TPU v7x, 32 devices: a whole 2x2x4 slice. The times are simulated.
32 devices in a mesh: tile: 4 (over y, core), orient: 8 (over z, x).
Axes of the slice: x: 2, y: 2, z: 4, core: 2. Of those that a mesh axis runs over, the one named last changes fastest.
Arguments:
- tile_spectra: bfloat16 [4, 2, 512, 512], P('tile', None, 'orient'), may hold values from -6 to 6
- template_spectra: bfloat16 [64, 2, 512, 512], P('orient', None, 'tile'), may hold values from -6 to 6
- peaks: int32 [4, 4, 2], P('tile'), may hold values from 0 to 511
- listed: int32 [4, 4, 48], P('tile'), may hold values from 0 to 63, as said below
Outputs:
- best: float32 [4, 4, 128, 128], P('tile')
- power: float32 [4, 4, 128, 128], P('tile')
Inputs may be any that keep to these rules, and one draw needn't show every extreme that they name: The 48 ids listed for one peak are distinct.
All inputs are finite; a program needn't handle non-finite values.
Results may differ from a plain program's by a relative error of at most 0.0026.
Values may be sent and summed in bfloat16 or wider, within the bound.
No kernel may reach another device: no remote copies, remote signals or barrier semaphores. Data moves between devices by JAX's collectives and lax.ppermute only.
A program may use at most 128 MiB of HBM per device.

v0:
```python
import math

import jax
import jax.numpy as jnp
from jax import lax
from jax.sharding import PartitionSpec as P

W = 128
LIST = 48


lowest_score = -1e30


def combined_all(shard, axis, combine):
    everything = jax.tree.map(lambda part: lax.all_gather(part, axis), shard)
    first = jax.tree.map(lambda part: part[0], everything)

    def lap(k, so_far):
        return combine(so_far, jax.tree.map(lambda part: part[k], everything))

    return lax.fori_loop(1, lax.axis_size(axis), lap, first)


def window_tables(peak_rows, size, width):
    offsets = jnp.arange(width, dtype=jnp.int32) - width // 2
    freqs = jnp.arange(size, dtype=jnp.int32)

    def tables_for(coords):
        position = (coords[:, None] + offsets[None, :]) % size
        phase = freqs[None, :, None] * position[:, None, :] % size
        angle = phase.astype(jnp.float32) * (2.0 * math.pi / size)
        return (jnp.cos(angle).astype(jnp.bfloat16), jnp.sin(angle).astype(jnp.bfloat16))

    cos_row, sin_row = tables_for(peak_rows[:, 0])
    cos_col, sin_col = tables_for(peak_rows[:, 1])
    upper = jnp.concatenate([cos_col, sin_col], axis=-1)
    lower = jnp.concatenate([-sin_col, cos_col], axis=-1)
    return (cos_row, sin_row, jnp.concatenate([upper, lower], axis=1))


def cross_spectrum(spectrum, template):
    image_re = spectrum[0].astype(jnp.float32)
    image_im = spectrum[1].astype(jnp.float32)
    tmpl_re = template[..., 0, :, :].astype(jnp.float32)
    tmpl_im = template[..., 1, :, :].astype(jnp.float32)
    mixed_re = image_re * tmpl_re + image_im * tmpl_im
    mixed_im = image_im * tmpl_re - image_re * tmpl_im
    return jnp.concatenate([mixed_re, mixed_im], axis=-1).astype(jnp.bfloat16)


def joint_reduce(first_pair, second_pair):
    return (jnp.maximum(first_pair[0], second_pair[0]), first_pair[1] + second_pair[1])


def reduce_orient(best_part, power_part):
    return combined_all((best_part, power_part), "orient", joint_reduce)


def local(tile_spectra, template_spectra, peaks, listed):
    size = tile_spectra.shape[3]
    width = W
    cos_row, sin_row, col_table = window_tables(peaks[0], size, width)
    listed_ids = listed[0]
    spectrum = lax.all_gather(tile_spectra, "orient", axis=2, tiled=True)[0]
    block_size = template_spectra.shape[0]
    mixed = cross_spectrum(spectrum, lax.all_gather(template_spectra, "tile", axis=2, tiled=True))
    partial_g = jnp.einsum(
        "jnk,pkw->pjnw", mixed, col_table, preferred_element_type=jnp.float32
    ).astype(jnp.bfloat16)
    update = jnp.einsum(
        "pna,pjnb->pjab", cos_row, partial_g[..., :width], preferred_element_type=jnp.float32
    )
    update = update - jnp.einsum(
        "pna,pjnb->pjab", sin_row, partial_g[..., width:], preferred_element_type=jnp.float32
    )
    scores = update / size
    global_ids = lax.axis_index("orient") * block_size + jnp.arange(block_size, dtype=jnp.int32)
    is_listed = jnp.any(listed_ids[:, :, None] == global_ids[None, None, :], axis=1)
    is_listed = is_listed[:, :, None, None]
    best_part = jnp.max(jnp.where(is_listed, scores, lowest_score), axis=1)
    power_part = jnp.sum(jnp.where(is_listed, scores * scores, 0.0), axis=1)
    best_all, power_all = reduce_orient(best_part, power_part)
    return (best_all[None], (power_all / LIST)[None])


def solution(mesh):
    placed = (
        P("tile", None, "orient", None),
        P("orient", None, "tile", None),
        P("tile", None, None),
        P("tile", None, None),
    )
    return jax.shard_map(
        local,
        mesh=mesh,
        in_specs=placed,
        out_specs=(P("tile", None, None, None), P("tile", None, None, None)),
        check_vma=False,
    )
```

profile of v0, /device:TPU:0, one launch (start us, length us, event | category | flops | bytes accessed | tf_op | source)
XLA Modules:
  0.0 261.0 jit_solution(14473625510305335943)
XLA Ops:
  7.2 0.0 all-gather.7.cloned.1.call-start
  7.2 0.7 all-gather.7.cloned.1.call-update
  7.9 0.0 all-gather.9.cloned.1.call-start
  8.0 3.1 %copy.14 = bf16[8,2,128,512]{3,2,0,1:T(8,128)(2,1)} copy(bf16[8,2,128,512]{3,2,1,0:T(8,128)(2,1)} %param.7) | data formatting | bytes 4194304 | tf_op args[1]
  11.1 0.0 all-gather.11.cloned.1.call-start
  11.2 0.2 compare_reduce_fusion
  11.5 0.1 add_select_fusion.4
  11.5 4.3 %fusion.39 = bf16[4,512,128]{1,2,0:T(8,128)(2,1)S(1)} fusion(s32[4,128]{1,0:T(4,128)S(1)} %get-tuple-element.160), kind=kLoop, calls=%fused_computation.60 | loop fusion | flops 4718592 | bytes 526336 | tf_op jit(solution)/shard_map/neg | solution.py:38
  15.8 5.6 %sine_convert_fusion.1 = (bf16[4,512,128]{1,2,0:T(8,128)(2,1)S(1)}, bf16[4,512,128]{1,2,0:T(8,128)(2,1)}) fusion(s32[4,128]{1,0:T(4,128)S(1)} %get-tuple-element.160), kind=kLoop, calls=%fused_computation.47 | loop fusion | flops 4194304 | bytes 1050624 | tf_op jit(solution)/shard_map/convert_element_type | solution.py:33
  21.4 31.8 %all-gather.7.cloned.1.call-done = bf16[1,2,512,512]{3,2,1,0:T(8,128)(2,1)} async-done(((bf16[1,2,64,512]{3,2,1,0:T(8,128)(2,1)}), bf16[1,2,512,512]{3,2,1,0:T(8,128)(2,1)}) %all-gather.7.cloned.1.call-update) | async-done | bytes 1048592 | tf_op jit(solution)/shard_map/all_gather | solution.py:65
  53.2 1.5 fusion.36
  54.7 57.1 %all-gather.9.cloned.1.call-done = bf16[8,2,512,512]{3,2,0,1:T(8,128)(2,1)} async-done(((bf16[8,2,128,512]{3,2,0,1:T(8,128)(2,1)}), bf16[8,2,512,512]{3,2,0,1:T(8,128)(2,1)}) %all-gather.9.cloned.1.call-update) | async-done | bytes 8388624 | tf_op jit(solution)/shard_map/all_gather | solution.py:67
  111.8 6.1 %fusion.1 = (bf16[8,512,512]{2,1,0:T(8,128)(2,1)S(1)}, bf16[8,512,512]{2,1,0:T(8,128)(2,1)}) fusion(f32[512,512]{1,0:T(8,128)S(1)} %get-tuple-element.154, f32[512,512]{1,0:T(8,128)S(1)} %get-tuple-element.153, bf16[8,2,512,512]{3,2,0,1:T(8,128)(2,1)} %all-gather.9.cloned.1.call-done), kind=kLoop, calls=%fused_computation.7 | loop fusion | flops 20971520 | bytes 18874368 | tf_op jit(solution)/shard_map/convert.4
  117.9 12.7 %convert_bitcast_fusion = bf16[4,8,512,256]{2,3,1,0:T(8,128)(2,1)} fusion(bf16[8,512,512]{2,1,0:T(8,128)(2,1)} %get-tuple-element.152, bf16[8,512,512]{2,1,0:T(8,128)(2,1)S(1)} %get-tuple-element.151, bf16[4,512,128]{1,2,0:T(8,128)(2,1)S(1)} %copy-done.1, bf16[4,512,128]{1,2,0:T(8,128)(2,1)S(1)} %fusion.39, bf16[4,512,128]{1,2,0:T(8,128)(2,1)S(1)} %get-tuple-element.155), kind=kOutput, calls=%fused_computation.14 | convolution fusion | flops 8619294720 | bytes 18350080 | tf_op jit(solution)/shard_map/jnk,pkw->pjnw/dot_general | solution.py:68
  130.7 7.2 %fusion.7 = f32[4,8,128,128]{3,2,1,0:T(8,128)S(1)} fusion(bf16[4,8,512,256]{2,3,1,0:T(8,128)(2,1)} %convert_bitcast_fusion, s32[4,128]{1,0:T(4,128)S(1)} %get-tuple-element.159), kind=kOutput, calls=%fused_computation.15 | convolution fusion | flops 540803072 | bytes 6293504 | tf_op jit(solution)/shard_map/pna,pjnb->pjab/dot_general | solution.py:74
  137.9 5.8 %select_reduce_fusion = (f32[4,128,128]{2,1,0:T(8,128)S(1)}, f32[4,128,128]{2,1,0:T(8,128)S(1)}) fusion(pred[4,8]{1,0:T(4,128)(4,1)S(1)} %compare_reduce_fusion, f32[4,8,128,128]{3,2,1,0:T(8,128)S(1)} %fusion.7, s32[4,128]{1,0:T(4,128)S(1)} %get-tuple-element.159, bf16[4,8,512,256]{2,3,1,0:T(8,128)(2,1)S(1)} %copy-done.4), kind=kOutput, calls=%fused_computation.28 | convolution fusion | flops 544342016 | bytes 6818304 | tf_op jit(solution)/shard_map/pna,pjnb->pjab/dot_general | solution.py:71
  143.7 0.8 copy.17
  144.6 0.0 all-gather.13.cloned.1.call-start
  144.6 0.8 copy.18
  145.5 48.5 %all-gather.11.cloned.1.call-done = f32[32,128,128]{2,1,0:T(8,128)} async-done(((f32[4,128,128]{2,1,0:T(8,128)}), f32[32,128,128]{2,1,0:T(8,128)}) %all-gather.11.cloned.1.call-update) | async-done | bytes 2097168 | tf_op jit(solution)/shard_map/all_gather | solution.py:16
  194.0 1.0 slice.50
  195.0 49.4 %all-gather.13.cloned.1.call-done = f32[32,128,128]{2,1,0:T(8,128)} async-done(((f32[4,128,128]{2,1,0:T(8,128)}), f32[32,128,128]{2,1,0:T(8,128)}) %all-gather.13.cloned.1.call-update) | async-done | bytes 2097168 | tf_op jit(solution)/shard_map/all_gather | solution.py:16
  244.4 1.0 slice.51
  245.3 8.4 %while.17 = (s32[]{:T(128)}, f32[4,128,128]{2,1,0:T(8,128)S(1)}, f32[4,128,128]{2,1,0:T(8,128)S(1)}, f32[8,4,128,128]{3,2,1,0:T(8,128)}, f32[8,4,128,128]{3,2,1,0:T(8,128)}, /*index=5*/s32[]{:T(128)}, s32[]{:T(128)}, s32[]{:T(128)}) while((s32[]{:T(128)}, f32[4,128,128]{2,1,0:T(8,128)S(1)}, f32[4,128,128]{2,1,0:T(8,128)S(1)}, ...), condition=%wide.region_4.5_spmd, body=%wide.region_3.4_spmd.sunk | while | flops 131077 | bytes 1572995 | solution.py:22
  245.4 1.2 bitcast_add_fusion.2
  246.5 1.2 bitcast_add_fusion.2
  247.7 1.2 bitcast_add_fusion.2
  248.9 1.2 bitcast_add_fusion.2
  250.1 1.2 bitcast_add_fusion.2
  251.3 1.2 bitcast_add_fusion.2
  252.5 1.2 bitcast_add_fusion.2
  253.7 0.8 multiply_bitcast_fusion
  (16 shorter events, 0.1 us)
Async XLA Ops:
  7.2 4.1 %copy-start.2 = (s32[1,4,48]{2,1,0:T(4,128)S(1)}, s32[1,4,48]{2,1,0:T(4,128)}, u32[]{:S(2)}) copy-start(s32[1,4,48]{2,1,0:T(4,128)} %param.9) | copy-start | bytes 2308
  7.2 4.3 %copy-start.3 = (s32[1,4,2]{1,2,0:T(2,128)S(1)}, s32[1,4,2]{1,2,0:T(2,128)}, u32[]{:S(2)}) copy-start(s32[1,4,2]{1,2,0:T(2,128)} %param.8) | copy-start | bytes 100
  7.2 46.0 %all-gather.7.cloned.1.call-start = ((), (), s32[]{:S(2)}) async-start(), calls=%async_computation | async-start | bytes 1179648 | tf_op jit(solution)/shard_map/all_gather | solution.py:65
  7.9 103.9 %all-gather.9.cloned.1.call-start = ((), (), s32[]{:S(2)}) async-start(), calls=%async_computation.1 | async-start | bytes 10485760 | tf_op jit(solution)/shard_map/all_gather | solution.py:67
  11.1 182.9 %all-gather.11.cloned.1.call-start = ((), (), s32[]{:S(2)}) async-start(), calls=%async_computation.2 | async-start | bytes 2359296 | tf_op jit(solution)/shard_map/all_gather | solution.py:16
  111.8 6.1 %copy-start.1 = (bf16[4,512,128]{1,2,0:T(8,128)(2,1)S(1)}, bf16[4,512,128]{1,2,0:T(8,128)(2,1)}, u32[]{:S(2)}) copy-start(bf16[4,512,128]{1,2,0:T(8,128)(2,1)} %get-tuple-element.156) | copy-start | bytes 1572868
  130.7 7.2 %copy-start.4 = (bf16[4,8,512,256]{2,3,1,0:T(8,128)(2,1)S(1)}, bf16[4,8,512,256]{2,3,1,0:T(8,128)(2,1)}, u32[]{:S(2)}) copy-start(bf16[4,8,512,256]{2,3,1,0:T(8,128)(2,1)} %convert_bitcast_fusion) | copy-start | bytes 25165828
  144.6 99.8 %all-gather.13.cloned.1.call-start = ((), (), s32[]{:S(2)}) async-start(), calls=%async_computation.3 | async-start | bytes 2359296 | tf_op jit(solution)/shard_map/all_gather | solution.py:16
  253.7 0.8 copy-start
Sparse Core Ops, SparseCore 0:
  10.2 42.9 all-gather.6
  54.7 57.0 all-gather.8
  144.7 49.2 all-gather.10
  196.6 47.7 all-gather.12
where the time goes:
time: 261 us
  waiting for transfers between devices  188 us (72%)
  other arithmetic  26.7 us (10%)
  matrix products  25.7 us (10%)
  between operations  13.9 us (5%)
  local copies, waits for them, and re-layouts  6.78 us (3%)
    all_gather x2, waiting for transfers between devices, combined_all(): everything = jax.tree.map(lambda part: lax.all_gather(part, axis), shard)  97.9 us
    all_gather x1, waiting for transfers between devices, local(): lax.all_gather(template_spectra, 'tile', axis=2, tiled=True)  57.1 us
    all_gather x1, waiting for transfers between devices, local(): spectrum = lax.all_gather(tile_spectra, 'orient', axis=2, tiled=True)[0]  31.8 us
    dot_general x1, matrix products, local(): jnp.einsum('jnk,pkw->pjnw', mixed, col_table, preferred_element_type=jnp....  12.7 us
    add x7, other arithmetic, joint_reduce(): first_pair[1] + second_pair[1]  8.2 us
    dot_general x1, matrix products, local(): jnp.einsum('pna,pjnb->pjab', sin_row, partial_g[..., width:], preferred_e...  7.18 us
    another operation x1, other arithmetic  6.12 us
    dot_general x1, matrix products, local(): jnp.einsum('pna,pjnb->pjab', cos_row, partial_g[..., :width], preferred_e...  5.83 us
  transfers between devices with their start and end apart: 4, of which 4 were waited for; matrix products, arithmetic and copies ran while one was open for 6% of the time, Pallas kernels for 0%

commit v1 on v0

v1 whole, which is shorter than its diff:
```python
import math

import jax
import jax.numpy as jnp
from jax import lax
from jax.sharding import Mesh
from jax.sharding import PartitionSpec as P

W = 128
LIST = 48


lowest_score = -1e30


def xor_pairs(n, k):
    return [(i, i ^ k) for i in range(n)]


def is_pow2(n):
    return n & (n - 1) == 0


def angle_tables(freqs, coords, size, width):
    offsets = jnp.arange(width, dtype=jnp.int32) - width // 2
    position = (coords[:, None] + offsets[None, :]) % size
    phase = freqs[None, :, None] * position[:, None, :] % size
    angle = phase.astype(jnp.float32) * (2.0 * math.pi / size)
    return (jnp.cos(angle).astype(jnp.bfloat16), jnp.sin(angle).astype(jnp.bfloat16))


def col_tables(peak_rows, size, width):
    freqs = jnp.arange(size, dtype=jnp.int32)
    cos_col, sin_col = angle_tables(freqs, peak_rows[:, 1], size, width)
    upper = jnp.concatenate([cos_col, sin_col], axis=-1)
    lower = jnp.concatenate([-sin_col, cos_col], axis=-1)
    return jnp.concatenate([upper, lower], axis=1)


def cross_spectrum(spectrum, template):
    image_re = spectrum[0].astype(jnp.float32)
    image_im = spectrum[1].astype(jnp.float32)
    tmpl_re = template[..., 0, :, :].astype(jnp.float32)
    tmpl_im = template[..., 1, :, :].astype(jnp.float32)
    mixed_re = image_re * tmpl_re + image_im * tmpl_im
    mixed_im = image_im * tmpl_re - image_re * tmpl_im
    return jnp.concatenate([mixed_re, mixed_im], axis=-1).astype(jnp.bfloat16)


def gather_rows(part, axis):
    n = lax.axis_size(axis)
    if not is_pow2(n):
        return lax.all_gather(part, axis)
    me = lax.axis_index(axis)
    blocks = part[None]
    k = n // 2
    while k >= 1:
        got = lax.ppermute(blocks, axis, xor_pairs(n, k))
        blocks = jnp.concatenate([blocks, got])
        k //= 2
    want = jnp.arange(n, dtype=jnp.int32) ^ me
    return blocks[order_of(want, n)]


def order_of(want, count):
    steps = int(math.log2(count))
    slot = jnp.zeros_like(want)
    for j in range(steps):
        k = count >> (j + 1)
        hit = (want & k) != 0
        slot = slot | jnp.where(hit, 1 << j, 0)
    return slot


def reduce_orient(best_part, power_part, axis):
    n = lax.axis_size(axis)
    if not is_pow2(n):
        best = lax.pmax(best_part, axis)
        power = lax.psum(power_part, axis)
        return best, power
    width = best_part.shape[-1]
    joined = jnp.stack([best_part.reshape(-1, width), power_part.reshape(-1, width)], axis=0)
    me = lax.axis_index(axis)
    cur = joined
    k = 1
    while k < n:
        half = cur.shape[1] // 2
        bit = (me // k) % 2
        keep = lax.dynamic_slice_in_dim(cur, bit * half, half, axis=1)
        send = lax.dynamic_slice_in_dim(cur, (1 - bit) * half, half, axis=1)
        got = lax.ppermute(send, axis, xor_pairs(n, k))
        cur = jnp.stack([jnp.maximum(keep[0], got[0]), keep[1] + got[1]])
        k *= 2
    k = n // 2
    while k >= 1:
        got = lax.ppermute(cur, axis, xor_pairs(n, k))
        bit = (me // k) % 2
        cur = jnp.where(bit == 1, jnp.concatenate([got, cur], axis=1), jnp.concatenate([cur, got], axis=1))
        k //= 2
    best = cur[0].reshape(best_part.shape)
    power = cur[1].reshape(power_part.shape)
    return best, power


def local(tile_spectra, template_spectra, peaks, listed):
    size = tile_spectra.shape[3]
    width = W
    chips = lax.axis_size("tchip")
    cores = lax.axis_size("tcore")
    rows_t = template_spectra.shape[2]
    tp = lax.all_gather(template_spectra, "tchip", axis=0)
    tp = lax.all_gather(tp, "tcore", axis=0)
    block_size = tp.shape[2]
    tp = jnp.moveaxis(tp, 2, 0)
    tp = jnp.moveaxis(tp, 3, 1)
    tmpl = tp.reshape(block_size, 2, size, size)
    spec = gather_rows(tile_spectra[0], "orient")
    spec = jnp.moveaxis(spec, 0, 1).reshape(2, size, size)
    spec = spec.reshape(2, chips, cores, rows_t, size)
    spec = jnp.swapaxes(spec, 1, 2).reshape(2, size, size)
    core_i = jnp.arange(cores, dtype=jnp.int32)[:, None, None]
    chip_i = jnp.arange(chips, dtype=jnp.int32)[None, :, None]
    r_i = jnp.arange(rows_t, dtype=jnp.int32)[None, None, :]
    freqs = ((chip_i * cores + core_i) * rows_t + r_i).reshape(size)
    cos_row, sin_row = angle_tables(freqs, peaks[0][:, 0], size, width)
    col_table = col_tables(peaks[0], size, width)
    listed_ids = listed[0]
    mixed = cross_spectrum(spec, tmpl)
    partial_g = jnp.einsum(
        "jnk,pkw->pjnw", mixed, col_table, preferred_element_type=jnp.float32
    ).astype(jnp.bfloat16)
    update = jnp.einsum(
        "pna,pjnb->pjab", cos_row, partial_g[..., :width], preferred_element_type=jnp.float32
    )
    update = update - jnp.einsum(
        "pna,pjnb->pjab", sin_row, partial_g[..., width:], preferred_element_type=jnp.float32
    )
    scores = update / size
    global_ids = lax.axis_index("orient") * block_size + jnp.arange(block_size, dtype=jnp.int32)
    is_listed = jnp.any(listed_ids[:, :, None] == global_ids[None, None, :], axis=1)
    is_listed = is_listed[:, :, None, None]
    best_part = jnp.max(jnp.where(is_listed, scores, lowest_score), axis=1)
    power_part = jnp.sum(jnp.where(is_listed, scores * scores, 0.0), axis=1)
    best_all, power_all = reduce_orient(best_part, power_part, "orient")
    return (best_all[None], (power_all / LIST)[None])


def solution(mesh):
    tiles = mesh.shape["tile"]
    orients = mesh.shape["orient"]
    split = Mesh(mesh.devices.reshape(tiles // 2, 2, orients), ("tchip", "tcore", "orient"))
    tile = ("tchip", "tcore")
    placed = (
        P(tile, None, "orient", None),
        P("orient", None, tile, None),
        P(tile, None, None),
        P(tile, None, None),
    )
    return jax.shard_map(
        local,
        mesh=split,
        in_specs=placed,
        out_specs=(P(tile, None, None, None), P(tile, None, None, None)),
        check_vma=False,
    )
```

time: 261 us -> 186 us (0.71)
  waiting for transfers between devices: 188 us -> 102 us
  starting transfers between devices: 0.16 us -> 16.4 us
  other arithmetic: 26.7 us -> 18.9 us
    all_gather x4 -> x2, waiting for transfers between devices: 187 us -> 61.1 us  [the longest x1 61.1 us: local(): tp = lax.all_gather(template_spectra, 'tchip', axis=0)]
    ppermute x0 -> x9, waiting for transfers between devices: none -> 40 us  [the longest x3 14.4 us: reduce_orient(): got = lax.ppermute(cur, axis, xor_pairs(n, k))]
    ppermute x0 -> x9, starting transfers between devices: none -> 16.3 us  [the longest x3 8.86 us: reduce_orient(): got = lax.ppermute(send, axis, xor_pairs(n, k))]
    add x7 -> x3, other arithmetic: 8.2 us -> 0.12 us  [the longest x1 0.07 us: local(): freqs = ((chip_i * cores + core_i) * rows_t + r_i).reshape(size)]
    all_gather x0 -> x1, local copies, waits for them, and re-layouts: none -> 7.67 us  [local(): tp = lax.all_gather(tp, 'tcore', axis=0)]
    unnamed x11 -> x10, local copies, waits for them, and re-layouts: 3.17 us -> 0.02 us
    another operation x1 -> x5, other arithmetic: 6.12 us -> 6.25 us
  transfers between devices with their start and end apart: 4 -> 11, of which waited for: 4 -> 10; matrix products, arithmetic and copies ran while one was open for 6% -> 7% of each run, Pallas kernels for 0% -> 0%
where the time goes in v1:
time: 186 us
  waiting for transfers between devices  102 us (55%)
  matrix products  25.8 us (14%)
  other arithmetic  18.9 us (10%)
  starting transfers between devices  16.4 us (9%)
  between operations  14.3 us (8%)
  local copies, waits for them, and re-layouts  8.79 us (5%)
    all_gather x1, waiting for transfers between devices, local(): tp = lax.all_gather(template_spectra, 'tchip', axis=0)  61.1 us
    ppermute x3, waiting for transfers between devices, reduce_orient(): got = lax.ppermute(cur, axis, xor_pairs(n, k))  14.4 us
    ppermute x3, waiting for transfers between devices, gather_rows(): got = lax.ppermute(blocks, axis, xor_pairs(n, k))  13.7 us
    dot_general x1, matrix products, local(): jnp.einsum('jnk,pkw->pjnw', mixed, col_table, preferred_element_type=jnp....  12.8 us
    ppermute x3, waiting for transfers between devices, reduce_orient(): got = lax.ppermute(send, axis, xor_pairs(n, k))  11.9 us
    ppermute x3, starting transfers between devices, reduce_orient(): got = lax.ppermute(send, axis, xor_pairs(n, k))  8.86 us
    all_gather x1, local copies, waits for them, and re-layouts, local(): tp = lax.all_gather(tp, 'tcore', axis=0)  7.67 us
    dot_general x1, matrix products, local(): jnp.einsum('pna,pjnb->pjab', sin_row, partial_g[..., width:], preferred_e...  7.17 us
  transfers between devices with their start and end apart: 11, of which 10 were waited for; matrix products, arithmetic and copies ran while one was open for 7% of the time, Pallas kernels for 0%

profile of v1, /device:TPU:0, one launch (start us, length us, event | category | flops | bytes accessed | tf_op | source)
XLA Modules:
  0.0 185.9 jit_solution(10141722668693653279)
XLA Ops:
  7.2 0.7 all-gather.5.cloned.1.call-update
  8.0 61.1 %all-gather.5.cloned.1.call-done = bf16[16,2,128,512]{3,2,1,0:T(8,128)(2,1)} async-done(((bf16[8,2,128,512]{3,2,1,0:T(8,128)(2,1)}), bf16[16,2,128,512]{3,2,1,0:T(8,128)(2,1)}) %all-gather.5.cloned.1.call-update) | async-done | bytes 4194320 | tf_op jit(solution)/shard_map/all_gather | solution.py:111
  69.1 2.5 %collective-permute-start = (bf16[1,2,64,512]{3,2,1,0:T(8,128)(2,1)S(1)}, bf16[1,2,64,512]{3,2,1,0:T(8,128)(2,1)S(1)}, u32[]{:S(2)}, u32[]{:S(2)}) collective-permute-start(bf16[1,2,64,512]{3,2,1,0:T(8,128)(2,1)S(1)} %copy-done), channel_id=1, source_target_pairs={{0,4},{1,5},{2,6},{3,7},{4,0},{5,1},{6,2},{7,3},{8,12},{9,13},{10,... | collective-permute-start | bytes 393224 | tf_op jit(solution)/shard_map/ppermute | solution.py:58
  71.7 0.2 compare_reduce_fusion
  71.9 6.2 %collective-permute-done = bf16[1,2,64,512]{3,2,1,0:T(8,128)(2,1)S(1)} collective-permute-done((bf16[1,2,64,512]{3,2,1,0:T(8,128)(2,1)S(1)}, bf16[1,2,64,512]{3,2,1,0:T(8,128)(2,1)S(1)}, u32[]{:S(2)}, u32[]{:S(2)}) %collective-permute-start) | collective-permute-done | bytes 131104 | tf_op jit(solution)/shard_map/ppermute | solution.py:58
  78.1 0.6 collective-permute-start.1
  78.8 6.7 %collective-permute-done.1 = bf16[2,2,64,512]{3,2,1,0:T(8,128)(2,1)S(1)} collective-permute-done((bf16[2,2,64,512]{3,2,1,0:T(8,128)(2,1)S(1)}, bf16[2,2,64,512]{3,2,1,0:T(8,128)(2,1)S(1)}, u32[]{:S(2)}, u32[]{:S(2)}) %collective-permute-start.1) | collective-permute-done | bytes 262176 | tf_op jit(solution)/shard_map/ppermute | solution.py:58
  85.5 1.5 collective-permute-start.2
  87.1 4.3 %fusion.36 = bf16[4,512,128]{1,2,0:T(8,128)(2,1)S(1)} fusion(s32[4,128]{1,0:T(4,128)S(1)} %get-tuple-element.27), kind=kLoop, calls=%fused_computation.75 | loop fusion | flops 4718592 | bytes 526336 | tf_op jit(solution)/shard_map/neg | solution.py:36
  91.3 5.6 %sine_convert_fusion.1 = (bf16[4,512,128]{1,2,0:T(8,128)(2,1)S(1)}, bf16[4,512,128]{1,2,0:T(8,128)(2,1)}) fusion(s32[4,128]{1,0:T(4,128)S(1)} %get-tuple-element.27), kind=kLoop, calls=%fused_computation.47 | loop fusion | flops 4194304 | bytes 1050624 | tf_op jit(solution)/shard_map/convert_element_type | solution.py:29
  96.9 0.8 collective-permute-done.2
  97.7 1.1 pad_maximum_fusion
  98.8 0.6 gather_fusion
  99.6 0.3 slice_convert_fusion.1
  100.0 7.7 %copy.34 = bf16[2,2,8,2,128,512]{5,4,1,0,2,3:T(8,128)(2,1)} copy(bf16[2,2,8,2,128,512]{5,4,3,2,1,0:T(8,128)(2,1)} %bitcast.65) | data formatting | bytes 16777216 | tf_op jit(solution)/shard_map/all_gather | solution.py:112
  107.7 6.2 %fusion.1 = (bf16[8,512,512]{2,1,0:T(8,128)(2,1)S(1)}, bf16[8,512,512]{2,1,0:T(8,128)(2,1)}) fusion(f32[512,512]{1,0:T(8,128)S(1)} %bitcast.66, f32[512,512]{1,0:T(8,128)S(1)} %bitcast.67, bf16[8,2,512,512]{3,2,0,1:T(8,128)(2,1)} %bitcast.64), kind=kLoop, calls=%fused_computation.6 | loop fusion | flops 20971520 | bytes 18874368 | tf_op jit(solution)/shard_map/convert.4
  113.8 12.8 %convert_bitcast_fusion = bf16[4,8,512,256]{2,3,1,0:T(8,128)(2,1)} fusion(bf16[8,512,512]{2,1,0:T(8,128)(2,1)} %get-tuple-element.5, bf16[8,512,512]{2,1,0:T(8,128)(2,1)S(1)} %get-tuple-element.4, bf16[4,512,128]{1,2,0:T(8,128)(2,1)S(1)} %copy-done.1, bf16[4,512,128]{1,2,0:T(8,128)(2,1)S(1)} %fusion.36, bf16[4,512,128]{1,2,0:T(8,128)(2,1)S(1)} %get-tuple-element.22), kind=kOutput, calls=%fused_computation.13 | convolution fusion | flops 8619294720 | bytes 18350080 | tf_op jit(solution)/shard_map/jnk,pkw->pjnw/dot_general | solution.py:129
  126.6 7.2 %fusion.7 = f32[4,8,128,128]{3,2,1,0:T(8,128)S(1)} fusion(bf16[4,8,512,256]{2,3,1,0:T(8,128)(2,1)} %convert_bitcast_fusion, s32[4,128]{1,0:T(4,128)S(1)} %get-tuple-element.26, s32[512]{0:T(512)S(1)} %bitcast.78), kind=kOutput, calls=%fused_computation.14 | convolution fusion | flops 540803072 | bytes 6295552 | tf_op jit(solution)/shard_map/pna,pjnb->pjab/dot_general | solution.py:135
  133.8 5.8 %select_reduce_fusion = (f32[4,128,128]{2,1,0:T(8,128)S(1)}, f32[4,128,128]{2,1,0:T(8,128)S(1)}) fusion(pred[4,8]{1,0:T(4,128)(4,1)S(1)} %compare_reduce_fusion, f32[4,8,128,128]{3,2,1,0:T(8,128)S(1)} %fusion.7, s32[4,128]{1,0:T(4,128)S(1)} %get-tuple-element.26, s32[512]{0:T(512)S(1)} %bitcast.79, bf16[4,8,512,256]{2,3,1,0:T(8,128)(2,1)S(1)} %copy-done.4), kind=kOutput, calls=%fused_computation.27 | convolution fusion | flops 544342016 | bytes 6820352 | tf_op jit(solution)/shard_map/pna,pjnb->pjab/dot_general | solution.py:132
  139.6 0.1 copy.38
  140.0 1.5 collective-permute-start.3
  141.5 4.9 %collective-permute-done.3 = f32[2,256,128]{2,1,0:T(8,128)S(1)} collective-permute-done((f32[2,256,128]{2,1,0:T(8,128)S(1)}, f32[2,256,128]{2,1,0:T(8,128)S(1)}, u32[]{:S(2)}, u32[]{:S(2)}) %collective-permute-start.3) | collective-permute-done | bytes 262176 | tf_op jit(solution)/shard_map/ppermute | solution.py:91
  146.5 2.6 %collective-permute-start.4 = (f32[2,128,128]{2,1,0:T(8,128)S(1)}, f32[2,128,128]{2,1,0:T(8,128)S(1)}, u32[]{:S(2)}, u32[]{:S(2)}) collective-permute-start(f32[2,128,128]{2,1,0:T(8,128)S(1)} %get-tuple-element.17), channel_id=1, source_target_pairs={{0,2},{1,3},{2,0},{3,1},{4,6},{5,7},{6,4},{7,5},{8,10},{9,11},{10,... | collective-permute-start | bytes 393224 | tf_op jit(solution)/shard_map/ppermute | solution.py:91
  149.1 2.9 %collective-permute-done.4 = f32[2,128,128]{2,1,0:T(8,128)S(1)} collective-permute-done((f32[2,128,128]{2,1,0:T(8,128)S(1)}, f32[2,128,128]{2,1,0:T(8,128)S(1)}, u32[]{:S(2)}, u32[]{:S(2)}) %collective-permute-start.4) | collective-permute-done | bytes 131104 | tf_op jit(solution)/shard_map/ppermute | solution.py:91
  152.1 4.7 %collective-permute-start.5 = (f32[2,64,128]{2,1,0:T(8,128)S(1)}, f32[2,64,128]{2,1,0:T(8,128)S(1)}, u32[]{:S(2)}, u32[]{:S(2)}) collective-permute-start(f32[2,64,128]{2,1,0:T(8,128)S(1)} %get-tuple-element.21), channel_id=1, source_target_pairs={{0,4},{1,5},{2,6},{3,7},{4,0},{5,1},{6,2},{7,3},{8,12},{9,13},{10,... | collective-permute-start | bytes 196616 | tf_op jit(solution)/shard_map/ppermute | solution.py:91
  156.8 4.1 %collective-permute-done.5 = f32[2,64,128]{2,1,0:T(8,128)S(1)} collective-permute-done((f32[2,64,128]{2,1,0:T(8,128)S(1)}, f32[2,64,128]{2,1,0:T(8,128)S(1)}, u32[]{:S(2)}, u32[]{:S(2)}) %collective-permute-start.5) | collective-permute-done | bytes 65568 | tf_op jit(solution)/shard_map/ppermute | solution.py:91
  160.9 1.2 collective-permute-start.6
  162.1 4.6 %collective-permute-done.6 = f32[2,64,128]{2,1,0:T(8,128)S(1)} collective-permute-done((f32[2,64,128]{2,1,0:T(8,128)S(1)}, f32[2,64,128]{2,1,0:T(8,128)S(1)}, u32[]{:S(2)}, u32[]{:S(2)}) %collective-permute-start.6) | collective-permute-done | bytes 65568 | tf_op jit(solution)/shard_map/ppermute | solution.py:96
  166.8 4.9 %collective-permute-done.7 = f32[2,128,128]{2,1,0:T(8,128)S(1)} collective-permute-done((f32[2,128,128]{2,1,0:T(8,128)S(1)}, f32[2,128,128]{2,1,0:T(8,128)S(1)}, u32[]{:S(2)}, u32[]{:S(2)}) %collective-permute-start.7) | collective-permute-done | bytes 131104 | tf_op jit(solution)/shard_map/ppermute | solution.py:96
  171.8 1.5 collective-permute-start.8
  173.3 4.9 %collective-permute-done.8 = f32[2,256,128]{2,1,0:T(8,128)S(1)} collective-permute-done((f32[2,256,128]{2,1,0:T(8,128)S(1)}, f32[2,256,128]{2,1,0:T(8,128)S(1)}, u32[]{:S(2)}, u32[]{:S(2)}) %collective-permute-start.8) | collective-permute-done | bytes 262176 | tf_op jit(solution)/shard_map/ppermute | solution.py:96
  178.2 0.8 slice_multiply_fusion
  (40 shorter events, 1.0 us)
Async XLA Ops:
  7.2 61.9 %copy-start = (bf16[1,2,64,512]{3,2,1,0:T(8,128)(2,1)S(1)}, bf16[1,2,64,512]{3,2,1,0:T(8,128)(2,1)}, u32[]{:S(2)}) copy-start(bf16[1,2,64,512]{3,2,1,0:T(8,128)(2,1)} %param.4) | copy-start | bytes 393220
  7.2 64.4 %copy-start.3 = (s32[1,4,2]{1,2,0:T(2,128)S(1)}, s32[1,4,2]{1,2,0:T(2,128)}, u32[]{:S(2)}) copy-start(s32[1,4,2]{1,2,0:T(2,128)} %param.6) | copy-start | bytes 100
  7.2 64.5 %copy-start.2 = (s32[1,4,48]{2,1,0:T(4,128)S(1)}, s32[1,4,48]{2,1,0:T(4,128)}, u32[]{:S(2)}) copy-start(s32[1,4,48]{2,1,0:T(4,128)} %param.7) | copy-start | bytes 2308
  7.2 61.9 %all-gather.5.cloned.1.call-start = ((), (), s32[]{:S(2)}) async-start(), calls=%async_computation | async-start | bytes 6291456 | tf_op jit(solution)/shard_map/all_gather | solution.py:111
  7.9 92.1 %all-gather.7.cloned.1.call-start = ((), (), s32[]{:S(2)}) async-start(), calls=%async_computation.1 | async-start | bytes 12582912 | tf_op jit(solution)/shard_map/all_gather | solution.py:112
  69.1 9.0 %collective-permute-start = (bf16[1,2,64,512]{3,2,1,0:T(8,128)(2,1)S(1)}, bf16[1,2,64,512]{3,2,1,0:T(8,128)(2,1)S(1)}, u32[]{:S(2)}, u32[]{:S(2)}) collective-permute-start(bf16[1,2,64,512]{3,2,1,0:T(8,128)(2,1)S(1)} %copy-done), channel_id=1, source_target_pairs={{0,4},{1,5},{2,6},{3,7},{4,0},{5,1},{6,2},{7,3},{8,12},{9,13},{10,... | collective-permute-start | bytes 393224 | tf_op jit(solution)/shard_map/ppermute | solution.py:58
  78.1 7.3 %collective-permute-start.1 = (bf16[2,2,64,512]{3,2,1,0:T(8,128)(2,1)S(1)}, bf16[2,2,64,512]{3,2,1,0:T(8,128)(2,1)S(1)}, u32[]{:S(2)}, u32[]{:S(2)}) collective-permute-start(bf16[2,2,64,512]{3,2,1,0:T(8,128)(2,1)S(1)} %pad_maximum_fusion.2), channel_id=1, source_target_pairs={{0,2},{1,3},{2,0},{3,1},{4,6},{5,7},{6,4},{7,5},{8,10},{9,11},{10,... | collective-permute-start | bytes 786440 | tf_op jit(solution)/shard_map/ppermute | solution.py:58
  85.5 12.2 %collective-permute-start.2 = (bf16[4,2,64,512]{3,2,1,0:T(8,128)(2,1)S(1)}, bf16[4,2,64,512]{3,2,1,0:T(8,128)(2,1)}, u32[]{:S(2)}, u32[]{:S(2)}) collective-permute-start(bf16[4,2,64,512]{3,2,1,0:T(8,128)(2,1)S(1)} %pad_maximum_fusion.1), channel_id=1, source_target_pairs={{0,1},{1,0},{2,3},{3,2},{4,5},{5,4},{6,7},{7,6},{8,9},{9,8},{10,11... | collective-permute-start | bytes 1572872 | tf_op jit(solution)/shard_map/ppermute | solution.py:58
  107.7 6.2 %copy-start.1 = (bf16[4,512,128]{1,2,0:T(8,128)(2,1)S(1)}, bf16[4,512,128]{1,2,0:T(8,128)(2,1)}, u32[]{:S(2)}) copy-start(bf16[4,512,128]{1,2,0:T(8,128)(2,1)} %get-tuple-element.23) | copy-start | bytes 1572868
  126.6 7.2 %copy-start.4 = (bf16[4,8,512,256]{2,3,1,0:T(8,128)(2,1)S(1)}, bf16[4,8,512,256]{2,3,1,0:T(8,128)(2,1)}, u32[]{:S(2)}) copy-start(bf16[4,8,512,256]{2,3,1,0:T(8,128)(2,1)} %convert_bitcast_fusion) | copy-start | bytes 25165828
  140.0 6.4 %collective-permute-start.3 = (f32[2,256,128]{2,1,0:T(8,128)S(1)}, f32[2,256,128]{2,1,0:T(8,128)S(1)}, u32[]{:S(2)}, u32[]{:S(2)}) collective-permute-start(f32[2,256,128]{2,1,0:T(8,128)S(1)} %get-tuple-element.13), channel_id=1, source_target_pairs={{0,1},{1,0},{2,3},{3,2},{4,5},{5,4},{6,7},{7,6},{8,9},{9,8},{10,11... | collective-permute-start | bytes 786440 | tf_op jit(solution)/shard_map/ppermute | solution.py:91
  146.5 5.6 %collective-permute-start.4 = (f32[2,128,128]{2,1,0:T(8,128)S(1)}, f32[2,128,128]{2,1,0:T(8,128)S(1)}, u32[]{:S(2)}, u32[]{:S(2)}) collective-permute-start(f32[2,128,128]{2,1,0:T(8,128)S(1)} %get-tuple-element.17), channel_id=1, source_target_pairs={{0,2},{1,3},{2,0},{3,1},{4,6},{5,7},{6,4},{7,5},{8,10},{9,11},{10,... | collective-permute-start | bytes 393224 | tf_op jit(solution)/shard_map/ppermute | solution.py:91
  152.1 8.8 %collective-permute-start.5 = (f32[2,64,128]{2,1,0:T(8,128)S(1)}, f32[2,64,128]{2,1,0:T(8,128)S(1)}, u32[]{:S(2)}, u32[]{:S(2)}) collective-permute-start(f32[2,64,128]{2,1,0:T(8,128)S(1)} %get-tuple-element.21), channel_id=1, source_target_pairs={{0,4},{1,5},{2,6},{3,7},{4,0},{5,1},{6,2},{7,3},{8,12},{9,13},{10,... | collective-permute-start | bytes 196616 | tf_op jit(solution)/shard_map/ppermute | solution.py:91
  160.9 5.8 %collective-permute-start.6 = (f32[2,64,128]{2,1,0:T(8,128)S(1)}, f32[2,64,128]{2,1,0:T(8,128)S(1)}, u32[]{:S(2)}, u32[]{:S(2)}) collective-permute-start(f32[2,64,128]{2,1,0:T(8,128)S(1)} %pad_maximum_fusion.3), channel_id=1, source_target_pairs={{0,4},{1,5},{2,6},{3,7},{4,0},{5,1},{6,2},{7,3},{8,12},{9,13},{10,... | collective-permute-start | bytes 196616 | tf_op jit(solution)/shard_map/ppermute | solution.py:96
  166.7 5.0 %collective-permute-start.7 = (f32[2,128,128]{2,1,0:T(8,128)S(1)}, f32[2,128,128]{2,1,0:T(8,128)S(1)}, u32[]{:S(2)}, u32[]{:S(2)}) collective-permute-start(f32[2,128,128]{2,1,0:T(8,128)S(1)} %maximum_select_fusion.2), channel_id=1, source_target_pairs={{0,2},{1,3},{2,0},{3,1},{4,6},{5,7},{6,4},{7,5},{8,10},{9,11},{10,... | collective-permute-start | bytes 393224 | tf_op jit(solution)/shard_map/ppermute | solution.py:96
  171.8 6.4 %collective-permute-start.8 = (f32[2,256,128]{2,1,0:T(8,128)S(1)}, f32[2,256,128]{2,1,0:T(8,128)S(1)}, u32[]{:S(2)}, u32[]{:S(2)}) collective-permute-start(f32[2,256,128]{2,1,0:T(8,128)S(1)} %maximum_select_fusion.1), channel_id=1, source_target_pairs={{0,1},{1,0},{2,3},{3,2},{4,5},{5,4},{6,7},{7,6},{8,9},{9,8},{10,11... | collective-permute-start | bytes 786440 | tf_op jit(solution)/shard_map/ppermute | solution.py:96
Sparse Core Ops, SparseCore 0:
  9.6 59.4 all-gather.4
  70.6 19.8 all-gather.6

commit v2 on v1

v2 whole, which is shorter than its diff:
```python
import functools
import math

import jax
import jax.numpy as jnp
from jax import lax
from jax.experimental import pallas as pl
from jax.experimental.pallas import tpu as pltpu
from jax.sharding import PartitionSpec as P

W = 128
LIST = 48


lowest_score = -1e30


def xor_pairs(n, k):
    return [(i, i ^ k) for i in range(n)]


def is_pow2(n):
    return n & (n - 1) == 0


def angle_tables(freqs, coords, size, width):
    offsets = jnp.arange(width, dtype=jnp.int32) - width // 2
    position = (coords[:, None] + offsets[None, :]) % size
    phase = freqs[None, :, None] * position[:, None, :] % size
    angle = phase.astype(jnp.float32) * (2.0 * math.pi / size)
    return (jnp.cos(angle).astype(jnp.bfloat16), jnp.sin(angle).astype(jnp.bfloat16))


def col_tables(peak_rows, size, width):
    freqs = jnp.arange(size, dtype=jnp.int32)
    cos_col, sin_col = angle_tables(freqs, peak_rows[:, 1], size, width)
    upper = jnp.concatenate([cos_col, sin_col], axis=-1)
    lower = jnp.concatenate([-sin_col, cos_col], axis=-1)
    return jnp.concatenate([upper, lower], axis=1)


def gather_rows(part, axis):
    n = lax.axis_size(axis)
    if not is_pow2(n):
        return lax.all_gather(part, axis)
    me = lax.axis_index(axis)
    blocks = part[None]
    k = n // 2
    while k >= 1:
        got = lax.ppermute(blocks, axis, xor_pairs(n, k))
        blocks = jnp.concatenate([blocks, got])
        k //= 2
    want = jnp.arange(n, dtype=jnp.int32) ^ me
    return blocks[order_of(want, n)]


def order_of(want, count):
    steps = int(math.log2(count))
    slot = jnp.zeros_like(want)
    for j in range(steps):
        k = count >> (j + 1)
        hit = (want & k) != 0
        slot = slot | jnp.where(hit, 1 << j, 0)
    return slot


def reduce_orient(best_part, power_part, axis):
    n = lax.axis_size(axis)
    if not is_pow2(n):
        best = lax.pmax(best_part, axis)
        power = lax.psum(power_part, axis)
        return best, power
    width = best_part.shape[-1]
    joined = jnp.stack([best_part.reshape(-1, width), power_part.reshape(-1, width)], axis=0)
    me = lax.axis_index(axis)
    cur = joined
    k = 1
    while k < n:
        half = cur.shape[1] // 2
        bit = (me // k) % 2
        keep = lax.dynamic_slice_in_dim(cur, bit * half, half, axis=1)
        send = lax.dynamic_slice_in_dim(cur, (1 - bit) * half, half, axis=1)
        got = lax.ppermute(send, axis, xor_pairs(n, k))
        cur = jnp.stack([jnp.maximum(keep[0], got[0]), keep[1] + got[1]])
        k *= 2
    k = n // 2
    while k >= 1:
        got = lax.ppermute(cur, axis, xor_pairs(n, k))
        bit = (me // k) % 2
        cur = jnp.where(bit == 1, jnp.concatenate([got, cur], axis=1), jnp.concatenate([cur, got], axis=1))
        k //= 2
    best = cur[0].reshape(best_part.shape)
    power = cur[1].reshape(power_part.shape)
    return best, power


def match_kernel(blocks, size, width, rows_t, tiles, peaks_n, l_ref, tm_ref, sp_ref, ct_ref, cr_ref, sr_ref, best_ref, pow_ref, m_ref):
    j = pl.program_id(0)

    @pl.when(j == 0)
    def _():
        best_ref[...] = jnp.full(best_ref.shape, lowest_score, jnp.float32)
        pow_ref[...] = jnp.zeros(pow_ref.shape, jnp.float32)

    for t in range(tiles):
        rows = pl.ds(t * rows_t, rows_t)
        image_re = sp_ref[0, rows, :].astype(jnp.float32)
        image_im = sp_ref[1, rows, :].astype(jnp.float32)
        tmpl_re = tm_ref[t, 0, 0].astype(jnp.float32)
        tmpl_im = tm_ref[t, 0, 1].astype(jnp.float32)
        m_ref[rows, pl.ds(0, size)] = (image_re * tmpl_re + image_im * tmpl_im).astype(jnp.bfloat16)
        m_ref[rows, pl.ds(size, size)] = (image_im * tmpl_re - image_re * tmpl_im).astype(jnp.bfloat16)

    for p in range(peaks_n):
        @pl.when(l_ref[p * blocks + j] > 0)
        def _():
            g = jnp.dot(m_ref[...], ct_ref[p], preferred_element_type=jnp.float32).astype(jnp.bfloat16)
            score = jnp.dot(cr_ref[p], g[:, :width], preferred_element_type=jnp.float32)
            score = score - jnp.dot(sr_ref[p], g[:, width:], preferred_element_type=jnp.float32)
            score = score / size
            best_ref[p] = jnp.maximum(best_ref[p], score)
            pow_ref[p] = pow_ref[p] + score * score


def match(flags, tmpl, spec, col_table, cos_t, sin_t):
    tiles, blocks, _, rows_t, size = tmpl.shape
    peaks_n, width = cos_t.shape[0], cos_t.shape[1]
    kernel = functools.partial(match_kernel, blocks, size, width, rows_t, tiles, peaks_n)
    flops = blocks * peaks_n * (2 * size * 2 * size * 2 * width + 2 * 2 * width * size * width)
    cost = pl.CostEstimate(flops=flops, transcendentals=0, bytes_accessed=tmpl.size * 2 + spec.size * 2 + col_table.size * 2)
    out = jax.ShapeDtypeStruct((peaks_n, width, width), jnp.float32)
    return pl.pallas_call(
        kernel,
        grid_spec=pltpu.PrefetchScalarGridSpec(
            num_scalar_prefetch=1,
            grid=(blocks,),
            in_specs=[
                pl.BlockSpec((tiles, 1, 2, rows_t, size), lambda j, l: (0, j, 0, 0, 0)),
                pl.BlockSpec((2, size, size), lambda j, l: (0, 0, 0)),
                pl.BlockSpec(col_table.shape, lambda j, l: (0, 0, 0)),
                pl.BlockSpec(cos_t.shape, lambda j, l: (0, 0, 0)),
                pl.BlockSpec(sin_t.shape, lambda j, l: (0, 0, 0)),
            ],
            out_specs=[
                pl.BlockSpec((peaks_n, width, width), lambda j, l: (0, 0, 0)),
                pl.BlockSpec((peaks_n, width, width), lambda j, l: (0, 0, 0)),
            ],
            scratch_shapes=[pltpu.VMEM((size, 2 * size), jnp.bfloat16)],
        ),
        out_shape=[out, out],
        compiler_params=pltpu.CompilerParams(dimension_semantics=("arbitrary",)),
        cost_estimate=cost,
    )(flags, tmpl, spec, col_table, cos_t, sin_t)


def local(tile_spectra, template_spectra, peaks, listed):
    size = tile_spectra.shape[3]
    width = W
    tmpl = lax.all_gather(template_spectra, "tile", axis=0)
    block_size = tmpl.shape[1]
    spec = gather_rows(tile_spectra[0], "orient")
    spec = jnp.moveaxis(spec, 0, 1).reshape(2, size, size)
    freqs = jnp.arange(size, dtype=jnp.int32)
    cos_row, sin_row = angle_tables(freqs, peaks[0][:, 0], size, width)
    cos_t = jnp.swapaxes(cos_row, 1, 2)
    sin_t = jnp.swapaxes(sin_row, 1, 2)
    col_table = col_tables(peaks[0], size, width)
    listed_ids = listed[0]
    global_ids = lax.axis_index("orient") * block_size + jnp.arange(block_size, dtype=jnp.int32)
    is_listed = jnp.any(listed_ids[:, :, None] == global_ids[None, None, :], axis=1)
    flags = is_listed.astype(jnp.int32).reshape(-1)
    best_part, power_part = match(flags, tmpl, spec, col_table, cos_t, sin_t)
    best_all, power_all = reduce_orient(best_part, power_part, "orient")
    return (best_all[None], (power_all / LIST)[None])


def solution(mesh):
    placed = (
        P("tile", None, "orient", None),
        P("orient", None, "tile", None),
        P("tile", None, None),
        P("tile", None, None),
    )
    return jax.shard_map(
        local,
        mesh=mesh,
        in_specs=placed,
        out_specs=(P("tile", None, None, None), P("tile", None, None, None)),
        check_vma=False,
    )
```

time: 186 us -> 143 us (0.77)
  waiting for transfers between devices: 102 us -> 59.5 us
  matrix products: 25.8 us -> 0 us
  Pallas kernels: 0 us -> 24.8 us
  local copies, waits for them, and re-layouts: 8.79 us -> 3.08 us
  starting transfers between devices: 16.4 us -> 21.1 us
    all_gather x2 -> x1, waiting for transfers between devices: 61.1 us -> 29.3 us  [local(): tmpl = lax.all_gather(template_spectra, 'tile', axis=0)]
    dot_general x3 -> x0, matrix products: 25.8 us -> none  [the longest x1 12.8 us: local(): jnp.einsum('jnk,pkw->pjnw', mixed, col_table, preferred_element_type=jnp....]
    pallas_call x0 -> x1, Pallas kernels: none -> 24.8 us  [match(): pl.pallas_call(kernel, grid_spec=pltpu.PrefetchScalarGridSpec(num_scalar_...]
    all_gather x1 -> x0, local copies, waits for them, and re-layouts: 7.67 us -> none  [local(): tp = lax.all_gather(tp, 'tcore', axis=0)]
    ppermute x3, waiting for transfers between devices: 13.7 us -> 6.06 us  [gather_rows(): got = lax.ppermute(blocks, axis, xor_pairs(n, k))]
    another operation x1 -> x0, other arithmetic: 6.15 us -> none
    convert_element_type x1 -> x2, other arithmetic: 5.56 us -> 10.1 us  [angle_tables(): jnp.sin(angle).astype(jnp.bfloat16)]
    ppermute x3, waiting for transfers between devices: 14.4 us -> 10.6 us  [reduce_orient(): got = lax.ppermute(cur, axis, xor_pairs(n, k))]
  transfers between devices with their start and end apart: 11 -> 10, of which waited for: 10 -> 10; matrix products, arithmetic and copies ran while one was open for 7% -> 15% of each run, Pallas kernels for 0% -> 0%
where the time goes in v2:
time: 143 us
  waiting for transfers between devices  59.5 us (42%)
  Pallas kernels  24.8 us (17%)
  starting transfers between devices  21.1 us (15%)
  other arithmetic  19.9 us (14%)
  between operations  14.1 us (10%)
  local copies, waits for them, and re-layouts  3.08 us (2%)
    all_gather x1, waiting for transfers between devices, local(): tmpl = lax.all_gather(template_spectra, 'tile', axis=0)  29.3 us
    pallas_call x1, Pallas kernels, match(): pl.pallas_call(kernel, grid_spec=pltpu.PrefetchScalarGridSpec(num_scalar_...  24.8 us
    ppermute x3, waiting for transfers between devices, reduce_orient(): got = lax.ppermute(send, axis, xor_pairs(n, k))  12.8 us
    ppermute x3, waiting for transfers between devices, reduce_orient(): got = lax.ppermute(cur, axis, xor_pairs(n, k))  10.6 us
    convert_element_type x2, other arithmetic, angle_tables(): jnp.sin(angle).astype(jnp.bfloat16)  10.1 us
    ppermute x3, starting transfers between devices, reduce_orient(): got = lax.ppermute(send, axis, xor_pairs(n, k))  8.33 us
    ppermute x3, starting transfers between devices, reduce_orient(): got = lax.ppermute(cur, axis, xor_pairs(n, k))  6.39 us
    ppermute x3, starting transfers between devices, gather_rows(): got = lax.ppermute(blocks, axis, xor_pairs(n, k))  6.38 us
  transfers between devices with their start and end apart: 10, of which 10 were waited for; matrix products, arithmetic and copies ran while one was open for 15% of the time, Pallas kernels for 0%

profile of v2, /device:TPU:0, one launch (start us, length us, event | category | flops | bytes accessed | tf_op | source)
XLA Modules:
  0.0 142.5 jit_solution(18046477464266703952)
XLA Ops:
  7.2 0.7 all-gather.3.cloned.1.call-update
  7.9 4.1 %collective-permute-start = (bf16[1,2,64,512]{3,2,1,0:T(8,128)(2,1)}, bf16[1,2,64,512]{3,2,1,0:T(8,128)(2,1)S(1)}, u32[]{:S(2)}, u32[]{:S(2)}) collective-permute-start(bf16[1,2,64,512]{3,2,1,0:T(8,128)(2,1)} %param.4), channel_id=1, source_target_pairs={{0,4},{1,5},{2,6},{3,7},{4,0},{5,1},{6,2},{7,3},{8,12},{9,13},{10,... | collective-permute-start | bytes 393224 | tf_op jit(solution)/shard_map/ppermute | solution.py:50
  12.0 0.8 slice_bitcast_fusion
  12.9 4.0 %fusion.14 = bf16[4,512,128]{2,1,0:T(8,128)(2,1)S(1)} fusion(s32[4,128]{1,0:T(4,128)S(1)} %get-tuple-element.27), kind=kLoop, calls=%fused_computation.44 | loop fusion | flops 4718592 | bytes 526336 | tf_op jit(solution)/shard_map/neg | solution.py:38
  16.9 0.9 compare_reduce_fusion
  17.8 0.8 collective-permute-done
  18.5 1.0 pad_maximum_fusion.2
  19.5 0.9 collective-permute-start.1
  20.4 0.6 reshape.152.l_ref
  21.0 4.4 %sine_convert_fusion.1 = (bf16[4,512,128]{2,1,0:T(8,128)(2,1)S(1)}, bf16[4,512,128]{2,1,0:T(8,128)(2,1)S(1)}) fusion(s32[4,128]{1,0:T(4,128)S(1)} %get-tuple-element.27), kind=kLoop, calls=%fused_computation.19 | loop fusion | flops 4194304 | bytes 1050624 | tf_op jit(solution)/shard_map/convert_element_type | solution.py:31
  25.4 1.6 %collective-permute-done.1 = bf16[2,2,64,512]{3,2,1,0:T(8,128)(2,1)S(1)} collective-permute-done((bf16[2,2,64,512]{3,2,1,0:T(8,128)(2,1)S(1)}, bf16[2,2,64,512]{3,2,1,0:T(8,128)(2,1)S(1)}, u32[]{:S(2)}, u32[]{:S(2)}) %collective-permute-start.1) | collective-permute-done | bytes 262176 | tf_op jit(solution)/shard_map/ppermute | solution.py:50
  27.1 1.4 collective-permute-start.2
  28.5 1.6 %maximum_maximum_fusion.ct_ref = bf16[4,1024,256]{2,1,0:T(8,128)(2,1)} fusion(bf16[4,512,128]{2,1,0:T(8,128)(2,1)S(1)} %get-tuple-element.23, bf16[4,512,128]{2,1,0:T(8,128)(2,1)S(1)} %fusion.14, bf16[4,512,128]{2,1,0:T(8,128)(2,1)S(1)} %get-tuple-element.22), kind=kLoop, calls=%fused_computation.1 | loop fusion | flops 8388608 | bytes 3670016 | tf_op jit(solution)/shard_map/concatenate | solution.py:39
  30.1 5.7 %sine_convert_fusion = (bf16[4,128,512]{2,1,0:T(8,128)(2,1)}, bf16[4,128,512]{2,1,0:T(8,128)(2,1)}) fusion(s32[4,128]{1,0:T(4,128)S(1)} %get-tuple-element.26), kind=kLoop, calls=%fused_computation.15 | loop fusion | flops 4194304 | bytes 1050624 | tf_op jit(solution)/shard_map/convert_element_type | solution.py:31
  35.8 3.7 %collective-permute-done.2 = bf16[4,2,64,512]{3,2,1,0:T(8,128)(2,1)S(1)} collective-permute-done((bf16[4,2,64,512]{3,2,1,0:T(8,128)(2,1)S(1)}, bf16[4,2,64,512]{3,2,1,0:T(8,128)(2,1)S(1)}, u32[]{:S(2)}, u32[]{:S(2)}) %collective-permute-start.2) | collective-permute-done | bytes 524320 | tf_op jit(solution)/shard_map/ppermute | solution.py:50
  40.2 1.1 copy.8
  41.3 29.3 %all-gather.3.cloned.1.call-done = bf16[32,2,128,512]{3,2,1,0:T(8,128)(2,1)} async-done(((bf16[8,2,128,512]{3,2,1,0:T(8,128)(2,1)}), bf16[32,2,128,512]{3,2,1,0:T(8,128)(2,1)}) %all-gather.3.cloned.1.call-update) | async-done | bytes 8388624 | tf_op jit(solution)/shard_map/all_gather | solution.py:159
  70.6 24.8 %shard_map.59 = (f32[4,128,128]{2,1,0:T(8,128)}, f32[4,128,128]{2,1,0:T(8,128)}) custom-call(s32[32]{0:T(128)} %reshape.152.l_ref, bf16[4,8,2,128,512]{4,3,2,1,0:T(8,128)(2,1)} %bitcast.23, bf16[2,512,512]{2,1,0:T(8,128)(2,1)} %bitcast.16, bf16[4,1024,256]{2,1,0:T(8,128)(2,1)} %maximum_maximum_fusion.ct_ref, bf16[4,128,512]{2,1,0:T(8,128)(2,1)} %get-tuple-element.21.cr_ref, ...), custom_call_target="tpu_custom_call" | custom-call | flops 9663676416 | bytes 11534336 | tf_op jit(solution)/shard_map/pallas_call | solution.py:132
  95.4 1.1 fusion.13
  96.5 2.2 %collective-permute-start.3 = (f32[2,256,128]{2,1,0:T(8,128)S(1)}, f32[2,256,128]{2,1,0:T(8,128)S(1)}, u32[]{:S(2)}, u32[]{:S(2)}) collective-permute-start(f32[2,256,128]{2,1,0:T(8,128)S(1)} %get-tuple-element.11), channel_id=1, source_target_pairs={{0,1},{1,0},{2,3},{3,2},{4,5},{5,4},{6,7},{7,6},{8,9},{9,8},{10,11... | collective-permute-start | bytes 786440 | tf_op jit(solution)/shard_map/ppermute | solution.py:83
  98.8 6.0 %collective-permute-done.3 = f32[2,256,128]{2,1,0:T(8,128)S(1)} collective-permute-done((f32[2,256,128]{2,1,0:T(8,128)S(1)}, f32[2,256,128]{2,1,0:T(8,128)S(1)}, u32[]{:S(2)}, u32[]{:S(2)}) %collective-permute-start.3) | collective-permute-done | bytes 262176 | tf_op jit(solution)/shard_map/ppermute | solution.py:83
  104.8 4.0 %collective-permute-start.4 = (f32[2,128,128]{2,1,0:T(8,128)S(1)}, f32[2,128,128]{2,1,0:T(8,128)S(1)}, u32[]{:S(2)}, u32[]{:S(2)}) collective-permute-start(f32[2,128,128]{2,1,0:T(8,128)S(1)} %get-tuple-element.15), channel_id=1, source_target_pairs={{0,2},{1,3},{2,0},{3,1},{4,6},{5,7},{6,4},{7,5},{8,10},{9,11},{10,... | collective-permute-start | bytes 393224 | tf_op jit(solution)/shard_map/ppermute | solution.py:83
  108.8 3.6 %collective-permute-done.4 = f32[2,128,128]{2,1,0:T(8,128)S(1)} collective-permute-done((f32[2,128,128]{2,1,0:T(8,128)S(1)}, f32[2,128,128]{2,1,0:T(8,128)S(1)}, u32[]{:S(2)}, u32[]{:S(2)}) %collective-permute-start.4) | collective-permute-done | bytes 131104 | tf_op jit(solution)/shard_map/ppermute | solution.py:83
  112.5 2.1 %collective-permute-start.5 = (f32[2,64,128]{2,1,0:T(8,128)S(1)}, f32[2,64,128]{2,1,0:T(8,128)S(1)}, u32[]{:S(2)}, u32[]{:S(2)}) collective-permute-start(f32[2,64,128]{2,1,0:T(8,128)S(1)} %get-tuple-element.19), channel_id=1, source_target_pairs={{0,4},{1,5},{2,6},{3,7},{4,0},{5,1},{6,2},{7,3},{8,12},{9,13},{10,... | collective-permute-start | bytes 196616 | tf_op jit(solution)/shard_map/ppermute | solution.py:83
  114.6 3.2 %collective-permute-done.5 = f32[2,64,128]{2,1,0:T(8,128)S(1)} collective-permute-done((f32[2,64,128]{2,1,0:T(8,128)S(1)}, f32[2,64,128]{2,1,0:T(8,128)S(1)}, u32[]{:S(2)}, u32[]{:S(2)}) %collective-permute-start.5) | collective-permute-done | bytes 65568 | tf_op jit(solution)/shard_map/ppermute | solution.py:83
  117.8 2.2 %collective-permute-start.6 = (f32[2,64,128]{2,1,0:T(8,128)S(1)}, f32[2,64,128]{2,1,0:T(8,128)S(1)}, u32[]{:S(2)}, u32[]{:S(2)}) collective-permute-start(f32[2,64,128]{2,1,0:T(8,128)S(1)} %pad_maximum_fusion.3), channel_id=1, source_target_pairs={{0,4},{1,5},{2,6},{3,7},{4,0},{5,1},{6,2},{7,3},{8,12},{9,13},{10,... | collective-permute-start | bytes 196616 | tf_op jit(solution)/shard_map/ppermute | solution.py:88
  119.9 3.1 %collective-permute-done.6 = f32[2,64,128]{2,1,0:T(8,128)S(1)} collective-permute-done((f32[2,64,128]{2,1,0:T(8,128)S(1)}, f32[2,64,128]{2,1,0:T(8,128)S(1)}, u32[]{:S(2)}, u32[]{:S(2)}) %collective-permute-start.6) | collective-permute-done | bytes 65568 | tf_op jit(solution)/shard_map/ppermute | solution.py:88
  123.0 2.4 %collective-permute-start.7 = (f32[2,128,128]{2,1,0:T(8,128)S(1)}, f32[2,128,128]{2,1,0:T(8,128)S(1)}, u32[]{:S(2)}, u32[]{:S(2)}) collective-permute-start(f32[2,128,128]{2,1,0:T(8,128)S(1)} %maximum_select_fusion.2), channel_id=1, source_target_pairs={{0,2},{1,3},{2,0},{3,1},{4,6},{5,7},{6,4},{7,5},{8,10},{9,11},{10,... | collective-permute-start | bytes 393224 | tf_op jit(solution)/shard_map/ppermute | solution.py:88
  125.4 2.9 %collective-permute-done.7 = f32[2,128,128]{2,1,0:T(8,128)S(1)} collective-permute-done((f32[2,128,128]{2,1,0:T(8,128)S(1)}, f32[2,128,128]{2,1,0:T(8,128)S(1)}, u32[]{:S(2)}, u32[]{:S(2)}) %collective-permute-start.7) | collective-permute-done | bytes 131104 | tf_op jit(solution)/shard_map/ppermute | solution.py:88
  128.4 1.8 %collective-permute-start.8 = (f32[2,256,128]{2,1,0:T(8,128)S(1)}, f32[2,256,128]{2,1,0:T(8,128)S(1)}, u32[]{:S(2)}, u32[]{:S(2)}) collective-permute-start(f32[2,256,128]{2,1,0:T(8,128)S(1)} %maximum_select_fusion.1), channel_id=1, source_target_pairs={{0,1},{1,0},{2,3},{3,2},{4,5},{5,4},{6,7},{7,6},{8,9},{9,8},{10,11... | collective-permute-start | bytes 786440 | tf_op jit(solution)/shard_map/ppermute | solution.py:88
  130.2 4.6 %collective-permute-done.8 = f32[2,256,128]{2,1,0:T(8,128)S(1)} collective-permute-done((f32[2,256,128]{2,1,0:T(8,128)S(1)}, f32[2,256,128]{2,1,0:T(8,128)S(1)}, u32[]{:S(2)}, u32[]{:S(2)}) %collective-permute-start.8) | collective-permute-done | bytes 262176 | tf_op jit(solution)/shard_map/ppermute | solution.py:88
  134.9 0.8 slice_multiply_fusion
  (21 shorter events, 1.1 us)
Async XLA Ops:
  7.2 19.9 %copy-start = (bf16[1,2,64,512]{3,2,1,0:T(8,128)(2,1)S(1)}, bf16[1,2,64,512]{3,2,1,0:T(8,128)(2,1)}, u32[]{:S(2)}) copy-start(bf16[1,2,64,512]{3,2,1,0:T(8,128)(2,1)} %param.4) | copy-start | bytes 393220
  7.2 63.4 %all-gather.3.cloned.1.call-start = ((), (), s32[]{:S(2)}) async-start(), calls=%async_computation | async-start | bytes 10485760 | tf_op jit(solution)/shard_map/all_gather | solution.py:159
  7.9 10.6 %collective-permute-start = (bf16[1,2,64,512]{3,2,1,0:T(8,128)(2,1)}, bf16[1,2,64,512]{3,2,1,0:T(8,128)(2,1)S(1)}, u32[]{:S(2)}, u32[]{:S(2)}) collective-permute-start(bf16[1,2,64,512]{3,2,1,0:T(8,128)(2,1)} %param.4), channel_id=1, source_target_pairs={{0,4},{1,5},{2,6},{3,7},{4,0},{5,1},{6,2},{7,3},{8,12},{9,13},{10,... | collective-permute-start | bytes 393224 | tf_op jit(solution)/shard_map/ppermute | solution.py:50
  19.5 7.6 %collective-permute-start.1 = (bf16[2,2,64,512]{3,2,1,0:T(8,128)(2,1)S(1)}, bf16[2,2,64,512]{3,2,1,0:T(8,128)(2,1)S(1)}, u32[]{:S(2)}, u32[]{:S(2)}) collective-permute-start(bf16[2,2,64,512]{3,2,1,0:T(8,128)(2,1)S(1)} %pad_maximum_fusion.2), channel_id=1, source_target_pairs={{0,2},{1,3},{2,0},{3,1},{4,6},{5,7},{6,4},{7,5},{8,10},{9,11},{10,... | collective-permute-start | bytes 786440 | tf_op jit(solution)/shard_map/ppermute | solution.py:50
  27.1 12.4 %collective-permute-start.2 = (bf16[4,2,64,512]{3,2,1,0:T(8,128)(2,1)S(1)}, bf16[4,2,64,512]{3,2,1,0:T(8,128)(2,1)S(1)}, u32[]{:S(2)}, u32[]{:S(2)}) collective-permute-start(bf16[4,2,64,512]{3,2,1,0:T(8,128)(2,1)S(1)} %pad_maximum_fusion.1), channel_id=1, source_target_pairs={{0,1},{1,0},{2,3},{3,2},{4,5},{5,4},{6,7},{7,6},{8,9},{9,8},{10,11... | collective-permute-start | bytes 1572872 | tf_op jit(solution)/shard_map/ppermute | solution.py:50
  96.5 8.2 %collective-permute-start.3 = (f32[2,256,128]{2,1,0:T(8,128)S(1)}, f32[2,256,128]{2,1,0:T(8,128)S(1)}, u32[]{:S(2)}, u32[]{:S(2)}) collective-permute-start(f32[2,256,128]{2,1,0:T(8,128)S(1)} %get-tuple-element.11), channel_id=1, source_target_pairs={{0,1},{1,0},{2,3},{3,2},{4,5},{5,4},{6,7},{7,6},{8,9},{9,8},{10,11... | collective-permute-start | bytes 786440 | tf_op jit(solution)/shard_map/ppermute | solution.py:83
  104.8 7.6 %collective-permute-start.4 = (f32[2,128,128]{2,1,0:T(8,128)S(1)}, f32[2,128,128]{2,1,0:T(8,128)S(1)}, u32[]{:S(2)}, u32[]{:S(2)}) collective-permute-start(f32[2,128,128]{2,1,0:T(8,128)S(1)} %get-tuple-element.15), channel_id=1, source_target_pairs={{0,2},{1,3},{2,0},{3,1},{4,6},{5,7},{6,4},{7,5},{8,10},{9,11},{10,... | collective-permute-start | bytes 393224 | tf_op jit(solution)/shard_map/ppermute | solution.py:83
  112.5 5.2 %collective-permute-start.5 = (f32[2,64,128]{2,1,0:T(8,128)S(1)}, f32[2,64,128]{2,1,0:T(8,128)S(1)}, u32[]{:S(2)}, u32[]{:S(2)}) collective-permute-start(f32[2,64,128]{2,1,0:T(8,128)S(1)} %get-tuple-element.19), channel_id=1, source_target_pairs={{0,4},{1,5},{2,6},{3,7},{4,0},{5,1},{6,2},{7,3},{8,12},{9,13},{10,... | collective-permute-start | bytes 196616 | tf_op jit(solution)/shard_map/ppermute | solution.py:83
  117.8 5.3 %collective-permute-start.6 = (f32[2,64,128]{2,1,0:T(8,128)S(1)}, f32[2,64,128]{2,1,0:T(8,128)S(1)}, u32[]{:S(2)}, u32[]{:S(2)}) collective-permute-start(f32[2,64,128]{2,1,0:T(8,128)S(1)} %pad_maximum_fusion.3), channel_id=1, source_target_pairs={{0,4},{1,5},{2,6},{3,7},{4,0},{5,1},{6,2},{7,3},{8,12},{9,13},{10,... | collective-permute-start | bytes 196616 | tf_op jit(solution)/shard_map/ppermute | solution.py:88
  123.0 5.3 %collective-permute-start.7 = (f32[2,128,128]{2,1,0:T(8,128)S(1)}, f32[2,128,128]{2,1,0:T(8,128)S(1)}, u32[]{:S(2)}, u32[]{:S(2)}) collective-permute-start(f32[2,128,128]{2,1,0:T(8,128)S(1)} %maximum_select_fusion.2), channel_id=1, source_target_pairs={{0,2},{1,3},{2,0},{3,1},{4,6},{5,7},{6,4},{7,5},{8,10},{9,11},{10,... | collective-permute-start | bytes 393224 | tf_op jit(solution)/shard_map/ppermute | solution.py:88
  128.4 6.4 %collective-permute-start.8 = (f32[2,256,128]{2,1,0:T(8,128)S(1)}, f32[2,256,128]{2,1,0:T(8,128)S(1)}, u32[]{:S(2)}, u32[]{:S(2)}) collective-permute-start(f32[2,256,128]{2,1,0:T(8,128)S(1)} %maximum_select_fusion.1), channel_id=1, source_target_pairs={{0,1},{1,0},{2,3},{3,2},{4,5},{5,4},{6,7},{7,6},{8,9},{9,8},{10,11... | collective-permute-start | bytes 786440 | tf_op jit(solution)/shard_map/ppermute | solution.py:88
Sparse Core Ops, SparseCore 0:
  9.6 60.9 all-gather.2

commit v3 on v2

--- a/solution.py
+++ b/solution.py
@@ -94,7 +94,7 @@
     return best, power
 
 
-def match_kernel(blocks, size, width, rows_t, tiles, peaks_n, l_ref, tm_ref, sp_ref, ct_ref, cr_ref, sr_ref, best_ref, pow_ref, m_ref):
+def match_kernel(blocks, size, width, rows_t, tiles, peaks_n, chunk, l_ref, tm_ref, sp_ref, ct_ref, cr_ref, sr_ref, best_ref, pow_ref, m_ref):
     j = pl.program_id(0)
 
     @pl.when(j == 0)
@@ -102,14 +102,21 @@
         best_ref[...] = jnp.full(best_ref.shape, lowest_score, jnp.float32)
         pow_ref[...] = jnp.zeros(pow_ref.shape, jnp.float32)
 
-    for t in range(tiles):
-        rows = pl.ds(t * rows_t, rows_t)
-        image_re = sp_ref[0, rows, :].astype(jnp.float32)
-        image_im = sp_ref[1, rows, :].astype(jnp.float32)
-        tmpl_re = tm_ref[t, 0, 0].astype(jnp.float32)
-        tmpl_im = tm_ref[t, 0, 1].astype(jnp.float32)
-        m_ref[rows, pl.ds(0, size)] = (image_re * tmpl_re + image_im * tmpl_im).astype(jnp.bfloat16)
-        m_ref[rows, pl.ds(size, size)] = (image_im * tmpl_re - image_re * tmpl_im).astype(jnp.bfloat16)
+    per_tile = rows_t // chunk
+
+    def mix(c, carry):
+        t = c // per_tile
+        row = pl.multiple_of(c * chunk, chunk)
+        local_row = pl.multiple_of((c % per_tile) * chunk, chunk)
+        image_re = sp_ref[0, pl.ds(row, chunk), :]
+        image_im = sp_ref[1, pl.ds(row, chunk), :]
+        tmpl_re = tm_ref[t, 0, 0, pl.ds(local_row, chunk), :].astype(jnp.float32)
+        tmpl_im = tm_ref[t, 0, 1, pl.ds(local_row, chunk), :].astype(jnp.float32)
+        m_ref[pl.ds(row, chunk), pl.ds(0, size)] = (image_re * tmpl_re + image_im * tmpl_im).astype(jnp.bfloat16)
+        m_ref[pl.ds(row, chunk), pl.ds(size, size)] = (image_im * tmpl_re - image_re * tmpl_im).astype(jnp.bfloat16)
+        return carry
+
+    lax.fori_loop(0, tiles * per_tile, mix, 0, unroll=4)
 
     for p in range(peaks_n):
         @pl.when(l_ref[p * blocks + j] > 0)
@@ -125,9 +132,10 @@
 def match(flags, tmpl, spec, col_table, cos_t, sin_t):
     tiles, blocks, _, rows_t, size = tmpl.shape
     peaks_n, width = cos_t.shape[0], cos_t.shape[1]
-    kernel = functools.partial(match_kernel, blocks, size, width, rows_t, tiles, peaks_n)
+    chunk = math.gcd(rows_t, 16)
+    kernel = functools.partial(match_kernel, blocks, size, width, rows_t, tiles, peaks_n, chunk)
     flops = blocks * peaks_n * (2 * size * 2 * size * 2 * width + 2 * 2 * width * size * width)
-    cost = pl.CostEstimate(flops=flops, transcendentals=0, bytes_accessed=tmpl.size * 2 + spec.size * 2 + col_table.size * 2)
+    cost = pl.CostEstimate(flops=flops, transcendentals=0, bytes_accessed=tmpl.size * 2 + spec.size * 4 + col_table.size * 2)
     out = jax.ShapeDtypeStruct((peaks_n, width, width), jnp.float32)
     return pl.pallas_call(
         kernel,
@@ -156,20 +164,29 @@
 def local(tile_spectra, template_spectra, peaks, listed):
     size = tile_spectra.shape[3]
     width = W
-    tmpl = lax.all_gather(template_spectra, "tile", axis=0)
-    block_size = tmpl.shape[1]
+    block_size = template_spectra.shape[0]
     spec = gather_rows(tile_spectra[0], "orient")
-    spec = jnp.moveaxis(spec, 0, 1).reshape(2, size, size)
+    spec = jnp.moveaxis(spec, 0, 1).reshape(2, size, size).astype(jnp.float32)
     freqs = jnp.arange(size, dtype=jnp.int32)
     cos_row, sin_row = angle_tables(freqs, peaks[0][:, 0], size, width)
     cos_t = jnp.swapaxes(cos_row, 1, 2)
     sin_t = jnp.swapaxes(sin_row, 1, 2)
     col_table = col_tables(peaks[0], size, width)
     listed_ids = listed[0]
-    global_ids = lax.axis_index("orient") * block_size + jnp.arange(block_size, dtype=jnp.int32)
-    is_listed = jnp.any(listed_ids[:, :, None] == global_ids[None, None, :], axis=1)
-    flags = is_listed.astype(jnp.int32).reshape(-1)
-    best_part, power_part = match(flags, tmpl, spec, col_table, cos_t, sin_t)
+    halves = 2 if block_size % 2 == 0 else 1
+    part = block_size // halves
+    best_part, power_part = None, None
+    for h in range(halves):
+        tmpl = lax.all_gather(template_spectra[h * part:(h + 1) * part], "tile", axis=0)
+        global_ids = lax.axis_index("orient") * block_size + h * part + jnp.arange(part, dtype=jnp.int32)
+        is_listed = jnp.any(listed_ids[:, :, None] == global_ids[None, None, :], axis=1)
+        flags = is_listed.astype(jnp.int32).reshape(-1)
+        best_h, power_h = match(flags, tmpl, spec, col_table, cos_t, sin_t)
+        if best_part is None:
+            best_part, power_part = best_h, power_h
+        else:
+            best_part = jnp.maximum(best_part, best_h)
+            power_part = power_part + power_h
     best_all, power_all = reduce_orient(best_part, power_part, "orient")
     return (best_all[None], (power_all / LIST)[None])
 

time: 143 us -> 146 us (1.021)
  Pallas kernels: 24.8 us -> 30.2 us
  starting transfers between devices: 21.1 us -> 16.9 us
  local copies, waits for them, and re-layouts: 3.08 us -> 6.62 us
  waiting for transfers between devices: 59.5 us -> 57.7 us
    pallas_call x1 -> x2, Pallas kernels: 24.8 us -> 30.2 us  [match(): pl.pallas_call(kernel, grid_spec=pltpu.PrefetchScalarGridSpec(num_scalar_...]
    all_gather x1 -> x2, waiting for transfers between devices: 29.3 us -> 25.1 us  [local(): lax.all_gather(template_spectra[h * part:(h + 1) * part], 'tile', axis=0)]
    ppermute x3, starting transfers between devices: 8.33 us -> 4.66 us  [reduce_orient(): got = lax.ppermute(send, axis, xor_pairs(n, k))]
    slice x0 -> x1, local copies, waits for them, and re-layouts: none -> 3.04 us  [local(): template_spectra[h * part:(h + 1) * part]]
    convert_element_type x0 -> x1, local copies, waits for them, and re-layouts: none -> 1.61 us  [local(): spec = jnp.moveaxis(spec, 0, 1).reshape(2, size, size).astype(jnp.float32)]
  transfers between devices with their start and end apart: 10 -> 11, of which waited for: 10 -> 11; matrix products, arithmetic and copies ran while one was open for 15% -> 14% of each run, Pallas kernels for 0% -> 10%
where the time goes in v3:
time: 146 us; the launch traced here: 145 us
  waiting for transfers between devices  57.7 us (40%)
  Pallas kernels  30.2 us (21%)
  other arithmetic  19.5 us (13%)
  starting transfers between devices  16.9 us (12%)
  between operations  14.2 us (10%)
  local copies, waits for them, and re-layouts  6.62 us (5%)
    pallas_call x2, Pallas kernels, match(): pl.pallas_call(kernel, grid_spec=pltpu.PrefetchScalarGridSpec(num_scalar_...  30.2 us
    all_gather x2, waiting for transfers between devices, local(): lax.all_gather(template_spectra[h * part:(h + 1) * part], 'tile', axis=0)  25.1 us
    ppermute x3, waiting for transfers between devices, reduce_orient(): got = lax.ppermute(send, axis, xor_pairs(n, k))  14.1 us
    ppermute x3, waiting for transfers between devices, reduce_orient(): got = lax.ppermute(cur, axis, xor_pairs(n, k))  10.7 us
    convert_element_type x2, other arithmetic, angle_tables(): jnp.sin(angle).astype(jnp.bfloat16)  10.1 us
    ppermute x3, waiting for transfers between devices, gather_rows(): got = lax.ppermute(blocks, axis, xor_pairs(n, k))  6.95 us
    ppermute x3, starting transfers between devices, gather_rows(): got = lax.ppermute(blocks, axis, xor_pairs(n, k))  6.14 us
    ppermute x3, starting transfers between devices, reduce_orient(): got = lax.ppermute(cur, axis, xor_pairs(n, k))  6.07 us
  transfers between devices with their start and end apart: 11, of which 11 were waited for; matrix products, arithmetic and copies ran while one was open for 14% of the time, Pallas kernels for 10%

profile of v3, /device:TPU:0, one launch (start us, length us, event | category | flops | bytes accessed | tf_op | source)
XLA Modules:
  0.0 145.1 jit_solution(13506989837808136921)
XLA Ops:
  7.2 3.0 %fusion.24 = (bf16[4,2,128,512]{3,2,1,0:T(8,128)(2,1)}, bf16[4,2,128,512]{3,2,1,0:T(8,128)(2,1)}) fusion(bf16[8,2,128,512]{3,2,1,0:T(8,128)(2,1)} %param.5), kind=kLoop, calls=%fused_computation.85 | loop fusion | bytes 4194304 | tf_op jit(solution)/shard_map/slice | solution.py:180
  10.3 0.7 all-gather.7.cloned.1.call-update
  11.2 4.0 %collective-permute-start = (bf16[1,2,64,512]{3,2,1,0:T(8,128)(2,1)S(1)}, bf16[1,2,64,512]{3,2,1,0:T(8,128)(2,1)S(1)}, u32[]{:S(2)}, u32[]{:S(2)}) collective-permute-start(bf16[1,2,64,512]{3,2,1,0:T(8,128)(2,1)S(1)} %copy-done), channel_id=1, source_target_pairs={{0,4},{1,5},{2,6},{3,7},{4,0},{5,1},{6,2},{7,3},{8,12},{9,13},{10,... | collective-permute-start | bytes 393224 | tf_op jit(solution)/shard_map/ppermute | solution.py:50
  15.3 4.0 %fusion.14 = bf16[4,512,128]{2,1,0:T(8,128)(2,1)S(1)} fusion(s32[4,128]{1,0:T(4,128)S(1)} %get-tuple-element.35), kind=kLoop, calls=%fused_computation.45 | loop fusion | flops 4718592 | bytes 526336 | tf_op jit(solution)/shard_map/neg | solution.py:38
  19.6 1.9 %collective-permute-done = bf16[1,2,64,512]{3,2,1,0:T(8,128)(2,1)S(1)} collective-permute-done((bf16[1,2,64,512]{3,2,1,0:T(8,128)(2,1)S(1)}, bf16[1,2,64,512]{3,2,1,0:T(8,128)(2,1)S(1)}, u32[]{:S(2)}, u32[]{:S(2)}) %collective-permute-start) | collective-permute-done | bytes 131104 | tf_op jit(solution)/shard_map/ppermute | solution.py:50
  21.5 0.8 collective-permute-start.1
  23.5 4.4 %sine_convert_fusion.1 = (bf16[4,512,128]{2,1,0:T(8,128)(2,1)S(1)}, bf16[4,512,128]{2,1,0:T(8,128)(2,1)S(1)}) fusion(s32[4,128]{1,0:T(4,128)S(1)} %get-tuple-element.35), kind=kLoop, calls=%fused_computation.20 | loop fusion | flops 4194304 | bytes 1050624 | tf_op jit(solution)/shard_map/convert_element_type | solution.py:31
  27.9 1.1 collective-permute-done.1
  29.1 1.3 collective-permute-start.2
  30.5 1.6 %maximum_maximum_fusion.ct_ref = bf16[4,1024,256]{2,1,0:T(8,128)(2,1)} fusion(bf16[4,512,128]{2,1,0:T(8,128)(2,1)S(1)} %get-tuple-element.31, bf16[4,512,128]{2,1,0:T(8,128)(2,1)S(1)} %fusion.14, bf16[4,512,128]{2,1,0:T(8,128)(2,1)S(1)} %get-tuple-element.30), kind=kLoop, calls=%fused_computation.1 | loop fusion | flops 8388608 | bytes 3670016 | tf_op jit(solution)/shard_map/concatenate | solution.py:39
  32.0 5.7 %sine_convert_fusion = (bf16[4,128,512]{2,1,0:T(8,128)(2,1)}, bf16[4,128,512]{2,1,0:T(8,128)(2,1)}) fusion(s32[4,128]{1,0:T(4,128)S(1)} %get-tuple-element.34), kind=kLoop, calls=%fused_computation.16 | loop fusion | flops 4194304 | bytes 1050624 | tf_op jit(solution)/shard_map/convert_element_type | solution.py:31
  37.7 3.9 %collective-permute-done.2 = bf16[4,2,64,512]{3,2,1,0:T(8,128)(2,1)S(1)} collective-permute-done((bf16[4,2,64,512]{3,2,1,0:T(8,128)(2,1)S(1)}, bf16[4,2,64,512]{3,2,1,0:T(8,128)(2,1)S(1)}, u32[]{:S(2)}, u32[]{:S(2)}) %collective-permute-start.2) | collective-permute-done | bytes 524320 | tf_op jit(solution)/shard_map/ppermute | solution.py:50
  42.7 1.6 %copy.8 = f32[2,8,64,512]{3,2,1,0:T(8,128)} copy(f32[2,8,64,512]{3,2,0,1:T(8,128)S(1)} %convert_bitcast_fusion) | data formatting | bytes 4194304 | tf_op jit(solution)/shard_map/convert_element_type | solution.py:169
  44.3 3.4 %all-gather.5.cloned.1.call-done = bf16[16,2,128,512]{3,2,1,0:T(8,128)(2,1)} async-done(((bf16[4,2,128,512]{3,2,1,0:T(8,128)(2,1)}), bf16[16,2,128,512]{3,2,1,0:T(8,128)(2,1)}) %all-gather.5.cloned.1.call-update) | async-done | bytes 4194320 | tf_op jit(solution)/shard_map/all_gather | solution.py:180
  47.6 14.3 %shard_map.59 = (f32[4,128,128]{2,1,0:T(8,128)}, f32[4,128,128]{2,1,0:T(8,128)}) custom-call(s32[16]{0:T(128)} %reshape.159.l_ref, bf16[4,4,2,128,512]{4,3,2,1,0:T(8,128)(2,1)} %bitcast.25, f32[2,512,512]{2,1,0:T(8,128)} %bitcast.17, bf16[4,1024,256]{2,1,0:T(8,128)(2,1)} %maximum_maximum_fusion.ct_ref, bf16[4,128,512]{2,1,0:T(8,128)(2,1)} %get-tuple-element.29.cr_ref, ...), custom_call_target="tpu_custom_call" | custom-call | flops 4831838208 | bytes 8388608 | tf_op jit(solution)/shard_map/pallas_call | solution.py:140
  61.9 21.8 %all-gather.7.cloned.1.call-done = bf16[16,2,128,512]{3,2,1,0:T(8,128)(2,1)} async-done(((bf16[4,2,128,512]{3,2,1,0:T(8,128)(2,1)}), bf16[16,2,128,512]{3,2,1,0:T(8,128)(2,1)}) %all-gather.7.cloned.1.call-update) | async-done | bytes 4194320 | tf_op jit(solution)/shard_map/all_gather | solution.py:180
  83.7 15.9 %shard_map.60 = (f32[4,128,128]{2,1,0:T(8,128)}, f32[4,128,128]{2,1,0:T(8,128)}) custom-call(s32[16]{0:T(128)} %reshape.161.l_ref, bf16[4,4,2,128,512]{4,3,2,1,0:T(8,128)(2,1)} %bitcast.26, f32[2,512,512]{2,1,0:T(8,128)} %bitcast.18, bf16[4,1024,256]{2,1,0:T(8,128)(2,1)} %maximum_maximum_fusion.ct_ref, bf16[4,128,512]{2,1,0:T(8,128)(2,1)} %get-tuple-element.29.cr_ref, ...), custom_call_target="tpu_custom_call" | custom-call | flops 4831838208 | bytes 8388608 | tf_op jit(solution)/shard_map/pallas_call | solution.py:140
  99.6 1.0 max.15
  100.6 1.0 add.175
  101.6 1.6 %collective-permute-start.3 = (f32[2,256,128]{2,1,0:T(8,128)S(1)}, f32[2,256,128]{2,1,0:T(8,128)S(1)}, u32[]{:S(2)}, u32[]{:S(2)}) collective-permute-start(f32[2,256,128]{2,1,0:T(8,128)S(1)} %get-tuple-element.19), channel_id=1, source_target_pairs={{0,1},{1,0},{2,3},{3,2},{4,5},{5,4},{6,7},{7,6},{8,9},{9,8},{10,11... | collective-permute-start | bytes 786440 | tf_op jit(solution)/shard_map/ppermute | solution.py:83
  103.2 7.0 %collective-permute-done.3 = f32[2,256,128]{2,1,0:T(8,128)S(1)} collective-permute-done((f32[2,256,128]{2,1,0:T(8,128)S(1)}, f32[2,256,128]{2,1,0:T(8,128)S(1)}, u32[]{:S(2)}, u32[]{:S(2)}) %collective-permute-start.3) | collective-permute-done | bytes 262176 | tf_op jit(solution)/shard_map/ppermute | solution.py:83
  110.2 1.3 collective-permute-start.4
  111.5 3.8 %collective-permute-done.4 = f32[2,128,128]{2,1,0:T(8,128)S(1)} collective-permute-done((f32[2,128,128]{2,1,0:T(8,128)S(1)}, f32[2,128,128]{2,1,0:T(8,128)S(1)}, u32[]{:S(2)}, u32[]{:S(2)}) %collective-permute-start.4) | collective-permute-done | bytes 131104 | tf_op jit(solution)/shard_map/ppermute | solution.py:83
  115.3 1.8 %collective-permute-start.5 = (f32[2,64,128]{2,1,0:T(8,128)S(1)}, f32[2,64,128]{2,1,0:T(8,128)S(1)}, u32[]{:S(2)}, u32[]{:S(2)}) collective-permute-start(f32[2,64,128]{2,1,0:T(8,128)S(1)} %get-tuple-element.27), channel_id=1, source_target_pairs={{0,4},{1,5},{2,6},{3,7},{4,0},{5,1},{6,2},{7,3},{8,12},{9,13},{10,... | collective-permute-start | bytes 196616 | tf_op jit(solution)/shard_map/ppermute | solution.py:83
  117.1 3.4 %collective-permute-done.5 = f32[2,64,128]{2,1,0:T(8,128)S(1)} collective-permute-done((f32[2,64,128]{2,1,0:T(8,128)S(1)}, f32[2,64,128]{2,1,0:T(8,128)S(1)}, u32[]{:S(2)}, u32[]{:S(2)}) %collective-permute-start.5) | collective-permute-done | bytes 65568 | tf_op jit(solution)/shard_map/ppermute | solution.py:83
  120.6 2.5 %collective-permute-start.6 = (f32[2,64,128]{2,1,0:T(8,128)S(1)}, f32[2,64,128]{2,1,0:T(8,128)S(1)}, u32[]{:S(2)}, u32[]{:S(2)}) collective-permute-start(f32[2,64,128]{2,1,0:T(8,128)S(1)} %pad_maximum_fusion.3), channel_id=1, source_target_pairs={{0,4},{1,5},{2,6},{3,7},{4,0},{5,1},{6,2},{7,3},{8,12},{9,13},{10,... | collective-permute-start | bytes 196616 | tf_op jit(solution)/shard_map/ppermute | solution.py:88
  123.1 2.8 %collective-permute-done.6 = f32[2,64,128]{2,1,0:T(8,128)S(1)} collective-permute-done((f32[2,64,128]{2,1,0:T(8,128)S(1)}, f32[2,64,128]{2,1,0:T(8,128)S(1)}, u32[]{:S(2)}, u32[]{:S(2)}) %collective-permute-start.6) | collective-permute-done | bytes 65568 | tf_op jit(solution)/shard_map/ppermute | solution.py:88
  125.9 2.0 %collective-permute-start.7 = (f32[2,128,128]{2,1,0:T(8,128)S(1)}, f32[2,128,128]{2,1,0:T(8,128)S(1)}, u32[]{:S(2)}, u32[]{:S(2)}) collective-permute-start(f32[2,128,128]{2,1,0:T(8,128)S(1)} %maximum_select_fusion.2), channel_id=1, source_target_pairs={{0,2},{1,3},{2,0},{3,1},{4,6},{5,7},{6,4},{7,5},{8,10},{9,11},{10,... | collective-permute-start | bytes 393224 | tf_op jit(solution)/shard_map/ppermute | solution.py:88
  127.9 3.0 %collective-permute-done.7 = f32[2,128,128]{2,1,0:T(8,128)S(1)} collective-permute-done((f32[2,128,128]{2,1,0:T(8,128)S(1)}, f32[2,128,128]{2,1,0:T(8,128)S(1)}, u32[]{:S(2)}, u32[]{:S(2)}) %collective-permute-start.7) | collective-permute-done | bytes 131104 | tf_op jit(solution)/shard_map/ppermute | solution.py:88
  131.0 1.5 %collective-permute-start.8 = (f32[2,256,128]{2,1,0:T(8,128)S(1)}, f32[2,256,128]{2,1,0:T(8,128)S(1)}, u32[]{:S(2)}, u32[]{:S(2)}) collective-permute-start(f32[2,256,128]{2,1,0:T(8,128)S(1)} %maximum_select_fusion.1), channel_id=1, source_target_pairs={{0,1},{1,0},{2,3},{3,2},{4,5},{5,4},{6,7},{7,6},{8,9},{9,8},{10,11... | collective-permute-start | bytes 786440 | tf_op jit(solution)/shard_map/ppermute | solution.py:88
  132.5 4.9 %collective-permute-done.8 = f32[2,256,128]{2,1,0:T(8,128)S(1)} collective-permute-done((f32[2,256,128]{2,1,0:T(8,128)S(1)}, f32[2,256,128]{2,1,0:T(8,128)S(1)}, u32[]{:S(2)}, u32[]{:S(2)}) %collective-permute-start.8) | collective-permute-done | bytes 262176 | tf_op jit(solution)/shard_map/ppermute | solution.py:88
  137.5 0.8 slice_multiply_fusion
  (39 shorter events, 3.1 us)
Async XLA Ops:
  7.2 40.5 %all-gather.5.cloned.1.call-start = ((), (), s32[]{:S(2)}) async-start(), calls=%async_computation | async-start | bytes 5242880 | tf_op jit(solution)/shard_map/all_gather | solution.py:180
  10.2 0.9 copy-start
  10.2 4.9 %copy-start.4 = (s32[1,4,2]{1,2,0:T(2,128)S(1)}, s32[1,4,2]{1,2,0:T(2,128)}, u32[]{:S(2)}) copy-start(s32[1,4,2]{1,2,0:T(2,128)} %param.6) | copy-start | bytes 100
  10.3 9.1 %copy-start.3 = (s32[1,4,48]{2,1,0:T(4,128)S(1)}, s32[1,4,48]{2,1,0:T(4,128)}, u32[]{:S(2)}) copy-start(s32[1,4,48]{2,1,0:T(4,128)} %param.7) | copy-start | bytes 2308
  10.3 73.4 %all-gather.7.cloned.1.call-start = ((), (), s32[]{:S(2)}) async-start(), calls=%async_computation.1 | async-start | bytes 5242880 | tf_op jit(solution)/shard_map/all_gather | solution.py:180
  11.2 10.3 %collective-permute-start = (bf16[1,2,64,512]{3,2,1,0:T(8,128)(2,1)S(1)}, bf16[1,2,64,512]{3,2,1,0:T(8,128)(2,1)S(1)}, u32[]{:S(2)}, u32[]{:S(2)}) collective-permute-start(bf16[1,2,64,512]{3,2,1,0:T(8,128)(2,1)S(1)} %copy-done), channel_id=1, source_target_pairs={{0,4},{1,5},{2,6},{3,7},{4,0},{5,1},{6,2},{7,3},{8,12},{9,13},{10,... | collective-permute-start | bytes 393224 | tf_op jit(solution)/shard_map/ppermute | solution.py:50
  21.5 7.6 %collective-permute-start.1 = (bf16[2,2,64,512]{3,2,1,0:T(8,128)(2,1)S(1)}, bf16[2,2,64,512]{3,2,1,0:T(8,128)(2,1)S(1)}, u32[]{:S(2)}, u32[]{:S(2)}) collective-permute-start(bf16[2,2,64,512]{3,2,1,0:T(8,128)(2,1)S(1)} %pad_maximum_fusion.2), channel_id=1, source_target_pairs={{0,2},{1,3},{2,0},{3,1},{4,6},{5,7},{6,4},{7,5},{8,10},{9,11},{10,... | collective-permute-start | bytes 786440 | tf_op jit(solution)/shard_map/ppermute | solution.py:50
  29.1 12.5 %collective-permute-start.2 = (bf16[4,2,64,512]{3,2,1,0:T(8,128)(2,1)S(1)}, bf16[4,2,64,512]{3,2,1,0:T(8,128)(2,1)S(1)}, u32[]{:S(2)}, u32[]{:S(2)}) collective-permute-start(bf16[4,2,64,512]{3,2,1,0:T(8,128)(2,1)S(1)} %pad_maximum_fusion.1), channel_id=1, source_target_pairs={{0,1},{1,0},{2,3},{3,2},{4,5},{5,4},{6,7},{7,6},{8,9},{9,8},{10,11... | collective-permute-start | bytes 1572872 | tf_op jit(solution)/shard_map/ppermute | solution.py:50
  83.7 15.9 %copy-start.2 = (f32[4,128,128]{2,1,0:T(8,128)S(1)}, f32[4,128,128]{2,1,0:T(8,128)}, u32[]{:S(2)}) copy-start(f32[4,128,128]{2,1,0:T(8,128)} %get-tuple-element.6) | copy-start | bytes 786436
  83.7 16.9 %copy-start.1 = (f32[4,128,128]{2,1,0:T(8,128)S(1)}, f32[4,128,128]{2,1,0:T(8,128)}, u32[]{:S(2)}) copy-start(f32[4,128,128]{2,1,0:T(8,128)} %get-tuple-element.8) | copy-start | bytes 786436
  101.6 8.5 %collective-permute-start.3 = (f32[2,256,128]{2,1,0:T(8,128)S(1)}, f32[2,256,128]{2,1,0:T(8,128)S(1)}, u32[]{:S(2)}, u32[]{:S(2)}) collective-permute-start(f32[2,256,128]{2,1,0:T(8,128)S(1)} %get-tuple-element.19), channel_id=1, source_target_pairs={{0,1},{1,0},{2,3},{3,2},{4,5},{5,4},{6,7},{7,6},{8,9},{9,8},{10,11... | collective-permute-start | bytes 786440 | tf_op jit(solution)/shard_map/ppermute | solution.py:83
  110.2 5.0 %collective-permute-start.4 = (f32[2,128,128]{2,1,0:T(8,128)S(1)}, f32[2,128,128]{2,1,0:T(8,128)S(1)}, u32[]{:S(2)}, u32[]{:S(2)}) collective-permute-start(f32[2,128,128]{2,1,0:T(8,128)S(1)} %get-tuple-element.23), channel_id=1, source_target_pairs={{0,2},{1,3},{2,0},{3,1},{4,6},{5,7},{6,4},{7,5},{8,10},{9,11},{10,... | collective-permute-start | bytes 393224 | tf_op jit(solution)/shard_map/ppermute | solution.py:83
  115.3 5.2 %collective-permute-start.5 = (f32[2,64,128]{2,1,0:T(8,128)S(1)}, f32[2,64,128]{2,1,0:T(8,128)S(1)}, u32[]{:S(2)}, u32[]{:S(2)}) collective-permute-start(f32[2,64,128]{2,1,0:T(8,128)S(1)} %get-tuple-element.27), channel_id=1, source_target_pairs={{0,4},{1,5},{2,6},{3,7},{4,0},{5,1},{6,2},{7,3},{8,12},{9,13},{10,... | collective-permute-start | bytes 196616 | tf_op jit(solution)/shard_map/ppermute | solution.py:83
  120.6 5.3 %collective-permute-start.6 = (f32[2,64,128]{2,1,0:T(8,128)S(1)}, f32[2,64,128]{2,1,0:T(8,128)S(1)}, u32[]{:S(2)}, u32[]{:S(2)}) collective-permute-start(f32[2,64,128]{2,1,0:T(8,128)S(1)} %pad_maximum_fusion.3), channel_id=1, source_target_pairs={{0,4},{1,5},{2,6},{3,7},{4,0},{5,1},{6,2},{7,3},{8,12},{9,13},{10,... | collective-permute-start | bytes 196616 | tf_op jit(solution)/shard_map/ppermute | solution.py:88
  125.9 5.0 %collective-permute-start.7 = (f32[2,128,128]{2,1,0:T(8,128)S(1)}, f32[2,128,128]{2,1,0:T(8,128)S(1)}, u32[]{:S(2)}, u32[]{:S(2)}) collective-permute-start(f32[2,128,128]{2,1,0:T(8,128)S(1)} %maximum_select_fusion.2), channel_id=1, source_target_pairs={{0,2},{1,3},{2,0},{3,1},{4,6},{5,7},{6,4},{7,5},{8,10},{9,11},{10,... | collective-permute-start | bytes 393224 | tf_op jit(solution)/shard_map/ppermute | solution.py:88
  131.0 6.4 %collective-permute-start.8 = (f32[2,256,128]{2,1,0:T(8,128)S(1)}, f32[2,256,128]{2,1,0:T(8,128)S(1)}, u32[]{:S(2)}, u32[]{:S(2)}) collective-permute-start(f32[2,256,128]{2,1,0:T(8,128)S(1)} %maximum_select_fusion.1), channel_id=1, source_target_pairs={{0,1},{1,0},{2,3},{3,2},{4,5},{5,4},{6,7},{7,6},{8,9},{9,8},{10,11... | collective-permute-start | bytes 786440 | tf_op jit(solution)/shard_map/ppermute | solution.py:88
Sparse Core Ops, SparseCore 0:
  10.4 37.1 all-gather.4
  49.2 34.4 all-gather.6

commit v4 on v2

--- a/solution.py
+++ b/solution.py
@@ -153,9 +153,108 @@
     )(flags, tmpl, spec, col_table, cos_t, sin_t)
 
 
+def rows_kernel(blocks, size, width, rows_t, peaks_n, chunk, n_steps, final, f_ref, tid_ref, rid_ref, tm_ref, sp_ref, ct_ref, cr_ref, sr_ref, *rest):
+    if final:
+        init_ref, best_ref, pow_ref, acc_ref, m_ref = rest
+    else:
+        part_ref, acc_ref, m_ref = rest
+    j = pl.program_id(0)
+    i = pl.program_id(1)
+
+    if final:
+        @pl.when((j == 0) & (i == 0))
+        def _():
+            best_ref[...] = jnp.full(best_ref.shape, lowest_score, jnp.float32)
+            pow_ref[...] = jnp.zeros(pow_ref.shape, jnp.float32)
+
+        @pl.when(i == 0)
+        def _():
+            acc_ref[...] = init_ref[:, 0]
+    else:
+        @pl.when(i == 0)
+        def _():
+            acc_ref[...] = jnp.zeros(acc_ref.shape, jnp.float32)
+
+    def mix(c, carry):
+        row = pl.multiple_of(c * chunk, chunk)
+        image_re = sp_ref[0, pl.ds(row, chunk), :]
+        image_im = sp_ref[1, pl.ds(row, chunk), :]
+        tmpl_re = tm_ref[0, 0, 0, pl.ds(row, chunk), :].astype(jnp.float32)
+        tmpl_im = tm_ref[0, 0, 1, pl.ds(row, chunk), :].astype(jnp.float32)
+        m_ref[pl.ds(row, chunk), pl.ds(0, size)] = (image_re * tmpl_re + image_im * tmpl_im).astype(jnp.bfloat16)
+        m_ref[pl.ds(row, chunk), pl.ds(size, size)] = (image_im * tmpl_re - image_re * tmpl_im).astype(jnp.bfloat16)
+        return carry
+
+    lax.fori_loop(0, rows_t // chunk, mix, 0, unroll=4)
+
+    for p in range(peaks_n):
+        @pl.when(f_ref[p * blocks + j] > 0)
+        def _():
+            g = jnp.dot(m_ref[...], ct_ref[p], preferred_element_type=jnp.float32).astype(jnp.bfloat16)
+            part = jnp.dot(cr_ref[p], g[:, :width], preferred_element_type=jnp.float32)
+            part = part - jnp.dot(sr_ref[p], g[:, width:], preferred_element_type=jnp.float32)
+            acc_ref[p] = acc_ref[p] + part
+
+    @pl.when(i == n_steps - 1)
+    def _():
+        if final:
+            for p in range(peaks_n):
+                @pl.when(f_ref[p * blocks + j] > 0)
+                def _():
+                    score = acc_ref[p] / size
+                    best_ref[p] = jnp.maximum(best_ref[p], score)
+                    pow_ref[p] = pow_ref[p] + score * score
+        else:
+            part_ref[:, 0] = acc_ref[...]
+
+
+def match_rows(flags, tids, rids, tmpl, spec, col_table, cos_t, sin_t, init=None):
+    _, blocks, _, rows_t, size = tmpl.shape
+    peaks_n, width = cos_t.shape[0], cos_t.shape[1]
+    n_steps = tids.shape[0]
+    final = init is not None
+    chunk = math.gcd(rows_t, 16)
+    kernel = functools.partial(rows_kernel, blocks, size, width, rows_t, peaks_n, chunk, n_steps, final)
+    flops = blocks * peaks_n * n_steps * (2 * rows_t * 2 * size * 2 * width + 2 * 2 * width * rows_t * width)
+    cost = pl.CostEstimate(flops=flops, transcendentals=0, bytes_accessed=n_steps * blocks * 2 * rows_t * size * 6 + col_table.size * 2)
+    in_specs = [
+        pl.BlockSpec((1, 1, 2, rows_t, size), lambda j, i, f, t, r: (t[i], j, 0, 0, 0)),
+        pl.BlockSpec((2, rows_t, size), lambda j, i, f, t, r: (0, r[i], 0)),
+        pl.BlockSpec(col_table.shape, lambda j, i, f, t, r: (0, 0, 0)),
+        pl.BlockSpec((peaks_n, width, rows_t), lambda j, i, f, t, r: (0, 0, r[i])),
+        pl.BlockSpec((peaks_n, width, rows_t), lambda j, i, f, t, r: (0, 0, r[i])),
+    ]
+    args = [flags, tids, rids, tmpl, spec, col_table, cos_t, sin_t]
+    part_spec = pl.BlockSpec((peaks_n, 1, width, width), lambda j, i, f, t, r: (0, j, 0, 0))
+    if final:
+        in_specs.append(part_spec)
+        args.append(init)
+        out = jax.ShapeDtypeStruct((peaks_n, width, width), jnp.float32)
+        out_shape = [out, out]
+        out_specs = [pl.BlockSpec((peaks_n, width, width), lambda j, i, f, t, r: (0, 0, 0))] * 2
+    else:
+        out_shape = jax.ShapeDtypeStruct((peaks_n, blocks, width, width), jnp.float32)
+        out_specs = part_spec
+    return pl.pallas_call(
+        kernel,
+        grid_spec=pltpu.PrefetchScalarGridSpec(
+            num_scalar_prefetch=3,
+            grid=(blocks, n_steps),
+            in_specs=in_specs,
+            out_specs=out_specs,
+            scratch_shapes=[pltpu.VMEM((peaks_n, width, width), jnp.float32), pltpu.VMEM((rows_t, 2 * size), jnp.bfloat16)],
+        ),
+        out_shape=out_shape,
+        compiler_params=pltpu.CompilerParams(dimension_semantics=("arbitrary", "arbitrary")),
+        cost_estimate=cost,
+    )(*args)
+
+
 def local(tile_spectra, template_spectra, peaks, listed):
     size = tile_spectra.shape[3]
     width = W
+    tiles = lax.axis_size("tile")
+    rows_t = template_spectra.shape[2]
     tmpl = lax.all_gather(template_spectra, "tile", axis=0)
     block_size = tmpl.shape[1]
     spec = gather_rows(tile_spectra[0], "orient")
@@ -169,9 +268,27 @@
     global_ids = lax.axis_index("orient") * block_size + jnp.arange(block_size, dtype=jnp.int32)
     is_listed = jnp.any(listed_ids[:, :, None] == global_ids[None, None, :], axis=1)
     flags = is_listed.astype(jnp.int32).reshape(-1)
-    best_part, power_part = match(flags, tmpl, spec, col_table, cos_t, sin_t)
+    if rows_t % 128 != 0 or tiles % 2 != 0:
+        best_part, power_part = match(flags, tmpl, spec, col_table, cos_t, sin_t)
+    else:
+        me = lax.axis_index("tile")
+        sibling = lax.ppermute(template_spectra, "tile", xor_pairs(tiles, 1))
+        near = jnp.stack([template_spectra, sibling])
+        spec32 = spec.astype(jnp.float32)
+        near_rows = jnp.stack([me, me ^ 1]).astype(jnp.int32)
+        partial = match_rows(flags, jnp.arange(2, dtype=jnp.int32), near_rows, near, spec32, col_table, cos_t, sin_t)
+        far_rows = far_blocks(me, tiles)
+        best_part, power_part = match_rows(flags, far_rows, far_rows, tmpl, spec32, col_table, cos_t, sin_t, init=partial)
     best_all, power_all = reduce_orient(best_part, power_part, "orient")
     return (best_all[None], (power_all / LIST)[None])
+
+
+def far_blocks(me, tiles):
+    steps = jnp.arange(tiles - 2, dtype=jnp.int32)
+    pair = steps // 2
+    chip = me // 2
+    pair = pair + (pair >= chip).astype(jnp.int32)
+    return pair * 2 + steps % 2
 
 
 def solution(mesh):

time: 143 us -> 157 us (1.098)
  Pallas kernels: 24.8 us -> 53.6 us
  waiting for transfers between devices: 59.5 us -> 38.7 us
  other arithmetic: 19.9 us -> 24.6 us
  local copies, waits for them, and re-layouts: 3.08 us -> 6.12 us
  starting transfers between devices: 21.1 us -> 18.2 us
    all_gather x1, waiting for transfers between devices: 29.3 us -> 0.01 us  [local(): tmpl = lax.all_gather(template_spectra, 'tile', axis=0)]
    pallas_call x1 -> x2, Pallas kernels: 24.8 us -> 53.6 us  [match_rows(): pl.pallas_call(kernel, grid_spec=pltpu.PrefetchScalarGridSpec(num_scalar_...]
    ppermute x3, waiting for transfers between devices: 10.6 us -> 15.8 us  [reduce_orient(): got = lax.ppermute(cur, axis, xor_pairs(n, k))]
    ppermute x3, starting transfers between devices: 6.39 us -> 1.6 us  [reduce_orient(): got = lax.ppermute(cur, axis, xor_pairs(n, k))]
    another operation x0 -> x2, other arithmetic: none -> 4.6 us  [the longest x1 3.96 us: local(): near = jnp.stack([template_spectra, sibling])]
    ppermute x3, starting transfers between devices: 8.33 us -> 10.3 us  [reduce_orient(): got = lax.ppermute(send, axis, xor_pairs(n, k))]
    ppermute x3, waiting for transfers between devices: 12.8 us -> 14.5 us  [reduce_orient(): got = lax.ppermute(send, axis, xor_pairs(n, k))]
    ppermute x3, waiting for transfers between devices: 6.06 us -> 7.71 us  [gather_rows(): got = lax.ppermute(blocks, axis, xor_pairs(n, k))]
  transfers between devices with their start and end apart: 10 -> 11, of which waited for: 10 -> 9; matrix products, arithmetic and copies ran while one was open for 15% -> 18% of each run, Pallas kernels for 0% -> 17%
where the time goes in v4:
time: 157 us; the launch traced here: 155 us
  Pallas kernels  53.6 us (34%)
  waiting for transfers between devices  38.7 us (25%)
  other arithmetic  24.6 us (16%)
  starting transfers between devices  18.2 us (12%)
  between operations  14.2 us (9%)
  local copies, waits for them, and re-layouts  6.12 us (4%)
    pallas_call x2, Pallas kernels, match_rows(): pl.pallas_call(kernel, grid_spec=pltpu.PrefetchScalarGridSpec(num_scalar_...  53.6 us
    ppermute x3, waiting for transfers between devices, reduce_orient(): got = lax.ppermute(cur, axis, xor_pairs(n, k))  15.8 us
    ppermute x3, waiting for transfers between devices, reduce_orient(): got = lax.ppermute(send, axis, xor_pairs(n, k))  14.5 us
    ppermute x3, starting transfers between devices, reduce_orient(): got = lax.ppermute(send, axis, xor_pairs(n, k))  10.3 us
    convert_element_type x2, other arithmetic, angle_tables(): jnp.sin(angle).astype(jnp.bfloat16)  10 us
    ppermute x3, waiting for transfers between devices, gather_rows(): got = lax.ppermute(blocks, axis, xor_pairs(n, k))  7.71 us
    ppermute x3, starting transfers between devices, gather_rows(): got = lax.ppermute(blocks, axis, xor_pairs(n, k))  5.89 us
    neg x1, other arithmetic, col_tables(): lower = jnp.concatenate([-sin_col, cos_col], axis=-1)  4.02 us
  transfers between devices with their start and end apart: 11, of which 9 were waited for; matrix products, arithmetic and copies ran while one was open for 18% of the time, Pallas kernels for 17%

profile of v4, /device:TPU:0, one launch (start us, length us, event | category | flops | bytes accessed | tf_op | source)
XLA Modules:
  0.0 155.4 jit_solution(8363082324093157381)
XLA Ops:
  7.2 0.7 all-gather.3.cloned.1.call-update
  7.9 0.8 copy-done
  9.2 3.6 %collective-permute-start = (bf16[1,2,64,512]{3,2,1,0:T(8,128)(2,1)}, bf16[1,2,64,512]{3,2,1,0:T(8,128)(2,1)S(1)}, u32[]{:S(2)}, u32[]{:S(2)}) collective-permute-start(bf16[1,2,64,512]{3,2,1,0:T(8,128)(2,1)} %param.4), channel_id=1, source_target_pairs={{0,4},{1,5},{2,6},{3,7},{4,0},{5,1},{6,2},{7,3},{8,12},{9,13},{10,... | collective-permute-start | bytes 393224 | tf_op jit(solution)/shard_map/ppermute | solution.py:50
  12.8 0.8 slice_bitcast_fusion
  13.7 4.0 %fusion.14 = bf16[4,512,128]{2,1,0:T(8,128)(2,1)S(1)} fusion(s32[4,128]{1,0:T(4,128)S(1)} %get-tuple-element.27), kind=kLoop, calls=%fused_computation.46 | loop fusion | flops 4718592 | bytes 526336 | tf_op jit(solution)/shard_map/neg | solution.py:38
  18.0 2.0 %collective-permute-done = bf16[1,2,64,512]{3,2,1,0:T(8,128)(2,1)S(1)} collective-permute-done((bf16[1,2,64,512]{3,2,1,0:T(8,128)(2,1)}, bf16[1,2,64,512]{3,2,1,0:T(8,128)(2,1)S(1)}, u32[]{:S(2)}, u32[]{:S(2)}) %collective-permute-start) | collective-permute-done | bytes 131104 | tf_op jit(solution)/shard_map/ppermute | solution.py:50
  20.0 0.9 collective-permute-start.1
  22.0 4.4 %sine_convert_fusion.1 = (bf16[4,512,128]{2,1,0:T(8,128)(2,1)S(1)}, bf16[4,512,128]{2,1,0:T(8,128)(2,1)S(1)}) fusion(s32[4,128]{1,0:T(4,128)S(1)} %get-tuple-element.27), kind=kLoop, calls=%fused_computation.21 | loop fusion | flops 4194304 | bytes 1050624 | tf_op jit(solution)/shard_map/convert_element_type | solution.py:31
  26.4 1.8 %collective-permute-done.1 = bf16[2,2,64,512]{3,2,1,0:T(8,128)(2,1)S(1)} collective-permute-done((bf16[2,2,64,512]{3,2,1,0:T(8,128)(2,1)S(1)}, bf16[2,2,64,512]{3,2,1,0:T(8,128)(2,1)S(1)}, u32[]{:S(2)}, u32[]{:S(2)}) %collective-permute-start.1) | collective-permute-done | bytes 262176 | tf_op jit(solution)/shard_map/ppermute | solution.py:50
  28.3 1.4 collective-permute-start.2
  29.7 0.6 pad_add_fusion.rid_ref
  30.3 1.5 maximum_maximum_fusion.ct_ref
  31.9 5.6 %sine_convert_fusion = (bf16[4,128,512]{2,1,0:T(8,128)(2,1)}, bf16[4,128,512]{2,1,0:T(8,128)(2,1)}) fusion(s32[4,128]{1,0:T(4,128)S(1)} %get-tuple-element.26), kind=kLoop, calls=%fused_computation.17 | loop fusion | flops 4194304 | bytes 1050624 | tf_op jit(solution)/shard_map/convert_element_type | solution.py:31
  37.5 3.9 %collective-permute-done.2 = bf16[4,2,64,512]{3,2,1,0:T(8,128)(2,1)S(1)} collective-permute-done((bf16[4,2,64,512]{3,2,1,0:T(8,128)(2,1)S(1)}, bf16[4,2,64,512]{3,2,1,0:T(8,128)(2,1)S(1)}, u32[]{:S(2)}, u32[]{:S(2)}) %collective-permute-start.2) | collective-permute-done | bytes 524320 | tf_op jit(solution)/shard_map/ppermute | solution.py:50
  41.4 1.1 pad_maximum_fusion.1
  42.5 1.8 %gather_fusion = bf16[8,2,64,512]{3,2,1,0:T(8,128)(2,1)S(1)} fusion(bf16[8,2,64,512]{3,2,1,0:T(8,128)(2,1)} %pad_maximum_fusion.1, s32[1024]{0:T(1024)S(1)} %pad_clamp_fusion), kind=kCustom, calls=%fused_computation | custom fusion | bytes 2097184 | tf_op jit(solution)/shard_map/gather | solution.py:54
  44.6 1.6 copy.8
  46.2 4.0 %pad_maximum_fusion.tm_ref = bf16[2,8,2,128,512]{4,3,2,1,0:T(8,128)(2,1)} fusion(bf16[1,8,2,128,512]{4,3,2,1,0:T(8,128)(2,1)} %bitcast.11, bf16[1,8,2,128,512]{4,3,2,1,0:T(8,128)(2,1)S(1)} %bitcast.20), kind=kLoop, calls=%fused_computation.1 | loop fusion | flops 2097152 | bytes 8388608 | tf_op jit(solution)/shard_map/stack | solution.py:276
  50.6 26.5 %shard_map.59.rest_0_ = f32[4,8,128,128]{3,2,1,0:T(8,128)} custom-call(s32[32]{0:T(128)} %reshape.151.f_ref, s32[2]{0:T(128)} %iota.38.tid_ref, s32[2]{0:T(128)} %pad_add_fusion.rid_ref, bf16[2,8,2,128,512]{4,3,2,1,0:T(8,128)(2,1)} %pad_maximum_fusion.tm_ref, f32[2,512,512]{2,1,0:T(8,128)} %bitcast.21, bf16[4,1024,256]{2,1,0:T(8,128)(2,1)} %maximum_maximum_fusion.ct_ref, ...), custom_call_target="tpu_custom_call" | custom-call | flops 4831838208 | bytes 14680064 | tf_op jit(solution)/shard_map/pallas_call | solution.py:238
  77.1 27.1 %shard_map.60 = (f32[4,128,128]{2,1,0:T(8,128)}, f32[4,128,128]{2,1,0:T(8,128)}) custom-call(s32[32]{0:T(128)} %reshape.151.f_ref, s32[2]{0:T(128)} %fusion.22.tid_ref.rid_ref, s32[2]{0:T(128)} %fusion.22.tid_ref.rid_ref, bf16[4,8,2,128,512]{4,3,2,1,0:T(8,128)(2,1)} %bitcast.29, f32[2,512,512]{2,1,0:T(8,128)} %bitcast.22, ...), custom_call_target="tpu_custom_call" | custom-call | flops 4831838208 | bytes 14680064 | tf_op jit(solution)/shard_map/pallas_call | solution.py:238
  104.2 1.1 fusion.13
  105.3 3.4 %collective-permute-start.4 = (f32[2,256,128]{2,1,0:T(8,128)S(1)}, f32[2,256,128]{2,1,0:T(8,128)S(1)}, u32[]{:S(2)}, u32[]{:S(2)}) collective-permute-start(f32[2,256,128]{2,1,0:T(8,128)S(1)} %get-tuple-element.11), channel_id=1, source_target_pairs={{0,1},{1,0},{2,3},{3,2},{4,5},{5,4},{6,7},{7,6},{8,9},{9,8},{10,11... | collective-permute-start | bytes 786440 | tf_op jit(solution)/shard_map/ppermute | solution.py:83
  108.8 6.5 %collective-permute-done.4 = f32[2,256,128]{2,1,0:T(8,128)S(1)} collective-permute-done((f32[2,256,128]{2,1,0:T(8,128)S(1)}, f32[2,256,128]{2,1,0:T(8,128)S(1)}, u32[]{:S(2)}, u32[]{:S(2)}) %collective-permute-start.4) | collective-permute-done | bytes 262176 | tf_op jit(solution)/shard_map/ppermute | solution.py:83
  115.3 1.8 %collective-permute-start.5 = (f32[2,128,128]{2,1,0:T(8,128)S(1)}, f32[2,128,128]{2,1,0:T(8,128)S(1)}, u32[]{:S(2)}, u32[]{:S(2)}) collective-permute-start(f32[2,128,128]{2,1,0:T(8,128)S(1)} %get-tuple-element.15), channel_id=1, source_target_pairs={{0,2},{1,3},{2,0},{3,1},{4,6},{5,7},{6,4},{7,5},{8,10},{9,11},{10,... | collective-permute-start | bytes 393224 | tf_op jit(solution)/shard_map/ppermute | solution.py:83
  117.1 4.2 %collective-permute-done.5 = f32[2,128,128]{2,1,0:T(8,128)S(1)} collective-permute-done((f32[2,128,128]{2,1,0:T(8,128)S(1)}, f32[2,128,128]{2,1,0:T(8,128)S(1)}, u32[]{:S(2)}, u32[]{:S(2)}) %collective-permute-start.5) | collective-permute-done | bytes 131104 | tf_op jit(solution)/shard_map/ppermute | solution.py:83
  121.3 5.1 %collective-permute-start.6 = (f32[2,64,128]{2,1,0:T(8,128)S(1)}, f32[2,64,128]{2,1,0:T(8,128)S(1)}, u32[]{:S(2)}, u32[]{:S(2)}) collective-permute-start(f32[2,64,128]{2,1,0:T(8,128)S(1)} %get-tuple-element.19), channel_id=1, source_target_pairs={{0,4},{1,5},{2,6},{3,7},{4,0},{5,1},{6,2},{7,3},{8,12},{9,13},{10,... | collective-permute-start | bytes 196616 | tf_op jit(solution)/shard_map/ppermute | solution.py:83
  126.4 3.8 %collective-permute-done.6 = f32[2,64,128]{2,1,0:T(8,128)S(1)} collective-permute-done((f32[2,64,128]{2,1,0:T(8,128)S(1)}, f32[2,64,128]{2,1,0:T(8,128)S(1)}, u32[]{:S(2)}, u32[]{:S(2)}) %collective-permute-start.6) | collective-permute-done | bytes 65568 | tf_op jit(solution)/shard_map/ppermute | solution.py:83
  130.2 1.5 collective-permute-start.7
  131.7 4.5 %collective-permute-done.7 = f32[2,64,128]{2,1,0:T(8,128)S(1)} collective-permute-done((f32[2,64,128]{2,1,0:T(8,128)S(1)}, f32[2,64,128]{2,1,0:T(8,128)S(1)}, u32[]{:S(2)}, u32[]{:S(2)}) %collective-permute-start.7) | collective-permute-done | bytes 65568 | tf_op jit(solution)/shard_map/ppermute | solution.py:88
  136.3 4.9 %collective-permute-done.8 = f32[2,128,128]{2,1,0:T(8,128)S(1)} collective-permute-done((f32[2,128,128]{2,1,0:T(8,128)S(1)}, f32[2,128,128]{2,1,0:T(8,128)S(1)}, u32[]{:S(2)}, u32[]{:S(2)}) %collective-permute-start.8) | collective-permute-done | bytes 131104 | tf_op jit(solution)/shard_map/ppermute | solution.py:88
  141.3 6.4 %collective-permute-done.9 = f32[2,256,128]{2,1,0:T(8,128)S(1)} collective-permute-done((f32[2,256,128]{2,1,0:T(8,128)S(1)}, f32[2,256,128]{2,1,0:T(8,128)S(1)}, u32[]{:S(2)}, u32[]{:S(2)}) %collective-permute-start.9) | collective-permute-done | bytes 262176 | tf_op jit(solution)/shard_map/ppermute | solution.py:88
  147.7 0.8 slice_multiply_fusion
  (33 shorter events, 3.1 us)
Async XLA Ops:
  7.2 1.6 %copy-start = (bf16[8,2,128,512]{3,2,1,0:T(8,128)(2,1)S(1)}, bf16[8,2,128,512]{3,2,1,0:T(8,128)(2,1)}, u32[]{:S(2)}) copy-start(bf16[8,2,128,512]{3,2,1,0:T(8,128)(2,1)} %param.5) | copy-start | bytes 6291460
  7.2 12.8 %copy-start.1 = (bf16[1,2,64,512]{3,2,1,0:T(8,128)(2,1)S(1)}, bf16[1,2,64,512]{3,2,1,0:T(8,128)(2,1)}, u32[]{:S(2)}) copy-start(bf16[1,2,64,512]{3,2,1,0:T(8,128)(2,1)} %param.4) | copy-start | bytes 393220
  7.2 10.6 %copy-start.2 = (s32[1,4,48]{2,1,0:T(4,128)S(1)}, s32[1,4,48]{2,1,0:T(4,128)}, u32[]{:S(2)}) copy-start(s32[1,4,48]{2,1,0:T(4,128)} %param.7) | copy-start | bytes 2308
  7.2 69.9 %all-gather.3.cloned.1.call-start = ((), (), s32[]{:S(2)}) async-start(), calls=%async_computation | async-start | bytes 10485760 | tf_op jit(solution)/shard_map/all_gather | solution.py:258
  8.8 37.4 %collective-permute-start.3 = (bf16[8,2,128,512]{3,2,1,0:T(8,128)(2,1)S(1)}, bf16[8,2,128,512]{3,2,1,0:T(8,128)(2,1)}, u32[]{:S(2)}, u32[]{:S(2)}) collective-permute-start(bf16[8,2,128,512]{3,2,1,0:T(8,128)(2,1)S(1)} %copy-done), channel_id=1, source_target_pairs={{0,8},{8,0},{16,24},{24,16},{1,9},{9,1},{17,25},{25,17},{2,10},{10... | collective-permute-start | bytes 6291464 | tf_op jit(solution)/shard_map/ppermute | solution.py:275
  9.2 10.8 %collective-permute-start = (bf16[1,2,64,512]{3,2,1,0:T(8,128)(2,1)}, bf16[1,2,64,512]{3,2,1,0:T(8,128)(2,1)S(1)}, u32[]{:S(2)}, u32[]{:S(2)}) collective-permute-start(bf16[1,2,64,512]{3,2,1,0:T(8,128)(2,1)} %param.4), channel_id=1, source_target_pairs={{0,4},{1,5},{2,6},{3,7},{4,0},{5,1},{6,2},{7,3},{8,12},{9,13},{10,... | collective-permute-start | bytes 393224 | tf_op jit(solution)/shard_map/ppermute | solution.py:50
  20.0 8.2 %collective-permute-start.1 = (bf16[2,2,64,512]{3,2,1,0:T(8,128)(2,1)S(1)}, bf16[2,2,64,512]{3,2,1,0:T(8,128)(2,1)S(1)}, u32[]{:S(2)}, u32[]{:S(2)}) collective-permute-start(bf16[2,2,64,512]{3,2,1,0:T(8,128)(2,1)S(1)} %pad_maximum_fusion.3), channel_id=1, source_target_pairs={{0,2},{1,3},{2,0},{3,1},{4,6},{5,7},{6,4},{7,5},{8,10},{9,11},{10,... | collective-permute-start | bytes 786440 | tf_op jit(solution)/shard_map/ppermute | solution.py:50
  28.3 13.1 %collective-permute-start.2 = (bf16[4,2,64,512]{3,2,1,0:T(8,128)(2,1)S(1)}, bf16[4,2,64,512]{3,2,1,0:T(8,128)(2,1)S(1)}, u32[]{:S(2)}, u32[]{:S(2)}) collective-permute-start(bf16[4,2,64,512]{3,2,1,0:T(8,128)(2,1)S(1)} %pad_maximum_fusion.2), channel_id=1, source_target_pairs={{0,1},{1,0},{2,3},{3,2},{4,5},{5,4},{6,7},{7,6},{8,9},{9,8},{10,11... | collective-permute-start | bytes 1572872 | tf_op jit(solution)/shard_map/ppermute | solution.py:50
  105.3 9.9 %collective-permute-start.4 = (f32[2,256,128]{2,1,0:T(8,128)S(1)}, f32[2,256,128]{2,1,0:T(8,128)S(1)}, u32[]{:S(2)}, u32[]{:S(2)}) collective-permute-start(f32[2,256,128]{2,1,0:T(8,128)S(1)} %get-tuple-element.11), channel_id=1, source_target_pairs={{0,1},{1,0},{2,3},{3,2},{4,5},{5,4},{6,7},{7,6},{8,9},{9,8},{10,11... | collective-permute-start | bytes 786440 | tf_op jit(solution)/shard_map/ppermute | solution.py:83
  115.3 6.0 %collective-permute-start.5 = (f32[2,128,128]{2,1,0:T(8,128)S(1)}, f32[2,128,128]{2,1,0:T(8,128)S(1)}, u32[]{:S(2)}, u32[]{:S(2)}) collective-permute-start(f32[2,128,128]{2,1,0:T(8,128)S(1)} %get-tuple-element.15), channel_id=1, source_target_pairs={{0,2},{1,3},{2,0},{3,1},{4,6},{5,7},{6,4},{7,5},{8,10},{9,11},{10,... | collective-permute-start | bytes 393224 | tf_op jit(solution)/shard_map/ppermute | solution.py:83
  121.3 8.9 %collective-permute-start.6 = (f32[2,64,128]{2,1,0:T(8,128)S(1)}, f32[2,64,128]{2,1,0:T(8,128)S(1)}, u32[]{:S(2)}, u32[]{:S(2)}) collective-permute-start(f32[2,64,128]{2,1,0:T(8,128)S(1)} %get-tuple-element.19), channel_id=1, source_target_pairs={{0,4},{1,5},{2,6},{3,7},{4,0},{5,1},{6,2},{7,3},{8,12},{9,13},{10,... | collective-permute-start | bytes 196616 | tf_op jit(solution)/shard_map/ppermute | solution.py:83
  130.2 5.9 %collective-permute-start.7 = (f32[2,64,128]{2,1,0:T(8,128)S(1)}, f32[2,64,128]{2,1,0:T(8,128)S(1)}, u32[]{:S(2)}, u32[]{:S(2)}) collective-permute-start(f32[2,64,128]{2,1,0:T(8,128)S(1)} %pad_maximum_fusion.4), channel_id=1, source_target_pairs={{0,4},{1,5},{2,6},{3,7},{4,0},{5,1},{6,2},{7,3},{8,12},{9,13},{10,... | collective-permute-start | bytes 196616 | tf_op jit(solution)/shard_map/ppermute | solution.py:88
  136.2 5.0 %collective-permute-start.8 = (f32[2,128,128]{2,1,0:T(8,128)S(1)}, f32[2,128,128]{2,1,0:T(8,128)S(1)}, u32[]{:S(2)}, u32[]{:S(2)}) collective-permute-start(f32[2,128,128]{2,1,0:T(8,128)S(1)} %maximum_select_fusion.2), channel_id=1, source_target_pairs={{0,2},{1,3},{2,0},{3,1},{4,6},{5,7},{6,4},{7,5},{8,10},{9,11},{10,... | collective-permute-start | bytes 393224 | tf_op jit(solution)/shard_map/ppermute | solution.py:88
  141.2 6.4 %collective-permute-start.9 = (f32[2,256,128]{2,1,0:T(8,128)S(1)}, f32[2,256,128]{2,1,0:T(8,128)S(1)}, u32[]{:S(2)}, u32[]{:S(2)}) collective-permute-start(f32[2,256,128]{2,1,0:T(8,128)S(1)} %maximum_select_fusion.1), channel_id=1, source_target_pairs={{0,1},{1,0},{2,3},{3,2},{4,5},{5,4},{6,7},{7,6},{8,9},{9,8},{10,11... | collective-permute-start | bytes 786440 | tf_op jit(solution)/shard_map/ppermute | solution.py:88
Sparse Core Ops, SparseCore 0:
  9.6 60.9 all-gather.2

commit v5 on v4

--- a/solution.py
+++ b/solution.py
@@ -153,7 +153,7 @@
     )(flags, tmpl, spec, col_table, cos_t, sin_t)
 
 
-def rows_kernel(blocks, size, width, rows_t, peaks_n, chunk, n_steps, final, f_ref, tid_ref, rid_ref, tm_ref, sp_ref, ct_ref, cr_ref, sr_ref, *rest):
+def rows_kernel(blocks, size, width, rows_t, peaks_n, chunk, n_steps, final, f_ref, ta_ref, tb_ref, rid_ref, tma_ref, tmb_ref, sp_ref, ct_ref, cr_ref, sr_ref, *rest):
     if final:
         init_ref, best_ref, pow_ref, acc_ref, m_ref = rest
     else:
@@ -175,17 +175,19 @@
         def _():
             acc_ref[...] = jnp.zeros(acc_ref.shape, jnp.float32)
 
-    def mix(c, carry):
-        row = pl.multiple_of(c * chunk, chunk)
-        image_re = sp_ref[0, pl.ds(row, chunk), :]
-        image_im = sp_ref[1, pl.ds(row, chunk), :]
-        tmpl_re = tm_ref[0, 0, 0, pl.ds(row, chunk), :].astype(jnp.float32)
-        tmpl_im = tm_ref[0, 0, 1, pl.ds(row, chunk), :].astype(jnp.float32)
-        m_ref[pl.ds(row, chunk), pl.ds(0, size)] = (image_re * tmpl_re + image_im * tmpl_im).astype(jnp.bfloat16)
-        m_ref[pl.ds(row, chunk), pl.ds(size, size)] = (image_im * tmpl_re - image_re * tmpl_im).astype(jnp.bfloat16)
-        return carry
-
-    lax.fori_loop(0, rows_t // chunk, mix, 0, unroll=4)
+    for u, tm_ref in enumerate((tma_ref, tmb_ref)):
+        def mix(c, carry, u=u, tm_ref=tm_ref):
+            row = pl.multiple_of(c * chunk, chunk)
+            out_row = pl.multiple_of(u * rows_t + c * chunk, chunk)
+            image_re = sp_ref[0, pl.ds(out_row, chunk), :]
+            image_im = sp_ref[1, pl.ds(out_row, chunk), :]
+            tmpl_re = tm_ref[0, 0, 0, pl.ds(row, chunk), :].astype(jnp.float32)
+            tmpl_im = tm_ref[0, 0, 1, pl.ds(row, chunk), :].astype(jnp.float32)
+            m_ref[pl.ds(out_row, chunk), pl.ds(0, size)] = (image_re * tmpl_re + image_im * tmpl_im).astype(jnp.bfloat16)
+            m_ref[pl.ds(out_row, chunk), pl.ds(size, size)] = (image_im * tmpl_re - image_re * tmpl_im).astype(jnp.bfloat16)
+            return carry
+
+        lax.fori_loop(0, rows_t // chunk, mix, 0, unroll=4)
 
     for p in range(peaks_n):
         @pl.when(f_ref[p * blocks + j] > 0)
@@ -208,41 +210,43 @@
             part_ref[:, 0] = acc_ref[...]
 
 
-def match_rows(flags, tids, rids, tmpl, spec, col_table, cos_t, sin_t, init=None):
-    _, blocks, _, rows_t, size = tmpl.shape
+def match_rows(flags, tas, tbs, rids, tmpl_a, tmpl_b, spec, col_table, cos_t, sin_t, init=None):
+    _, blocks, _, rows_t, size = tmpl_a.shape
     peaks_n, width = cos_t.shape[0], cos_t.shape[1]
-    n_steps = tids.shape[0]
+    n_steps = tas.shape[0]
     final = init is not None
     chunk = math.gcd(rows_t, 16)
+    span = 2 * rows_t
     kernel = functools.partial(rows_kernel, blocks, size, width, rows_t, peaks_n, chunk, n_steps, final)
-    flops = blocks * peaks_n * n_steps * (2 * rows_t * 2 * size * 2 * width + 2 * 2 * width * rows_t * width)
-    cost = pl.CostEstimate(flops=flops, transcendentals=0, bytes_accessed=n_steps * blocks * 2 * rows_t * size * 6 + col_table.size * 2)
+    flops = blocks * peaks_n * n_steps * (2 * span * 2 * size * 2 * width + 2 * 2 * width * span * width)
+    cost = pl.CostEstimate(flops=flops, transcendentals=0, bytes_accessed=n_steps * blocks * 2 * span * size * 6 + col_table.size * 2)
     in_specs = [
-        pl.BlockSpec((1, 1, 2, rows_t, size), lambda j, i, f, t, r: (t[i], j, 0, 0, 0)),
-        pl.BlockSpec((2, rows_t, size), lambda j, i, f, t, r: (0, r[i], 0)),
-        pl.BlockSpec(col_table.shape, lambda j, i, f, t, r: (0, 0, 0)),
-        pl.BlockSpec((peaks_n, width, rows_t), lambda j, i, f, t, r: (0, 0, r[i])),
-        pl.BlockSpec((peaks_n, width, rows_t), lambda j, i, f, t, r: (0, 0, r[i])),
+        pl.BlockSpec((1, 1, 2, rows_t, size), lambda j, i, f, ta, tb, r: (ta[i], j, 0, 0, 0)),
+        pl.BlockSpec((1, 1, 2, rows_t, size), lambda j, i, f, ta, tb, r: (tb[i], j, 0, 0, 0)),
+        pl.BlockSpec((2, span, size), lambda j, i, f, ta, tb, r: (0, r[i], 0)),
+        pl.BlockSpec(col_table.shape, lambda j, i, f, ta, tb, r: (0, 0, 0)),
+        pl.BlockSpec((peaks_n, width, span), lambda j, i, f, ta, tb, r: (0, 0, r[i])),
+        pl.BlockSpec((peaks_n, width, span), lambda j, i, f, ta, tb, r: (0, 0, r[i])),
     ]
-    args = [flags, tids, rids, tmpl, spec, col_table, cos_t, sin_t]
-    part_spec = pl.BlockSpec((peaks_n, 1, width, width), lambda j, i, f, t, r: (0, j, 0, 0))
+    args = [flags, tas, tbs, rids, tmpl_a, tmpl_b, spec, col_table, cos_t, sin_t]
+    part_spec = pl.BlockSpec((peaks_n, 1, width, width), lambda j, i, f, ta, tb, r: (0, j, 0, 0))
     if final:
         in_specs.append(part_spec)
         args.append(init)
         out = jax.ShapeDtypeStruct((peaks_n, width, width), jnp.float32)
         out_shape = [out, out]
-        out_specs = [pl.BlockSpec((peaks_n, width, width), lambda j, i, f, t, r: (0, 0, 0))] * 2
+        out_specs = [pl.BlockSpec((peaks_n, width, width), lambda j, i, f, ta, tb, r: (0, 0, 0))] * 2
     else:
         out_shape = jax.ShapeDtypeStruct((peaks_n, blocks, width, width), jnp.float32)
         out_specs = part_spec
     return pl.pallas_call(
         kernel,
         grid_spec=pltpu.PrefetchScalarGridSpec(
-            num_scalar_prefetch=3,
+            num_scalar_prefetch=4,
             grid=(blocks, n_steps),
             in_specs=in_specs,
             out_specs=out_specs,
-            scratch_shapes=[pltpu.VMEM((peaks_n, width, width), jnp.float32), pltpu.VMEM((rows_t, 2 * size), jnp.bfloat16)],
+            scratch_shapes=[pltpu.VMEM((peaks_n, width, width), jnp.float32), pltpu.VMEM((span, 2 * size), jnp.bfloat16)],
         ),
         out_shape=out_shape,
         compiler_params=pltpu.CompilerParams(dimension_semantics=("arbitrary", "arbitrary")),
@@ -275,20 +279,18 @@
         sibling = lax.ppermute(template_spectra, "tile", xor_pairs(tiles, 1))
         near = jnp.stack([template_spectra, sibling])
         spec32 = spec.astype(jnp.float32)
-        near_rows = jnp.stack([me, me ^ 1]).astype(jnp.int32)
-        partial = match_rows(flags, jnp.arange(2, dtype=jnp.int32), near_rows, near, spec32, col_table, cos_t, sin_t)
-        far_rows = far_blocks(me, tiles)
-        best_part, power_part = match_rows(flags, far_rows, far_rows, tmpl, spec32, col_table, cos_t, sin_t, init=partial)
+        chip = me // 2
+        odd = (me % 2)[None].astype(jnp.int32)
+        partial = match_rows(flags, odd, 1 - odd, chip[None].astype(jnp.int32), near, near, spec32, col_table, cos_t, sin_t)
+        far = far_chips(chip, tiles // 2)
+        best_part, power_part = match_rows(flags, far * 2, far * 2 + 1, far, tmpl, tmpl, spec32, col_table, cos_t, sin_t, init=partial)
     best_all, power_all = reduce_orient(best_part, power_part, "orient")
     return (best_all[None], (power_all / LIST)[None])
 
 
-def far_blocks(me, tiles):
-    steps = jnp.arange(tiles - 2, dtype=jnp.int32)
-    pair = steps // 2
-    chip = me // 2
-    pair = pair + (pair >= chip).astype(jnp.int32)
-    return pair * 2 + steps % 2
+def far_chips(chip, chips):
+    steps = jnp.arange(chips - 1, dtype=jnp.int32)
+    return steps + (steps >= chip).astype(jnp.int32)
 
 
 def solution(mesh):

time: 157 us -> 137 us (0.87); the launches traced: 155 us -> 137 us
  Pallas kernels: 53.6 us -> 40 us
  starting transfers between devices: 18.2 us -> 9.37 us
  waiting for transfers between devices: 38.7 us -> 44.4 us
    pallas_call x2, Pallas kernels: 53.6 us -> 40 us  [match_rows(): pl.pallas_call(kernel, grid_spec=pltpu.PrefetchScalarGridSpec(num_scalar_...]
    ppermute x3, starting transfers between devices: 10.3 us -> 1.12 us  [reduce_orient(): got = lax.ppermute(send, axis, xor_pairs(n, k))]
    ppermute x3, waiting for transfers between devices: 14.5 us -> 18.7 us  [reduce_orient(): got = lax.ppermute(send, axis, xor_pairs(n, k))]
  transfers between devices with their start and end apart: 11 -> 11, of which waited for: 9 -> 10; matrix products, arithmetic and copies ran while one was open for 18% -> 19% of each run, Pallas kernels for 17% -> 14%
where the time goes in v5:
time: 137 us
  waiting for transfers between devices  44.4 us (32%)
  Pallas kernels  40 us (29%)
  other arithmetic  23.4 us (17%)
  between operations  14.3 us (10%)
  starting transfers between devices  9.37 us (7%)
  local copies, waits for them, and re-layouts  5.6 us (4%)
    pallas_call x2, Pallas kernels, match_rows(): pl.pallas_call(kernel, grid_spec=pltpu.PrefetchScalarGridSpec(num_scalar_...  40 us
    ppermute x3, waiting for transfers between devices, reduce_orient(): got = lax.ppermute(send, axis, xor_pairs(n, k))  18.7 us
    ppermute x3, waiting for transfers between devices, reduce_orient(): got = lax.ppermute(cur, axis, xor_pairs(n, k))  15.3 us
    convert_element_type x2, other arithmetic, angle_tables(): jnp.sin(angle).astype(jnp.bfloat16)  10 us
    ppermute x3, waiting for transfers between devices, gather_rows(): got = lax.ppermute(blocks, axis, xor_pairs(n, k))  8.88 us
    ppermute x3, starting transfers between devices, gather_rows(): got = lax.ppermute(blocks, axis, xor_pairs(n, k))  5.89 us
    neg x1, other arithmetic, col_tables(): lower = jnp.concatenate([-sin_col, cos_col], axis=-1)  4 us
    another operation x1, other arithmetic, local(): near = jnp.stack([template_spectra, sibling])  3.96 us
  transfers between devices with their start and end apart: 11, of which 10 were waited for; matrix products, arithmetic and copies ran while one was open for 19% of the time, Pallas kernels for 14%

profile of v5, /device:TPU:0, one launch (start us, length us, event | category | flops | bytes accessed | tf_op | source)
XLA Modules:
  0.0 137.1 jit_solution(3349473313273172562)
XLA Ops:
  7.2 0.7 all-gather.3.cloned.1.call-update
  7.9 0.8 copy-done
  8.8 0.5 collective-permute-start.3
  9.2 3.6 %collective-permute-start = (bf16[1,2,64,512]{3,2,1,0:T(8,128)(2,1)}, bf16[1,2,64,512]{3,2,1,0:T(8,128)(2,1)S(1)}, u32[]{:S(2)}, u32[]{:S(2)}) collective-permute-start(bf16[1,2,64,512]{3,2,1,0:T(8,128)(2,1)} %param.4), channel_id=1, source_target_pairs={{0,4},{1,5},{2,6},{3,7},{4,0},{5,1},{6,2},{7,3},{8,12},{9,13},{10,... | collective-permute-start | bytes 393224 | tf_op jit(solution)/shard_map/ppermute | solution.py:50
  12.8 0.8 slice_bitcast_fusion
  13.7 4.0 %fusion.14 = bf16[4,512,128]{2,1,0:T(8,128)(2,1)S(1)} fusion(s32[4,128]{1,0:T(4,128)S(1)} %get-tuple-element.27), kind=kLoop, calls=%fused_computation.46 | loop fusion | flops 4718592 | bytes 526336 | tf_op jit(solution)/shard_map/neg | solution.py:38
  17.9 2.1 %collective-permute-done = bf16[1,2,64,512]{3,2,1,0:T(8,128)(2,1)S(1)} collective-permute-done((bf16[1,2,64,512]{3,2,1,0:T(8,128)(2,1)}, bf16[1,2,64,512]{3,2,1,0:T(8,128)(2,1)S(1)}, u32[]{:S(2)}, u32[]{:S(2)}) %collective-permute-start) | collective-permute-done | bytes 131104 | tf_op jit(solution)/shard_map/ppermute | solution.py:50
  20.0 0.9 collective-permute-start.1
  20.9 0.6 reshape.152.f_ref
  21.5 4.4 %sine_convert_fusion.1 = (bf16[4,512,128]{2,1,0:T(8,128)(2,1)S(1)}, bf16[4,512,128]{2,1,0:T(8,128)(2,1)S(1)}) fusion(s32[4,128]{1,0:T(4,128)S(1)} %get-tuple-element.27), kind=kLoop, calls=%fused_computation.21 | loop fusion | flops 4194304 | bytes 1050624 | tf_op jit(solution)/shard_map/convert_element_type | solution.py:31
  25.9 2.3 %collective-permute-done.1 = bf16[2,2,64,512]{3,2,1,0:T(8,128)(2,1)S(1)} collective-permute-done((bf16[2,2,64,512]{3,2,1,0:T(8,128)(2,1)S(1)}, bf16[2,2,64,512]{3,2,1,0:T(8,128)(2,1)S(1)}, u32[]{:S(2)}, u32[]{:S(2)}) %collective-permute-start.1) | collective-permute-done | bytes 262176 | tf_op jit(solution)/shard_map/ppermute | solution.py:50
  28.3 1.4 %collective-permute-start.2 = (bf16[4,2,64,512]{3,2,1,0:T(8,128)(2,1)S(1)}, bf16[4,2,64,512]{3,2,1,0:T(8,128)(2,1)S(1)}, u32[]{:S(2)}, u32[]{:S(2)}) collective-permute-start(bf16[4,2,64,512]{3,2,1,0:T(8,128)(2,1)S(1)} %pad_maximum_fusion.2), channel_id=1, source_target_pairs={{0,1},{1,0},{2,3},{3,2},{4,5},{5,4},{6,7},{7,6},{8,9},{9,8},{10,11... | collective-permute-start | bytes 1572872 | tf_op jit(solution)/shard_map/ppermute | solution.py:50
  29.7 1.5 %maximum_maximum_fusion.ct_ref = bf16[4,1024,256]{2,1,0:T(8,128)(2,1)} fusion(bf16[4,512,128]{2,1,0:T(8,128)(2,1)S(1)} %get-tuple-element.23, bf16[4,512,128]{2,1,0:T(8,128)(2,1)S(1)} %fusion.14, bf16[4,512,128]{2,1,0:T(8,128)(2,1)S(1)} %get-tuple-element.22), kind=kLoop, calls=%fused_computation.2 | loop fusion | flops 8388608 | bytes 3670016 | tf_op jit(solution)/shard_map/concatenate | solution.py:39
  31.2 5.6 %sine_convert_fusion = (bf16[4,128,512]{2,1,0:T(8,128)(2,1)}, bf16[4,128,512]{2,1,0:T(8,128)(2,1)}) fusion(s32[4,128]{1,0:T(4,128)S(1)} %get-tuple-element.26), kind=kLoop, calls=%fused_computation.17 | loop fusion | flops 4194304 | bytes 1050624 | tf_op jit(solution)/shard_map/convert_element_type | solution.py:31
  36.9 4.5 %collective-permute-done.2 = bf16[4,2,64,512]{3,2,1,0:T(8,128)(2,1)S(1)} collective-permute-done((bf16[4,2,64,512]{3,2,1,0:T(8,128)(2,1)S(1)}, bf16[4,2,64,512]{3,2,1,0:T(8,128)(2,1)S(1)}, u32[]{:S(2)}, u32[]{:S(2)}) %collective-permute-start.2) | collective-permute-done | bytes 524320 | tf_op jit(solution)/shard_map/ppermute | solution.py:50
  41.4 1.1 pad_maximum_fusion.1
  42.5 1.8 %gather_fusion = bf16[8,2,64,512]{3,2,1,0:T(8,128)(2,1)S(1)} fusion(bf16[8,2,64,512]{3,2,1,0:T(8,128)(2,1)} %pad_maximum_fusion.1, s32[1024]{0:T(1024)S(1)} %pad_clamp_fusion), kind=kCustom, calls=%fused_computation | custom fusion | bytes 2097184 | tf_op jit(solution)/shard_map/gather | solution.py:54
  44.6 1.6 %copy.8 = f32[2,8,64,512]{3,2,1,0:T(8,128)} copy(f32[2,8,64,512]{3,2,0,1:T(8,128)S(1)} %convert_bitcast_fusion) | data formatting | bytes 4194304 | tf_op jit(solution)/shard_map/convert_element_type | solution.py:281
  46.2 4.0 %pad_maximum_fusion.tma_ref.tmb_ref = bf16[2,8,2,128,512]{4,3,2,1,0:T(8,128)(2,1)} fusion(bf16[1,8,2,128,512]{4,3,2,1,0:T(8,128)(2,1)} %bitcast.11, bf16[1,8,2,128,512]{4,3,2,1,0:T(8,128)(2,1)S(1)} %bitcast.24), kind=kLoop, calls=%fused_computation.1 | loop fusion | flops 2097152 | bytes 8388608 | tf_op jit(solution)/shard_map/stack | solution.py:280
  50.1 19.7 %shard_map.59.rest_0_ = f32[4,8,128,128]{3,2,1,0:T(8,128)} custom-call(s32[32]{0:T(128)} %reshape.152.f_ref, s32[1]{0:T(128)} %bitcast.9.ta_ref, s32[1]{0:T(128)S(6)} %sub.36.tb_ref, s32[1]{0:T(128)} %bitcast.1.rid_ref, bf16[2,8,2,128,512]{4,3,2,1,0:T(8,128)(2,1)} %pad_maximum_fusion.tma_ref.tmb_ref, ...), custom_call_target="tpu_custom_call" | custom-call | flops 4831838208 | bytes 14680064 | tf_op jit(solution)/shard_map/pallas_call | solution.py:242
  69.8 0.8 all-gather.3.cloned.1.call-done
  70.6 20.3 %shard_map.60 = (f32[4,128,128]{2,1,0:T(8,128)}, f32[4,128,128]{2,1,0:T(8,128)}) custom-call(s32[32]{0:T(128)} %reshape.152.f_ref, s32[1]{0:T(128)S(6)} %mul.62.ta_ref, s32[1]{0:T(128)S(6)} %add.151.tb_ref, s32[1]{0:T(128)S(6)} %convert_element_type.41.rid_ref, bf16[4,8,2,128,512]{4,3,2,1,0:T(8,128)(2,1)} %bitcast.20, bf16[4,8,2,128,512]{4,3,2,1,0:T(8,128)(2,1)} %bitcast.21, ...), custom_call_target="tpu_custom_call" | custom-call | flops 4831838208 | bytes 14680064 | tf_op jit(solution)/shard_map/pallas_call | solution.py:242
  91.0 1.1 fusion.13
  92.2 8.7 %collective-permute-done.4 = f32[2,256,128]{2,1,0:T(8,128)S(1)} collective-permute-done((f32[2,256,128]{2,1,0:T(8,128)S(1)}, f32[2,256,128]{2,1,0:T(8,128)S(1)}, u32[]{:S(2)}, u32[]{:S(2)}) %collective-permute-start.4) | collective-permute-done | bytes 262176 | tf_op jit(solution)/shard_map/ppermute | solution.py:83
  101.1 5.1 %collective-permute-done.5 = f32[2,128,128]{2,1,0:T(8,128)S(1)} collective-permute-done((f32[2,128,128]{2,1,0:T(8,128)S(1)}, f32[2,128,128]{2,1,0:T(8,128)S(1)}, u32[]{:S(2)}, u32[]{:S(2)}) %collective-permute-start.5) | collective-permute-done | bytes 131104 | tf_op jit(solution)/shard_map/ppermute | solution.py:83
  106.2 1.0 collective-permute-start.6
  107.2 5.0 %collective-permute-done.6 = f32[2,64,128]{2,1,0:T(8,128)S(1)} collective-permute-done((f32[2,64,128]{2,1,0:T(8,128)S(1)}, f32[2,64,128]{2,1,0:T(8,128)S(1)}, u32[]{:S(2)}, u32[]{:S(2)}) %collective-permute-start.6) | collective-permute-done | bytes 65568 | tf_op jit(solution)/shard_map/ppermute | solution.py:83
  112.5 5.3 %collective-permute-done.7 = f32[2,64,128]{2,1,0:T(8,128)S(1)} collective-permute-done((f32[2,64,128]{2,1,0:T(8,128)S(1)}, f32[2,64,128]{2,1,0:T(8,128)S(1)}, u32[]{:S(2)}, u32[]{:S(2)}) %collective-permute-start.7) | collective-permute-done | bytes 65568 | tf_op jit(solution)/shard_map/ppermute | solution.py:88
  118.1 4.8 %collective-permute-done.8 = f32[2,128,128]{2,1,0:T(8,128)S(1)} collective-permute-done((f32[2,128,128]{2,1,0:T(8,128)S(1)}, f32[2,128,128]{2,1,0:T(8,128)S(1)}, u32[]{:S(2)}, u32[]{:S(2)}) %collective-permute-start.8) | collective-permute-done | bytes 131104 | tf_op jit(solution)/shard_map/ppermute | solution.py:88
  122.9 1.3 collective-permute-start.9
  124.3 5.1 %collective-permute-done.9 = f32[2,256,128]{2,1,0:T(8,128)S(1)} collective-permute-done((f32[2,256,128]{2,1,0:T(8,128)S(1)}, f32[2,256,128]{2,1,0:T(8,128)S(1)}, u32[]{:S(2)}, u32[]{:S(2)}) %collective-permute-start.9) | collective-permute-done | bytes 262176 | tf_op jit(solution)/shard_map/ppermute | solution.py:88
  129.4 0.8 slice_multiply_fusion
  (30 shorter events, 1.6 us)
Async XLA Ops:
  7.2 1.6 %copy-start = (bf16[8,2,128,512]{3,2,1,0:T(8,128)(2,1)S(1)}, bf16[8,2,128,512]{3,2,1,0:T(8,128)(2,1)}, u32[]{:S(2)}) copy-start(bf16[8,2,128,512]{3,2,1,0:T(8,128)(2,1)} %param.5) | copy-start | bytes 6291460
  7.2 12.8 %copy-start.1 = (bf16[1,2,64,512]{3,2,1,0:T(8,128)(2,1)S(1)}, bf16[1,2,64,512]{3,2,1,0:T(8,128)(2,1)}, u32[]{:S(2)}) copy-start(bf16[1,2,64,512]{3,2,1,0:T(8,128)(2,1)} %param.4) | copy-start | bytes 393220
  7.2 10.5 %copy-start.2 = (s32[1,4,48]{2,1,0:T(4,128)S(1)}, s32[1,4,48]{2,1,0:T(4,128)}, u32[]{:S(2)}) copy-start(s32[1,4,48]{2,1,0:T(4,128)} %param.7) | copy-start | bytes 2308
  7.2 63.4 %all-gather.3.cloned.1.call-start = ((), (), s32[]{:S(2)}) async-start(), calls=%async_computation | async-start | bytes 10485760 | tf_op jit(solution)/shard_map/all_gather | solution.py:262
  8.8 37.4 %collective-permute-start.3 = (bf16[8,2,128,512]{3,2,1,0:T(8,128)(2,1)S(1)}, bf16[8,2,128,512]{3,2,1,0:T(8,128)(2,1)}, u32[]{:S(2)}, u32[]{:S(2)}) collective-permute-start(bf16[8,2,128,512]{3,2,1,0:T(8,128)(2,1)S(1)} %copy-done), channel_id=1, source_target_pairs={{0,8},{8,0},{16,24},{24,16},{1,9},{9,1},{17,25},{25,17},{2,10},{10... | collective-permute-start | bytes 6291464 | tf_op jit(solution)/shard_map/ppermute | solution.py:279
  9.2 10.8 %collective-permute-start = (bf16[1,2,64,512]{3,2,1,0:T(8,128)(2,1)}, bf16[1,2,64,512]{3,2,1,0:T(8,128)(2,1)S(1)}, u32[]{:S(2)}, u32[]{:S(2)}) collective-permute-start(bf16[1,2,64,512]{3,2,1,0:T(8,128)(2,1)} %param.4), channel_id=1, source_target_pairs={{0,4},{1,5},{2,6},{3,7},{4,0},{5,1},{6,2},{7,3},{8,12},{9,13},{10,... | collective-permute-start | bytes 393224 | tf_op jit(solution)/shard_map/ppermute | solution.py:50
  20.0 8.2 %collective-permute-start.1 = (bf16[2,2,64,512]{3,2,1,0:T(8,128)(2,1)S(1)}, bf16[2,2,64,512]{3,2,1,0:T(8,128)(2,1)S(1)}, u32[]{:S(2)}, u32[]{:S(2)}) collective-permute-start(bf16[2,2,64,512]{3,2,1,0:T(8,128)(2,1)S(1)} %pad_maximum_fusion.3), channel_id=1, source_target_pairs={{0,2},{1,3},{2,0},{3,1},{4,6},{5,7},{6,4},{7,5},{8,10},{9,11},{10,... | collective-permute-start | bytes 786440 | tf_op jit(solution)/shard_map/ppermute | solution.py:50
  28.3 13.1 %collective-permute-start.2 = (bf16[4,2,64,512]{3,2,1,0:T(8,128)(2,1)S(1)}, bf16[4,2,64,512]{3,2,1,0:T(8,128)(2,1)S(1)}, u32[]{:S(2)}, u32[]{:S(2)}) collective-permute-start(bf16[4,2,64,512]{3,2,1,0:T(8,128)(2,1)S(1)} %pad_maximum_fusion.2), channel_id=1, source_target_pairs={{0,1},{1,0},{2,3},{3,2},{4,5},{5,4},{6,7},{7,6},{8,9},{9,8},{10,11... | collective-permute-start | bytes 1572872 | tf_op jit(solution)/shard_map/ppermute | solution.py:50
  92.1 8.8 %collective-permute-start.4 = (f32[2,256,128]{2,1,0:T(8,128)S(1)}, f32[2,256,128]{2,1,0:T(8,128)S(1)}, u32[]{:S(2)}, u32[]{:S(2)}) collective-permute-start(f32[2,256,128]{2,1,0:T(8,128)S(1)} %get-tuple-element.11), channel_id=1, source_target_pairs={{0,1},{1,0},{2,3},{3,2},{4,5},{5,4},{6,7},{7,6},{8,9},{9,8},{10,11... | collective-permute-start | bytes 786440 | tf_op jit(solution)/shard_map/ppermute | solution.py:83
  101.0 5.2 %collective-permute-start.5 = (f32[2,128,128]{2,1,0:T(8,128)S(1)}, f32[2,128,128]{2,1,0:T(8,128)S(1)}, u32[]{:S(2)}, u32[]{:S(2)}) collective-permute-start(f32[2,128,128]{2,1,0:T(8,128)S(1)} %get-tuple-element.15), channel_id=1, source_target_pairs={{0,2},{1,3},{2,0},{3,1},{4,6},{5,7},{6,4},{7,5},{8,10},{9,11},{10,... | collective-permute-start | bytes 393224 | tf_op jit(solution)/shard_map/ppermute | solution.py:83
  106.2 5.9 %collective-permute-start.6 = (f32[2,64,128]{2,1,0:T(8,128)S(1)}, f32[2,64,128]{2,1,0:T(8,128)S(1)}, u32[]{:S(2)}, u32[]{:S(2)}) collective-permute-start(f32[2,64,128]{2,1,0:T(8,128)S(1)} %get-tuple-element.19), channel_id=1, source_target_pairs={{0,4},{1,5},{2,6},{3,7},{4,0},{5,1},{6,2},{7,3},{8,12},{9,13},{10,... | collective-permute-start | bytes 196616 | tf_op jit(solution)/shard_map/ppermute | solution.py:83
  112.2 5.7 %collective-permute-start.7 = (f32[2,64,128]{2,1,0:T(8,128)S(1)}, f32[2,64,128]{2,1,0:T(8,128)S(1)}, u32[]{:S(2)}, u32[]{:S(2)}) collective-permute-start(f32[2,64,128]{2,1,0:T(8,128)S(1)} %pad_maximum_fusion.4), channel_id=1, source_target_pairs={{0,4},{1,5},{2,6},{3,7},{4,0},{5,1},{6,2},{7,3},{8,12},{9,13},{10,... | collective-permute-start | bytes 196616 | tf_op jit(solution)/shard_map/ppermute | solution.py:88
  117.9 5.0 %collective-permute-start.8 = (f32[2,128,128]{2,1,0:T(8,128)S(1)}, f32[2,128,128]{2,1,0:T(8,128)S(1)}, u32[]{:S(2)}, u32[]{:S(2)}) collective-permute-start(f32[2,128,128]{2,1,0:T(8,128)S(1)} %maximum_select_fusion.2), channel_id=1, source_target_pairs={{0,2},{1,3},{2,0},{3,1},{4,6},{5,7},{6,4},{7,5},{8,10},{9,11},{10,... | collective-permute-start | bytes 393224 | tf_op jit(solution)/shard_map/ppermute | solution.py:88
  122.9 6.4 %collective-permute-start.9 = (f32[2,256,128]{2,1,0:T(8,128)S(1)}, f32[2,256,128]{2,1,0:T(8,128)S(1)}, u32[]{:S(2)}, u32[]{:S(2)}) collective-permute-start(f32[2,256,128]{2,1,0:T(8,128)S(1)} %maximum_select_fusion.1), channel_id=1, source_target_pairs={{0,1},{1,0},{2,3},{3,2},{4,5},{5,4},{6,7},{7,6},{8,9},{9,8},{10,11... | collective-permute-start | bytes 786440 | tf_op jit(solution)/shard_map/ppermute | solution.py:88
Sparse Core Ops, SparseCore 0:
  9.6 60.9 all-gather.2

commit v6 on v5

--- a/solution.py
+++ b/solution.py
@@ -72,6 +72,15 @@
         return best, power
     width = best_part.shape[-1]
     joined = jnp.stack([best_part.reshape(-1, width), power_part.reshape(-1, width)], axis=0)
+    return reduce_joined(joined, best_part.shape, axis)
+
+
+def reduce_joined(joined, shape, axis):
+    n = lax.axis_size(axis)
+    if not is_pow2(n):
+        best = lax.pmax(joined[0], axis)
+        power = lax.psum(joined[1], axis)
+        return best.reshape(shape), power.reshape(shape)
     me = lax.axis_index(axis)
     cur = joined
     k = 1
@@ -89,9 +98,7 @@
         bit = (me // k) % 2
         cur = jnp.where(bit == 1, jnp.concatenate([got, cur], axis=1), jnp.concatenate([cur, got], axis=1))
         k //= 2
-    best = cur[0].reshape(best_part.shape)
-    power = cur[1].reshape(power_part.shape)
-    return best, power
+    return cur[0].reshape(shape), cur[1].reshape(shape)
 
 
 def match_kernel(blocks, size, width, rows_t, tiles, peaks_n, l_ref, tm_ref, sp_ref, ct_ref, cr_ref, sr_ref, best_ref, pow_ref, m_ref):
@@ -153,9 +160,10 @@
     )(flags, tmpl, spec, col_table, cos_t, sin_t)
 
 
-def rows_kernel(blocks, size, width, rows_t, peaks_n, chunk, n_steps, final, f_ref, ta_ref, tb_ref, rid_ref, tma_ref, tmb_ref, sp_ref, ct_ref, cr_ref, sr_ref, *rest):
+def rows_kernel(blocks, size, width, rows_t, peaks_n, chunk, n_steps, final, f_ref, ta_ref, tb_ref, rid_ref, off_ref, tma_ref, tmb_ref, sp_ref, ct_ref, cr_ref, sr_ref, *rest):
     if final:
-        init_ref, best_ref, pow_ref, acc_ref, m_ref = rest
+        init_ref, out_ref, acc_ref, m_ref = rest
+        best_ref, pow_ref = out_ref.at[0], out_ref.at[1]
     else:
         part_ref, acc_ref, m_ref = rest
     j = pl.program_id(0)
@@ -178,7 +186,7 @@
     for u, tm_ref in enumerate((tma_ref, tmb_ref)):
         def mix(c, carry, u=u, tm_ref=tm_ref):
             row = pl.multiple_of(c * chunk, chunk)
-            out_row = pl.multiple_of(u * rows_t + c * chunk, chunk)
+            out_row = pl.multiple_of(off_ref[u] + c * chunk, chunk)
             image_re = sp_ref[0, pl.ds(out_row, chunk), :]
             image_im = sp_ref[1, pl.ds(out_row, chunk), :]
             tmpl_re = tm_ref[0, 0, 0, pl.ds(row, chunk), :].astype(jnp.float32)
@@ -210,7 +218,7 @@
             part_ref[:, 0] = acc_ref[...]
 
 
-def match_rows(flags, tas, tbs, rids, tmpl_a, tmpl_b, spec, col_table, cos_t, sin_t, init=None):
+def match_rows(flags, tas, tbs, rids, offs, tmpl_a, tmpl_b, spec, col_table, cos_t, sin_t, init=None):
     _, blocks, _, rows_t, size = tmpl_a.shape
     peaks_n, width = cos_t.shape[0], cos_t.shape[1]
     n_steps = tas.shape[0]
@@ -221,28 +229,27 @@
     flops = blocks * peaks_n * n_steps * (2 * span * 2 * size * 2 * width + 2 * 2 * width * span * width)
     cost = pl.CostEstimate(flops=flops, transcendentals=0, bytes_accessed=n_steps * blocks * 2 * span * size * 6 + col_table.size * 2)
     in_specs = [
-        pl.BlockSpec((1, 1, 2, rows_t, size), lambda j, i, f, ta, tb, r: (ta[i], j, 0, 0, 0)),
-        pl.BlockSpec((1, 1, 2, rows_t, size), lambda j, i, f, ta, tb, r: (tb[i], j, 0, 0, 0)),
-        pl.BlockSpec((2, span, size), lambda j, i, f, ta, tb, r: (0, r[i], 0)),
-        pl.BlockSpec(col_table.shape, lambda j, i, f, ta, tb, r: (0, 0, 0)),
-        pl.BlockSpec((peaks_n, width, span), lambda j, i, f, ta, tb, r: (0, 0, r[i])),
-        pl.BlockSpec((peaks_n, width, span), lambda j, i, f, ta, tb, r: (0, 0, r[i])),
+        pl.BlockSpec((1, 1, 2, rows_t, size), lambda j, i, f, ta, tb, r, o: (ta[i], j, 0, 0, 0)),
+        pl.BlockSpec((1, 1, 2, rows_t, size), lambda j, i, f, ta, tb, r, o: (tb[i], j, 0, 0, 0)),
+        pl.BlockSpec((2, span, size), lambda j, i, f, ta, tb, r, o: (0, r[i], 0)),
+        pl.BlockSpec(col_table.shape, lambda j, i, f, ta, tb, r, o: (0, 0, 0)),
+        pl.BlockSpec((peaks_n, width, span), lambda j, i, f, ta, tb, r, o: (0, 0, r[i])),
+        pl.BlockSpec((peaks_n, width, span), lambda j, i, f, ta, tb, r, o: (0, 0, r[i])),
     ]
-    args = [flags, tas, tbs, rids, tmpl_a, tmpl_b, spec, col_table, cos_t, sin_t]
-    part_spec = pl.BlockSpec((peaks_n, 1, width, width), lambda j, i, f, ta, tb, r: (0, j, 0, 0))
+    args = [flags, tas, tbs, rids, offs, tmpl_a, tmpl_b, spec, col_table, cos_t, sin_t]
+    part_spec = pl.BlockSpec((peaks_n, 1, width, width), lambda j, i, f, ta, tb, r, o: (0, j, 0, 0))
     if final:
         in_specs.append(part_spec)
         args.append(init)
-        out = jax.ShapeDtypeStruct((peaks_n, width, width), jnp.float32)
-        out_shape = [out, out]
-        out_specs = [pl.BlockSpec((peaks_n, width, width), lambda j, i, f, ta, tb, r: (0, 0, 0))] * 2
+        out_shape = jax.ShapeDtypeStruct((2, peaks_n, width, width), jnp.float32)
+        out_specs = pl.BlockSpec((2, peaks_n, width, width), lambda j, i, f, ta, tb, r, o: (0, 0, 0, 0))
     else:
         out_shape = jax.ShapeDtypeStruct((peaks_n, blocks, width, width), jnp.float32)
         out_specs = part_spec
     return pl.pallas_call(
         kernel,
         grid_spec=pltpu.PrefetchScalarGridSpec(
-            num_scalar_prefetch=4,
+            num_scalar_prefetch=5,
             grid=(blocks, n_steps),
             in_specs=in_specs,
             out_specs=out_specs,
@@ -272,18 +279,24 @@
     global_ids = lax.axis_index("orient") * block_size + jnp.arange(block_size, dtype=jnp.int32)
     is_listed = jnp.any(listed_ids[:, :, None] == global_ids[None, None, :], axis=1)
     flags = is_listed.astype(jnp.int32).reshape(-1)
+    best_shape = (listed.shape[1], width, width)
     if rows_t % 128 != 0 or tiles % 2 != 0:
         best_part, power_part = match(flags, tmpl, spec, col_table, cos_t, sin_t)
     else:
         me = lax.axis_index("tile")
         sibling = lax.ppermute(template_spectra, "tile", xor_pairs(tiles, 1))
-        near = jnp.stack([template_spectra, sibling])
         spec32 = spec.astype(jnp.float32)
         chip = me // 2
-        odd = (me % 2)[None].astype(jnp.int32)
-        partial = match_rows(flags, odd, 1 - odd, chip[None].astype(jnp.int32), near, near, spec32, col_table, cos_t, sin_t)
+        odd = (me % 2).astype(jnp.int32)
+        zero = jnp.zeros((1,), jnp.int32)
+        near_offs = jnp.stack([odd, 1 - odd]) * rows_t
+        own, sib = template_spectra[None], sibling[None]
+        partial = match_rows(flags, zero, zero, chip[None].astype(jnp.int32), near_offs, own, sib, spec32, col_table, cos_t, sin_t)
         far = far_chips(chip, tiles // 2)
-        best_part, power_part = match_rows(flags, far * 2, far * 2 + 1, far, tmpl, tmpl, spec32, col_table, cos_t, sin_t, init=partial)
+        far_offs = jnp.array([0, rows_t], jnp.int32)
+        joined = match_rows(flags, far * 2, far * 2 + 1, far, far_offs, tmpl, tmpl, spec32, col_table, cos_t, sin_t, init=partial)
+        best_all, power_all = reduce_joined(joined.reshape(2, -1, width), best_shape, "orient")
+        return (best_all[None], (power_all / LIST)[None])
     best_all, power_all = reduce_orient(best_part, power_part, "orient")
     return (best_all[None], (power_all / LIST)[None])
 

time: 137 us -> 137 us (level)
  starting transfers between devices: 9.37 us -> 17.8 us
  waiting for transfers between devices: 44.4 us -> 38.6 us
  other arithmetic: 23.4 us -> 19.5 us
  Pallas kernels: 40 us -> 42.3 us
  local copies, waits for them, and re-layouts: 5.6 us -> 3.77 us
    ppermute x6, waiting for transfers between devices: 34 us -> 23 us  [the longest x3 12.7 us: reduce_joined(): got = lax.ppermute(send, axis, xor_pairs(n, k))]
    ppermute x6, starting transfers between devices: 2.99 us -> 11.4 us  [the longest x3 6.41 us: reduce_joined(): got = lax.ppermute(cur, axis, xor_pairs(n, k))]
    all_gather x1, waiting for transfers between devices: 0.84 us -> 7.04 us  [local(): tmpl = lax.all_gather(template_spectra, 'tile', axis=0)]
    another operation x5 -> x4, other arithmetic: 5.14 us -> 0.63 us  [the longest x1 3.96 us: local(): near = jnp.stack([template_spectra, sibling])]
    pallas_call x2, Pallas kernels: 40 us -> 42.3 us  [match_rows(): pl.pallas_call(kernel, grid_spec=pltpu.PrefetchScalarGridSpec(num_scalar_...]
  transfers between devices with their start and end apart: 11 -> 11, of which waited for: 10 -> 10; matrix products, arithmetic and copies ran while one was open for 19% -> 15% of each run, Pallas kernels for 14% -> 15%
where the time goes in v6:
time: 137 us; the launch traced here: 136 us
  Pallas kernels  42.3 us (31%)
  waiting for transfers between devices  38.6 us (28%)
  other arithmetic  19.5 us (14%)
  starting transfers between devices  17.8 us (13%)
  between operations  14.2 us (10%)
  local copies, waits for them, and re-layouts  3.77 us (3%)
    pallas_call x2, Pallas kernels, match_rows(): pl.pallas_call(kernel, grid_spec=pltpu.PrefetchScalarGridSpec(num_scalar_...  42.3 us
    ppermute x3, waiting for transfers between devices, reduce_joined(): got = lax.ppermute(send, axis, xor_pairs(n, k))  12.7 us
    ppermute x3, waiting for transfers between devices, reduce_joined(): got = lax.ppermute(cur, axis, xor_pairs(n, k))  10.3 us
    convert_element_type x2, other arithmetic, angle_tables(): jnp.sin(angle).astype(jnp.bfloat16)  10 us
    ppermute x3, waiting for transfers between devices, gather_rows(): got = lax.ppermute(blocks, axis, xor_pairs(n, k))  7.95 us
    all_gather x1, waiting for transfers between devices, local(): tmpl = lax.all_gather(template_spectra, 'tile', axis=0)  7.04 us
    ppermute x3, starting transfers between devices, reduce_joined(): got = lax.ppermute(cur, axis, xor_pairs(n, k))  6.41 us
    ppermute x3, starting transfers between devices, gather_rows(): got = lax.ppermute(blocks, axis, xor_pairs(n, k))  5.92 us
  transfers between devices with their start and end apart: 11, of which 10 were waited for; matrix products, arithmetic and copies ran while one was open for 15% of the time, Pallas kernels for 15%

profile of v6, /device:TPU:0, one launch (start us, length us, event | category | flops | bytes accessed | tf_op | source)
XLA Modules:
  0.0 136.3 jit_solution(2685185378722533341)
XLA Ops:
  7.2 0.7 all-gather.3.cloned.1.call-update
  8.4 3.7 %collective-permute-start = (bf16[1,2,64,512]{3,2,1,0:T(8,128)(2,1)S(1)}, bf16[1,2,64,512]{3,2,1,0:T(8,128)(2,1)S(1)}, u32[]{:S(2)}, u32[]{:S(2)}) collective-permute-start(bf16[1,2,64,512]{3,2,1,0:T(8,128)(2,1)S(1)} %copy-done), channel_id=1, source_target_pairs={{0,4},{1,5},{2,6},{3,7},{4,0},{5,1},{6,2},{7,3},{8,12},{9,13},{10,... | collective-permute-start | bytes 393224 | tf_op jit(solution)/shard_map/ppermute | solution.py:50
  12.2 4.0 %fusion.12 = bf16[4,512,128]{2,1,0:T(8,128)(2,1)S(1)} fusion(s32[4,128]{1,0:T(4,128)S(1)} %get-tuple-element.21), kind=kLoop, calls=%fused_computation.39 | loop fusion | flops 4718592 | bytes 526336 | tf_op jit(solution)/shard_map/neg | solution.py:38
  16.5 2.5 %collective-permute-done = bf16[1,2,64,512]{3,2,1,0:T(8,128)(2,1)S(1)} collective-permute-done((bf16[1,2,64,512]{3,2,1,0:T(8,128)(2,1)S(1)}, bf16[1,2,64,512]{3,2,1,0:T(8,128)(2,1)S(1)}, u32[]{:S(2)}, u32[]{:S(2)}) %collective-permute-start) | collective-permute-done | bytes 131104 | tf_op jit(solution)/shard_map/ppermute | solution.py:50
  19.0 0.8 collective-permute-start.1
  20.4 0.6 reshape.156.f_ref
  21.0 4.4 %sine_convert_fusion.1 = (bf16[4,512,128]{2,1,0:T(8,128)(2,1)S(1)}, bf16[4,512,128]{2,1,0:T(8,128)(2,1)S(1)}) fusion(s32[4,128]{1,0:T(4,128)S(1)} %get-tuple-element.21), kind=kLoop, calls=%fused_computation.20 | loop fusion | flops 4194304 | bytes 1050624 | tf_op jit(solution)/shard_map/convert_element_type | solution.py:31
  25.4 1.7 %collective-permute-done.1 = bf16[2,2,64,512]{3,2,1,0:T(8,128)(2,1)S(1)} collective-permute-done((bf16[2,2,64,512]{3,2,1,0:T(8,128)(2,1)S(1)}, bf16[2,2,64,512]{3,2,1,0:T(8,128)(2,1)S(1)}, u32[]{:S(2)}, u32[]{:S(2)}) %collective-permute-start.1) | collective-permute-done | bytes 262176 | tf_op jit(solution)/shard_map/ppermute | solution.py:50
  27.2 1.4 %collective-permute-start.2 = (bf16[4,2,64,512]{3,2,1,0:T(8,128)(2,1)S(1)}, bf16[4,2,64,512]{3,2,1,0:T(8,128)(2,1)S(1)}, u32[]{:S(2)}, u32[]{:S(2)}) collective-permute-start(bf16[4,2,64,512]{3,2,1,0:T(8,128)(2,1)S(1)} %pad_maximum_fusion.1), channel_id=1, source_target_pairs={{0,1},{1,0},{2,3},{3,2},{4,5},{5,4},{6,7},{7,6},{8,9},{9,8},{10,11... | collective-permute-start | bytes 1572872 | tf_op jit(solution)/shard_map/ppermute | solution.py:50
  28.6 0.6 add_multiply_fusion.off_ref
  29.3 1.6 %maximum_maximum_fusion.ct_ref = bf16[4,1024,256]{2,1,0:T(8,128)(2,1)} fusion(bf16[4,512,128]{2,1,0:T(8,128)(2,1)S(1)} %get-tuple-element.17, bf16[4,512,128]{2,1,0:T(8,128)(2,1)S(1)} %fusion.12, bf16[4,512,128]{2,1,0:T(8,128)(2,1)S(1)} %get-tuple-element.16), kind=kLoop, calls=%fused_computation.1 | loop fusion | flops 8388608 | bytes 3670016 | tf_op jit(solution)/shard_map/concatenate | solution.py:39
  30.8 5.6 %sine_convert_fusion = (bf16[4,128,512]{2,1,0:T(8,128)(2,1)}, bf16[4,128,512]{2,1,0:T(8,128)(2,1)}) fusion(s32[4,128]{1,0:T(4,128)S(1)} %get-tuple-element.20), kind=kLoop, calls=%fused_computation.16 | loop fusion | flops 4194304 | bytes 1050624 | tf_op jit(solution)/shard_map/convert_element_type | solution.py:31
  36.4 3.7 %collective-permute-done.2 = bf16[4,2,64,512]{3,2,1,0:T(8,128)(2,1)S(1)} collective-permute-done((bf16[4,2,64,512]{3,2,1,0:T(8,128)(2,1)S(1)}, bf16[4,2,64,512]{3,2,1,0:T(8,128)(2,1)S(1)}, u32[]{:S(2)}, u32[]{:S(2)}) %collective-permute-start.2) | collective-permute-done | bytes 524320 | tf_op jit(solution)/shard_map/ppermute | solution.py:50
  40.3 0.6 gather_fusion
  41.2 1.6 %copy.9 = f32[2,8,64,512]{3,2,1,0:T(8,128)} copy(f32[2,8,64,512]{3,2,0,1:T(8,128)S(1)} %convert_bitcast_fusion) | data formatting | bytes 4194304 | tf_op jit(solution)/shard_map/convert_element_type | solution.py:288
  42.8 20.8 %shard_map.68.rest_0_ = f32[4,8,128,128]{3,2,1,0:T(8,128)} custom-call(s32[32]{0:T(128)} %reshape.156.f_ref, s32[1]{0:T(128)} %constant.139.clone.1.ta_ref.tb_ref, s32[1]{0:T(128)} %constant.139.clone.1.ta_ref.tb_ref, s32[1]{0:T(128)} %bitcast.1.rid_ref, s32[2]{0:T(128)} %add_multiply_fusion.off_ref, bf16[1,8,2,128,512]{4,3,2,1,0:T(8,128)(2,1)} %bitcast.11.tma_ref, ...), custom_call_target="tpu_custom_call" | custom-call | flops 4831838208 | bytes 14680064 | tf_op jit(solution)/shard_map/pallas_call | solution.py:249
  63.6 7.0 %all-gather.3.cloned.1.call-done = bf16[32,2,128,512]{3,2,1,0:T(8,128)(2,1)} async-done(((bf16[8,2,128,512]{3,2,1,0:T(8,128)(2,1)}), bf16[32,2,128,512]{3,2,1,0:T(8,128)(2,1)}) %all-gather.3.cloned.1.call-update) | async-done | bytes 8388624 | tf_op jit(solution)/shard_map/all_gather | solution.py:269
  70.6 21.5 %shard_map.69 = f32[2,4,128,128]{3,2,1,0:T(8,128)} custom-call(s32[32]{0:T(128)} %reshape.156.f_ref, s32[1]{0:T(128)S(6)} %mul.65.ta_ref, s32[1]{0:T(128)S(6)} %add.151.tb_ref, s32[1]{0:T(128)S(6)} %convert_element_type.41.rid_ref, s32[2]{0:T(128)} %iota_multiply_fusion.off_ref, bf16[4,8,2,128,512]{4,3,2,1,0:T(8,128)(2,1)} %bitcast.20, ...), custom_call_target="tpu_custom_call" | custom-call | flops 4831838208 | bytes 14680064 | tf_op jit(solution)/shard_map/pallas_call | solution.py:249
  92.1 1.0 constant_dynamic-slice_fusion
  93.2 6.3 %collective-permute-done.4 = f32[2,256,128]{2,1,0:T(8,128)S(1)} collective-permute-done((f32[2,256,128]{2,1,0:T(8,128)S(1)}, f32[2,256,128]{2,1,0:T(8,128)S(1)}, u32[]{:S(2)}, u32[]{:S(2)}) %collective-permute-start.4) | collective-permute-done | bytes 262176 | tf_op jit(solution)/shard_map/ppermute | solution.py:92
  99.5 1.0 slice_add_fusion
  100.6 1.9 %collective-permute-start.5 = (f32[2,128,128]{2,1,0:T(8,128)S(1)}, f32[2,128,128]{2,1,0:T(8,128)S(1)}, u32[]{:S(2)}, u32[]{:S(2)}) collective-permute-start(f32[2,128,128]{2,1,0:T(8,128)S(1)} %get-tuple-element.9), channel_id=1, source_target_pairs={{0,2},{1,3},{2,0},{3,1},{4,6},{5,7},{6,4},{7,5},{8,10},{9,11},{10,... | collective-permute-start | bytes 393224 | tf_op jit(solution)/shard_map/ppermute | solution.py:92
  102.5 3.8 %collective-permute-done.5 = f32[2,128,128]{2,1,0:T(8,128)S(1)} collective-permute-done((f32[2,128,128]{2,1,0:T(8,128)S(1)}, f32[2,128,128]{2,1,0:T(8,128)S(1)}, u32[]{:S(2)}, u32[]{:S(2)}) %collective-permute-start.5) | collective-permute-done | bytes 131104 | tf_op jit(solution)/shard_map/ppermute | solution.py:92
  106.4 2.9 %collective-permute-start.6 = (f32[2,64,128]{2,1,0:T(8,128)S(1)}, f32[2,64,128]{2,1,0:T(8,128)S(1)}, u32[]{:S(2)}, u32[]{:S(2)}) collective-permute-start(f32[2,64,128]{2,1,0:T(8,128)S(1)} %get-tuple-element.13), channel_id=1, source_target_pairs={{0,4},{1,5},{2,6},{3,7},{4,0},{5,1},{6,2},{7,3},{8,12},{9,13},{10,... | collective-permute-start | bytes 196616 | tf_op jit(solution)/shard_map/ppermute | solution.py:92
  109.3 2.5 %collective-permute-done.6 = f32[2,64,128]{2,1,0:T(8,128)S(1)} collective-permute-done((f32[2,64,128]{2,1,0:T(8,128)S(1)}, f32[2,64,128]{2,1,0:T(8,128)S(1)}, u32[]{:S(2)}, u32[]{:S(2)}) %collective-permute-start.6) | collective-permute-done | bytes 65568 | tf_op jit(solution)/shard_map/ppermute | solution.py:92
  111.9 2.7 %collective-permute-start.7 = (f32[2,64,128]{2,1,0:T(8,128)S(1)}, f32[2,64,128]{2,1,0:T(8,128)S(1)}, u32[]{:S(2)}, u32[]{:S(2)}) collective-permute-start(f32[2,64,128]{2,1,0:T(8,128)S(1)} %pad_maximum_fusion.3), channel_id=1, source_target_pairs={{0,4},{1,5},{2,6},{3,7},{4,0},{5,1},{6,2},{7,3},{8,12},{9,13},{10,... | collective-permute-start | bytes 196616 | tf_op jit(solution)/shard_map/ppermute | solution.py:97
  114.6 2.5 %collective-permute-done.7 = f32[2,64,128]{2,1,0:T(8,128)S(1)} collective-permute-done((f32[2,64,128]{2,1,0:T(8,128)S(1)}, f32[2,64,128]{2,1,0:T(8,128)S(1)}, u32[]{:S(2)}, u32[]{:S(2)}) %collective-permute-start.7) | collective-permute-done | bytes 65568 | tf_op jit(solution)/shard_map/ppermute | solution.py:97
  117.1 1.9 %collective-permute-start.8 = (f32[2,128,128]{2,1,0:T(8,128)S(1)}, f32[2,128,128]{2,1,0:T(8,128)S(1)}, u32[]{:S(2)}, u32[]{:S(2)}) collective-permute-start(f32[2,128,128]{2,1,0:T(8,128)S(1)} %maximum_select_fusion.2), channel_id=1, source_target_pairs={{0,2},{1,3},{2,0},{3,1},{4,6},{5,7},{6,4},{7,5},{8,10},{9,11},{10,... | collective-permute-start | bytes 393224 | tf_op jit(solution)/shard_map/ppermute | solution.py:97
  119.1 3.1 %collective-permute-done.8 = f32[2,128,128]{2,1,0:T(8,128)S(1)} collective-permute-done((f32[2,128,128]{2,1,0:T(8,128)S(1)}, f32[2,128,128]{2,1,0:T(8,128)S(1)}, u32[]{:S(2)}, u32[]{:S(2)}) %collective-permute-start.8) | collective-permute-done | bytes 131104 | tf_op jit(solution)/shard_map/ppermute | solution.py:97
  122.2 1.7 %collective-permute-start.9 = (f32[2,256,128]{2,1,0:T(8,128)S(1)}, f32[2,256,128]{2,1,0:T(8,128)S(1)}, u32[]{:S(2)}, u32[]{:S(2)}) collective-permute-start(f32[2,256,128]{2,1,0:T(8,128)S(1)} %maximum_select_fusion.1), channel_id=1, source_target_pairs={{0,1},{1,0},{2,3},{3,2},{4,5},{5,4},{6,7},{7,6},{8,9},{9,8},{10,11... | collective-permute-start | bytes 786440 | tf_op jit(solution)/shard_map/ppermute | solution.py:97
  123.9 4.7 %collective-permute-done.9 = f32[2,256,128]{2,1,0:T(8,128)S(1)} collective-permute-done((f32[2,256,128]{2,1,0:T(8,128)S(1)}, f32[2,256,128]{2,1,0:T(8,128)S(1)}, u32[]{:S(2)}, u32[]{:S(2)}) %collective-permute-start.9) | collective-permute-done | bytes 262176 | tf_op jit(solution)/shard_map/ppermute | solution.py:97
  128.6 0.8 slice_multiply_fusion
  (31 shorter events, 2.2 us)
Async XLA Ops:
  7.2 1.3 copy-start
  7.2 5.0 %copy-start.2 = (s32[1,4,2]{1,2,0:T(2,128)S(1)}, s32[1,4,2]{1,2,0:T(2,128)}, u32[]{:S(2)}) copy-start(s32[1,4,2]{1,2,0:T(2,128)} %param.7) | copy-start | bytes 100
  7.2 9.1 %copy-start.1 = (s32[1,4,48]{2,1,0:T(4,128)S(1)}, s32[1,4,48]{2,1,0:T(4,128)}, u32[]{:S(2)}) copy-start(s32[1,4,48]{2,1,0:T(4,128)} %param.8) | copy-start | bytes 2308
  7.2 63.4 %all-gather.3.cloned.1.call-start = ((), (), s32[]{:S(2)}) async-start(), calls=%async_computation | async-start | bytes 10485760 | tf_op jit(solution)/shard_map/all_gather | solution.py:269
  7.9 34.8 %collective-permute-start.3 = (bf16[8,2,128,512]{3,2,1,0:T(8,128)(2,1)}, bf16[8,2,128,512]{3,2,1,0:T(8,128)(2,1)}, u32[]{:S(2)}, u32[]{:S(2)}) collective-permute-start(bf16[8,2,128,512]{3,2,1,0:T(8,128)(2,1)} %param.6), channel_id=1, source_target_pairs={{0,8},{8,0},{16,24},{24,16},{1,9},{9,1},{17,25},{25,17},{2,10},{10... | collective-permute-start | bytes 6291464 | tf_op jit(solution)/shard_map/ppermute | solution.py:287
  8.4 10.6 %collective-permute-start = (bf16[1,2,64,512]{3,2,1,0:T(8,128)(2,1)S(1)}, bf16[1,2,64,512]{3,2,1,0:T(8,128)(2,1)S(1)}, u32[]{:S(2)}, u32[]{:S(2)}) collective-permute-start(bf16[1,2,64,512]{3,2,1,0:T(8,128)(2,1)S(1)} %copy-done), channel_id=1, source_target_pairs={{0,4},{1,5},{2,6},{3,7},{4,0},{5,1},{6,2},{7,3},{8,12},{9,13},{10,... | collective-permute-start | bytes 393224 | tf_op jit(solution)/shard_map/ppermute | solution.py:50
  19.0 8.1 %collective-permute-start.1 = (bf16[2,2,64,512]{3,2,1,0:T(8,128)(2,1)S(1)}, bf16[2,2,64,512]{3,2,1,0:T(8,128)(2,1)S(1)}, u32[]{:S(2)}, u32[]{:S(2)}) collective-permute-start(bf16[2,2,64,512]{3,2,1,0:T(8,128)(2,1)S(1)} %pad_maximum_fusion.2), channel_id=1, source_target_pairs={{0,2},{1,3},{2,0},{3,1},{4,6},{5,7},{6,4},{7,5},{8,10},{9,11},{10,... | collective-permute-start | bytes 786440 | tf_op jit(solution)/shard_map/ppermute | solution.py:50
  27.2 13.0 %collective-permute-start.2 = (bf16[4,2,64,512]{3,2,1,0:T(8,128)(2,1)S(1)}, bf16[4,2,64,512]{3,2,1,0:T(8,128)(2,1)S(1)}, u32[]{:S(2)}, u32[]{:S(2)}) collective-permute-start(bf16[4,2,64,512]{3,2,1,0:T(8,128)(2,1)S(1)} %pad_maximum_fusion.1), channel_id=1, source_target_pairs={{0,1},{1,0},{2,3},{3,2},{4,5},{5,4},{6,7},{7,6},{8,9},{9,8},{10,11... | collective-permute-start | bytes 1572872 | tf_op jit(solution)/shard_map/ppermute | solution.py:50
  93.1 6.4 %collective-permute-start.4 = (f32[2,256,128]{2,1,0:T(8,128)S(1)}, f32[2,256,128]{2,1,0:T(8,128)S(1)}, u32[]{:S(2)}, u32[]{:S(2)}) collective-permute-start(f32[2,256,128]{2,1,0:T(8,128)S(1)} %constant_dynamic-slice_fusion), channel_id=1, source_target_pairs={{0,1},{1,0},{2,3},{3,2},{4,5},{5,4},{6,7},{7,6},{8,9},{9,8},{10,11... | collective-permute-start | bytes 786440 | tf_op jit(solution)/shard_map/ppermute | solution.py:92
  100.6 5.7 %collective-permute-start.5 = (f32[2,128,128]{2,1,0:T(8,128)S(1)}, f32[2,128,128]{2,1,0:T(8,128)S(1)}, u32[]{:S(2)}, u32[]{:S(2)}) collective-permute-start(f32[2,128,128]{2,1,0:T(8,128)S(1)} %get-tuple-element.9), channel_id=1, source_target_pairs={{0,2},{1,3},{2,0},{3,1},{4,6},{5,7},{6,4},{7,5},{8,10},{9,11},{10,... | collective-permute-start | bytes 393224 | tf_op jit(solution)/shard_map/ppermute | solution.py:92
  106.4 5.5 %collective-permute-start.6 = (f32[2,64,128]{2,1,0:T(8,128)S(1)}, f32[2,64,128]{2,1,0:T(8,128)S(1)}, u32[]{:S(2)}, u32[]{:S(2)}) collective-permute-start(f32[2,64,128]{2,1,0:T(8,128)S(1)} %get-tuple-element.13), channel_id=1, source_target_pairs={{0,4},{1,5},{2,6},{3,7},{4,0},{5,1},{6,2},{7,3},{8,12},{9,13},{10,... | collective-permute-start | bytes 196616 | tf_op jit(solution)/shard_map/ppermute | solution.py:92
  111.9 5.2 %collective-permute-start.7 = (f32[2,64,128]{2,1,0:T(8,128)S(1)}, f32[2,64,128]{2,1,0:T(8,128)S(1)}, u32[]{:S(2)}, u32[]{:S(2)}) collective-permute-start(f32[2,64,128]{2,1,0:T(8,128)S(1)} %pad_maximum_fusion.3), channel_id=1, source_target_pairs={{0,4},{1,5},{2,6},{3,7},{4,0},{5,1},{6,2},{7,3},{8,12},{9,13},{10,... | collective-permute-start | bytes 196616 | tf_op jit(solution)/shard_map/ppermute | solution.py:97
  117.1 5.0 %collective-permute-start.8 = (f32[2,128,128]{2,1,0:T(8,128)S(1)}, f32[2,128,128]{2,1,0:T(8,128)S(1)}, u32[]{:S(2)}, u32[]{:S(2)}) collective-permute-start(f32[2,128,128]{2,1,0:T(8,128)S(1)} %maximum_select_fusion.2), channel_id=1, source_target_pairs={{0,2},{1,3},{2,0},{3,1},{4,6},{5,7},{6,4},{7,5},{8,10},{9,11},{10,... | collective-permute-start | bytes 393224 | tf_op jit(solution)/shard_map/ppermute | solution.py:97
  122.2 6.4 %collective-permute-start.9 = (f32[2,256,128]{2,1,0:T(8,128)S(1)}, f32[2,256,128]{2,1,0:T(8,128)S(1)}, u32[]{:S(2)}, u32[]{:S(2)}) collective-permute-start(f32[2,256,128]{2,1,0:T(8,128)S(1)} %maximum_select_fusion.1), channel_id=1, source_target_pairs={{0,1},{1,0},{2,3},{3,2},{4,5},{5,4},{6,7},{7,6},{8,9},{9,8},{10,11... | collective-permute-start | bytes 786440 | tf_op jit(solution)/shard_map/ppermute | solution.py:97
Sparse Core Ops, SparseCore 0:
  9.6 60.9 all-gather.2

commit v7 on v6

--- a/solution.py
+++ b/solution.py
@@ -160,7 +160,7 @@
     )(flags, tmpl, spec, col_table, cos_t, sin_t)
 
 
-def rows_kernel(blocks, size, width, rows_t, peaks_n, chunk, n_steps, final, f_ref, ta_ref, tb_ref, rid_ref, off_ref, tma_ref, tmb_ref, sp_ref, ct_ref, cr_ref, sr_ref, *rest):
+def rows_kernel(blocks, size, width, rows_t, peaks_n, peak_lo, chunk, n_steps, final, f_ref, ta_ref, tb_ref, rid_ref, off_ref, tma_ref, tmb_ref, sp_ref, ct_ref, cr_ref, sr_ref, *rest):
     if final:
         init_ref, out_ref, acc_ref, m_ref = rest
         best_ref, pow_ref = out_ref.at[0], out_ref.at[1]
@@ -198,7 +198,7 @@
         lax.fori_loop(0, rows_t // chunk, mix, 0, unroll=4)
 
     for p in range(peaks_n):
-        @pl.when(f_ref[p * blocks + j] > 0)
+        @pl.when(f_ref[(peak_lo + p) * blocks + j] > 0)
         def _():
             g = jnp.dot(m_ref[...], ct_ref[p], preferred_element_type=jnp.float32).astype(jnp.bfloat16)
             part = jnp.dot(cr_ref[p], g[:, :width], preferred_element_type=jnp.float32)
@@ -209,7 +209,7 @@
     def _():
         if final:
             for p in range(peaks_n):
-                @pl.when(f_ref[p * blocks + j] > 0)
+                @pl.when(f_ref[(peak_lo + p) * blocks + j] > 0)
                 def _():
                     score = acc_ref[p] / size
                     best_ref[p] = jnp.maximum(best_ref[p], score)
@@ -218,26 +218,28 @@
             part_ref[:, 0] = acc_ref[...]
 
 
-def match_rows(flags, tas, tbs, rids, offs, tmpl_a, tmpl_b, spec, col_table, cos_t, sin_t, init=None):
+def match_rows(flags, tas, tbs, rids, offs, tmpl_a, tmpl_b, spec, col_table, cos_t, sin_t, init=None, peak_lo=0, peaks_n=None):
     _, blocks, _, rows_t, size = tmpl_a.shape
-    peaks_n, width = cos_t.shape[0], cos_t.shape[1]
+    width = cos_t.shape[1]
+    peaks_n = cos_t.shape[0] if peaks_n is None else peaks_n
+    h = peak_lo // peaks_n
     n_steps = tas.shape[0]
     final = init is not None
     chunk = math.gcd(rows_t, 16)
     span = 2 * rows_t
-    kernel = functools.partial(rows_kernel, blocks, size, width, rows_t, peaks_n, chunk, n_steps, final)
+    kernel = functools.partial(rows_kernel, blocks, size, width, rows_t, peaks_n, peak_lo, chunk, n_steps, final)
     flops = blocks * peaks_n * n_steps * (2 * span * 2 * size * 2 * width + 2 * 2 * width * span * width)
-    cost = pl.CostEstimate(flops=flops, transcendentals=0, bytes_accessed=n_steps * blocks * 2 * span * size * 6 + col_table.size * 2)
+    cost = pl.CostEstimate(flops=flops, transcendentals=0, bytes_accessed=n_steps * blocks * 2 * span * size * 6 + col_table.size * 2 * peaks_n // col_table.shape[0])
     in_specs = [
         pl.BlockSpec((1, 1, 2, rows_t, size), lambda j, i, f, ta, tb, r, o: (ta[i], j, 0, 0, 0)),
         pl.BlockSpec((1, 1, 2, rows_t, size), lambda j, i, f, ta, tb, r, o: (tb[i], j, 0, 0, 0)),
         pl.BlockSpec((2, span, size), lambda j, i, f, ta, tb, r, o: (0, r[i], 0)),
-        pl.BlockSpec(col_table.shape, lambda j, i, f, ta, tb, r, o: (0, 0, 0)),
-        pl.BlockSpec((peaks_n, width, span), lambda j, i, f, ta, tb, r, o: (0, 0, r[i])),
-        pl.BlockSpec((peaks_n, width, span), lambda j, i, f, ta, tb, r, o: (0, 0, r[i])),
+        pl.BlockSpec((peaks_n,) + col_table.shape[1:], lambda j, i, f, ta, tb, r, o: (h, 0, 0)),
+        pl.BlockSpec((peaks_n, width, span), lambda j, i, f, ta, tb, r, o: (h, 0, r[i])),
+        pl.BlockSpec((peaks_n, width, span), lambda j, i, f, ta, tb, r, o: (h, 0, r[i])),
     ]
     args = [flags, tas, tbs, rids, offs, tmpl_a, tmpl_b, spec, col_table, cos_t, sin_t]
-    part_spec = pl.BlockSpec((peaks_n, 1, width, width), lambda j, i, f, ta, tb, r, o: (0, j, 0, 0))
+    part_spec = pl.BlockSpec((peaks_n, 1, width, width), lambda j, i, f, ta, tb, r, o: (h, j, 0, 0))
     if final:
         in_specs.append(part_spec)
         args.append(init)
@@ -294,8 +296,17 @@
         partial = match_rows(flags, zero, zero, chip[None].astype(jnp.int32), near_offs, own, sib, spec32, col_table, cos_t, sin_t)
         far = far_chips(chip, tiles // 2)
         far_offs = jnp.array([0, rows_t], jnp.int32)
-        joined = match_rows(flags, far * 2, far * 2 + 1, far, far_offs, tmpl, tmpl, spec32, col_table, cos_t, sin_t, init=partial)
-        best_all, power_all = reduce_joined(joined.reshape(2, -1, width), best_shape, "orient")
+        peaks_n = best_shape[0]
+        half = peaks_n // 2 if peaks_n % 2 == 0 else peaks_n
+        bests, powers = [], []
+        for lo in range(0, peaks_n, half):
+            joined = match_rows(flags, far * 2, far * 2 + 1, far, far_offs, tmpl, tmpl, spec32, col_table, cos_t, sin_t,
+                                init=partial, peak_lo=lo, peaks_n=half)
+            best_h, power_h = reduce_joined(joined.reshape(2, -1, width), (half,) + best_shape[1:], "orient")
+            bests.append(best_h)
+            powers.append(power_h)
+        best_all = jnp.concatenate(bests)
+        power_all = jnp.concatenate(powers)
         return (best_all[None], (power_all / LIST)[None])
     best_all, power_all = reduce_orient(best_part, power_part, "orient")
     return (best_all[None], (power_all / LIST)[None])

time: 137 us -> 139 us (1.015)
  waiting for transfers between devices: 38.6 us -> 25.5 us
  starting transfers between devices: 17.8 us -> 28.5 us
  Pallas kernels: 42.3 us -> 45.9 us
    ppermute x3 -> x6, waiting for transfers between devices: 12.7 us -> 2.47 us  [reduce_joined(): got = lax.ppermute(send, axis, xor_pairs(n, k))]
    ppermute x3 -> x6, starting transfers between devices: 4.94 us -> 12.1 us  [reduce_joined(): got = lax.ppermute(send, axis, xor_pairs(n, k))]
    ppermute x3 -> x6, waiting for transfers between devices: 10.3 us -> 6.37 us  [reduce_joined(): got = lax.ppermute(cur, axis, xor_pairs(n, k))]
    pallas_call x2 -> x3, Pallas kernels: 42.3 us -> 45.9 us  [match_rows(): pl.pallas_call(kernel, grid_spec=pltpu.PrefetchScalarGridSpec(num_scalar_...]
    ppermute x3 -> x6, starting transfers between devices: 6.41 us -> 9.94 us  [reduce_joined(): got = lax.ppermute(cur, axis, xor_pairs(n, k))]
  transfers between devices with their start and end apart: 11 -> 17, of which waited for: 10 -> 9; matrix products, arithmetic and copies ran while one was open for 15% -> 16% of each run, Pallas kernels for 15% -> 23%
where the time goes in v7:
time: 139 us
  Pallas kernels  45.9 us (33%)
  starting transfers between devices  28.5 us (21%)
  waiting for transfers between devices  25.5 us (18%)
  other arithmetic  20 us (14%)
  between operations  14.3 us (10%)
  local copies, waits for them, and re-layouts  4.76 us (3%)
    pallas_call x3, Pallas kernels, match_rows(): pl.pallas_call(kernel, grid_spec=pltpu.PrefetchScalarGridSpec(num_scalar_...  45.9 us
    ppermute x6, starting transfers between devices, reduce_joined(): got = lax.ppermute(send, axis, xor_pairs(n, k))  12.1 us
    convert_element_type x2, other arithmetic, angle_tables(): jnp.sin(angle).astype(jnp.bfloat16)  10 us
    ppermute x6, starting transfers between devices, reduce_joined(): got = lax.ppermute(cur, axis, xor_pairs(n, k))  9.94 us
    all_gather x1, waiting for transfers between devices, local(): tmpl = lax.all_gather(template_spectra, 'tile', axis=0)  8.03 us
    ppermute x3, waiting for transfers between devices, gather_rows(): got = lax.ppermute(blocks, axis, xor_pairs(n, k))  7.98 us
    ppermute x6, waiting for transfers between devices, reduce_joined(): got = lax.ppermute(cur, axis, xor_pairs(n, k))  6.37 us
    ppermute x3, starting transfers between devices, gather_rows(): got = lax.ppermute(blocks, axis, xor_pairs(n, k))  5.92 us
  transfers between devices with their start and end apart: 17, of which 9 were waited for; matrix products, arithmetic and copies ran while one was open for 16% of the time, Pallas kernels for 23%

profile of v7, /device:TPU:0, one launch (start us, length us, event | category | flops | bytes accessed | tf_op | source)
XLA Modules:
  0.0 138.9 jit_solution(10374575482874727814)
XLA Ops:
  8.4 3.7 %collective-permute-start = (bf16[1,2,64,512]{3,2,1,0:T(8,128)(2,1)S(1)}, bf16[1,2,64,512]{3,2,1,0:T(8,128)(2,1)S(1)}, u32[]{:S(2)}, u32[]{:S(2)}) collective-permute-start(bf16[1,2,64,512]{3,2,1,0:T(8,128)(2,1)S(1)} %copy-done), channel_id=1, source_target_pairs={{0,4},{1,5},{2,6},{3,7},{4,0},{5,1},{6,2},{7,3},{8,12},{9,13},{10,... | collective-permute-start | bytes 393224 | tf_op jit(solution)/shard_map/ppermute | solution.py:50
  12.2 4.0 %fusion.12 = bf16[4,512,128]{2,1,0:T(8,128)(2,1)S(1)} fusion(s32[4,128]{1,0:T(4,128)S(1)} %get-tuple-element.33), kind=kLoop, calls=%fused_computation.40 | loop fusion | flops 4718592 | bytes 526336 | tf_op jit(solution)/shard_map/neg | solution.py:38
  16.5 2.5 %collective-permute-done = bf16[1,2,64,512]{3,2,1,0:T(8,128)(2,1)S(1)} collective-permute-done((bf16[1,2,64,512]{3,2,1,0:T(8,128)(2,1)S(1)}, bf16[1,2,64,512]{3,2,1,0:T(8,128)(2,1)S(1)}, u32[]{:S(2)}, u32[]{:S(2)}) %collective-permute-start) | collective-permute-done | bytes 131104 | tf_op jit(solution)/shard_map/ppermute | solution.py:50
  19.0 0.8 collective-permute-start.1
  21.0 4.4 %sine_convert_fusion.1 = (bf16[4,512,128]{2,1,0:T(8,128)(2,1)S(1)}, bf16[4,512,128]{2,1,0:T(8,128)(2,1)S(1)}) fusion(s32[4,128]{1,0:T(4,128)S(1)} %get-tuple-element.33), kind=kLoop, calls=%fused_computation.20 | loop fusion | flops 4194304 | bytes 1050624 | tf_op jit(solution)/shard_map/convert_element_type | solution.py:31
  25.4 1.8 %collective-permute-done.1 = bf16[2,2,64,512]{3,2,1,0:T(8,128)(2,1)S(1)} collective-permute-done((bf16[2,2,64,512]{3,2,1,0:T(8,128)(2,1)S(1)}, bf16[2,2,64,512]{3,2,1,0:T(8,128)(2,1)S(1)}, u32[]{:S(2)}, u32[]{:S(2)}) %collective-permute-start.1) | collective-permute-done | bytes 262176 | tf_op jit(solution)/shard_map/ppermute | solution.py:50
  27.2 1.4 %collective-permute-start.2 = (bf16[4,2,64,512]{3,2,1,0:T(8,128)(2,1)S(1)}, bf16[4,2,64,512]{3,2,1,0:T(8,128)(2,1)S(1)}, u32[]{:S(2)}, u32[]{:S(2)}) collective-permute-start(bf16[4,2,64,512]{3,2,1,0:T(8,128)(2,1)S(1)} %pad_maximum_fusion.1), channel_id=1, source_target_pairs={{0,1},{1,0},{2,3},{3,2},{4,5},{5,4},{6,7},{7,6},{8,9},{9,8},{10,11... | collective-permute-start | bytes 1572872 | tf_op jit(solution)/shard_map/ppermute | solution.py:50
  29.3 1.5 %maximum_maximum_fusion.ct_ref = bf16[4,1024,256]{2,1,0:T(8,128)(2,1)} fusion(bf16[4,512,128]{2,1,0:T(8,128)(2,1)S(1)} %get-tuple-element.29, bf16[4,512,128]{2,1,0:T(8,128)(2,1)S(1)} %fusion.12, bf16[4,512,128]{2,1,0:T(8,128)(2,1)S(1)} %get-tuple-element.28), kind=kLoop, calls=%fused_computation.1 | loop fusion | flops 8388608 | bytes 3670016 | tf_op jit(solution)/shard_map/concatenate | solution.py:39
  30.8 5.7 %sine_convert_fusion = (bf16[4,128,512]{2,1,0:T(8,128)(2,1)}, bf16[4,128,512]{2,1,0:T(8,128)(2,1)}) fusion(s32[4,128]{1,0:T(4,128)S(1)} %get-tuple-element.32), kind=kLoop, calls=%fused_computation.16 | loop fusion | flops 4194304 | bytes 1050624 | tf_op jit(solution)/shard_map/convert_element_type | solution.py:31
  36.5 3.7 %collective-permute-done.2 = bf16[4,2,64,512]{3,2,1,0:T(8,128)(2,1)S(1)} collective-permute-done((bf16[4,2,64,512]{3,2,1,0:T(8,128)(2,1)S(1)}, bf16[4,2,64,512]{3,2,1,0:T(8,128)(2,1)S(1)}, u32[]{:S(2)}, u32[]{:S(2)}) %collective-permute-start.2) | collective-permute-done | bytes 524320 | tf_op jit(solution)/shard_map/ppermute | solution.py:50
  41.2 1.6 %copy.9 = f32[2,8,64,512]{3,2,1,0:T(8,128)} copy(f32[2,8,64,512]{3,2,0,1:T(8,128)S(1)} %convert_bitcast_fusion) | data formatting | bytes 4194304 | tf_op jit(solution)/shard_map/convert_element_type | solution.py:290
  42.8 19.8 %shard_map.68.rest_0_ = f32[4,8,128,128]{3,2,1,0:T(8,128)} custom-call(s32[32]{0:T(128)} %reshape.179.f_ref, s32[1]{0:T(128)} %constant.164.clone.1.ta_ref.tb_ref, s32[1]{0:T(128)} %constant.164.clone.1.ta_ref.tb_ref, s32[1]{0:T(128)} %bitcast.1.rid_ref, s32[2]{0:T(128)} %add_multiply_fusion.off_ref, bf16[1,8,2,128,512]{4,3,2,1,0:T(8,128)(2,1)} %bitcast.11.tma_ref, ...), custom_call_target="tpu_custom_call" | custom-call | flops 4831838208 | bytes 14680064 | tf_op jit(solution)/shard_map/pallas_call | solution.py:251
  62.6 8.0 %all-gather.3.cloned.1.call-done = bf16[32,2,128,512]{3,2,1,0:T(8,128)(2,1)} async-done(((bf16[8,2,128,512]{3,2,1,0:T(8,128)(2,1)}), bf16[32,2,128,512]{3,2,1,0:T(8,128)(2,1)}) %all-gather.3.cloned.1.call-update) | async-done | bytes 8388624 | tf_op jit(solution)/shard_map/all_gather | solution.py:271
  70.6 13.7 %shard_map.69 = f32[2,2,128,128]{3,2,1,0:T(8,128)} custom-call(s32[32]{0:T(128)} %reshape.179.f_ref, s32[1]{0:T(128)S(6)} %mul.73.ta_ref, s32[1]{0:T(128)S(6)} %add.176.tb_ref, s32[1]{0:T(128)S(6)} %convert_element_type.41.rid_ref, s32[2]{0:T(128)} %iota_multiply_fusion.off_ref, bf16[4,8,2,128,512]{4,3,2,1,0:T(8,128)(2,1)} %bitcast.25, ...), custom_call_target="tpu_custom_call" | custom-call | flops 2415919104 | bytes 13631488 | tf_op jit(solution)/shard_map/pallas_call | solution.py:251
  84.3 0.9 constant_dynamic-slice_fusion.1
  85.2 0.8 collective-permute-start.4
  86.0 12.4 %shard_map.70 = f32[2,2,128,128]{3,2,1,0:T(8,128)} custom-call(s32[32]{0:T(128)} %reshape.179.f_ref, s32[1]{0:T(128)S(6)} %mul.73.ta_ref, s32[1]{0:T(128)S(6)} %add.176.tb_ref, s32[1]{0:T(128)S(6)} %convert_element_type.41.rid_ref, s32[2]{0:T(128)} %iota_multiply_fusion.off_ref, bf16[4,8,2,128,512]{4,3,2,1,0:T(8,128)(2,1)} %bitcast.27, ...), custom_call_target="tpu_custom_call" | custom-call | flops 2415919104 | bytes 13631488 | tf_op jit(solution)/shard_map/pallas_call | solution.py:251
  98.4 0.9 constant_dynamic-slice_fusion
  99.3 1.9 %collective-permute-start.10 = (f32[2,128,128]{2,1,0:T(8,128)S(1)}, f32[2,128,128]{2,1,0:T(8,128)S(1)}, u32[]{:S(2)}, u32[]{:S(2)}) collective-permute-start(f32[2,128,128]{2,1,0:T(8,128)S(1)} %constant_dynamic-slice_fusion), channel_id=1, source_target_pairs={{0,1},{1,0},{2,3},{3,2},{4,5},{5,4},{6,7},{7,6},{8,9},{9,8},{10,11... | collective-permute-start | bytes 393224 | tf_op jit(solution)/shard_map/ppermute | solution.py:92
  101.3 1.2 collective-permute-start.5
  102.5 2.4 %collective-permute-done.10 = f32[2,128,128]{2,1,0:T(8,128)S(1)} collective-permute-done((f32[2,128,128]{2,1,0:T(8,128)S(1)}, f32[2,128,128]{2,1,0:T(8,128)S(1)}, u32[]{:S(2)}, u32[]{:S(2)}) %collective-permute-start.10) | collective-permute-done | bytes 131104 | tf_op jit(solution)/shard_map/ppermute | solution.py:92
  104.9 0.9 slice_add_fusion
  105.8 1.7 %collective-permute-start.11 = (f32[2,64,128]{2,1,0:T(8,128)S(1)}, f32[2,64,128]{2,1,0:T(8,128)S(1)}, u32[]{:S(2)}, u32[]{:S(2)}) collective-permute-start(f32[2,64,128]{2,1,0:T(8,128)S(1)} %get-tuple-element.17), channel_id=1, source_target_pairs={{0,2},{1,3},{2,0},{3,1},{4,6},{5,7},{6,4},{7,5},{8,10},{9,11},{10,... | collective-permute-start | bytes 196616 | tf_op jit(solution)/shard_map/ppermute | solution.py:92
  107.6 3.8 %collective-permute-start.6 = (f32[2,32,128]{2,1,0:T(8,128)S(1)}, f32[2,32,128]{2,1,0:T(8,128)S(1)}, u32[]{:S(2)}, u32[]{:S(2)}) collective-permute-start(f32[2,32,128]{2,1,0:T(8,128)S(1)} %get-tuple-element.21), channel_id=1, source_target_pairs={{0,4},{1,5},{2,6},{3,7},{4,0},{5,1},{6,2},{7,3},{8,12},{9,13},{10,... | collective-permute-start | bytes 98312 | tf_op jit(solution)/shard_map/ppermute | solution.py:92
  111.4 2.7 %collective-permute-start.12 = (f32[2,32,128]{2,1,0:T(8,128)S(1)}, f32[2,32,128]{2,1,0:T(8,128)S(1)}, u32[]{:S(2)}, u32[]{:S(2)}) collective-permute-start(f32[2,32,128]{2,1,0:T(8,128)S(1)} %get-tuple-element.25), channel_id=1, source_target_pairs={{0,4},{1,5},{2,6},{3,7},{4,0},{5,1},{6,2},{7,3},{8,12},{9,13},{10,... | collective-permute-start | bytes 98312 | tf_op jit(solution)/shard_map/ppermute | solution.py:92
  114.1 2.1 %collective-permute-start.7 = (f32[2,32,128]{2,1,0:T(8,128)S(1)}, f32[2,32,128]{2,1,0:T(8,128)S(1)}, u32[]{:S(2)}, u32[]{:S(2)}) collective-permute-start(f32[2,32,128]{2,1,0:T(8,128)S(1)} %pad_maximum_fusion.3), channel_id=1, source_target_pairs={{0,4},{1,5},{2,6},{3,7},{4,0},{5,1},{6,2},{7,3},{8,12},{9,13},{10,... | collective-permute-start | bytes 98312 | tf_op jit(solution)/shard_map/ppermute | solution.py:97
  116.3 3.0 %collective-permute-start.13 = (f32[2,32,128]{2,1,0:T(8,128)S(1)}, f32[2,32,128]{2,1,0:T(8,128)S(1)}, u32[]{:S(2)}, u32[]{:S(2)}) collective-permute-start(f32[2,32,128]{2,1,0:T(8,128)S(1)} %pad_maximum_fusion.4), channel_id=1, source_target_pairs={{0,4},{1,5},{2,6},{3,7},{4,0},{5,1},{6,2},{7,3},{8,12},{9,13},{10,... | collective-permute-start | bytes 98312 | tf_op jit(solution)/shard_map/ppermute | solution.py:97
  119.3 1.9 %collective-permute-start.8 = (f32[2,64,128]{2,1,0:T(8,128)S(1)}, f32[2,64,128]{2,1,0:T(8,128)S(1)}, u32[]{:S(2)}, u32[]{:S(2)}) collective-permute-start(f32[2,64,128]{2,1,0:T(8,128)S(1)} %maximum_select_fusion.4), channel_id=1, source_target_pairs={{0,2},{1,3},{2,0},{3,1},{4,6},{5,7},{6,4},{7,5},{8,10},{9,11},{10,... | collective-permute-start | bytes 196616 | tf_op jit(solution)/shard_map/ppermute | solution.py:97
  121.2 2.0 %collective-permute-start.14 = (f32[2,64,128]{2,1,0:T(8,128)S(1)}, f32[2,64,128]{2,1,0:T(8,128)S(1)}, u32[]{:S(2)}, u32[]{:S(2)}) collective-permute-start(f32[2,64,128]{2,1,0:T(8,128)S(1)} %maximum_select_fusion.5), channel_id=1, source_target_pairs={{0,2},{1,3},{2,0},{3,1},{4,6},{5,7},{6,4},{7,5},{8,10},{9,11},{10,... | collective-permute-start | bytes 196616 | tf_op jit(solution)/shard_map/ppermute | solution.py:97
  124.1 1.4 %collective-permute-done.14 = f32[2,64,128]{2,1,0:T(8,128)S(1)} collective-permute-done((f32[2,64,128]{2,1,0:T(8,128)S(1)}, f32[2,64,128]{2,1,0:T(8,128)S(1)}, u32[]{:S(2)}, u32[]{:S(2)}) %collective-permute-start.14) | collective-permute-done | bytes 65568 | tf_op jit(solution)/shard_map/ppermute | solution.py:97
  126.0 2.7 %collective-permute-done.9 = f32[2,128,128]{2,1,0:T(8,128)S(1)} collective-permute-done((f32[2,128,128]{2,1,0:T(8,128)S(1)}, f32[2,128,128]{2,1,0:T(8,128)S(1)}, u32[]{:S(2)}, u32[]{:S(2)}) %collective-permute-start.9) | collective-permute-done | bytes 131104 | tf_op jit(solution)/shard_map/ppermute | solution.py:97
  128.7 1.9 %collective-permute-done.15 = f32[2,128,128]{2,1,0:T(8,128)S(1)} collective-permute-done((f32[2,128,128]{2,1,0:T(8,128)S(1)}, f32[2,128,128]{2,1,0:T(8,128)S(1)}, u32[]{:S(2)}, u32[]{:S(2)}) %collective-permute-start.15) | collective-permute-done | bytes 131104 | tf_op jit(solution)/shard_map/ppermute | solution.py:97
  (59 shorter events, 7.5 us)
Async XLA Ops:
  7.2 1.3 copy-start
  7.2 5.0 %copy-start.3 = (s32[1,4,2]{1,2,0:T(2,128)S(1)}, s32[1,4,2]{1,2,0:T(2,128)}, u32[]{:S(2)}) copy-start(s32[1,4,2]{1,2,0:T(2,128)} %param.7) | copy-start | bytes 100
  7.2 9.1 %copy-start.2 = (s32[1,4,48]{2,1,0:T(4,128)S(1)}, s32[1,4,48]{2,1,0:T(4,128)}, u32[]{:S(2)}) copy-start(s32[1,4,48]{2,1,0:T(4,128)} %param.8) | copy-start | bytes 2308
  7.2 63.4 %all-gather.3.cloned.1.call-start = ((), (), s32[]{:S(2)}) async-start(), calls=%async_computation | async-start | bytes 10485760 | tf_op jit(solution)/shard_map/all_gather | solution.py:271
  7.9 34.9 %collective-permute-start.3 = (bf16[8,2,128,512]{3,2,1,0:T(8,128)(2,1)}, bf16[8,2,128,512]{3,2,1,0:T(8,128)(2,1)}, u32[]{:S(2)}, u32[]{:S(2)}) collective-permute-start(bf16[8,2,128,512]{3,2,1,0:T(8,128)(2,1)} %param.6), channel_id=1, source_target_pairs={{0,8},{8,0},{16,24},{24,16},{1,9},{9,1},{17,25},{25,17},{2,10},{10... | collective-permute-start | bytes 6291464 | tf_op jit(solution)/shard_map/ppermute | solution.py:289
  8.4 10.6 %collective-permute-start = (bf16[1,2,64,512]{3,2,1,0:T(8,128)(2,1)S(1)}, bf16[1,2,64,512]{3,2,1,0:T(8,128)(2,1)S(1)}, u32[]{:S(2)}, u32[]{:S(2)}) collective-permute-start(bf16[1,2,64,512]{3,2,1,0:T(8,128)(2,1)S(1)} %copy-done), channel_id=1, source_target_pairs={{0,4},{1,5},{2,6},{3,7},{4,0},{5,1},{6,2},{7,3},{8,12},{9,13},{10,... | collective-permute-start | bytes 393224 | tf_op jit(solution)/shard_map/ppermute | solution.py:50
  19.0 8.1 %collective-permute-start.1 = (bf16[2,2,64,512]{3,2,1,0:T(8,128)(2,1)S(1)}, bf16[2,2,64,512]{3,2,1,0:T(8,128)(2,1)S(1)}, u32[]{:S(2)}, u32[]{:S(2)}) collective-permute-start(bf16[2,2,64,512]{3,2,1,0:T(8,128)(2,1)S(1)} %pad_maximum_fusion.2), channel_id=1, source_target_pairs={{0,2},{1,3},{2,0},{3,1},{4,6},{5,7},{6,4},{7,5},{8,10},{9,11},{10,... | collective-permute-start | bytes 786440 | tf_op jit(solution)/shard_map/ppermute | solution.py:50
  27.2 13.0 %collective-permute-start.2 = (bf16[4,2,64,512]{3,2,1,0:T(8,128)(2,1)S(1)}, bf16[4,2,64,512]{3,2,1,0:T(8,128)(2,1)S(1)}, u32[]{:S(2)}, u32[]{:S(2)}) collective-permute-start(bf16[4,2,64,512]{3,2,1,0:T(8,128)(2,1)S(1)} %pad_maximum_fusion.1), channel_id=1, source_target_pairs={{0,1},{1,0},{2,3},{3,2},{4,5},{5,4},{6,7},{7,6},{8,9},{9,8},{10,11... | collective-permute-start | bytes 1572872 | tf_op jit(solution)/shard_map/ppermute | solution.py:50
  85.2 16.0 %copy-start.1 = (f32[2,2,128,128]{3,2,1,0:T(8,128)S(1)}, f32[2,2,128,128]{3,2,1,0:T(8,128)}, u32[]{:S(2)}) copy-start(f32[2,2,128,128]{3,2,1,0:T(8,128)} %shard_map.69) | copy-start | bytes 786436
  85.2 16.0 %collective-permute-start.4 = (f32[2,128,128]{2,1,0:T(8,128)S(1)}, f32[2,128,128]{2,1,0:T(8,128)S(1)}, u32[]{:S(2)}, u32[]{:S(2)}) collective-permute-start(f32[2,128,128]{2,1,0:T(8,128)S(1)} %constant_dynamic-slice_fusion.1), channel_id=1, source_target_pairs={{0,1},{1,0},{2,3},{3,2},{4,5},{5,4},{6,7},{7,6},{8,9},{9,8},{10,11... | collective-permute-start | bytes 393224 | tf_op jit(solution)/shard_map/ppermute | solution.py:92
  99.3 5.6 %collective-permute-start.10 = (f32[2,128,128]{2,1,0:T(8,128)S(1)}, f32[2,128,128]{2,1,0:T(8,128)S(1)}, u32[]{:S(2)}, u32[]{:S(2)}) collective-permute-start(f32[2,128,128]{2,1,0:T(8,128)S(1)} %constant_dynamic-slice_fusion), channel_id=1, source_target_pairs={{0,1},{1,0},{2,3},{3,2},{4,5},{5,4},{6,7},{7,6},{8,9},{9,8},{10,11... | collective-permute-start | bytes 393224 | tf_op jit(solution)/shard_map/ppermute | solution.py:92
  101.3 6.2 %collective-permute-start.5 = (f32[2,64,128]{2,1,0:T(8,128)S(1)}, f32[2,64,128]{2,1,0:T(8,128)S(1)}, u32[]{:S(2)}, u32[]{:S(2)}) collective-permute-start(f32[2,64,128]{2,1,0:T(8,128)S(1)} %get-tuple-element.13), channel_id=1, source_target_pairs={{0,2},{1,3},{2,0},{3,1},{4,6},{5,7},{6,4},{7,5},{8,10},{9,11},{10,... | collective-permute-start | bytes 196616 | tf_op jit(solution)/shard_map/ppermute | solution.py:92
  105.8 5.6 %collective-permute-start.11 = (f32[2,64,128]{2,1,0:T(8,128)S(1)}, f32[2,64,128]{2,1,0:T(8,128)S(1)}, u32[]{:S(2)}, u32[]{:S(2)}) collective-permute-start(f32[2,64,128]{2,1,0:T(8,128)S(1)} %get-tuple-element.17), channel_id=1, source_target_pairs={{0,2},{1,3},{2,0},{3,1},{4,6},{5,7},{6,4},{7,5},{8,10},{9,11},{10,... | collective-permute-start | bytes 196616 | tf_op jit(solution)/shard_map/ppermute | solution.py:92
  107.6 6.6 %collective-permute-start.6 = (f32[2,32,128]{2,1,0:T(8,128)S(1)}, f32[2,32,128]{2,1,0:T(8,128)S(1)}, u32[]{:S(2)}, u32[]{:S(2)}) collective-permute-start(f32[2,32,128]{2,1,0:T(8,128)S(1)} %get-tuple-element.21), channel_id=1, source_target_pairs={{0,4},{1,5},{2,6},{3,7},{4,0},{5,1},{6,2},{7,3},{8,12},{9,13},{10,... | collective-permute-start | bytes 98312 | tf_op jit(solution)/shard_map/ppermute | solution.py:92
  111.4 4.9 %collective-permute-start.12 = (f32[2,32,128]{2,1,0:T(8,128)S(1)}, f32[2,32,128]{2,1,0:T(8,128)S(1)}, u32[]{:S(2)}, u32[]{:S(2)}) collective-permute-start(f32[2,32,128]{2,1,0:T(8,128)S(1)} %get-tuple-element.25), channel_id=1, source_target_pairs={{0,4},{1,5},{2,6},{3,7},{4,0},{5,1},{6,2},{7,3},{8,12},{9,13},{10,... | collective-permute-start | bytes 98312 | tf_op jit(solution)/shard_map/ppermute | solution.py:92
  114.1 5.2 %collective-permute-start.7 = (f32[2,32,128]{2,1,0:T(8,128)S(1)}, f32[2,32,128]{2,1,0:T(8,128)S(1)}, u32[]{:S(2)}, u32[]{:S(2)}) collective-permute-start(f32[2,32,128]{2,1,0:T(8,128)S(1)} %pad_maximum_fusion.3), channel_id=1, source_target_pairs={{0,4},{1,5},{2,6},{3,7},{4,0},{5,1},{6,2},{7,3},{8,12},{9,13},{10,... | collective-permute-start | bytes 98312 | tf_op jit(solution)/shard_map/ppermute | solution.py:97
  116.3 4.9 %collective-permute-start.13 = (f32[2,32,128]{2,1,0:T(8,128)S(1)}, f32[2,32,128]{2,1,0:T(8,128)S(1)}, u32[]{:S(2)}, u32[]{:S(2)}) collective-permute-start(f32[2,32,128]{2,1,0:T(8,128)S(1)} %pad_maximum_fusion.4), channel_id=1, source_target_pairs={{0,4},{1,5},{2,6},{3,7},{4,0},{5,1},{6,2},{7,3},{8,12},{9,13},{10,... | collective-permute-start | bytes 98312 | tf_op jit(solution)/shard_map/ppermute | solution.py:97
  119.3 4.3 %collective-permute-start.8 = (f32[2,64,128]{2,1,0:T(8,128)S(1)}, f32[2,64,128]{2,1,0:T(8,128)S(1)}, u32[]{:S(2)}, u32[]{:S(2)}) collective-permute-start(f32[2,64,128]{2,1,0:T(8,128)S(1)} %maximum_select_fusion.4), channel_id=1, source_target_pairs={{0,2},{1,3},{2,0},{3,1},{4,6},{5,7},{6,4},{7,5},{8,10},{9,11},{10,... | collective-permute-start | bytes 196616 | tf_op jit(solution)/shard_map/ppermute | solution.py:97
  121.2 4.3 %collective-permute-start.14 = (f32[2,64,128]{2,1,0:T(8,128)S(1)}, f32[2,64,128]{2,1,0:T(8,128)S(1)}, u32[]{:S(2)}, u32[]{:S(2)}) collective-permute-start(f32[2,64,128]{2,1,0:T(8,128)S(1)} %maximum_select_fusion.5), channel_id=1, source_target_pairs={{0,2},{1,3},{2,0},{3,1},{4,6},{5,7},{6,4},{7,5},{8,10},{9,11},{10,... | collective-permute-start | bytes 196616 | tf_op jit(solution)/shard_map/ppermute | solution.py:97
  123.7 5.0 %collective-permute-start.9 = (f32[2,128,128]{2,1,0:T(8,128)S(1)}, f32[2,128,128]{2,1,0:T(8,128)S(1)}, u32[]{:S(2)}, u32[]{:S(2)}) collective-permute-start(f32[2,128,128]{2,1,0:T(8,128)S(1)} %maximum_select_fusion.2), channel_id=1, source_target_pairs={{0,1},{1,0},{2,3},{3,2},{4,5},{5,4},{6,7},{7,6},{8,9},{9,8},{10,11... | collective-permute-start | bytes 393224 | tf_op jit(solution)/shard_map/ppermute | solution.py:97
  125.6 5.0 %collective-permute-start.15 = (f32[2,128,128]{2,1,0:T(8,128)S(1)}, f32[2,128,128]{2,1,0:T(8,128)S(1)}, u32[]{:S(2)}, u32[]{:S(2)}) collective-permute-start(f32[2,128,128]{2,1,0:T(8,128)S(1)} %maximum_select_fusion.3), channel_id=1, source_target_pairs={{0,1},{1,0},{2,3},{3,2},{4,5},{5,4},{6,7},{7,6},{8,9},{9,8},{10,11... | collective-permute-start | bytes 393224 | tf_op jit(solution)/shard_map/ppermute | solution.py:97
Sparse Core Ops, SparseCore 0:
  9.6 60.9 all-gather.2

commit v8 on v6

--- a/solution.py
+++ b/solution.py
@@ -166,56 +166,65 @@
         best_ref, pow_ref = out_ref.at[0], out_ref.at[1]
     else:
         part_ref, acc_ref, m_ref = rest
-    j = pl.program_id(0)
+    jj = pl.program_id(0)
     i = pl.program_id(1)
+    span = 2 * rows_t
 
     if final:
-        @pl.when((j == 0) & (i == 0))
+        @pl.when((jj == 0) & (i == 0))
         def _():
             best_ref[...] = jnp.full(best_ref.shape, lowest_score, jnp.float32)
             pow_ref[...] = jnp.zeros(pow_ref.shape, jnp.float32)
 
         @pl.when(i == 0)
         def _():
-            acc_ref[...] = init_ref[:, 0]
+            acc_ref[...] = init_ref[...]
     else:
         @pl.when(i == 0)
         def _():
             acc_ref[...] = jnp.zeros(acc_ref.shape, jnp.float32)
 
-    for u, tm_ref in enumerate((tma_ref, tmb_ref)):
-        def mix(c, carry, u=u, tm_ref=tm_ref):
-            row = pl.multiple_of(c * chunk, chunk)
-            out_row = pl.multiple_of(off_ref[u] + c * chunk, chunk)
-            image_re = sp_ref[0, pl.ds(out_row, chunk), :]
-            image_im = sp_ref[1, pl.ds(out_row, chunk), :]
-            tmpl_re = tm_ref[0, 0, 0, pl.ds(row, chunk), :].astype(jnp.float32)
-            tmpl_im = tm_ref[0, 0, 1, pl.ds(row, chunk), :].astype(jnp.float32)
-            m_ref[pl.ds(out_row, chunk), pl.ds(0, size)] = (image_re * tmpl_re + image_im * tmpl_im).astype(jnp.bfloat16)
-            m_ref[pl.ds(out_row, chunk), pl.ds(size, size)] = (image_im * tmpl_re - image_re * tmpl_im).astype(jnp.bfloat16)
-            return carry
-
-        lax.fori_loop(0, rows_t // chunk, mix, 0, unroll=4)
+    for o in range(2):
+        for u, tm_ref in enumerate((tma_ref, tmb_ref)):
+            def mix(c, carry, u=u, o=o, tm_ref=tm_ref):
+                row = pl.multiple_of(c * chunk, chunk)
+                in_row = pl.multiple_of(off_ref[u] + c * chunk, chunk)
+                out_row = pl.multiple_of(o * span + off_ref[u] + c * chunk, chunk)
+                image_re = sp_ref[0, pl.ds(in_row, chunk), :]
+                image_im = sp_ref[1, pl.ds(in_row, chunk), :]
+                tmpl_re = tm_ref[0, o, 0, pl.ds(row, chunk), :].astype(jnp.float32)
+                tmpl_im = tm_ref[0, o, 1, pl.ds(row, chunk), :].astype(jnp.float32)
+                m_ref[pl.ds(out_row, chunk), pl.ds(0, size)] = (image_re * tmpl_re + image_im * tmpl_im).astype(jnp.bfloat16)
+                m_ref[pl.ds(out_row, chunk), pl.ds(size, size)] = (image_im * tmpl_re - image_re * tmpl_im).astype(jnp.bfloat16)
+                return carry
+
+            lax.fori_loop(0, rows_t // chunk, mix, 0, unroll=4)
 
     for p in range(peaks_n):
-        @pl.when(f_ref[p * blocks + j] > 0)
+        first = f_ref[p * blocks + 2 * jj]
+        second = f_ref[p * blocks + 2 * jj + 1]
+
+        @pl.when((first > 0) | (second > 0))
         def _():
             g = jnp.dot(m_ref[...], ct_ref[p], preferred_element_type=jnp.float32).astype(jnp.bfloat16)
-            part = jnp.dot(cr_ref[p], g[:, :width], preferred_element_type=jnp.float32)
-            part = part - jnp.dot(sr_ref[p], g[:, width:], preferred_element_type=jnp.float32)
-            acc_ref[p] = acc_ref[p] + part
+            for o in range(2):
+                rows = slice(o * span, (o + 1) * span)
+                part = jnp.dot(cr_ref[p], g[rows, :width], preferred_element_type=jnp.float32)
+                part = part - jnp.dot(sr_ref[p], g[rows, width:], preferred_element_type=jnp.float32)
+                acc_ref[p, o] = acc_ref[p, o] + part
 
     @pl.when(i == n_steps - 1)
     def _():
         if final:
             for p in range(peaks_n):
-                @pl.when(f_ref[p * blocks + j] > 0)
-                def _():
-                    score = acc_ref[p] / size
-                    best_ref[p] = jnp.maximum(best_ref[p], score)
-                    pow_ref[p] = pow_ref[p] + score * score
+                for o in range(2):
+                    @pl.when(f_ref[p * blocks + 2 * jj + o] > 0)
+                    def _():
+                        score = acc_ref[p, o] / size
+                        best_ref[p] = jnp.maximum(best_ref[p], score)
+                        pow_ref[p] = pow_ref[p] + score * score
         else:
-            part_ref[:, 0] = acc_ref[...]
+            part_ref[...] = acc_ref[...]
 
 
 def match_rows(flags, tas, tbs, rids, offs, tmpl_a, tmpl_b, spec, col_table, cos_t, sin_t, init=None):
@@ -229,15 +238,15 @@
     flops = blocks * peaks_n * n_steps * (2 * span * 2 * size * 2 * width + 2 * 2 * width * span * width)
     cost = pl.CostEstimate(flops=flops, transcendentals=0, bytes_accessed=n_steps * blocks * 2 * span * size * 6 + col_table.size * 2)
     in_specs = [
-        pl.BlockSpec((1, 1, 2, rows_t, size), lambda j, i, f, ta, tb, r, o: (ta[i], j, 0, 0, 0)),
-        pl.BlockSpec((1, 1, 2, rows_t, size), lambda j, i, f, ta, tb, r, o: (tb[i], j, 0, 0, 0)),
+        pl.BlockSpec((1, 2, 2, rows_t, size), lambda j, i, f, ta, tb, r, o: (ta[i], j, 0, 0, 0)),
+        pl.BlockSpec((1, 2, 2, rows_t, size), lambda j, i, f, ta, tb, r, o: (tb[i], j, 0, 0, 0)),
         pl.BlockSpec((2, span, size), lambda j, i, f, ta, tb, r, o: (0, r[i], 0)),
         pl.BlockSpec(col_table.shape, lambda j, i, f, ta, tb, r, o: (0, 0, 0)),
         pl.BlockSpec((peaks_n, width, span), lambda j, i, f, ta, tb, r, o: (0, 0, r[i])),
         pl.BlockSpec((peaks_n, width, span), lambda j, i, f, ta, tb, r, o: (0, 0, r[i])),
     ]
     args = [flags, tas, tbs, rids, offs, tmpl_a, tmpl_b, spec, col_table, cos_t, sin_t]
-    part_spec = pl.BlockSpec((peaks_n, 1, width, width), lambda j, i, f, ta, tb, r, o: (0, j, 0, 0))
+    part_spec = pl.BlockSpec((peaks_n, 2, width, width), lambda j, i, f, ta, tb, r, o: (0, j, 0, 0))
     if final:
         in_specs.append(part_spec)
         args.append(init)
@@ -250,10 +259,10 @@
         kernel,
         grid_spec=pltpu.PrefetchScalarGridSpec(
             num_scalar_prefetch=5,
-            grid=(blocks, n_steps),
+            grid=(blocks // 2, n_steps),
             in_specs=in_specs,
             out_specs=out_specs,
-            scratch_shapes=[pltpu.VMEM((peaks_n, width, width), jnp.float32), pltpu.VMEM((span, 2 * size), jnp.bfloat16)],
+            scratch_shapes=[pltpu.VMEM((peaks_n, 2, width, width), jnp.float32), pltpu.VMEM((2 * span, 2 * size), jnp.bfloat16)],
         ),
         out_shape=out_shape,
         compiler_params=pltpu.CompilerParams(dimension_semantics=("arbitrary", "arbitrary")),
@@ -280,7 +289,7 @@
     is_listed = jnp.any(listed_ids[:, :, None] == global_ids[None, None, :], axis=1)
     flags = is_listed.astype(jnp.int32).reshape(-1)
     best_shape = (listed.shape[1], width, width)
-    if rows_t % 128 != 0 or tiles % 2 != 0:
+    if rows_t % 128 != 0 or tiles % 2 != 0 or block_size % 2 != 0:
         best_part, power_part = match(flags, tmpl, spec, col_table, cos_t, sin_t)
     else:
         me = lax.axis_index("tile")

time: 137 us -> 135 us (0.985)
  waiting for transfers between devices: 38.6 us -> 49.6 us
  Pallas kernels: 42.3 us -> 31.5 us
  starting transfers between devices: 17.8 us -> 16.1 us
    pallas_call x2, Pallas kernels: 42.3 us -> 31.5 us  [match_rows(): pl.pallas_call(kernel, grid_spec=pltpu.PrefetchScalarGridSpec(num_scalar_...]
    all_gather x1, waiting for transfers between devices: 7.04 us -> 12.4 us  [local(): tmpl = lax.all_gather(template_spectra, 'tile', axis=0)]
    ppermute x3, waiting for transfers between devices: 10.3 us -> 14.5 us  [reduce_joined(): got = lax.ppermute(cur, axis, xor_pairs(n, k))]
    ppermute x3, starting transfers between devices: 6.41 us -> 2.97 us  [reduce_joined(): got = lax.ppermute(cur, axis, xor_pairs(n, k))]
    ppermute x3, starting transfers between devices: 4.94 us -> 6.66 us  [reduce_joined(): got = lax.ppermute(send, axis, xor_pairs(n, k))]
    ppermute x3, waiting for transfers between devices: 12.7 us -> 14.1 us  [reduce_joined(): got = lax.ppermute(send, axis, xor_pairs(n, k))]
  transfers between devices with their start and end apart: 11 -> 11, of which waited for: 10 -> 10; matrix products, arithmetic and copies ran while one was open for 15% -> 15% of each run, Pallas kernels for 15% -> 11%
where the time goes in v8:
time: 135 us
  waiting for transfers between devices  49.6 us (37%)
  Pallas kernels  31.5 us (23%)
  other arithmetic  19.5 us (14%)
  starting transfers between devices  16.1 us (12%)
  between operations  14.2 us (11%)
  local copies, waits for them, and re-layouts  3.77 us (3%)
    pallas_call x2, Pallas kernels, match_rows(): pl.pallas_call(kernel, grid_spec=pltpu.PrefetchScalarGridSpec(num_scalar_...  31.5 us
    ppermute x3, waiting for transfers between devices, reduce_joined(): got = lax.ppermute(cur, axis, xor_pairs(n, k))  14.5 us
    ppermute x3, waiting for transfers between devices, reduce_joined(): got = lax.ppermute(send, axis, xor_pairs(n, k))  14.1 us
    all_gather x1, waiting for transfers between devices, local(): tmpl = lax.all_gather(template_spectra, 'tile', axis=0)  12.4 us
    convert_element_type x2, other arithmetic, angle_tables(): jnp.sin(angle).astype(jnp.bfloat16)  10 us
    ppermute x3, waiting for transfers between devices, gather_rows(): got = lax.ppermute(blocks, axis, xor_pairs(n, k))  7.95 us
    ppermute x3, starting transfers between devices, reduce_joined(): got = lax.ppermute(send, axis, xor_pairs(n, k))  6.66 us
    ppermute x3, starting transfers between devices, gather_rows(): got = lax.ppermute(blocks, axis, xor_pairs(n, k))  5.92 us
  transfers between devices with their start and end apart: 11, of which 10 were waited for; matrix products, arithmetic and copies ran while one was open for 15% of the time, Pallas kernels for 11%

profile of v8, /device:TPU:0, one launch (start us, length us, event | category | flops | bytes accessed | tf_op | source)
XLA Modules:
  0.0 134.7 jit_solution(2100577112882520880)
XLA Ops:
  7.2 0.7 all-gather.3.cloned.1.call-update
  8.4 3.7 %collective-permute-start = (bf16[1,2,64,512]{3,2,1,0:T(8,128)(2,1)S(1)}, bf16[1,2,64,512]{3,2,1,0:T(8,128)(2,1)S(1)}, u32[]{:S(2)}, u32[]{:S(2)}) collective-permute-start(bf16[1,2,64,512]{3,2,1,0:T(8,128)(2,1)S(1)} %copy-done), channel_id=1, source_target_pairs={{0,4},{1,5},{2,6},{3,7},{4,0},{5,1},{6,2},{7,3},{8,12},{9,13},{10,... | collective-permute-start | bytes 393224 | tf_op jit(solution)/shard_map/ppermute | solution.py:50
  12.2 4.0 %fusion.12 = bf16[4,512,128]{2,1,0:T(8,128)(2,1)S(1)} fusion(s32[4,128]{1,0:T(4,128)S(1)} %get-tuple-element.21), kind=kLoop, calls=%fused_computation.39 | loop fusion | flops 4718592 | bytes 526336 | tf_op jit(solution)/shard_map/neg | solution.py:38
  16.5 2.5 %collective-permute-done = bf16[1,2,64,512]{3,2,1,0:T(8,128)(2,1)S(1)} collective-permute-done((bf16[1,2,64,512]{3,2,1,0:T(8,128)(2,1)S(1)}, bf16[1,2,64,512]{3,2,1,0:T(8,128)(2,1)S(1)}, u32[]{:S(2)}, u32[]{:S(2)}) %collective-permute-start) | collective-permute-done | bytes 131104 | tf_op jit(solution)/shard_map/ppermute | solution.py:50
  19.0 0.8 collective-permute-start.1
  19.9 0.6 iota_multiply_fusion.off_ref
  20.4 0.6 reshape.156.f_ref
  21.0 4.4 %sine_convert_fusion.1 = (bf16[4,512,128]{2,1,0:T(8,128)(2,1)S(1)}, bf16[4,512,128]{2,1,0:T(8,128)(2,1)S(1)}) fusion(s32[4,128]{1,0:T(4,128)S(1)} %get-tuple-element.21), kind=kLoop, calls=%fused_computation.20 | loop fusion | flops 4194304 | bytes 1050624 | tf_op jit(solution)/shard_map/convert_element_type | solution.py:31
  25.4 1.7 %collective-permute-done.1 = bf16[2,2,64,512]{3,2,1,0:T(8,128)(2,1)S(1)} collective-permute-done((bf16[2,2,64,512]{3,2,1,0:T(8,128)(2,1)S(1)}, bf16[2,2,64,512]{3,2,1,0:T(8,128)(2,1)S(1)}, u32[]{:S(2)}, u32[]{:S(2)}) %collective-permute-start.1) | collective-permute-done | bytes 262176 | tf_op jit(solution)/shard_map/ppermute | solution.py:50
  27.2 1.4 %collective-permute-start.2 = (bf16[4,2,64,512]{3,2,1,0:T(8,128)(2,1)S(1)}, bf16[4,2,64,512]{3,2,1,0:T(8,128)(2,1)S(1)}, u32[]{:S(2)}, u32[]{:S(2)}) collective-permute-start(bf16[4,2,64,512]{3,2,1,0:T(8,128)(2,1)S(1)} %pad_maximum_fusion.1), channel_id=1, source_target_pairs={{0,1},{1,0},{2,3},{3,2},{4,5},{5,4},{6,7},{7,6},{8,9},{9,8},{10,11... | collective-permute-start | bytes 1572872 | tf_op jit(solution)/shard_map/ppermute | solution.py:50
  28.6 0.6 add_multiply_fusion.off_ref
  29.3 1.6 %maximum_maximum_fusion.ct_ref = bf16[4,1024,256]{2,1,0:T(8,128)(2,1)} fusion(bf16[4,512,128]{2,1,0:T(8,128)(2,1)S(1)} %get-tuple-element.17, bf16[4,512,128]{2,1,0:T(8,128)(2,1)S(1)} %fusion.12, bf16[4,512,128]{2,1,0:T(8,128)(2,1)S(1)} %get-tuple-element.16), kind=kLoop, calls=%fused_computation.1 | loop fusion | flops 8388608 | bytes 3670016 | tf_op jit(solution)/shard_map/concatenate | solution.py:39
  30.8 5.6 %sine_convert_fusion = (bf16[4,128,512]{2,1,0:T(8,128)(2,1)}, bf16[4,128,512]{2,1,0:T(8,128)(2,1)}) fusion(s32[4,128]{1,0:T(4,128)S(1)} %get-tuple-element.20), kind=kLoop, calls=%fused_computation.16 | loop fusion | flops 4194304 | bytes 1050624 | tf_op jit(solution)/shard_map/convert_element_type | solution.py:31
  36.4 3.7 %collective-permute-done.2 = bf16[4,2,64,512]{3,2,1,0:T(8,128)(2,1)S(1)} collective-permute-done((bf16[4,2,64,512]{3,2,1,0:T(8,128)(2,1)S(1)}, bf16[4,2,64,512]{3,2,1,0:T(8,128)(2,1)S(1)}, u32[]{:S(2)}, u32[]{:S(2)}) %collective-permute-start.2) | collective-permute-done | bytes 524320 | tf_op jit(solution)/shard_map/ppermute | solution.py:50
  40.3 0.6 gather_fusion
  41.2 1.6 %copy.9 = f32[2,8,64,512]{3,2,1,0:T(8,128)} copy(f32[2,8,64,512]{3,2,0,1:T(8,128)S(1)} %convert_bitcast_fusion) | data formatting | bytes 4194304 | tf_op jit(solution)/shard_map/convert_element_type | solution.py:297
  42.8 15.5 %shard_map.68.rest_0_ = f32[4,8,128,128]{3,2,1,0:T(8,128)} custom-call(s32[32]{0:T(128)} %reshape.156.f_ref, s32[1]{0:T(128)} %constant.139.clone.1.ta_ref.tb_ref, s32[1]{0:T(128)} %constant.139.clone.1.ta_ref.tb_ref, s32[1]{0:T(128)} %bitcast.1.rid_ref, s32[2]{0:T(128)} %add_multiply_fusion.off_ref, bf16[1,8,2,128,512]{4,3,2,1,0:T(8,128)(2,1)} %bitcast.11.tma_ref, ...), custom_call_target="tpu_custom_call" | custom-call | flops 4831838208 | bytes 14680064 | tf_op jit(solution)/shard_map/pallas_call | solution.py:258
  58.2 12.4 %all-gather.3.cloned.1.call-done = bf16[32,2,128,512]{3,2,1,0:T(8,128)(2,1)} async-done(((bf16[8,2,128,512]{3,2,1,0:T(8,128)(2,1)}), bf16[32,2,128,512]{3,2,1,0:T(8,128)(2,1)}) %all-gather.3.cloned.1.call-update) | async-done | bytes 8388624 | tf_op jit(solution)/shard_map/all_gather | solution.py:278
  70.6 16.0 %shard_map.69 = f32[2,4,128,128]{3,2,1,0:T(8,128)} custom-call(s32[32]{0:T(128)} %reshape.156.f_ref, s32[1]{0:T(128)S(6)} %mul.65.ta_ref, s32[1]{0:T(128)S(6)} %add.151.tb_ref, s32[1]{0:T(128)S(6)} %convert_element_type.41.rid_ref, s32[2]{0:T(128)} %iota_multiply_fusion.off_ref, bf16[4,8,2,128,512]{4,3,2,1,0:T(8,128)(2,1)} %bitcast.20, ...), custom_call_target="tpu_custom_call" | custom-call | flops 4831838208 | bytes 14680064 | tf_op jit(solution)/shard_map/pallas_call | solution.py:258
  86.6 1.0 constant_dynamic-slice_fusion
  87.6 2.2 %collective-permute-start.4 = (f32[2,256,128]{2,1,0:T(8,128)S(1)}, f32[2,256,128]{2,1,0:T(8,128)S(1)}, u32[]{:S(2)}, u32[]{:S(2)}) collective-permute-start(f32[2,256,128]{2,1,0:T(8,128)S(1)} %constant_dynamic-slice_fusion), channel_id=1, source_target_pairs={{0,1},{1,0},{2,3},{3,2},{4,5},{5,4},{6,7},{7,6},{8,9},{9,8},{10,11... | collective-permute-start | bytes 786440 | tf_op jit(solution)/shard_map/ppermute | solution.py:92
  89.8 7.0 %collective-permute-done.4 = f32[2,256,128]{2,1,0:T(8,128)S(1)} collective-permute-done((f32[2,256,128]{2,1,0:T(8,128)S(1)}, f32[2,256,128]{2,1,0:T(8,128)S(1)}, u32[]{:S(2)}, u32[]{:S(2)}) %collective-permute-start.4) | collective-permute-done | bytes 262176 | tf_op jit(solution)/shard_map/ppermute | solution.py:92
  96.8 1.0 slice_add_fusion
  97.9 1.3 collective-permute-start.5
  99.1 4.1 %collective-permute-done.5 = f32[2,128,128]{2,1,0:T(8,128)S(1)} collective-permute-done((f32[2,128,128]{2,1,0:T(8,128)S(1)}, f32[2,128,128]{2,1,0:T(8,128)S(1)}, u32[]{:S(2)}, u32[]{:S(2)}) %collective-permute-start.5) | collective-permute-done | bytes 131104 | tf_op jit(solution)/shard_map/ppermute | solution.py:92
  103.3 3.2 %collective-permute-start.6 = (f32[2,64,128]{2,1,0:T(8,128)S(1)}, f32[2,64,128]{2,1,0:T(8,128)S(1)}, u32[]{:S(2)}, u32[]{:S(2)}) collective-permute-start(f32[2,64,128]{2,1,0:T(8,128)S(1)} %get-tuple-element.13), channel_id=1, source_target_pairs={{0,4},{1,5},{2,6},{3,7},{4,0},{5,1},{6,2},{7,3},{8,12},{9,13},{10,... | collective-permute-start | bytes 196616 | tf_op jit(solution)/shard_map/ppermute | solution.py:92
  106.5 2.9 %collective-permute-done.6 = f32[2,64,128]{2,1,0:T(8,128)S(1)} collective-permute-done((f32[2,64,128]{2,1,0:T(8,128)S(1)}, f32[2,64,128]{2,1,0:T(8,128)S(1)}, u32[]{:S(2)}, u32[]{:S(2)}) %collective-permute-start.6) | collective-permute-done | bytes 65568 | tf_op jit(solution)/shard_map/ppermute | solution.py:92
  109.5 2.4 %collective-permute-start.7 = (f32[2,64,128]{2,1,0:T(8,128)S(1)}, f32[2,64,128]{2,1,0:T(8,128)S(1)}, u32[]{:S(2)}, u32[]{:S(2)}) collective-permute-start(f32[2,64,128]{2,1,0:T(8,128)S(1)} %pad_maximum_fusion.3), channel_id=1, source_target_pairs={{0,4},{1,5},{2,6},{3,7},{4,0},{5,1},{6,2},{7,3},{8,12},{9,13},{10,... | collective-permute-start | bytes 196616 | tf_op jit(solution)/shard_map/ppermute | solution.py:97
  111.8 3.6 %collective-permute-done.7 = f32[2,64,128]{2,1,0:T(8,128)S(1)} collective-permute-done((f32[2,64,128]{2,1,0:T(8,128)S(1)}, f32[2,64,128]{2,1,0:T(8,128)S(1)}, u32[]{:S(2)}, u32[]{:S(2)}) %collective-permute-start.7) | collective-permute-done | bytes 65568 | tf_op jit(solution)/shard_map/ppermute | solution.py:97
  116.0 4.5 %collective-permute-done.8 = f32[2,128,128]{2,1,0:T(8,128)S(1)} collective-permute-done((f32[2,128,128]{2,1,0:T(8,128)S(1)}, f32[2,128,128]{2,1,0:T(8,128)S(1)}, u32[]{:S(2)}, u32[]{:S(2)}) %collective-permute-start.8) | collective-permute-done | bytes 131104 | tf_op jit(solution)/shard_map/ppermute | solution.py:97
  120.7 6.4 %collective-permute-done.9 = f32[2,256,128]{2,1,0:T(8,128)S(1)} collective-permute-done((f32[2,256,128]{2,1,0:T(8,128)S(1)}, f32[2,256,128]{2,1,0:T(8,128)S(1)}, u32[]{:S(2)}, u32[]{:S(2)}) %collective-permute-start.9) | collective-permute-done | bytes 262176 | tf_op jit(solution)/shard_map/ppermute | solution.py:97
  127.0 0.8 slice_multiply_fusion
  (31 shorter events, 2.1 us)
Async XLA Ops:
  7.2 1.3 copy-start
  7.2 5.0 %copy-start.2 = (s32[1,4,2]{1,2,0:T(2,128)S(1)}, s32[1,4,2]{1,2,0:T(2,128)}, u32[]{:S(2)}) copy-start(s32[1,4,2]{1,2,0:T(2,128)} %param.7) | copy-start | bytes 100
  7.2 9.1 %copy-start.1 = (s32[1,4,48]{2,1,0:T(4,128)S(1)}, s32[1,4,48]{2,1,0:T(4,128)}, u32[]{:S(2)}) copy-start(s32[1,4,48]{2,1,0:T(4,128)} %param.8) | copy-start | bytes 2308
  7.2 63.4 %all-gather.3.cloned.1.call-start = ((), (), s32[]{:S(2)}) async-start(), calls=%async_computation | async-start | bytes 10485760 | tf_op jit(solution)/shard_map/all_gather | solution.py:278
  7.9 34.8 %collective-permute-start.3 = (bf16[8,2,128,512]{3,2,1,0:T(8,128)(2,1)}, bf16[8,2,128,512]{3,2,1,0:T(8,128)(2,1)}, u32[]{:S(2)}, u32[]{:S(2)}) collective-permute-start(bf16[8,2,128,512]{3,2,1,0:T(8,128)(2,1)} %param.6), channel_id=1, source_target_pairs={{0,8},{8,0},{16,24},{24,16},{1,9},{9,1},{17,25},{25,17},{2,10},{10... | collective-permute-start | bytes 6291464 | tf_op jit(solution)/shard_map/ppermute | solution.py:296
  8.4 10.6 %collective-permute-start = (bf16[1,2,64,512]{3,2,1,0:T(8,128)(2,1)S(1)}, bf16[1,2,64,512]{3,2,1,0:T(8,128)(2,1)S(1)}, u32[]{:S(2)}, u32[]{:S(2)}) collective-permute-start(bf16[1,2,64,512]{3,2,1,0:T(8,128)(2,1)S(1)} %copy-done), channel_id=1, source_target_pairs={{0,4},{1,5},{2,6},{3,7},{4,0},{5,1},{6,2},{7,3},{8,12},{9,13},{10,... | collective-permute-start | bytes 393224 | tf_op jit(solution)/shard_map/ppermute | solution.py:50
  19.0 8.1 %collective-permute-start.1 = (bf16[2,2,64,512]{3,2,1,0:T(8,128)(2,1)S(1)}, bf16[2,2,64,512]{3,2,1,0:T(8,128)(2,1)S(1)}, u32[]{:S(2)}, u32[]{:S(2)}) collective-permute-start(bf16[2,2,64,512]{3,2,1,0:T(8,128)(2,1)S(1)} %pad_maximum_fusion.2), channel_id=1, source_target_pairs={{0,2},{1,3},{2,0},{3,1},{4,6},{5,7},{6,4},{7,5},{8,10},{9,11},{10,... | collective-permute-start | bytes 786440 | tf_op jit(solution)/shard_map/ppermute | solution.py:50
  27.2 13.0 %collective-permute-start.2 = (bf16[4,2,64,512]{3,2,1,0:T(8,128)(2,1)S(1)}, bf16[4,2,64,512]{3,2,1,0:T(8,128)(2,1)S(1)}, u32[]{:S(2)}, u32[]{:S(2)}) collective-permute-start(bf16[4,2,64,512]{3,2,1,0:T(8,128)(2,1)S(1)} %pad_maximum_fusion.1), channel_id=1, source_target_pairs={{0,1},{1,0},{2,3},{3,2},{4,5},{5,4},{6,7},{7,6},{8,9},{9,8},{10,11... | collective-permute-start | bytes 1572872 | tf_op jit(solution)/shard_map/ppermute | solution.py:50
  87.6 9.2 %collective-permute-start.4 = (f32[2,256,128]{2,1,0:T(8,128)S(1)}, f32[2,256,128]{2,1,0:T(8,128)S(1)}, u32[]{:S(2)}, u32[]{:S(2)}) collective-permute-start(f32[2,256,128]{2,1,0:T(8,128)S(1)} %constant_dynamic-slice_fusion), channel_id=1, source_target_pairs={{0,1},{1,0},{2,3},{3,2},{4,5},{5,4},{6,7},{7,6},{8,9},{9,8},{10,11... | collective-permute-start | bytes 786440 | tf_op jit(solution)/shard_map/ppermute | solution.py:92
  97.9 5.4 %collective-permute-start.5 = (f32[2,128,128]{2,1,0:T(8,128)S(1)}, f32[2,128,128]{2,1,0:T(8,128)S(1)}, u32[]{:S(2)}, u32[]{:S(2)}) collective-permute-start(f32[2,128,128]{2,1,0:T(8,128)S(1)} %get-tuple-element.9), channel_id=1, source_target_pairs={{0,2},{1,3},{2,0},{3,1},{4,6},{5,7},{6,4},{7,5},{8,10},{9,11},{10,... | collective-permute-start | bytes 393224 | tf_op jit(solution)/shard_map/ppermute | solution.py:92
  103.3 6.1 %collective-permute-start.6 = (f32[2,64,128]{2,1,0:T(8,128)S(1)}, f32[2,64,128]{2,1,0:T(8,128)S(1)}, u32[]{:S(2)}, u32[]{:S(2)}) collective-permute-start(f32[2,64,128]{2,1,0:T(8,128)S(1)} %get-tuple-element.13), channel_id=1, source_target_pairs={{0,4},{1,5},{2,6},{3,7},{4,0},{5,1},{6,2},{7,3},{8,12},{9,13},{10,... | collective-permute-start | bytes 196616 | tf_op jit(solution)/shard_map/ppermute | solution.py:92
  109.5 6.0 %collective-permute-start.7 = (f32[2,64,128]{2,1,0:T(8,128)S(1)}, f32[2,64,128]{2,1,0:T(8,128)S(1)}, u32[]{:S(2)}, u32[]{:S(2)}) collective-permute-start(f32[2,64,128]{2,1,0:T(8,128)S(1)} %pad_maximum_fusion.3), channel_id=1, source_target_pairs={{0,4},{1,5},{2,6},{3,7},{4,0},{5,1},{6,2},{7,3},{8,12},{9,13},{10,... | collective-permute-start | bytes 196616 | tf_op jit(solution)/shard_map/ppermute | solution.py:97
  115.5 5.0 %collective-permute-start.8 = (f32[2,128,128]{2,1,0:T(8,128)S(1)}, f32[2,128,128]{2,1,0:T(8,128)S(1)}, u32[]{:S(2)}, u32[]{:S(2)}) collective-permute-start(f32[2,128,128]{2,1,0:T(8,128)S(1)} %maximum_select_fusion.2), channel_id=1, source_target_pairs={{0,2},{1,3},{2,0},{3,1},{4,6},{5,7},{6,4},{7,5},{8,10},{9,11},{10,... | collective-permute-start | bytes 393224 | tf_op jit(solution)/shard_map/ppermute | solution.py:97
  120.6 6.4 %collective-permute-start.9 = (f32[2,256,128]{2,1,0:T(8,128)S(1)}, f32[2,256,128]{2,1,0:T(8,128)S(1)}, u32[]{:S(2)}, u32[]{:S(2)}) collective-permute-start(f32[2,256,128]{2,1,0:T(8,128)S(1)} %maximum_select_fusion.1), channel_id=1, source_target_pairs={{0,1},{1,0},{2,3},{3,2},{4,5},{5,4},{6,7},{7,6},{8,9},{9,8},{10,11... | collective-permute-start | bytes 786440 | tf_op jit(solution)/shard_map/ppermute | solution.py:97
Sparse Core Ops, SparseCore 0:
  9.6 60.9 all-gather.2

commit v9 on v8

--- a/solution.py
+++ b/solution.py
@@ -160,7 +160,7 @@
     )(flags, tmpl, spec, col_table, cos_t, sin_t)
 
 
-def rows_kernel(blocks, size, width, rows_t, peaks_n, chunk, n_steps, final, f_ref, ta_ref, tb_ref, rid_ref, off_ref, tma_ref, tmb_ref, sp_ref, ct_ref, cr_ref, sr_ref, *rest):
+def rows_kernel(blocks, size, width, rows_t, peaks_n, chunk, n_steps, final, per, f_ref, ta_ref, tb_ref, rid_ref, off_ref, tma_ref, tmb_ref, sp_ref, ct_ref, cr_ref, sr_ref, *rest):
     if final:
         init_ref, out_ref, acc_ref, m_ref = rest
         best_ref, pow_ref = out_ref.at[0], out_ref.at[1]
@@ -184,7 +184,7 @@
         def _():
             acc_ref[...] = jnp.zeros(acc_ref.shape, jnp.float32)
 
-    for o in range(2):
+    for o in range(per):
         for u, tm_ref in enumerate((tma_ref, tmb_ref)):
             def mix(c, carry, u=u, o=o, tm_ref=tm_ref):
                 row = pl.multiple_of(c * chunk, chunk)
@@ -201,13 +201,14 @@
             lax.fori_loop(0, rows_t // chunk, mix, 0, unroll=4)
 
     for p in range(peaks_n):
-        first = f_ref[p * blocks + 2 * jj]
-        second = f_ref[p * blocks + 2 * jj + 1]
-
-        @pl.when((first > 0) | (second > 0))
+        count = f_ref[p * blocks + per * jj]
+        for o in range(1, per):
+            count = count + f_ref[p * blocks + per * jj + o]
+
+        @pl.when(count > 0)
         def _():
             g = jnp.dot(m_ref[...], ct_ref[p], preferred_element_type=jnp.float32).astype(jnp.bfloat16)
-            for o in range(2):
+            for o in range(per):
                 rows = slice(o * span, (o + 1) * span)
                 part = jnp.dot(cr_ref[p], g[rows, :width], preferred_element_type=jnp.float32)
                 part = part - jnp.dot(sr_ref[p], g[rows, width:], preferred_element_type=jnp.float32)
@@ -217,8 +218,8 @@
     def _():
         if final:
             for p in range(peaks_n):
-                for o in range(2):
-                    @pl.when(f_ref[p * blocks + 2 * jj + o] > 0)
+                for o in range(per):
+                    @pl.when(f_ref[p * blocks + per * jj + o] > 0)
                     def _():
                         score = acc_ref[p, o] / size
                         best_ref[p] = jnp.maximum(best_ref[p], score)
@@ -234,19 +235,20 @@
     final = init is not None
     chunk = math.gcd(rows_t, 16)
     span = 2 * rows_t
-    kernel = functools.partial(rows_kernel, blocks, size, width, rows_t, peaks_n, chunk, n_steps, final)
+    per = 4 if blocks % 4 == 0 else 2
+    kernel = functools.partial(rows_kernel, blocks, size, width, rows_t, peaks_n, chunk, n_steps, final, per)
     flops = blocks * peaks_n * n_steps * (2 * span * 2 * size * 2 * width + 2 * 2 * width * span * width)
     cost = pl.CostEstimate(flops=flops, transcendentals=0, bytes_accessed=n_steps * blocks * 2 * span * size * 6 + col_table.size * 2)
     in_specs = [
-        pl.BlockSpec((1, 2, 2, rows_t, size), lambda j, i, f, ta, tb, r, o: (ta[i], j, 0, 0, 0)),
-        pl.BlockSpec((1, 2, 2, rows_t, size), lambda j, i, f, ta, tb, r, o: (tb[i], j, 0, 0, 0)),
+        pl.BlockSpec((1, per, 2, rows_t, size), lambda j, i, f, ta, tb, r, o: (ta[i], j, 0, 0, 0)),
+        pl.BlockSpec((1, per, 2, rows_t, size), lambda j, i, f, ta, tb, r, o: (tb[i], j, 0, 0, 0)),
         pl.BlockSpec((2, span, size), lambda j, i, f, ta, tb, r, o: (0, r[i], 0)),
         pl.BlockSpec(col_table.shape, lambda j, i, f, ta, tb, r, o: (0, 0, 0)),
         pl.BlockSpec((peaks_n, width, span), lambda j, i, f, ta, tb, r, o: (0, 0, r[i])),
         pl.BlockSpec((peaks_n, width, span), lambda j, i, f, ta, tb, r, o: (0, 0, r[i])),
     ]
     args = [flags, tas, tbs, rids, offs, tmpl_a, tmpl_b, spec, col_table, cos_t, sin_t]
-    part_spec = pl.BlockSpec((peaks_n, 2, width, width), lambda j, i, f, ta, tb, r, o: (0, j, 0, 0))
+    part_spec = pl.BlockSpec((peaks_n, per, width, width), lambda j, i, f, ta, tb, r, o: (0, j, 0, 0))
     if final:
         in_specs.append(part_spec)
         args.append(init)
@@ -259,10 +261,10 @@
         kernel,
         grid_spec=pltpu.PrefetchScalarGridSpec(
             num_scalar_prefetch=5,
-            grid=(blocks // 2, n_steps),
+            grid=(blocks // per, n_steps),
             in_specs=in_specs,
             out_specs=out_specs,
-            scratch_shapes=[pltpu.VMEM((peaks_n, 2, width, width), jnp.float32), pltpu.VMEM((2 * span, 2 * size), jnp.bfloat16)],
+            scratch_shapes=[pltpu.VMEM((peaks_n, per, width, width), jnp.float32), pltpu.VMEM((per * span, 2 * size), jnp.bfloat16)],
         ),
         out_shape=out_shape,
         compiler_params=pltpu.CompilerParams(dimension_semantics=("arbitrary", "arbitrary")),

time: 135 us -> 131 us (0.970)
  waiting for transfers between devices: 49.6 us -> 46.7 us
  Pallas kernels: 31.5 us -> 29.5 us
    ppermute x3, waiting for transfers between devices: 14.5 us -> 11.1 us  [reduce_joined(): got = lax.ppermute(cur, axis, xor_pairs(n, k))]
    ppermute x3, starting transfers between devices: 2.97 us -> 5.69 us  [reduce_joined(): got = lax.ppermute(cur, axis, xor_pairs(n, k))]
    pallas_call x2, Pallas kernels: 31.5 us -> 29.5 us  [match_rows(): pl.pallas_call(kernel, grid_spec=pltpu.PrefetchScalarGridSpec(num_scalar_...]
    ppermute x3, starting transfers between devices: 6.66 us -> 5.25 us  [reduce_joined(): got = lax.ppermute(send, axis, xor_pairs(n, k))]
  transfers between devices with their start and end apart: 11 -> 11, of which waited for: 10 -> 10; matrix products, arithmetic and copies ran while one was open for 15% -> 16% of each run, Pallas kernels for 11% -> 11%
where the time goes in v9:
time: 131 us
  waiting for transfers between devices  46.7 us (36%)
  Pallas kernels  29.5 us (23%)
  other arithmetic  19.5 us (15%)
  starting transfers between devices  17.4 us (13%)
  between operations  14.2 us (11%)
  local copies, waits for them, and re-layouts  3.77 us (3%)
    pallas_call x2, Pallas kernels, match_rows(): pl.pallas_call(kernel, grid_spec=pltpu.PrefetchScalarGridSpec(num_scalar_...  29.5 us
    ppermute x3, waiting for transfers between devices, reduce_joined(): got = lax.ppermute(send, axis, xor_pairs(n, k))  13.6 us
    all_gather x1, waiting for transfers between devices, local(): tmpl = lax.all_gather(template_spectra, 'tile', axis=0)  13.3 us
    ppermute x3, waiting for transfers between devices, reduce_joined(): got = lax.ppermute(cur, axis, xor_pairs(n, k))  11.1 us
    convert_element_type x2, other arithmetic, angle_tables(): jnp.sin(angle).astype(jnp.bfloat16)  10 us
    ppermute x3, waiting for transfers between devices, gather_rows(): got = lax.ppermute(blocks, axis, xor_pairs(n, k))  7.95 us
    ppermute x3, starting transfers between devices, gather_rows(): got = lax.ppermute(blocks, axis, xor_pairs(n, k))  5.92 us
    ppermute x3, starting transfers between devices, reduce_joined(): got = lax.ppermute(cur, axis, xor_pairs(n, k))  5.69 us
  transfers between devices with their start and end apart: 11, of which 10 were waited for; matrix products, arithmetic and copies ran while one was open for 16% of the time, Pallas kernels for 11%

profile of v9, /device:TPU:0, one launch (start us, length us, event | category | flops | bytes accessed | tf_op | source)
XLA Modules:
  0.0 131.1 jit_solution(15861483102041185086)
XLA Ops:
  7.2 0.7 all-gather.3.cloned.1.call-update
  8.4 3.7 %collective-permute-start = (bf16[1,2,64,512]{3,2,1,0:T(8,128)(2,1)S(1)}, bf16[1,2,64,512]{3,2,1,0:T(8,128)(2,1)S(1)}, u32[]{:S(2)}, u32[]{:S(2)}) collective-permute-start(bf16[1,2,64,512]{3,2,1,0:T(8,128)(2,1)S(1)} %copy-done), channel_id=1, source_target_pairs={{0,4},{1,5},{2,6},{3,7},{4,0},{5,1},{6,2},{7,3},{8,12},{9,13},{10,... | collective-permute-start | bytes 393224 | tf_op jit(solution)/shard_map/ppermute | solution.py:50
  12.2 4.0 %fusion.12 = bf16[4,512,128]{2,1,0:T(8,128)(2,1)S(1)} fusion(s32[4,128]{1,0:T(4,128)S(1)} %get-tuple-element.21), kind=kLoop, calls=%fused_computation.39 | loop fusion | flops 4718592 | bytes 526336 | tf_op jit(solution)/shard_map/neg | solution.py:38
  16.5 2.5 %collective-permute-done = bf16[1,2,64,512]{3,2,1,0:T(8,128)(2,1)S(1)} collective-permute-done((bf16[1,2,64,512]{3,2,1,0:T(8,128)(2,1)S(1)}, bf16[1,2,64,512]{3,2,1,0:T(8,128)(2,1)S(1)}, u32[]{:S(2)}, u32[]{:S(2)}) %collective-permute-start) | collective-permute-done | bytes 131104 | tf_op jit(solution)/shard_map/ppermute | solution.py:50
  19.0 0.8 collective-permute-start.1
  21.0 4.4 %sine_convert_fusion.1 = (bf16[4,512,128]{2,1,0:T(8,128)(2,1)S(1)}, bf16[4,512,128]{2,1,0:T(8,128)(2,1)S(1)}) fusion(s32[4,128]{1,0:T(4,128)S(1)} %get-tuple-element.21), kind=kLoop, calls=%fused_computation.20 | loop fusion | flops 4194304 | bytes 1050624 | tf_op jit(solution)/shard_map/convert_element_type | solution.py:31
  25.4 1.7 %collective-permute-done.1 = bf16[2,2,64,512]{3,2,1,0:T(8,128)(2,1)S(1)} collective-permute-done((bf16[2,2,64,512]{3,2,1,0:T(8,128)(2,1)S(1)}, bf16[2,2,64,512]{3,2,1,0:T(8,128)(2,1)S(1)}, u32[]{:S(2)}, u32[]{:S(2)}) %collective-permute-start.1) | collective-permute-done | bytes 262176 | tf_op jit(solution)/shard_map/ppermute | solution.py:50
  27.2 1.4 %collective-permute-start.2 = (bf16[4,2,64,512]{3,2,1,0:T(8,128)(2,1)S(1)}, bf16[4,2,64,512]{3,2,1,0:T(8,128)(2,1)S(1)}, u32[]{:S(2)}, u32[]{:S(2)}) collective-permute-start(bf16[4,2,64,512]{3,2,1,0:T(8,128)(2,1)S(1)} %pad_maximum_fusion.1), channel_id=1, source_target_pairs={{0,1},{1,0},{2,3},{3,2},{4,5},{5,4},{6,7},{7,6},{8,9},{9,8},{10,11... | collective-permute-start | bytes 1572872 | tf_op jit(solution)/shard_map/ppermute | solution.py:50
  28.6 0.6 add_multiply_fusion.off_ref
  29.3 1.6 %maximum_maximum_fusion.ct_ref = bf16[4,1024,256]{2,1,0:T(8,128)(2,1)} fusion(bf16[4,512,128]{2,1,0:T(8,128)(2,1)S(1)} %get-tuple-element.17, bf16[4,512,128]{2,1,0:T(8,128)(2,1)S(1)} %fusion.12, bf16[4,512,128]{2,1,0:T(8,128)(2,1)S(1)} %get-tuple-element.16), kind=kLoop, calls=%fused_computation.1 | loop fusion | flops 8388608 | bytes 3670016 | tf_op jit(solution)/shard_map/concatenate | solution.py:39
  30.8 5.6 %sine_convert_fusion = (bf16[4,128,512]{2,1,0:T(8,128)(2,1)}, bf16[4,128,512]{2,1,0:T(8,128)(2,1)}) fusion(s32[4,128]{1,0:T(4,128)S(1)} %get-tuple-element.20), kind=kLoop, calls=%fused_computation.16 | loop fusion | flops 4194304 | bytes 1050624 | tf_op jit(solution)/shard_map/convert_element_type | solution.py:31
  36.4 3.7 %collective-permute-done.2 = bf16[4,2,64,512]{3,2,1,0:T(8,128)(2,1)S(1)} collective-permute-done((bf16[4,2,64,512]{3,2,1,0:T(8,128)(2,1)S(1)}, bf16[4,2,64,512]{3,2,1,0:T(8,128)(2,1)S(1)}, u32[]{:S(2)}, u32[]{:S(2)}) %collective-permute-start.2) | collective-permute-done | bytes 524320 | tf_op jit(solution)/shard_map/ppermute | solution.py:50
  40.3 0.6 gather_fusion
  41.2 1.6 %copy.9 = f32[2,8,64,512]{3,2,1,0:T(8,128)} copy(f32[2,8,64,512]{3,2,0,1:T(8,128)S(1)} %convert_bitcast_fusion) | data formatting | bytes 4194304 | tf_op jit(solution)/shard_map/convert_element_type | solution.py:299
  42.8 14.5 %shard_map.68.rest_0_ = f32[4,8,128,128]{3,2,1,0:T(8,128)} custom-call(s32[32]{0:T(128)} %reshape.156.f_ref, s32[1]{0:T(128)} %constant.139.clone.1.ta_ref.tb_ref, s32[1]{0:T(128)} %constant.139.clone.1.ta_ref.tb_ref, s32[1]{0:T(128)} %bitcast.1.rid_ref, s32[2]{0:T(128)} %add_multiply_fusion.off_ref, bf16[1,8,2,128,512]{4,3,2,1,0:T(8,128)(2,1)} %bitcast.11.tma_ref, ...), custom_call_target="tpu_custom_call" | custom-call | flops 4831838208 | bytes 14680064 | tf_op jit(solution)/shard_map/pallas_call | solution.py:260
  57.3 13.3 %all-gather.3.cloned.1.call-done = bf16[32,2,128,512]{3,2,1,0:T(8,128)(2,1)} async-done(((bf16[8,2,128,512]{3,2,1,0:T(8,128)(2,1)}), bf16[32,2,128,512]{3,2,1,0:T(8,128)(2,1)}) %all-gather.3.cloned.1.call-update) | async-done | bytes 8388624 | tf_op jit(solution)/shard_map/all_gather | solution.py:280
  70.6 15.0 %shard_map.69 = f32[2,4,128,128]{3,2,1,0:T(8,128)} custom-call(s32[32]{0:T(128)} %reshape.156.f_ref, s32[1]{0:T(128)S(6)} %mul.65.ta_ref, s32[1]{0:T(128)S(6)} %add.151.tb_ref, s32[1]{0:T(128)S(6)} %convert_element_type.41.rid_ref, s32[2]{0:T(128)} %iota_multiply_fusion.off_ref, bf16[4,8,2,128,512]{4,3,2,1,0:T(8,128)(2,1)} %bitcast.20, ...), custom_call_target="tpu_custom_call" | custom-call | flops 4831838208 | bytes 14680064 | tf_op jit(solution)/shard_map/pallas_call | solution.py:260
  85.6 1.0 constant_dynamic-slice_fusion
  86.6 1.5 %collective-permute-start.4 = (f32[2,256,128]{2,1,0:T(8,128)S(1)}, f32[2,256,128]{2,1,0:T(8,128)S(1)}, u32[]{:S(2)}, u32[]{:S(2)}) collective-permute-start(f32[2,256,128]{2,1,0:T(8,128)S(1)} %constant_dynamic-slice_fusion), channel_id=1, source_target_pairs={{0,1},{1,0},{2,3},{3,2},{4,5},{5,4},{6,7},{7,6},{8,9},{9,8},{10,11... | collective-permute-start | bytes 786440 | tf_op jit(solution)/shard_map/ppermute | solution.py:92
  88.1 7.0 %collective-permute-done.4 = f32[2,256,128]{2,1,0:T(8,128)S(1)} collective-permute-done((f32[2,256,128]{2,1,0:T(8,128)S(1)}, f32[2,256,128]{2,1,0:T(8,128)S(1)}, u32[]{:S(2)}, u32[]{:S(2)}) %collective-permute-start.4) | collective-permute-done | bytes 262176 | tf_op jit(solution)/shard_map/ppermute | solution.py:92
  95.2 1.0 slice_add_fusion
  96.2 1.2 collective-permute-start.5
  97.4 3.8 %collective-permute-done.5 = f32[2,128,128]{2,1,0:T(8,128)S(1)} collective-permute-done((f32[2,128,128]{2,1,0:T(8,128)S(1)}, f32[2,128,128]{2,1,0:T(8,128)S(1)}, u32[]{:S(2)}, u32[]{:S(2)}) %collective-permute-start.5) | collective-permute-done | bytes 131104 | tf_op jit(solution)/shard_map/ppermute | solution.py:92
  101.3 2.5 %collective-permute-start.6 = (f32[2,64,128]{2,1,0:T(8,128)S(1)}, f32[2,64,128]{2,1,0:T(8,128)S(1)}, u32[]{:S(2)}, u32[]{:S(2)}) collective-permute-start(f32[2,64,128]{2,1,0:T(8,128)S(1)} %get-tuple-element.13), channel_id=1, source_target_pairs={{0,4},{1,5},{2,6},{3,7},{4,0},{5,1},{6,2},{7,3},{8,12},{9,13},{10,... | collective-permute-start | bytes 196616 | tf_op jit(solution)/shard_map/ppermute | solution.py:92
  103.7 2.8 %collective-permute-done.6 = f32[2,64,128]{2,1,0:T(8,128)S(1)} collective-permute-done((f32[2,64,128]{2,1,0:T(8,128)S(1)}, f32[2,64,128]{2,1,0:T(8,128)S(1)}, u32[]{:S(2)}, u32[]{:S(2)}) %collective-permute-start.6) | collective-permute-done | bytes 65568 | tf_op jit(solution)/shard_map/ppermute | solution.py:92
  106.5 2.5 %collective-permute-start.7 = (f32[2,64,128]{2,1,0:T(8,128)S(1)}, f32[2,64,128]{2,1,0:T(8,128)S(1)}, u32[]{:S(2)}, u32[]{:S(2)}) collective-permute-start(f32[2,64,128]{2,1,0:T(8,128)S(1)} %pad_maximum_fusion.3), channel_id=1, source_target_pairs={{0,4},{1,5},{2,6},{3,7},{4,0},{5,1},{6,2},{7,3},{8,12},{9,13},{10,... | collective-permute-start | bytes 196616 | tf_op jit(solution)/shard_map/ppermute | solution.py:97
  109.1 2.8 %collective-permute-done.7 = f32[2,64,128]{2,1,0:T(8,128)S(1)} collective-permute-done((f32[2,64,128]{2,1,0:T(8,128)S(1)}, f32[2,64,128]{2,1,0:T(8,128)S(1)}, u32[]{:S(2)}, u32[]{:S(2)}) %collective-permute-start.7) | collective-permute-done | bytes 65568 | tf_op jit(solution)/shard_map/ppermute | solution.py:97
  111.9 1.6 %collective-permute-start.8 = (f32[2,128,128]{2,1,0:T(8,128)S(1)}, f32[2,128,128]{2,1,0:T(8,128)S(1)}, u32[]{:S(2)}, u32[]{:S(2)}) collective-permute-start(f32[2,128,128]{2,1,0:T(8,128)S(1)} %maximum_select_fusion.2), channel_id=1, source_target_pairs={{0,2},{1,3},{2,0},{3,1},{4,6},{5,7},{6,4},{7,5},{8,10},{9,11},{10,... | collective-permute-start | bytes 393224 | tf_op jit(solution)/shard_map/ppermute | solution.py:97
  113.5 3.4 %collective-permute-done.8 = f32[2,128,128]{2,1,0:T(8,128)S(1)} collective-permute-done((f32[2,128,128]{2,1,0:T(8,128)S(1)}, f32[2,128,128]{2,1,0:T(8,128)S(1)}, u32[]{:S(2)}, u32[]{:S(2)}) %collective-permute-start.8) | collective-permute-done | bytes 131104 | tf_op jit(solution)/shard_map/ppermute | solution.py:97
  116.9 1.5 %collective-permute-start.9 = (f32[2,256,128]{2,1,0:T(8,128)S(1)}, f32[2,256,128]{2,1,0:T(8,128)S(1)}, u32[]{:S(2)}, u32[]{:S(2)}) collective-permute-start(f32[2,256,128]{2,1,0:T(8,128)S(1)} %maximum_select_fusion.1), channel_id=1, source_target_pairs={{0,1},{1,0},{2,3},{3,2},{4,5},{5,4},{6,7},{7,6},{8,9},{9,8},{10,11... | collective-permute-start | bytes 786440 | tf_op jit(solution)/shard_map/ppermute | solution.py:97
  118.5 4.9 %collective-permute-done.9 = f32[2,256,128]{2,1,0:T(8,128)S(1)} collective-permute-done((f32[2,256,128]{2,1,0:T(8,128)S(1)}, f32[2,256,128]{2,1,0:T(8,128)S(1)}, u32[]{:S(2)}, u32[]{:S(2)}) %collective-permute-start.9) | collective-permute-done | bytes 262176 | tf_op jit(solution)/shard_map/ppermute | solution.py:97
  123.4 0.8 slice_multiply_fusion
  (31 shorter events, 2.7 us)
Async XLA Ops:
  7.2 1.3 copy-start
  7.2 5.0 %copy-start.2 = (s32[1,4,2]{1,2,0:T(2,128)S(1)}, s32[1,4,2]{1,2,0:T(2,128)}, u32[]{:S(2)}) copy-start(s32[1,4,2]{1,2,0:T(2,128)} %param.7) | copy-start | bytes 100
  7.2 9.1 %copy-start.1 = (s32[1,4,48]{2,1,0:T(4,128)S(1)}, s32[1,4,48]{2,1,0:T(4,128)}, u32[]{:S(2)}) copy-start(s32[1,4,48]{2,1,0:T(4,128)} %param.8) | copy-start | bytes 2308
  7.2 63.4 %all-gather.3.cloned.1.call-start = ((), (), s32[]{:S(2)}) async-start(), calls=%async_computation | async-start | bytes 10485760 | tf_op jit(solution)/shard_map/all_gather | solution.py:280
  7.9 34.8 %collective-permute-start.3 = (bf16[8,2,128,512]{3,2,1,0:T(8,128)(2,1)}, bf16[8,2,128,512]{3,2,1,0:T(8,128)(2,1)}, u32[]{:S(2)}, u32[]{:S(2)}) collective-permute-start(bf16[8,2,128,512]{3,2,1,0:T(8,128)(2,1)} %param.6), channel_id=1, source_target_pairs={{0,8},{8,0},{16,24},{24,16},{1,9},{9,1},{17,25},{25,17},{2,10},{10... | collective-permute-start | bytes 6291464 | tf_op jit(solution)/shard_map/ppermute | solution.py:298
  8.4 10.6 %collective-permute-start = (bf16[1,2,64,512]{3,2,1,0:T(8,128)(2,1)S(1)}, bf16[1,2,64,512]{3,2,1,0:T(8,128)(2,1)S(1)}, u32[]{:S(2)}, u32[]{:S(2)}) collective-permute-start(bf16[1,2,64,512]{3,2,1,0:T(8,128)(2,1)S(1)} %copy-done), channel_id=1, source_target_pairs={{0,4},{1,5},{2,6},{3,7},{4,0},{5,1},{6,2},{7,3},{8,12},{9,13},{10,... | collective-permute-start | bytes 393224 | tf_op jit(solution)/shard_map/ppermute | solution.py:50
  19.0 8.1 %collective-permute-start.1 = (bf16[2,2,64,512]{3,2,1,0:T(8,128)(2,1)S(1)}, bf16[2,2,64,512]{3,2,1,0:T(8,128)(2,1)S(1)}, u32[]{:S(2)}, u32[]{:S(2)}) collective-permute-start(bf16[2,2,64,512]{3,2,1,0:T(8,128)(2,1)S(1)} %pad_maximum_fusion.2), channel_id=1, source_target_pairs={{0,2},{1,3},{2,0},{3,1},{4,6},{5,7},{6,4},{7,5},{8,10},{9,11},{10,... | collective-permute-start | bytes 786440 | tf_op jit(solution)/shard_map/ppermute | solution.py:50
  27.2 13.0 %collective-permute-start.2 = (bf16[4,2,64,512]{3,2,1,0:T(8,128)(2,1)S(1)}, bf16[4,2,64,512]{3,2,1,0:T(8,128)(2,1)S(1)}, u32[]{:S(2)}, u32[]{:S(2)}) collective-permute-start(bf16[4,2,64,512]{3,2,1,0:T(8,128)(2,1)S(1)} %pad_maximum_fusion.1), channel_id=1, source_target_pairs={{0,1},{1,0},{2,3},{3,2},{4,5},{5,4},{6,7},{7,6},{8,9},{9,8},{10,11... | collective-permute-start | bytes 1572872 | tf_op jit(solution)/shard_map/ppermute | solution.py:50
  86.6 8.6 %collective-permute-start.4 = (f32[2,256,128]{2,1,0:T(8,128)S(1)}, f32[2,256,128]{2,1,0:T(8,128)S(1)}, u32[]{:S(2)}, u32[]{:S(2)}) collective-permute-start(f32[2,256,128]{2,1,0:T(8,128)S(1)} %constant_dynamic-slice_fusion), channel_id=1, source_target_pairs={{0,1},{1,0},{2,3},{3,2},{4,5},{5,4},{6,7},{7,6},{8,9},{9,8},{10,11... | collective-permute-start | bytes 786440 | tf_op jit(solution)/shard_map/ppermute | solution.py:92
  96.2 5.0 %collective-permute-start.5 = (f32[2,128,128]{2,1,0:T(8,128)S(1)}, f32[2,128,128]{2,1,0:T(8,128)S(1)}, u32[]{:S(2)}, u32[]{:S(2)}) collective-permute-start(f32[2,128,128]{2,1,0:T(8,128)S(1)} %get-tuple-element.9), channel_id=1, source_target_pairs={{0,2},{1,3},{2,0},{3,1},{4,6},{5,7},{6,4},{7,5},{8,10},{9,11},{10,... | collective-permute-start | bytes 393224 | tf_op jit(solution)/shard_map/ppermute | solution.py:92
  101.3 5.2 %collective-permute-start.6 = (f32[2,64,128]{2,1,0:T(8,128)S(1)}, f32[2,64,128]{2,1,0:T(8,128)S(1)}, u32[]{:S(2)}, u32[]{:S(2)}) collective-permute-start(f32[2,64,128]{2,1,0:T(8,128)S(1)} %get-tuple-element.13), channel_id=1, source_target_pairs={{0,4},{1,5},{2,6},{3,7},{4,0},{5,1},{6,2},{7,3},{8,12},{9,13},{10,... | collective-permute-start | bytes 196616 | tf_op jit(solution)/shard_map/ppermute | solution.py:92
  106.5 5.3 %collective-permute-start.7 = (f32[2,64,128]{2,1,0:T(8,128)S(1)}, f32[2,64,128]{2,1,0:T(8,128)S(1)}, u32[]{:S(2)}, u32[]{:S(2)}) collective-permute-start(f32[2,64,128]{2,1,0:T(8,128)S(1)} %pad_maximum_fusion.3), channel_id=1, source_target_pairs={{0,4},{1,5},{2,6},{3,7},{4,0},{5,1},{6,2},{7,3},{8,12},{9,13},{10,... | collective-permute-start | bytes 196616 | tf_op jit(solution)/shard_map/ppermute | solution.py:97
  111.9 5.0 %collective-permute-start.8 = (f32[2,128,128]{2,1,0:T(8,128)S(1)}, f32[2,128,128]{2,1,0:T(8,128)S(1)}, u32[]{:S(2)}, u32[]{:S(2)}) collective-permute-start(f32[2,128,128]{2,1,0:T(8,128)S(1)} %maximum_select_fusion.2), channel_id=1, source_target_pairs={{0,2},{1,3},{2,0},{3,1},{4,6},{5,7},{6,4},{7,5},{8,10},{9,11},{10,... | collective-permute-start | bytes 393224 | tf_op jit(solution)/shard_map/ppermute | solution.py:97
  116.9 6.4 %collective-permute-start.9 = (f32[2,256,128]{2,1,0:T(8,128)S(1)}, f32[2,256,128]{2,1,0:T(8,128)S(1)}, u32[]{:S(2)}, u32[]{:S(2)}) collective-permute-start(f32[2,256,128]{2,1,0:T(8,128)S(1)} %maximum_select_fusion.1), channel_id=1, source_target_pairs={{0,1},{1,0},{2,3},{3,2},{4,5},{5,4},{6,7},{7,6},{8,9},{9,8},{10,11... | collective-permute-start | bytes 786440 | tf_op jit(solution)/shard_map/ppermute | solution.py:97
Sparse Core Ops, SparseCore 0:
  9.6 60.9 all-gather.2

commit v10 on v9

--- a/solution.py
+++ b/solution.py
@@ -77,28 +77,30 @@
 
 def reduce_joined(joined, shape, axis):
     n = lax.axis_size(axis)
-    if not is_pow2(n):
+    rows = joined.shape[1]
+    if not is_pow2(n) or rows % n != 0:
         best = lax.pmax(joined[0], axis)
         power = lax.psum(joined[1], axis)
         return best.reshape(shape), power.reshape(shape)
     me = lax.axis_index(axis)
-    cur = joined
-    k = 1
-    while k < n:
-        half = cur.shape[1] // 2
-        bit = (me // k) % 2
-        keep = lax.dynamic_slice_in_dim(cur, bit * half, half, axis=1)
-        send = lax.dynamic_slice_in_dim(cur, (1 - bit) * half, half, axis=1)
+    piece = rows // n
+    own = lax.dynamic_slice_in_dim(joined, me * piece, piece, axis=1)
+    bests, powers = [own[0]], [own[1]]
+    for k in range(1, n):
+        send = lax.dynamic_slice_in_dim(joined, (me ^ k) * piece, piece, axis=1)
         got = lax.ppermute(send, axis, xor_pairs(n, k))
-        cur = jnp.stack([jnp.maximum(keep[0], got[0]), keep[1] + got[1]])
-        k *= 2
-    k = n // 2
-    while k >= 1:
-        got = lax.ppermute(cur, axis, xor_pairs(n, k))
-        bit = (me // k) % 2
-        cur = jnp.where(bit == 1, jnp.concatenate([got, cur], axis=1), jnp.concatenate([cur, got], axis=1))
-        k //= 2
-    return cur[0].reshape(shape), cur[1].reshape(shape)
+        bests.append(got[0])
+        powers.append(got[1])
+    best = bests[0]
+    power = powers[0]
+    for b, p in zip(bests[1:], powers[1:]):
+        best = jnp.maximum(best, b)
+        power = power + p
+    done = jnp.stack([best, power])
+    slots = [done] + [lax.ppermute(done, axis, xor_pairs(n, k)) for k in range(1, n)]
+    pieces = jnp.stack(slots)[jnp.arange(n, dtype=jnp.int32) ^ me]
+    whole = jnp.moveaxis(pieces, 0, 1).reshape(2, rows, joined.shape[2])
+    return whole[0].reshape(shape), whole[1].reshape(shape)
 
 
 def match_kernel(blocks, size, width, rows_t, tiles, peaks_n, l_ref, tm_ref, sp_ref, ct_ref, cr_ref, sr_ref, best_ref, pow_ref, m_ref):

time: 131 us -> 130 us (level)
  waiting for transfers between devices: 46.7 us -> 33.1 us
  starting transfers between devices: 17.4 us -> 29.1 us
    ppermute x3 -> x7, waiting for transfers between devices: 13.6 us -> 6.61 us  [reduce_joined(): got = lax.ppermute(send, axis, xor_pairs(n, k))]
    ppermute x3 -> x7, waiting for transfers between devices: 11.1 us -> 4.47 us  [reduce_joined(): lax.ppermute(done, axis, xor_pairs(n, k))]
    ppermute x3 -> x7, starting transfers between devices: 5.25 us -> 11.3 us  [reduce_joined(): got = lax.ppermute(send, axis, xor_pairs(n, k))]
    ppermute x3 -> x7, starting transfers between devices: 5.69 us -> 11.3 us  [reduce_joined(): lax.ppermute(done, axis, xor_pairs(n, k))]
  transfers between devices with their start and end apart: 11 -> 19, of which waited for: 10 -> 8; matrix products, arithmetic and copies ran while one was open for 16% -> 16% of each run, Pallas kernels for 11% -> 11%
where the time goes in v10:
time: 130 us
  waiting for transfers between devices  33.1 us (25%)
  Pallas kernels  29.5 us (23%)
  starting transfers between devices  29.1 us (22%)
  other arithmetic  19.2 us (15%)
  between operations  14.2 us (11%)
  local copies, waits for them, and re-layouts  4.5 us (3%)
    pallas_call x2, Pallas kernels, match_rows(): pl.pallas_call(kernel, grid_spec=pltpu.PrefetchScalarGridSpec(num_scalar_...  29.5 us
    all_gather x1, waiting for transfers between devices, local(): tmpl = lax.all_gather(template_spectra, 'tile', axis=0)  13.3 us
    ppermute x7, starting transfers between devices, reduce_joined(): lax.ppermute(done, axis, xor_pairs(n, k))  11.3 us
    ppermute x7, starting transfers between devices, reduce_joined(): got = lax.ppermute(send, axis, xor_pairs(n, k))  11.3 us
    convert_element_type x2, other arithmetic, angle_tables(): jnp.sin(angle).astype(jnp.bfloat16)  10.1 us
    ppermute x3, waiting for transfers between devices, gather_rows(): got = lax.ppermute(blocks, axis, xor_pairs(n, k))  8 us
    ppermute x7, waiting for transfers between devices, reduce_joined(): got = lax.ppermute(send, axis, xor_pairs(n, k))  6.61 us
    ppermute x3, starting transfers between devices, gather_rows(): got = lax.ppermute(blocks, axis, xor_pairs(n, k))  5.92 us
  transfers between devices with their start and end apart: 19, of which 8 were waited for; matrix products, arithmetic and copies ran while one was open for 16% of the time, Pallas kernels for 11%

profile of v10, /device:TPU:0, one launch (start us, length us, event | category | flops | bytes accessed | tf_op | source)
XLA Modules:
  0.0 129.6 jit_solution(472942792350604212)
XLA Ops:
  7.2 0.7 all-gather.3.cloned.1.call-update
  8.4 3.7 %collective-permute-start = (bf16[1,2,64,512]{3,2,1,0:T(8,128)(2,1)S(1)}, bf16[1,2,64,512]{3,2,1,0:T(8,128)(2,1)S(1)}, u32[]{:S(2)}, u32[]{:S(2)}) collective-permute-start(bf16[1,2,64,512]{3,2,1,0:T(8,128)(2,1)S(1)} %copy-done), channel_id=1, source_target_pairs={{0,4},{1,5},{2,6},{3,7},{4,0},{5,1},{6,2},{7,3},{8,12},{9,13},{10,... | collective-permute-start | bytes 393224 | tf_op jit(solution)/shard_map/ppermute | solution.py:50
  12.2 4.0 %fusion.12 = bf16[4,512,128]{2,1,0:T(8,128)(2,1)S(1)} fusion(s32[4,128]{1,0:T(4,128)S(1)} %get-tuple-element.20), kind=kLoop, calls=%fused_computation.30 | loop fusion | flops 4718592 | bytes 526336 | tf_op jit(solution)/shard_map/neg | solution.py:38
  16.5 2.5 %collective-permute-done = bf16[1,2,64,512]{3,2,1,0:T(8,128)(2,1)S(1)} collective-permute-done((bf16[1,2,64,512]{3,2,1,0:T(8,128)(2,1)S(1)}, bf16[1,2,64,512]{3,2,1,0:T(8,128)(2,1)S(1)}, u32[]{:S(2)}, u32[]{:S(2)}) %collective-permute-start) | collective-permute-done | bytes 131104 | tf_op jit(solution)/shard_map/ppermute | solution.py:50
  19.0 0.8 collective-permute-start.1
  21.0 4.4 %sine_convert_fusion.1 = (bf16[4,512,128]{2,1,0:T(8,128)(2,1)S(1)}, bf16[4,512,128]{2,1,0:T(8,128)(2,1)S(1)}) fusion(s32[4,128]{1,0:T(4,128)S(1)} %get-tuple-element.20), kind=kLoop, calls=%fused_computation.21 | loop fusion | flops 4194304 | bytes 1050624 | tf_op jit(solution)/shard_map/convert_element_type | solution.py:31
  25.4 1.7 %collective-permute-done.1 = bf16[2,2,64,512]{3,2,1,0:T(8,128)(2,1)S(1)} collective-permute-done((bf16[2,2,64,512]{3,2,1,0:T(8,128)(2,1)S(1)}, bf16[2,2,64,512]{3,2,1,0:T(8,128)(2,1)S(1)}, u32[]{:S(2)}, u32[]{:S(2)}) %collective-permute-start.1) | collective-permute-done | bytes 262176 | tf_op jit(solution)/shard_map/ppermute | solution.py:50
  27.2 1.4 %collective-permute-start.2 = (bf16[4,2,64,512]{3,2,1,0:T(8,128)(2,1)S(1)}, bf16[4,2,64,512]{3,2,1,0:T(8,128)(2,1)S(1)}, u32[]{:S(2)}, u32[]{:S(2)}) collective-permute-start(bf16[4,2,64,512]{3,2,1,0:T(8,128)(2,1)S(1)} %pad_maximum_fusion.1), channel_id=1, source_target_pairs={{0,1},{1,0},{2,3},{3,2},{4,5},{5,4},{6,7},{7,6},{8,9},{9,8},{10,11... | collective-permute-start | bytes 1572872 | tf_op jit(solution)/shard_map/ppermute | solution.py:50
  29.2 1.5 %maximum_maximum_fusion.ct_ref = bf16[4,1024,256]{2,1,0:T(8,128)(2,1)} fusion(bf16[4,512,128]{2,1,0:T(8,128)(2,1)S(1)} %get-tuple-element.16, bf16[4,512,128]{2,1,0:T(8,128)(2,1)S(1)} %fusion.12, bf16[4,512,128]{2,1,0:T(8,128)(2,1)S(1)} %get-tuple-element.15), kind=kLoop, calls=%fused_computation.2 | loop fusion | flops 8388608 | bytes 3670016 | tf_op jit(solution)/shard_map/concatenate | solution.py:39
  30.7 5.7 %sine_convert_fusion = (bf16[4,128,512]{2,1,0:T(8,128)(2,1)}, bf16[4,128,512]{2,1,0:T(8,128)(2,1)}) fusion(s32[4,128]{1,0:T(4,128)S(1)} %get-tuple-element.19), kind=kLoop, calls=%fused_computation.17 | loop fusion | flops 4194304 | bytes 1050624 | tf_op jit(solution)/shard_map/convert_element_type | solution.py:31
  36.4 3.8 %collective-permute-done.2 = bf16[4,2,64,512]{3,2,1,0:T(8,128)(2,1)S(1)} collective-permute-done((bf16[4,2,64,512]{3,2,1,0:T(8,128)(2,1)S(1)}, bf16[4,2,64,512]{3,2,1,0:T(8,128)(2,1)S(1)}, u32[]{:S(2)}, u32[]{:S(2)}) %collective-permute-start.2) | collective-permute-done | bytes 524320 | tf_op jit(solution)/shard_map/ppermute | solution.py:50
  41.2 1.6 %copy.9 = f32[2,8,64,512]{3,2,1,0:T(8,128)} copy(f32[2,8,64,512]{3,2,0,1:T(8,128)S(1)} %convert_bitcast_fusion) | data formatting | bytes 4194304 | tf_op jit(solution)/shard_map/convert_element_type | solution.py:301
  42.8 14.5 %shard_map.68.rest_0_ = f32[4,8,128,128]{3,2,1,0:T(8,128)} custom-call(s32[32]{0:T(128)} %reshape.171.f_ref, s32[1]{0:T(128)} %constant.92.clone.1.ta_ref.tb_ref, s32[1]{0:T(128)} %constant.92.clone.1.ta_ref.tb_ref, s32[1]{0:T(128)} %bitcast.1.rid_ref, s32[2]{0:T(128)} %add_multiply_fusion.off_ref, bf16[1,8,2,128,512]{4,3,2,1,0:T(8,128)(2,1)} %bitcast.11.tma_ref, ...), custom_call_target="tpu_custom_call" | custom-call | flops 4831838208 | bytes 14680064 | tf_op jit(solution)/shard_map/pallas_call | solution.py:262
  57.3 13.3 %all-gather.3.cloned.1.call-done = bf16[32,2,128,512]{3,2,1,0:T(8,128)(2,1)} async-done(((bf16[8,2,128,512]{3,2,1,0:T(8,128)(2,1)}), bf16[32,2,128,512]{3,2,1,0:T(8,128)(2,1)}) %all-gather.3.cloned.1.call-update) | async-done | bytes 8388624 | tf_op jit(solution)/shard_map/all_gather | solution.py:282
  70.6 15.1 %shard_map.69 = f32[2,4,128,128]{3,2,1,0:T(8,128)} custom-call(s32[32]{0:T(128)} %reshape.171.f_ref, s32[1]{0:T(128)S(6)} %mul.71.ta_ref, s32[1]{0:T(128)S(6)} %add.165.tb_ref, s32[1]{0:T(128)S(6)} %convert_element_type.41.rid_ref, s32[2]{0:T(128)} %iota_multiply_fusion.off_ref, bf16[4,8,2,128,512]{4,3,2,1,0:T(8,128)(2,1)} %bitcast.39, ...), custom_call_target="tpu_custom_call" | custom-call | flops 4831838208 | bytes 14680064 | tf_op jit(solution)/shard_map/pallas_call | solution.py:262
  85.7 1.1 constant_dynamic-slice_fusion.6
  86.7 4.3 %collective-permute-start.10 = (f32[2,64,128]{2,1,0:T(8,128)S(1)}, f32[2,64,128]{2,1,0:T(8,128)S(1)}, u32[]{:S(2)}, u32[]{:S(2)}) collective-permute-start(f32[2,64,128]{2,1,0:T(8,128)S(1)} %get-tuple-element.7), channel_id=1, source_target_pairs={{0,7},{1,6},{2,5},{3,4},{4,3},{5,2},{6,1},{7,0},{8,15},{9,14},{10,... | collective-permute-start | bytes 196616 | tf_op jit(solution)/shard_map/ppermute | solution.py:91
  91.6 2.9 %collective-permute-start.6 = (f32[2,64,128]{2,1,0:T(8,128)S(1)}, f32[2,64,128]{2,1,0:T(8,128)S(1)}, u32[]{:S(2)}, u32[]{:S(2)}) collective-permute-start(f32[2,64,128]{2,1,0:T(8,128)S(1)} %get-tuple-element.11), channel_id=1, source_target_pairs={{0,3},{1,2},{2,1},{3,0},{4,7},{5,6},{6,5},{7,4},{8,11},{9,10},{10,... | collective-permute-start | bytes 196616 | tf_op jit(solution)/shard_map/ppermute | solution.py:91
  94.5 2.9 %collective-permute-start.8 = (f32[2,64,128]{2,1,0:T(8,128)S(1)}, f32[2,64,128]{2,1,0:T(8,128)S(1)}, u32[]{:S(2)}, u32[]{:S(2)}) collective-permute-start(f32[2,64,128]{2,1,0:T(8,128)S(1)} %get-tuple-element.9), channel_id=1, source_target_pairs={{0,5},{1,4},{2,7},{3,6},{4,1},{5,0},{6,3},{7,2},{8,13},{9,12},{10,... | collective-permute-start | bytes 196616 | tf_op jit(solution)/shard_map/ppermute | solution.py:91
  98.0 4.2 %collective-permute-done.7 = f32[2,64,128]{2,1,0:T(8,128)S(1)} collective-permute-done((f32[2,64,128]{2,1,0:T(8,128)S(1)}, f32[2,64,128]{2,1,0:T(8,128)S(1)}, u32[]{:S(2)}, u32[]{:S(2)}) %collective-permute-start.7) | collective-permute-done | bytes 65568 | tf_op jit(solution)/shard_map/ppermute | solution.py:91
  102.2 2.4 %collective-permute-done.8 = f32[2,64,128]{2,1,0:T(8,128)S(1)} collective-permute-done((f32[2,64,128]{2,1,0:T(8,128)S(1)}, f32[2,64,128]{2,1,0:T(8,128)S(1)}, u32[]{:S(2)}, u32[]{:S(2)}) %collective-permute-start.8) | collective-permute-done | bytes 65568 | tf_op jit(solution)/shard_map/ppermute | solution.py:91
  104.6 0.8 slice_maximum_fusion
  105.5 1.2 collective-permute-start.11
  106.7 0.7 collective-permute-start.12
  107.4 1.6 %collective-permute-start.13 = (f32[2,64,128]{2,1,0:T(8,128)S(1)}, f32[2,64,128]{2,1,0:T(8,128)S(1)}, u32[]{:S(2)}, u32[]{:S(2)}) collective-permute-start(f32[2,64,128]{2,1,0:T(8,128)S(1)} %pad_maximum_fusion.3), channel_id=1, source_target_pairs={{0,3},{1,2},{2,1},{3,0},{4,7},{5,6},{6,5},{7,4},{8,11},{9,10},{10,... | collective-permute-start | bytes 196616 | tf_op jit(solution)/shard_map/ppermute | solution.py:100
  109.0 1.4 %collective-permute-start.14 = (f32[2,64,128]{2,1,0:T(8,128)S(1)}, f32[2,64,128]{2,1,0:T(8,128)S(1)}, u32[]{:S(2)}, u32[]{:S(2)}) collective-permute-start(f32[2,64,128]{2,1,0:T(8,128)S(1)} %pad_maximum_fusion.3), channel_id=1, source_target_pairs={{0,4},{1,5},{2,6},{3,7},{4,0},{5,1},{6,2},{7,3},{8,12},{9,13},{10,... | collective-permute-start | bytes 196616 | tf_op jit(solution)/shard_map/ppermute | solution.py:100
  110.4 2.2 %collective-permute-start.15 = (f32[2,64,128]{2,1,0:T(8,128)S(1)}, f32[2,64,128]{2,1,0:T(8,128)S(1)}, u32[]{:S(2)}, u32[]{:S(2)}) collective-permute-start(f32[2,64,128]{2,1,0:T(8,128)S(1)} %pad_maximum_fusion.3), channel_id=1, source_target_pairs={{0,5},{1,4},{2,7},{3,6},{4,1},{5,0},{6,3},{7,2},{8,13},{9,12},{10,... | collective-permute-start | bytes 196616 | tf_op jit(solution)/shard_map/ppermute | solution.py:100
  112.6 1.4 %collective-permute-start.16 = (f32[2,64,128]{2,1,0:T(8,128)S(1)}, f32[2,64,128]{2,1,0:T(8,128)S(1)}, u32[]{:S(2)}, u32[]{:S(2)}) collective-permute-start(f32[2,64,128]{2,1,0:T(8,128)S(1)} %pad_maximum_fusion.3), channel_id=1, source_target_pairs={{0,6},{1,7},{2,4},{3,5},{4,2},{5,3},{6,0},{7,1},{8,14},{9,15},{10,... | collective-permute-start | bytes 196616 | tf_op jit(solution)/shard_map/ppermute | solution.py:100
  113.9 2.9 %collective-permute-start.17 = (f32[2,64,128]{2,1,0:T(8,128)S(1)}, f32[2,64,128]{2,1,0:T(8,128)S(1)}, u32[]{:S(2)}, u32[]{:S(2)}) collective-permute-start(f32[2,64,128]{2,1,0:T(8,128)S(1)} %pad_maximum_fusion.3), channel_id=1, source_target_pairs={{0,7},{1,6},{2,5},{3,4},{4,3},{5,2},{6,1},{7,0},{8,15},{9,14},{10,... | collective-permute-start | bytes 196616 | tf_op jit(solution)/shard_map/ppermute | solution.py:100
  116.8 2.0 %collective-permute-done.14 = f32[2,64,128]{2,1,0:T(8,128)S(1)} collective-permute-done((f32[2,64,128]{2,1,0:T(8,128)S(1)}, f32[2,64,128]{2,1,0:T(8,128)S(1)}, u32[]{:S(2)}, u32[]{:S(2)}) %collective-permute-start.14) | collective-permute-done | bytes 65568 | tf_op jit(solution)/shard_map/ppermute | solution.py:100
  118.8 2.5 %collective-permute-done.15 = f32[2,64,128]{2,1,0:T(8,128)S(1)} collective-permute-done((f32[2,64,128]{2,1,0:T(8,128)S(1)}, f32[2,64,128]{2,1,0:T(8,128)S(1)}, u32[]{:S(2)}, u32[]{:S(2)}) %collective-permute-start.15) | collective-permute-done | bytes 65568 | tf_op jit(solution)/shard_map/ppermute | solution.py:100
  122.0 0.8 slice_multiply_fusion
  (51 shorter events, 5.5 us)
Async XLA Ops:
  7.2 1.3 copy-start
  7.2 5.0 %copy-start.2 = (s32[1,4,2]{1,2,0:T(2,128)S(1)}, s32[1,4,2]{1,2,0:T(2,128)}, u32[]{:S(2)}) copy-start(s32[1,4,2]{1,2,0:T(2,128)} %param.7) | copy-start | bytes 100
  7.2 9.1 %copy-start.1 = (s32[1,4,48]{2,1,0:T(4,128)S(1)}, s32[1,4,48]{2,1,0:T(4,128)}, u32[]{:S(2)}) copy-start(s32[1,4,48]{2,1,0:T(4,128)} %param.8) | copy-start | bytes 2308
  7.2 63.4 %all-gather.3.cloned.1.call-start = ((), (), s32[]{:S(2)}) async-start(), calls=%async_computation | async-start | bytes 10485760 | tf_op jit(solution)/shard_map/all_gather | solution.py:282
  7.9 34.9 %collective-permute-start.3 = (bf16[8,2,128,512]{3,2,1,0:T(8,128)(2,1)}, bf16[8,2,128,512]{3,2,1,0:T(8,128)(2,1)}, u32[]{:S(2)}, u32[]{:S(2)}) collective-permute-start(bf16[8,2,128,512]{3,2,1,0:T(8,128)(2,1)} %param.6), channel_id=1, source_target_pairs={{0,8},{8,0},{16,24},{24,16},{1,9},{9,1},{17,25},{25,17},{2,10},{10... | collective-permute-start | bytes 6291464 | tf_op jit(solution)/shard_map/ppermute | solution.py:300
  8.4 10.6 %collective-permute-start = (bf16[1,2,64,512]{3,2,1,0:T(8,128)(2,1)S(1)}, bf16[1,2,64,512]{3,2,1,0:T(8,128)(2,1)S(1)}, u32[]{:S(2)}, u32[]{:S(2)}) collective-permute-start(bf16[1,2,64,512]{3,2,1,0:T(8,128)(2,1)S(1)} %copy-done), channel_id=1, source_target_pairs={{0,4},{1,5},{2,6},{3,7},{4,0},{5,1},{6,2},{7,3},{8,12},{9,13},{10,... | collective-permute-start | bytes 393224 | tf_op jit(solution)/shard_map/ppermute | solution.py:50
  19.0 8.1 %collective-permute-start.1 = (bf16[2,2,64,512]{3,2,1,0:T(8,128)(2,1)S(1)}, bf16[2,2,64,512]{3,2,1,0:T(8,128)(2,1)S(1)}, u32[]{:S(2)}, u32[]{:S(2)}) collective-permute-start(bf16[2,2,64,512]{3,2,1,0:T(8,128)(2,1)S(1)} %pad_maximum_fusion.2), channel_id=1, source_target_pairs={{0,2},{1,3},{2,0},{3,1},{4,6},{5,7},{6,4},{7,5},{8,10},{9,11},{10,... | collective-permute-start | bytes 786440 | tf_op jit(solution)/shard_map/ppermute | solution.py:50
  27.2 13.0 %collective-permute-start.2 = (bf16[4,2,64,512]{3,2,1,0:T(8,128)(2,1)S(1)}, bf16[4,2,64,512]{3,2,1,0:T(8,128)(2,1)S(1)}, u32[]{:S(2)}, u32[]{:S(2)}) collective-permute-start(bf16[4,2,64,512]{3,2,1,0:T(8,128)(2,1)S(1)} %pad_maximum_fusion.1), channel_id=1, source_target_pairs={{0,1},{1,0},{2,3},{3,2},{4,5},{5,4},{6,7},{7,6},{8,9},{9,8},{10,11... | collective-permute-start | bytes 1572872 | tf_op jit(solution)/shard_map/ppermute | solution.py:50
  86.7 7.8 %collective-permute-start.10 = (f32[2,64,128]{2,1,0:T(8,128)S(1)}, f32[2,64,128]{2,1,0:T(8,128)S(1)}, u32[]{:S(2)}, u32[]{:S(2)}) collective-permute-start(f32[2,64,128]{2,1,0:T(8,128)S(1)} %get-tuple-element.7), channel_id=1, source_target_pairs={{0,7},{1,6},{2,5},{3,4},{4,3},{5,2},{6,1},{7,0},{8,15},{9,14},{10,... | collective-permute-start | bytes 196616 | tf_op jit(solution)/shard_map/ppermute | solution.py:91
  91.0 6.4 %collective-permute-start.4 = (f32[2,64,128]{2,1,0:T(8,128)S(1)}, f32[2,64,128]{2,1,0:T(8,128)S(1)}, u32[]{:S(2)}, u32[]{:S(2)}) collective-permute-start(f32[2,64,128]{2,1,0:T(8,128)S(1)} %get-tuple-element.6), channel_id=1, source_target_pairs={{0,1},{1,0},{2,3},{3,2},{4,5},{5,4},{6,7},{7,6},{8,9},{9,8},{10,11... | collective-permute-start | bytes 196616 | tf_op jit(solution)/shard_map/ppermute | solution.py:91
  91.6 6.4 %collective-permute-start.5 = (f32[2,64,128]{2,1,0:T(8,128)S(1)}, f32[2,64,128]{2,1,0:T(8,128)S(1)}, u32[]{:S(2)}, u32[]{:S(2)}) collective-permute-start(f32[2,64,128]{2,1,0:T(8,128)S(1)} %get-tuple-element.12), channel_id=1, source_target_pairs={{0,2},{1,3},{2,0},{3,1},{4,6},{5,7},{6,4},{7,5},{8,10},{9,11},{10,... | collective-permute-start | bytes 196616 | tf_op jit(solution)/shard_map/ppermute | solution.py:91
  91.6 6.4 %collective-permute-start.6 = (f32[2,64,128]{2,1,0:T(8,128)S(1)}, f32[2,64,128]{2,1,0:T(8,128)S(1)}, u32[]{:S(2)}, u32[]{:S(2)}) collective-permute-start(f32[2,64,128]{2,1,0:T(8,128)S(1)} %get-tuple-element.11), channel_id=1, source_target_pairs={{0,3},{1,2},{2,1},{3,0},{4,7},{5,6},{6,5},{7,4},{8,11},{9,10},{10,... | collective-permute-start | bytes 196616 | tf_op jit(solution)/shard_map/ppermute | solution.py:91
  94.5 7.7 %collective-permute-start.7 = (f32[2,64,128]{2,1,0:T(8,128)S(1)}, f32[2,64,128]{2,1,0:T(8,128)S(1)}, u32[]{:S(2)}, u32[]{:S(2)}) collective-permute-start(f32[2,64,128]{2,1,0:T(8,128)S(1)} %get-tuple-element.10), channel_id=1, source_target_pairs={{0,4},{1,5},{2,6},{3,7},{4,0},{5,1},{6,2},{7,3},{8,12},{9,13},{10,... | collective-permute-start | bytes 196616 | tf_op jit(solution)/shard_map/ppermute | solution.py:91
  94.5 10.1 %collective-permute-start.8 = (f32[2,64,128]{2,1,0:T(8,128)S(1)}, f32[2,64,128]{2,1,0:T(8,128)S(1)}, u32[]{:S(2)}, u32[]{:S(2)}) collective-permute-start(f32[2,64,128]{2,1,0:T(8,128)S(1)} %get-tuple-element.9), channel_id=1, source_target_pairs={{0,5},{1,4},{2,7},{3,6},{4,1},{5,0},{6,3},{7,2},{8,13},{9,12},{10,... | collective-permute-start | bytes 196616 | tf_op jit(solution)/shard_map/ppermute | solution.py:91
  97.5 7.2 %collective-permute-start.9 = (f32[2,64,128]{2,1,0:T(8,128)S(1)}, f32[2,64,128]{2,1,0:T(8,128)S(1)}, u32[]{:S(2)}, u32[]{:S(2)}) collective-permute-start(f32[2,64,128]{2,1,0:T(8,128)S(1)} %get-tuple-element.8), channel_id=1, source_target_pairs={{0,6},{1,7},{2,4},{3,5},{4,2},{5,3},{6,0},{7,1},{8,14},{9,15},{10,... | collective-permute-start | bytes 196616 | tf_op jit(solution)/shard_map/ppermute | solution.py:91
  105.5 7.1 %collective-permute-start.11 = (f32[2,64,128]{2,1,0:T(8,128)S(1)}, f32[2,64,128]{2,1,0:T(8,128)S(1)}, u32[]{:S(2)}, u32[]{:S(2)}) collective-permute-start(f32[2,64,128]{2,1,0:T(8,128)S(1)} %pad_maximum_fusion.3), channel_id=1, source_target_pairs={{0,1},{1,0},{2,3},{3,2},{4,5},{5,4},{6,7},{7,6},{8,9},{9,8},{10,11... | collective-permute-start | bytes 196616 | tf_op jit(solution)/shard_map/ppermute | solution.py:100
  106.7 7.2 %collective-permute-start.12 = (f32[2,64,128]{2,1,0:T(8,128)S(1)}, f32[2,64,128]{2,1,0:T(8,128)S(1)}, u32[]{:S(2)}, u32[]{:S(2)}) collective-permute-start(f32[2,64,128]{2,1,0:T(8,128)S(1)} %pad_maximum_fusion.3), channel_id=1, source_target_pairs={{0,2},{1,3},{2,0},{3,1},{4,6},{5,7},{6,4},{7,5},{8,10},{9,11},{10,... | collective-permute-start | bytes 196616 | tf_op jit(solution)/shard_map/ppermute | solution.py:100
  107.4 9.4 %collective-permute-start.13 = (f32[2,64,128]{2,1,0:T(8,128)S(1)}, f32[2,64,128]{2,1,0:T(8,128)S(1)}, u32[]{:S(2)}, u32[]{:S(2)}) collective-permute-start(f32[2,64,128]{2,1,0:T(8,128)S(1)} %pad_maximum_fusion.3), channel_id=1, source_target_pairs={{0,3},{1,2},{2,1},{3,0},{4,7},{5,6},{6,5},{7,4},{8,11},{9,10},{10,... | collective-permute-start | bytes 196616 | tf_op jit(solution)/shard_map/ppermute | solution.py:100
  109.0 9.8 %collective-permute-start.14 = (f32[2,64,128]{2,1,0:T(8,128)S(1)}, f32[2,64,128]{2,1,0:T(8,128)S(1)}, u32[]{:S(2)}, u32[]{:S(2)}) collective-permute-start(f32[2,64,128]{2,1,0:T(8,128)S(1)} %pad_maximum_fusion.3), channel_id=1, source_target_pairs={{0,4},{1,5},{2,6},{3,7},{4,0},{5,1},{6,2},{7,3},{8,12},{9,13},{10,... | collective-permute-start | bytes 196616 | tf_op jit(solution)/shard_map/ppermute | solution.py:100
  110.4 10.9 %collective-permute-start.15 = (f32[2,64,128]{2,1,0:T(8,128)S(1)}, f32[2,64,128]{2,1,0:T(8,128)S(1)}, u32[]{:S(2)}, u32[]{:S(2)}) collective-permute-start(f32[2,64,128]{2,1,0:T(8,128)S(1)} %pad_maximum_fusion.3), channel_id=1, source_target_pairs={{0,5},{1,4},{2,7},{3,6},{4,1},{5,0},{6,3},{7,2},{8,13},{9,12},{10,... | collective-permute-start | bytes 196616 | tf_op jit(solution)/shard_map/ppermute | solution.py:100
  112.6 8.8 %collective-permute-start.16 = (f32[2,64,128]{2,1,0:T(8,128)S(1)}, f32[2,64,128]{2,1,0:T(8,128)S(1)}, u32[]{:S(2)}, u32[]{:S(2)}) collective-permute-start(f32[2,64,128]{2,1,0:T(8,128)S(1)} %pad_maximum_fusion.3), channel_id=1, source_target_pairs={{0,6},{1,7},{2,4},{3,5},{4,2},{5,3},{6,0},{7,1},{8,14},{9,15},{10,... | collective-permute-start | bytes 196616 | tf_op jit(solution)/shard_map/ppermute | solution.py:100
  113.9 7.4 %collective-permute-start.17 = (f32[2,64,128]{2,1,0:T(8,128)S(1)}, f32[2,64,128]{2,1,0:T(8,128)S(1)}, u32[]{:S(2)}, u32[]{:S(2)}) collective-permute-start(f32[2,64,128]{2,1,0:T(8,128)S(1)} %pad_maximum_fusion.3), channel_id=1, source_target_pairs={{0,7},{1,6},{2,5},{3,4},{4,3},{5,2},{6,1},{7,0},{8,15},{9,14},{10,... | collective-permute-start | bytes 196616 | tf_op jit(solution)/shard_map/ppermute | solution.py:100
Sparse Core Ops, SparseCore 0:
  9.6 60.9 all-gather.2

commit v11 on v10

--- a/solution.py
+++ b/solution.py
@@ -162,7 +162,7 @@
     )(flags, tmpl, spec, col_table, cos_t, sin_t)
 
 
-def rows_kernel(blocks, size, width, rows_t, peaks_n, chunk, n_steps, final, per, f_ref, ta_ref, tb_ref, rid_ref, off_ref, tma_ref, tmb_ref, sp_ref, ct_ref, cr_ref, sr_ref, *rest):
+def rows_kernel(blocks, size, width, rows_t, peaks_n, chunk, n_steps, final, per, f_ref, ta_ref, tb_ref, rid_ref, off_ref, tma_ref, tmb_ref, sp_ref, ct_ref, cr_ref, *rest):
     if final:
         init_ref, out_ref, acc_ref, m_ref = rest
         best_ref, pow_ref = out_ref.at[0], out_ref.at[1]
@@ -212,8 +212,8 @@
             g = jnp.dot(m_ref[...], ct_ref[p], preferred_element_type=jnp.float32).astype(jnp.bfloat16)
             for o in range(per):
                 rows = slice(o * span, (o + 1) * span)
-                part = jnp.dot(cr_ref[p], g[rows, :width], preferred_element_type=jnp.float32)
-                part = part - jnp.dot(sr_ref[p], g[rows, width:], preferred_element_type=jnp.float32)
+                stacked = jnp.concatenate([g[rows, :width], g[rows, width:]], axis=0)
+                part = jnp.dot(cr_ref[p, 0], stacked, preferred_element_type=jnp.float32)
                 acc_ref[p, o] = acc_ref[p, o] + part
 
     @pl.when(i == n_steps - 1)
@@ -246,10 +246,12 @@
         pl.BlockSpec((1, per, 2, rows_t, size), lambda j, i, f, ta, tb, r, o: (tb[i], j, 0, 0, 0)),
         pl.BlockSpec((2, span, size), lambda j, i, f, ta, tb, r, o: (0, r[i], 0)),
         pl.BlockSpec(col_table.shape, lambda j, i, f, ta, tb, r, o: (0, 0, 0)),
-        pl.BlockSpec((peaks_n, width, span), lambda j, i, f, ta, tb, r, o: (0, 0, r[i])),
-        pl.BlockSpec((peaks_n, width, span), lambda j, i, f, ta, tb, r, o: (0, 0, r[i])),
+        pl.BlockSpec((peaks_n, 1, width, 2 * span), lambda j, i, f, ta, tb, r, o: (0, r[i], 0, 0)),
     ]
-    args = [flags, tas, tbs, rids, offs, tmpl_a, tmpl_b, spec, col_table, cos_t, sin_t]
+    chips = cos_t.shape[2] // span
+    row_table = jnp.concatenate([cos_t.reshape(peaks_n, width, chips, span), -sin_t.reshape(peaks_n, width, chips, span)], axis=3)
+    row_table = jnp.swapaxes(row_table, 1, 2)
+    args = [flags, tas, tbs, rids, offs, tmpl_a, tmpl_b, spec, col_table, row_table]
     part_spec = pl.BlockSpec((peaks_n, per, width, width), lambda j, i, f, ta, tb, r, o: (0, j, 0, 0))
     if final:
         in_specs.append(part_spec)

time: 130 us -> 130 us (level)
  waiting for transfers between devices: 33.1 us -> 28.2 us
  other arithmetic: 19.2 us -> 23.2 us
    convert_element_type x2 -> x1, other arithmetic: 10.1 us -> 4.39 us  [angle_tables(): jnp.sin(angle).astype(jnp.bfloat16)]
    neg x0 -> x1, other arithmetic: none -> 4.31 us  [match_rows(): -sin_t.reshape(peaks_n, width, chips, span)]
    convert_element_type x0 -> x1, other arithmetic: none -> 4.23 us  [angle_tables(): jnp.cos(angle).astype(jnp.bfloat16)]
    all_gather x1, waiting for transfers between devices: 13.3 us -> 9.51 us  [local(): tmpl = lax.all_gather(template_spectra, 'tile', axis=0)]
  transfers between devices with their start and end apart: 19 -> 19, of which waited for: 8 -> 7; matrix products, arithmetic and copies ran while one was open for 16% -> 19% of each run, Pallas kernels for 11% -> 11%
where the time goes in v11:
time: 130 us
  starting transfers between devices  30 us (23%)
  Pallas kernels  29.8 us (23%)
  waiting for transfers between devices  28.2 us (22%)
  other arithmetic  23.2 us (18%)
  between operations  14.3 us (11%)
  local copies, waits for them, and re-layouts  4.49 us (3%)
    pallas_call x2, Pallas kernels, match_rows(): pl.pallas_call(kernel, grid_spec=pltpu.PrefetchScalarGridSpec(num_scalar_...  29.8 us
    ppermute x7, starting transfers between devices, reduce_joined(): lax.ppermute(done, axis, xor_pairs(n, k))  11.3 us
    ppermute x7, starting transfers between devices, reduce_joined(): got = lax.ppermute(send, axis, xor_pairs(n, k))  11.2 us
    all_gather x1, waiting for transfers between devices, local(): tmpl = lax.all_gather(template_spectra, 'tile', axis=0)  9.51 us
    ppermute x3, starting transfers between devices, gather_rows(): got = lax.ppermute(blocks, axis, xor_pairs(n, k))  6.87 us
    ppermute x3, waiting for transfers between devices, gather_rows(): got = lax.ppermute(blocks, axis, xor_pairs(n, k))  6.84 us
    ppermute x7, waiting for transfers between devices, reduce_joined(): got = lax.ppermute(send, axis, xor_pairs(n, k))  6.68 us
    ppermute x7, waiting for transfers between devices, reduce_joined(): lax.ppermute(done, axis, xor_pairs(n, k))  4.48 us
  transfers between devices with their start and end apart: 19, of which 7 were waited for; matrix products, arithmetic and copies ran while one was open for 19% of the time, Pallas kernels for 11%

profile of v11, /device:TPU:0, one launch (start us, length us, event | category | flops | bytes accessed | tf_op | source)
XLA Modules:
  0.0 129.9 jit_solution(9980365749701328314)
XLA Ops:
  8.4 3.7 %collective-permute-start = (bf16[1,2,64,512]{3,2,1,0:T(8,128)(2,1)S(1)}, bf16[1,2,64,512]{3,2,1,0:T(8,128)(2,1)S(1)}, u32[]{:S(2)}, u32[]{:S(2)}) collective-permute-start(bf16[1,2,64,512]{3,2,1,0:T(8,128)(2,1)S(1)} %copy-done), channel_id=1, source_target_pairs={{0,4},{1,5},{2,6},{3,7},{4,0},{5,1},{6,2},{7,3},{8,12},{9,13},{10,... | collective-permute-start | bytes 393224 | tf_op jit(solution)/shard_map/ppermute | solution.py:50
  12.3 4.2 %cosine_convert_fusion = bf16[4,128,2,256]{3,1,2,0:T(8,128)(2,1)S(1)} fusion(s32[4,128]{1,0:T(4,128)S(1)} %get-tuple-element.17, s32[2,256]{1,0:T(2,128)S(1)} %multiply_add_fusion), kind=kLoop, calls=%fused_computation.21 | loop fusion | flops 3932160 | bytes 528384 | tf_op jit(solution)/shard_map/convert_element_type | solution.py:31
  16.7 4.3 %fusion.9 = bf16[4,128,2,256]{3,1,2,0:T(8,128)(2,1)S(1)} fusion(s32[4,128]{1,0:T(4,128)S(1)} %get-tuple-element.17, s32[2,256]{1,0:T(2,128)S(1)} %multiply_add_fusion), kind=kLoop, calls=%fused_computation.27 | loop fusion | flops 4718592 | bytes 528384 | tf_op jit(solution)/shard_map/neg | solution.py:252
  21.1 1.1 maximum_bitcast_fusion.cr_ref
  22.2 1.6 %collective-permute-start.1 = (bf16[2,2,64,512]{3,2,1,0:T(8,128)(2,1)S(1)}, bf16[2,2,64,512]{3,2,1,0:T(8,128)(2,1)S(1)}, u32[]{:S(2)}, u32[]{:S(2)}) collective-permute-start(bf16[2,2,64,512]{3,2,1,0:T(8,128)(2,1)S(1)} %pad_maximum_fusion.2), channel_id=1, source_target_pairs={{0,2},{1,3},{2,0},{3,1},{4,6},{5,7},{6,4},{7,5},{8,10},{9,11},{10,... | collective-permute-start | bytes 786440 | tf_op jit(solution)/shard_map/ppermute | solution.py:50
  25.0 4.0 %fusion.10 = bf16[4,512,128]{2,1,0:T(8,128)(2,1)S(1)} fusion(s32[4,128]{1,0:T(4,128)S(1)} %get-tuple-element.18), kind=kLoop, calls=%fused_computation.31 | loop fusion | flops 4718592 | bytes 526336 | tf_op jit(solution)/shard_map/neg | solution.py:38
  29.0 1.6 %collective-permute-done.1 = bf16[2,2,64,512]{3,2,1,0:T(8,128)(2,1)S(1)} collective-permute-done((bf16[2,2,64,512]{3,2,1,0:T(8,128)(2,1)S(1)}, bf16[2,2,64,512]{3,2,1,0:T(8,128)(2,1)S(1)}, u32[]{:S(2)}, u32[]{:S(2)}) %collective-permute-start.1) | collective-permute-done | bytes 262176 | tf_op jit(solution)/shard_map/ppermute | solution.py:50
  30.7 1.6 %collective-permute-start.2 = (bf16[4,2,64,512]{3,2,1,0:T(8,128)(2,1)S(1)}, bf16[4,2,64,512]{3,2,1,0:T(8,128)(2,1)S(1)}, u32[]{:S(2)}, u32[]{:S(2)}) collective-permute-start(bf16[4,2,64,512]{3,2,1,0:T(8,128)(2,1)S(1)} %pad_maximum_fusion.1), channel_id=1, source_target_pairs={{0,1},{1,0},{2,3},{3,2},{4,5},{5,4},{6,7},{7,6},{8,9},{9,8},{10,11... | collective-permute-start | bytes 1572872 | tf_op jit(solution)/shard_map/ppermute | solution.py:50
  32.9 4.4 %sine_convert_fusion.1 = (bf16[4,512,128]{2,1,0:T(8,128)(2,1)S(1)}, bf16[4,512,128]{2,1,0:T(8,128)(2,1)S(1)}) fusion(s32[4,128]{1,0:T(4,128)S(1)} %get-tuple-element.18), kind=kLoop, calls=%fused_computation.22 | loop fusion | flops 4194304 | bytes 1050624 | tf_op jit(solution)/shard_map/convert_element_type | solution.py:31
  37.3 1.5 %maximum_maximum_fusion.ct_ref = bf16[4,1024,256]{2,1,0:T(8,128)(2,1)} fusion(bf16[4,512,128]{2,1,0:T(8,128)(2,1)S(1)} %get-tuple-element.14, bf16[4,512,128]{2,1,0:T(8,128)(2,1)S(1)} %fusion.10, bf16[4,512,128]{2,1,0:T(8,128)(2,1)S(1)} %get-tuple-element.13), kind=kLoop, calls=%fused_computation.2 | loop fusion | flops 8388608 | bytes 3670016 | tf_op jit(solution)/shard_map/concatenate | solution.py:39
  38.8 5.2 %collective-permute-done.2 = bf16[4,2,64,512]{3,2,1,0:T(8,128)(2,1)S(1)} collective-permute-done((bf16[4,2,64,512]{3,2,1,0:T(8,128)(2,1)S(1)}, bf16[4,2,64,512]{3,2,1,0:T(8,128)(2,1)S(1)}, u32[]{:S(2)}, u32[]{:S(2)}) %collective-permute-start.2) | collective-permute-done | bytes 524320 | tf_op jit(solution)/shard_map/ppermute | solution.py:50
  45.0 1.6 %copy.9 = f32[2,8,64,512]{3,2,1,0:T(8,128)} copy(f32[2,8,64,512]{3,2,0,1:T(8,128)S(1)} %convert_bitcast_fusion) | data formatting | bytes 4194304 | tf_op jit(solution)/shard_map/convert_element_type | solution.py:303
  46.6 14.5 %shard_map.68.rest_0_ = f32[4,8,128,128]{3,2,1,0:T(8,128)} custom-call(s32[32]{0:T(128)} %reshape.177.f_ref, s32[1]{0:T(128)} %constant.94.clone.1.ta_ref.tb_ref, s32[1]{0:T(128)} %constant.94.clone.1.ta_ref.tb_ref, s32[1]{0:T(128)} %bitcast.1.rid_ref, s32[2]{0:T(128)} %add_multiply_fusion.off_ref, bf16[1,8,2,128,512]{4,3,2,1,0:T(8,128)(2,1)} %bitcast.12.tma_ref, ...), custom_call_target="tpu_custom_call" | custom-call | flops 4831838208 | bytes 14680064 | tf_op jit(solution)/shard_map/pallas_call | solution.py:264
  61.1 9.5 %all-gather.3.cloned.1.call-done = bf16[32,2,128,512]{3,2,1,0:T(8,128)(2,1)} async-done(((bf16[8,2,128,512]{3,2,1,0:T(8,128)(2,1)}), bf16[32,2,128,512]{3,2,1,0:T(8,128)(2,1)}) %all-gather.3.cloned.1.call-update) | async-done | bytes 8388624 | tf_op jit(solution)/shard_map/all_gather | solution.py:284
  70.6 15.3 %shard_map.69 = f32[2,4,128,128]{3,2,1,0:T(8,128)} custom-call(s32[32]{0:T(128)} %reshape.177.f_ref, s32[1]{0:T(128)S(6)} %mul.81.ta_ref, s32[1]{0:T(128)S(6)} %add.169.tb_ref, s32[1]{0:T(128)S(6)} %convert_element_type.45.rid_ref, s32[2]{0:T(128)} %iota_multiply_fusion.off_ref, bf16[4,8,2,128,512]{4,3,2,1,0:T(8,128)(2,1)} %bitcast.41, ...), custom_call_target="tpu_custom_call" | custom-call | flops 4831838208 | bytes 14680064 | tf_op jit(solution)/shard_map/pallas_call | solution.py:264
  85.9 1.1 constant_dynamic-slice_fusion.6
  86.9 4.3 %collective-permute-start.10 = (f32[2,64,128]{2,1,0:T(8,128)S(1)}, f32[2,64,128]{2,1,0:T(8,128)S(1)}, u32[]{:S(2)}, u32[]{:S(2)}) collective-permute-start(f32[2,64,128]{2,1,0:T(8,128)S(1)} %get-tuple-element.7), channel_id=1, source_target_pairs={{0,7},{1,6},{2,5},{3,4},{4,3},{5,2},{6,1},{7,0},{8,15},{9,14},{10,... | collective-permute-start | bytes 196616 | tf_op jit(solution)/shard_map/ppermute | solution.py:91
  91.8 2.9 %collective-permute-start.6 = (f32[2,64,128]{2,1,0:T(8,128)S(1)}, f32[2,64,128]{2,1,0:T(8,128)S(1)}, u32[]{:S(2)}, u32[]{:S(2)}) collective-permute-start(f32[2,64,128]{2,1,0:T(8,128)S(1)} %get-tuple-element.11), channel_id=1, source_target_pairs={{0,3},{1,2},{2,1},{3,0},{4,7},{5,6},{6,5},{7,4},{8,11},{9,10},{10,... | collective-permute-start | bytes 196616 | tf_op jit(solution)/shard_map/ppermute | solution.py:91
  94.7 2.9 %collective-permute-start.8 = (f32[2,64,128]{2,1,0:T(8,128)S(1)}, f32[2,64,128]{2,1,0:T(8,128)S(1)}, u32[]{:S(2)}, u32[]{:S(2)}) collective-permute-start(f32[2,64,128]{2,1,0:T(8,128)S(1)} %get-tuple-element.9), channel_id=1, source_target_pairs={{0,5},{1,4},{2,7},{3,6},{4,1},{5,0},{6,3},{7,2},{8,13},{9,12},{10,... | collective-permute-start | bytes 196616 | tf_op jit(solution)/shard_map/ppermute | solution.py:91
  98.2 4.2 %collective-permute-done.7 = f32[2,64,128]{2,1,0:T(8,128)S(1)} collective-permute-done((f32[2,64,128]{2,1,0:T(8,128)S(1)}, f32[2,64,128]{2,1,0:T(8,128)S(1)}, u32[]{:S(2)}, u32[]{:S(2)}) %collective-permute-start.7) | collective-permute-done | bytes 65568 | tf_op jit(solution)/shard_map/ppermute | solution.py:91
  102.4 2.4 %collective-permute-done.8 = f32[2,64,128]{2,1,0:T(8,128)S(1)} collective-permute-done((f32[2,64,128]{2,1,0:T(8,128)S(1)}, f32[2,64,128]{2,1,0:T(8,128)S(1)}, u32[]{:S(2)}, u32[]{:S(2)}) %collective-permute-start.8) | collective-permute-done | bytes 65568 | tf_op jit(solution)/shard_map/ppermute | solution.py:91
  104.9 0.8 slice_maximum_fusion
  105.7 1.2 collective-permute-start.11
  106.9 0.8 collective-permute-start.12
  107.7 1.6 %collective-permute-start.13 = (f32[2,64,128]{2,1,0:T(8,128)S(1)}, f32[2,64,128]{2,1,0:T(8,128)S(1)}, u32[]{:S(2)}, u32[]{:S(2)}) collective-permute-start(f32[2,64,128]{2,1,0:T(8,128)S(1)} %pad_maximum_fusion.3), channel_id=1, source_target_pairs={{0,3},{1,2},{2,1},{3,0},{4,7},{5,6},{6,5},{7,4},{8,11},{9,10},{10,... | collective-permute-start | bytes 196616 | tf_op jit(solution)/shard_map/ppermute | solution.py:100
  109.3 1.3 %collective-permute-start.14 = (f32[2,64,128]{2,1,0:T(8,128)S(1)}, f32[2,64,128]{2,1,0:T(8,128)S(1)}, u32[]{:S(2)}, u32[]{:S(2)}) collective-permute-start(f32[2,64,128]{2,1,0:T(8,128)S(1)} %pad_maximum_fusion.3), channel_id=1, source_target_pairs={{0,4},{1,5},{2,6},{3,7},{4,0},{5,1},{6,2},{7,3},{8,12},{9,13},{10,... | collective-permute-start | bytes 196616 | tf_op jit(solution)/shard_map/ppermute | solution.py:100
  110.6 2.2 %collective-permute-start.15 = (f32[2,64,128]{2,1,0:T(8,128)S(1)}, f32[2,64,128]{2,1,0:T(8,128)S(1)}, u32[]{:S(2)}, u32[]{:S(2)}) collective-permute-start(f32[2,64,128]{2,1,0:T(8,128)S(1)} %pad_maximum_fusion.3), channel_id=1, source_target_pairs={{0,5},{1,4},{2,7},{3,6},{4,1},{5,0},{6,3},{7,2},{8,13},{9,12},{10,... | collective-permute-start | bytes 196616 | tf_op jit(solution)/shard_map/ppermute | solution.py:100
  112.8 1.3 %collective-permute-start.16 = (f32[2,64,128]{2,1,0:T(8,128)S(1)}, f32[2,64,128]{2,1,0:T(8,128)S(1)}, u32[]{:S(2)}, u32[]{:S(2)}) collective-permute-start(f32[2,64,128]{2,1,0:T(8,128)S(1)} %pad_maximum_fusion.3), channel_id=1, source_target_pairs={{0,6},{1,7},{2,4},{3,5},{4,2},{5,3},{6,0},{7,1},{8,14},{9,15},{10,... | collective-permute-start | bytes 196616 | tf_op jit(solution)/shard_map/ppermute | solution.py:100
  114.1 3.0 %collective-permute-start.17 = (f32[2,64,128]{2,1,0:T(8,128)S(1)}, f32[2,64,128]{2,1,0:T(8,128)S(1)}, u32[]{:S(2)}, u32[]{:S(2)}) collective-permute-start(f32[2,64,128]{2,1,0:T(8,128)S(1)} %pad_maximum_fusion.3), channel_id=1, source_target_pairs={{0,7},{1,6},{2,5},{3,4},{4,3},{5,2},{6,1},{7,0},{8,15},{9,14},{10,... | collective-permute-start | bytes 196616 | tf_op jit(solution)/shard_map/ppermute | solution.py:100
  117.1 1.9 %collective-permute-done.14 = f32[2,64,128]{2,1,0:T(8,128)S(1)} collective-permute-done((f32[2,64,128]{2,1,0:T(8,128)S(1)}, f32[2,64,128]{2,1,0:T(8,128)S(1)}, u32[]{:S(2)}, u32[]{:S(2)}) %collective-permute-start.14) | collective-permute-done | bytes 65568 | tf_op jit(solution)/shard_map/ppermute | solution.py:100
  119.0 2.5 %collective-permute-done.15 = f32[2,64,128]{2,1,0:T(8,128)S(1)} collective-permute-done((f32[2,64,128]{2,1,0:T(8,128)S(1)}, f32[2,64,128]{2,1,0:T(8,128)S(1)}, u32[]{:S(2)}, u32[]{:S(2)}) %collective-permute-start.15) | collective-permute-done | bytes 65568 | tf_op jit(solution)/shard_map/ppermute | solution.py:100
  122.2 0.8 slice_multiply_fusion
  (54 shorter events, 6.2 us)
Async XLA Ops:
  7.2 1.3 copy-start
  7.2 5.0 %copy-start.2 = (s32[1,4,2]{1,2,0:T(2,128)S(1)}, s32[1,4,2]{1,2,0:T(2,128)}, u32[]{:S(2)}) copy-start(s32[1,4,2]{1,2,0:T(2,128)} %param.7) | copy-start | bytes 100
  7.2 9.3 %copy-start.1 = (s32[1,4,48]{2,1,0:T(4,128)S(1)}, s32[1,4,48]{2,1,0:T(4,128)}, u32[]{:S(2)}) copy-start(s32[1,4,48]{2,1,0:T(4,128)} %param.8) | copy-start | bytes 2308
  7.2 63.4 %all-gather.3.cloned.1.call-start = ((), (), s32[]{:S(2)}) async-start(), calls=%async_computation | async-start | bytes 10485760 | tf_op jit(solution)/shard_map/all_gather | solution.py:284
  7.9 38.7 %collective-permute-start.3 = (bf16[8,2,128,512]{3,2,1,0:T(8,128)(2,1)}, bf16[8,2,128,512]{3,2,1,0:T(8,128)(2,1)}, u32[]{:S(2)}, u32[]{:S(2)}) collective-permute-start(bf16[8,2,128,512]{3,2,1,0:T(8,128)(2,1)} %param.6), channel_id=1, source_target_pairs={{0,8},{8,0},{16,24},{24,16},{1,9},{9,1},{17,25},{25,17},{2,10},{10... | collective-permute-start | bytes 6291464 | tf_op jit(solution)/shard_map/ppermute | solution.py:302
  8.4 13.7 %collective-permute-start = (bf16[1,2,64,512]{3,2,1,0:T(8,128)(2,1)S(1)}, bf16[1,2,64,512]{3,2,1,0:T(8,128)(2,1)S(1)}, u32[]{:S(2)}, u32[]{:S(2)}) collective-permute-start(bf16[1,2,64,512]{3,2,1,0:T(8,128)(2,1)S(1)} %copy-done), channel_id=1, source_target_pairs={{0,4},{1,5},{2,6},{3,7},{4,0},{5,1},{6,2},{7,3},{8,12},{9,13},{10,... | collective-permute-start | bytes 393224 | tf_op jit(solution)/shard_map/ppermute | solution.py:50
  22.2 8.4 %collective-permute-start.1 = (bf16[2,2,64,512]{3,2,1,0:T(8,128)(2,1)S(1)}, bf16[2,2,64,512]{3,2,1,0:T(8,128)(2,1)S(1)}, u32[]{:S(2)}, u32[]{:S(2)}) collective-permute-start(bf16[2,2,64,512]{3,2,1,0:T(8,128)(2,1)S(1)} %pad_maximum_fusion.2), channel_id=1, source_target_pairs={{0,2},{1,3},{2,0},{3,1},{4,6},{5,7},{6,4},{7,5},{8,10},{9,11},{10,... | collective-permute-start | bytes 786440 | tf_op jit(solution)/shard_map/ppermute | solution.py:50
  30.7 13.3 %collective-permute-start.2 = (bf16[4,2,64,512]{3,2,1,0:T(8,128)(2,1)S(1)}, bf16[4,2,64,512]{3,2,1,0:T(8,128)(2,1)S(1)}, u32[]{:S(2)}, u32[]{:S(2)}) collective-permute-start(bf16[4,2,64,512]{3,2,1,0:T(8,128)(2,1)S(1)} %pad_maximum_fusion.1), channel_id=1, source_target_pairs={{0,1},{1,0},{2,3},{3,2},{4,5},{5,4},{6,7},{7,6},{8,9},{9,8},{10,11... | collective-permute-start | bytes 1572872 | tf_op jit(solution)/shard_map/ppermute | solution.py:50
  86.9 7.8 %collective-permute-start.10 = (f32[2,64,128]{2,1,0:T(8,128)S(1)}, f32[2,64,128]{2,1,0:T(8,128)S(1)}, u32[]{:S(2)}, u32[]{:S(2)}) collective-permute-start(f32[2,64,128]{2,1,0:T(8,128)S(1)} %get-tuple-element.7), channel_id=1, source_target_pairs={{0,7},{1,6},{2,5},{3,4},{4,3},{5,2},{6,1},{7,0},{8,15},{9,14},{10,... | collective-permute-start | bytes 196616 | tf_op jit(solution)/shard_map/ppermute | solution.py:91
  91.2 6.4 %collective-permute-start.4 = (f32[2,64,128]{2,1,0:T(8,128)S(1)}, f32[2,64,128]{2,1,0:T(8,128)S(1)}, u32[]{:S(2)}, u32[]{:S(2)}) collective-permute-start(f32[2,64,128]{2,1,0:T(8,128)S(1)} %get-tuple-element.6), channel_id=1, source_target_pairs={{0,1},{1,0},{2,3},{3,2},{4,5},{5,4},{6,7},{7,6},{8,9},{9,8},{10,11... | collective-permute-start | bytes 196616 | tf_op jit(solution)/shard_map/ppermute | solution.py:91
  91.8 6.4 %collective-permute-start.5 = (f32[2,64,128]{2,1,0:T(8,128)S(1)}, f32[2,64,128]{2,1,0:T(8,128)S(1)}, u32[]{:S(2)}, u32[]{:S(2)}) collective-permute-start(f32[2,64,128]{2,1,0:T(8,128)S(1)} %get-tuple-element.12), channel_id=1, source_target_pairs={{0,2},{1,3},{2,0},{3,1},{4,6},{5,7},{6,4},{7,5},{8,10},{9,11},{10,... | collective-permute-start | bytes 196616 | tf_op jit(solution)/shard_map/ppermute | solution.py:91
  91.8 6.4 %collective-permute-start.6 = (f32[2,64,128]{2,1,0:T(8,128)S(1)}, f32[2,64,128]{2,1,0:T(8,128)S(1)}, u32[]{:S(2)}, u32[]{:S(2)}) collective-permute-start(f32[2,64,128]{2,1,0:T(8,128)S(1)} %get-tuple-element.11), channel_id=1, source_target_pairs={{0,3},{1,2},{2,1},{3,0},{4,7},{5,6},{6,5},{7,4},{8,11},{9,10},{10,... | collective-permute-start | bytes 196616 | tf_op jit(solution)/shard_map/ppermute | solution.py:91
  94.7 7.7 %collective-permute-start.7 = (f32[2,64,128]{2,1,0:T(8,128)S(1)}, f32[2,64,128]{2,1,0:T(8,128)S(1)}, u32[]{:S(2)}, u32[]{:S(2)}) collective-permute-start(f32[2,64,128]{2,1,0:T(8,128)S(1)} %get-tuple-element.10), channel_id=1, source_target_pairs={{0,4},{1,5},{2,6},{3,7},{4,0},{5,1},{6,2},{7,3},{8,12},{9,13},{10,... | collective-permute-start | bytes 196616 | tf_op jit(solution)/shard_map/ppermute | solution.py:91
  94.7 10.1 %collective-permute-start.8 = (f32[2,64,128]{2,1,0:T(8,128)S(1)}, f32[2,64,128]{2,1,0:T(8,128)S(1)}, u32[]{:S(2)}, u32[]{:S(2)}) collective-permute-start(f32[2,64,128]{2,1,0:T(8,128)S(1)} %get-tuple-element.9), channel_id=1, source_target_pairs={{0,5},{1,4},{2,7},{3,6},{4,1},{5,0},{6,3},{7,2},{8,13},{9,12},{10,... | collective-permute-start | bytes 196616 | tf_op jit(solution)/shard_map/ppermute | solution.py:91
  97.6 7.2 %collective-permute-start.9 = (f32[2,64,128]{2,1,0:T(8,128)S(1)}, f32[2,64,128]{2,1,0:T(8,128)S(1)}, u32[]{:S(2)}, u32[]{:S(2)}) collective-permute-start(f32[2,64,128]{2,1,0:T(8,128)S(1)} %get-tuple-element.8), channel_id=1, source_target_pairs={{0,6},{1,7},{2,4},{3,5},{4,2},{5,3},{6,0},{7,1},{8,14},{9,15},{10,... | collective-permute-start | bytes 196616 | tf_op jit(solution)/shard_map/ppermute | solution.py:91
  105.7 7.1 %collective-permute-start.11 = (f32[2,64,128]{2,1,0:T(8,128)S(1)}, f32[2,64,128]{2,1,0:T(8,128)S(1)}, u32[]{:S(2)}, u32[]{:S(2)}) collective-permute-start(f32[2,64,128]{2,1,0:T(8,128)S(1)} %pad_maximum_fusion.3), channel_id=1, source_target_pairs={{0,1},{1,0},{2,3},{3,2},{4,5},{5,4},{6,7},{7,6},{8,9},{9,8},{10,11... | collective-permute-start | bytes 196616 | tf_op jit(solution)/shard_map/ppermute | solution.py:100
  106.9 7.2 %collective-permute-start.12 = (f32[2,64,128]{2,1,0:T(8,128)S(1)}, f32[2,64,128]{2,1,0:T(8,128)S(1)}, u32[]{:S(2)}, u32[]{:S(2)}) collective-permute-start(f32[2,64,128]{2,1,0:T(8,128)S(1)} %pad_maximum_fusion.3), channel_id=1, source_target_pairs={{0,2},{1,3},{2,0},{3,1},{4,6},{5,7},{6,4},{7,5},{8,10},{9,11},{10,... | collective-permute-start | bytes 196616 | tf_op jit(solution)/shard_map/ppermute | solution.py:100
  107.7 9.4 %collective-permute-start.13 = (f32[2,64,128]{2,1,0:T(8,128)S(1)}, f32[2,64,128]{2,1,0:T(8,128)S(1)}, u32[]{:S(2)}, u32[]{:S(2)}) collective-permute-start(f32[2,64,128]{2,1,0:T(8,128)S(1)} %pad_maximum_fusion.3), channel_id=1, source_target_pairs={{0,3},{1,2},{2,1},{3,0},{4,7},{5,6},{6,5},{7,4},{8,11},{9,10},{10,... | collective-permute-start | bytes 196616 | tf_op jit(solution)/shard_map/ppermute | solution.py:100
  109.3 9.8 %collective-permute-start.14 = (f32[2,64,128]{2,1,0:T(8,128)S(1)}, f32[2,64,128]{2,1,0:T(8,128)S(1)}, u32[]{:S(2)}, u32[]{:S(2)}) collective-permute-start(f32[2,64,128]{2,1,0:T(8,128)S(1)} %pad_maximum_fusion.3), channel_id=1, source_target_pairs={{0,4},{1,5},{2,6},{3,7},{4,0},{5,1},{6,2},{7,3},{8,12},{9,13},{10,... | collective-permute-start | bytes 196616 | tf_op jit(solution)/shard_map/ppermute | solution.py:100
  110.6 11.0 %collective-permute-start.15 = (f32[2,64,128]{2,1,0:T(8,128)S(1)}, f32[2,64,128]{2,1,0:T(8,128)S(1)}, u32[]{:S(2)}, u32[]{:S(2)}) collective-permute-start(f32[2,64,128]{2,1,0:T(8,128)S(1)} %pad_maximum_fusion.3), channel_id=1, source_target_pairs={{0,5},{1,4},{2,7},{3,6},{4,1},{5,0},{6,3},{7,2},{8,13},{9,12},{10,... | collective-permute-start | bytes 196616 | tf_op jit(solution)/shard_map/ppermute | solution.py:100
  112.8 8.8 %collective-permute-start.16 = (f32[2,64,128]{2,1,0:T(8,128)S(1)}, f32[2,64,128]{2,1,0:T(8,128)S(1)}, u32[]{:S(2)}, u32[]{:S(2)}) collective-permute-start(f32[2,64,128]{2,1,0:T(8,128)S(1)} %pad_maximum_fusion.3), channel_id=1, source_target_pairs={{0,6},{1,7},{2,4},{3,5},{4,2},{5,3},{6,0},{7,1},{8,14},{9,15},{10,... | collective-permute-start | bytes 196616 | tf_op jit(solution)/shard_map/ppermute | solution.py:100
  114.1 7.5 %collective-permute-start.17 = (f32[2,64,128]{2,1,0:T(8,128)S(1)}, f32[2,64,128]{2,1,0:T(8,128)S(1)}, u32[]{:S(2)}, u32[]{:S(2)}) collective-permute-start(f32[2,64,128]{2,1,0:T(8,128)S(1)} %pad_maximum_fusion.3), channel_id=1, source_target_pairs={{0,7},{1,6},{2,5},{3,4},{4,3},{5,2},{6,1},{7,0},{8,15},{9,14},{10,... | collective-permute-start | bytes 196616 | tf_op jit(solution)/shard_map/ppermute | solution.py:100
Sparse Core Ops, SparseCore 0:
  9.6 60.9 all-gather.2

commit v12 on v11

--- a/solution.py
+++ b/solution.py
@@ -281,10 +281,7 @@
     width = W
     tiles = lax.axis_size("tile")
     rows_t = template_spectra.shape[2]
-    tmpl = lax.all_gather(template_spectra, "tile", axis=0)
-    block_size = tmpl.shape[1]
-    spec = gather_rows(tile_spectra[0], "orient")
-    spec = jnp.moveaxis(spec, 0, 1).reshape(2, size, size)
+    block_size = template_spectra.shape[0]
     freqs = jnp.arange(size, dtype=jnp.int32)
     cos_row, sin_row = angle_tables(freqs, peaks[0][:, 0], size, width)
     cos_t = jnp.swapaxes(cos_row, 1, 2)
@@ -295,24 +292,26 @@
     is_listed = jnp.any(listed_ids[:, :, None] == global_ids[None, None, :], axis=1)
     flags = is_listed.astype(jnp.int32).reshape(-1)
     best_shape = (listed.shape[1], width, width)
-    if rows_t % 128 != 0 or tiles % 2 != 0 or block_size % 2 != 0:
+    if rows_t % 128 != 0 or tiles != 4 or block_size % 4 != 0:
+        tmpl = lax.all_gather(template_spectra, "tile", axis=0)
+        spec = gather_rows(tile_spectra[0], "orient")
+        spec = jnp.moveaxis(spec, 0, 1).reshape(2, size, size)
         best_part, power_part = match(flags, tmpl, spec, col_table, cos_t, sin_t)
-    else:
-        me = lax.axis_index("tile")
-        sibling = lax.ppermute(template_spectra, "tile", xor_pairs(tiles, 1))
-        spec32 = spec.astype(jnp.float32)
-        chip = me // 2
-        odd = (me % 2).astype(jnp.int32)
-        zero = jnp.zeros((1,), jnp.int32)
-        near_offs = jnp.stack([odd, 1 - odd]) * rows_t
-        own, sib = template_spectra[None], sibling[None]
-        partial = match_rows(flags, zero, zero, chip[None].astype(jnp.int32), near_offs, own, sib, spec32, col_table, cos_t, sin_t)
-        far = far_chips(chip, tiles // 2)
-        far_offs = jnp.array([0, rows_t], jnp.int32)
-        joined = match_rows(flags, far * 2, far * 2 + 1, far, far_offs, tmpl, tmpl, spec32, col_table, cos_t, sin_t, init=partial)
-        best_all, power_all = reduce_joined(joined.reshape(2, -1, width), best_shape, "orient")
+        best_all, power_all = reduce_orient(best_part, power_part, "orient")
         return (best_all[None], (power_all / LIST)[None])
-    best_all, power_all = reduce_orient(best_part, power_part, "orient")
+    me = lax.axis_index("tile")
+    spec = lax.all_gather(tile_spectra, "orient", axis=2, tiled=True)[0]
+    spec32 = spec.astype(jnp.float32)
+    sibling = lax.ppermute(template_spectra, "tile", xor_pairs(tiles, 1))
+    far_own = lax.ppermute(template_spectra, "tile", xor_pairs(tiles, 2))
+    far_sib = lax.ppermute(far_own, "tile", xor_pairs(tiles, 1))
+    chip = (me // 2).astype(jnp.int32)
+    odd = (me % 2).astype(jnp.int32)
+    zero = jnp.zeros((1,), jnp.int32)
+    offs = jnp.stack([odd, 1 - odd]) * rows_t
+    partial = match_rows(flags, zero, zero, chip[None], offs, template_spectra[None], sibling[None], spec32, col_table, cos_t, sin_t)
+    joined = match_rows(flags, zero, zero, (1 - chip)[None], offs, far_own[None], far_sib[None], spec32, col_table, cos_t, sin_t, init=partial)
+    best_all, power_all = reduce_joined(joined.reshape(2, -1, width), best_shape, "orient")
     return (best_all[None], (power_all / LIST)[None])
 
 

time: 130 us -> 155 us (1.19)
  waiting for transfers between devices: 28.2 us -> 55.9 us
  starting transfers between devices: 30 us -> 26 us
  other arithmetic: 23.2 us -> 25.9 us
    ppermute x3 -> x2, waiting for transfers between devices: 6.84 us -> 44.1 us  [the longest x1 44.1 us: local(): far_own = lax.ppermute(template_spectra, 'tile', xor_pairs(tiles, 2))]
    all_gather x1, waiting for transfers between devices: 9.51 us -> 0.01 us  [local(): spec = lax.all_gather(tile_spectra, 'orient', axis=2, tiled=True)[0]]
    ppermute x3 -> x2, starting transfers between devices: 6.87 us -> 3.03 us  [the longest x1 3.03 us: local(): far_own = lax.ppermute(template_spectra, 'tile', xor_pairs(tiles, 2))]
    convert_element_type x1, other arithmetic: 0.28 us -> 2.85 us  [local(): spec32 = spec.astype(jnp.float32)]
    convert_element_type x1 -> x0, local copies, waits for them, and re-layouts: 1.57 us -> none  [local(): spec32 = spec.astype(jnp.float32)]
  transfers between devices with their start and end apart: 19 -> 18, of which waited for: 7 -> 5; matrix products, arithmetic and copies ran while one was open for 19% -> 17% of each run, Pallas kernels for 11% -> 9%
where the time goes in v12:
time: 155 us
  waiting for transfers between devices  55.9 us (36%)
  Pallas kernels  29.7 us (19%)
  starting transfers between devices  26 us (17%)
  other arithmetic  25.9 us (17%)
  between operations  14.2 us (9%)
  local copies, waits for them, and re-layouts  3.05 us (2%)
    ppermute x1, waiting for transfers between devices, local(): far_own = lax.ppermute(template_spectra, 'tile', xor_pairs(tiles, 2))  44.1 us
    pallas_call x2, Pallas kernels, match_rows(): pl.pallas_call(kernel, grid_spec=pltpu.PrefetchScalarGridSpec(num_scalar_...  29.7 us
    ppermute x7, starting transfers between devices, reduce_joined(): lax.ppermute(done, axis, xor_pairs(n, k))  11.7 us
    ppermute x7, starting transfers between devices, reduce_joined(): got = lax.ppermute(send, axis, xor_pairs(n, k))  11.2 us
    ppermute x7, waiting for transfers between devices, reduce_joined(): got = lax.ppermute(send, axis, xor_pairs(n, k))  7.04 us
    ppermute x7, waiting for transfers between devices, reduce_joined(): lax.ppermute(done, axis, xor_pairs(n, k))  4.76 us
    convert_element_type x1, other arithmetic, angle_tables(): jnp.sin(angle).astype(jnp.bfloat16)  4.41 us
    neg x1, other arithmetic, match_rows(): -sin_t.reshape(peaks_n, width, chips, span)  4.31 us
  transfers between devices with their start and end apart: 18, of which 5 were waited for; matrix products, arithmetic and copies ran while one was open for 17% of the time, Pallas kernels for 9%

profile of v12, /device:TPU:0, one launch (start us, length us, event | category | flops | bytes accessed | tf_op | source)
XLA Modules:
  0.0 154.8 jit_solution(1321109665241598203)
XLA Ops:
  7.2 3.0 %collective-permute-start = (bf16[8,2,128,512]{3,2,1,0:T(8,128)(2,1)}, bf16[8,2,128,512]{3,2,1,0:T(8,128)(2,1)S(1)}, u32[]{:S(2)}, u32[]{:S(2)}) collective-permute-start(bf16[8,2,128,512]{3,2,1,0:T(8,128)(2,1)} %param.5), channel_id=1, source_target_pairs={{0,16},{8,24},{16,0},{24,8},{1,17},{9,25},{17,1},{25,9},{2,18},{10... | collective-permute-start | bytes 6291464 | tf_op jit(solution)/shard_map/ppermute | solution.py:306
  10.3 0.8 slice_bitcast_fusion
  11.1 0.9 compare_reduce_fusion
  12.0 44.1 %collective-permute-done = bf16[8,2,128,512]{3,2,1,0:T(8,128)(2,1)S(1)} collective-permute-done((bf16[8,2,128,512]{3,2,1,0:T(8,128)(2,1)}, bf16[8,2,128,512]{3,2,1,0:T(8,128)(2,1)S(1)}, u32[]{:S(2)}, u32[]{:S(2)}) %collective-permute-start) | collective-permute-done | bytes 2097184 | tf_op jit(solution)/shard_map/ppermute | solution.py:306
  56.1 0.7 add_multiply_fusion.off_ref
  56.8 0.6 reshape.132.f_ref
  57.4 4.2 %cosine_convert_fusion = bf16[4,128,2,256]{3,1,2,0:T(8,128)(2,1)S(1)} fusion(s32[4,128]{1,0:T(4,128)S(1)} %get-tuple-element.17, s32[2,256]{1,0:T(2,128)S(1)} %multiply_add_fusion), kind=kLoop, calls=%fused_computation.19 | loop fusion | flops 3932160 | bytes 528384 | tf_op jit(solution)/shard_map/convert_element_type | solution.py:31
  61.6 4.3 %fusion.9 = bf16[4,128,2,256]{3,1,2,0:T(8,128)(2,1)S(1)} fusion(s32[4,128]{1,0:T(4,128)S(1)} %get-tuple-element.17, s32[2,256]{1,0:T(2,128)S(1)} %multiply_add_fusion), kind=kLoop, calls=%fused_computation.25 | loop fusion | flops 4718592 | bytes 528384 | tf_op jit(solution)/shard_map/neg | solution.py:252
  65.9 1.1 maximum_bitcast_fusion.cr_ref
  67.0 4.0 %fusion.10 = bf16[4,512,128]{2,1,0:T(8,128)(2,1)S(1)} fusion(s32[4,128]{1,0:T(4,128)S(1)} %get-tuple-element.18), kind=kLoop, calls=%fused_computation.27 | loop fusion | flops 4718592 | bytes 526336 | tf_op jit(solution)/shard_map/neg | solution.py:38
  71.1 4.4 %sine_convert_fusion.1 = (bf16[4,512,128]{2,1,0:T(8,128)(2,1)S(1)}, bf16[4,512,128]{2,1,0:T(8,128)(2,1)S(1)}) fusion(s32[4,128]{1,0:T(4,128)S(1)} %get-tuple-element.18), kind=kLoop, calls=%fused_computation.20 | loop fusion | flops 4194304 | bytes 1050624 | tf_op jit(solution)/shard_map/convert_element_type | solution.py:31
  75.5 1.6 %maximum_maximum_fusion.ct_ref = bf16[4,1024,256]{2,1,0:T(8,128)(2,1)} fusion(bf16[4,512,128]{2,1,0:T(8,128)(2,1)S(1)} %get-tuple-element.14, bf16[4,512,128]{2,1,0:T(8,128)(2,1)S(1)} %fusion.10, bf16[4,512,128]{2,1,0:T(8,128)(2,1)S(1)} %get-tuple-element.13), kind=kLoop, calls=%fused_computation.1 | loop fusion | flops 8388608 | bytes 3670016 | tf_op jit(solution)/shard_map/concatenate | solution.py:39
  77.1 2.9 %bitcast_convert_fusion.sp_ref = f32[2,512,512]{2,1,0:T(8,128)} fusion(bf16[1,2,512,512]{3,2,1,0:T(8,128)(2,1)} %all-gather.2.cloned.1.call-done), kind=kLoop, calls=%fused_computation.17 | loop fusion | flops 524288 | bytes 3145728 | tf_op jit(solution)/shard_map/convert_element_type | solution.py:304
  79.9 14.5 %shard_map.59.rest_0_ = f32[4,8,128,128]{3,2,1,0:T(8,128)} custom-call(s32[32]{0:T(128)} %reshape.132.f_ref, s32[1]{0:T(128)} %constant.80.clone.1.ta_ref.tb_ref, s32[1]{0:T(128)} %constant.80.clone.1.ta_ref.tb_ref, s32[1]{0:T(128)} %bitcast.11.rid_ref, s32[2]{0:T(128)} %add_multiply_fusion.off_ref, bf16[1,8,2,128,512]{4,3,2,1,0:T(8,128)(2,1)} %bitcast.48, ...), custom_call_target="tpu_custom_call" | custom-call | flops 4831838208 | bytes 14680064 | tf_op jit(solution)/shard_map/pallas_call | solution.py:264
  94.4 15.2 %shard_map.60 = f32[2,4,128,128]{3,2,1,0:T(8,128)} custom-call(s32[32]{0:T(128)} %reshape.132.f_ref, s32[1]{0:T(128)} %constant.80.clone.1.ta_ref.tb_ref, s32[1]{0:T(128)} %constant.80.clone.1.ta_ref.tb_ref, s32[1]{0:T(128)} %bitcast.1.rid_ref, s32[2]{0:T(128)} %add_multiply_fusion.off_ref, bf16[1,8,2,128,512]{4,3,2,1,0:T(8,128)(2,1)} %bitcast.49, ...), custom_call_target="tpu_custom_call" | custom-call | flops 4831838208 | bytes 14680064 | tf_op jit(solution)/shard_map/pallas_call | solution.py:264
  109.7 1.1 constant_dynamic-slice_fusion.6
  110.8 3.2 %collective-permute-start.4 = (f32[2,64,128]{2,1,0:T(8,128)S(1)}, f32[2,64,128]{2,1,0:T(8,128)S(1)}, u32[]{:S(2)}, u32[]{:S(2)}) collective-permute-start(f32[2,64,128]{2,1,0:T(8,128)S(1)} %get-tuple-element.12), channel_id=1, source_target_pairs={{0,2},{1,3},{2,0},{3,1},{4,6},{5,7},{6,4},{7,5},{8,10},{9,11},{10,... | collective-permute-start | bytes 196616 | tf_op jit(solution)/shard_map/ppermute | solution.py:91
  114.3 2.8 %collective-permute-start.6 = (f32[2,64,128]{2,1,0:T(8,128)S(1)}, f32[2,64,128]{2,1,0:T(8,128)S(1)}, u32[]{:S(2)}, u32[]{:S(2)}) collective-permute-start(f32[2,64,128]{2,1,0:T(8,128)S(1)} %get-tuple-element.10), channel_id=1, source_target_pairs={{0,4},{1,5},{2,6},{3,7},{4,0},{5,1},{6,2},{7,3},{8,12},{9,13},{10,... | collective-permute-start | bytes 196616 | tf_op jit(solution)/shard_map/ppermute | solution.py:91
  117.2 0.9 collective-permute-start.7
  118.1 3.9 %collective-permute-start.8 = (f32[2,64,128]{2,1,0:T(8,128)S(1)}, f32[2,64,128]{2,1,0:T(8,128)S(1)}, u32[]{:S(2)}, u32[]{:S(2)}) collective-permute-start(f32[2,64,128]{2,1,0:T(8,128)S(1)} %get-tuple-element.8), channel_id=1, source_target_pairs={{0,6},{1,7},{2,4},{3,5},{4,2},{5,3},{6,0},{7,1},{8,14},{9,15},{10,... | collective-permute-start | bytes 196616 | tf_op jit(solution)/shard_map/ppermute | solution.py:91
  122.1 5.3 %collective-permute-done.7 = f32[2,64,128]{2,1,0:T(8,128)S(1)} collective-permute-done((f32[2,64,128]{2,1,0:T(8,128)S(1)}, f32[2,64,128]{2,1,0:T(8,128)S(1)}, u32[]{:S(2)}, u32[]{:S(2)}) %collective-permute-start.7) | collective-permute-done | bytes 65568 | tf_op jit(solution)/shard_map/ppermute | solution.py:91
  127.3 1.8 %collective-permute-done.9 = f32[2,64,128]{2,1,0:T(8,128)S(1)} collective-permute-done((f32[2,64,128]{2,1,0:T(8,128)S(1)}, f32[2,64,128]{2,1,0:T(8,128)S(1)}, u32[]{:S(2)}, u32[]{:S(2)}) %collective-permute-start.9) | collective-permute-done | bytes 65568 | tf_op jit(solution)/shard_map/ppermute | solution.py:91
  129.1 0.8 slice_maximum_fusion
  129.9 0.5 collective-permute-start.10
  130.5 2.5 %collective-permute-start.11 = (f32[2,64,128]{2,1,0:T(8,128)S(1)}, f32[2,64,128]{2,1,0:T(8,128)S(1)}, u32[]{:S(2)}, u32[]{:S(2)}) collective-permute-start(f32[2,64,128]{2,1,0:T(8,128)S(1)} %pad_maximum_fusion), channel_id=1, source_target_pairs={{0,2},{1,3},{2,0},{3,1},{4,6},{5,7},{6,4},{7,5},{8,10},{9,11},{10,... | collective-permute-start | bytes 196616 | tf_op jit(solution)/shard_map/ppermute | solution.py:100
  133.5 3.3 %collective-permute-start.13 = (f32[2,64,128]{2,1,0:T(8,128)S(1)}, f32[2,64,128]{2,1,0:T(8,128)S(1)}, u32[]{:S(2)}, u32[]{:S(2)}) collective-permute-start(f32[2,64,128]{2,1,0:T(8,128)S(1)} %pad_maximum_fusion), channel_id=1, source_target_pairs={{0,4},{1,5},{2,6},{3,7},{4,0},{5,1},{6,2},{7,3},{8,12},{9,13},{10,... | collective-permute-start | bytes 196616 | tf_op jit(solution)/shard_map/ppermute | solution.py:100
  136.8 2.4 %collective-permute-start.15 = (f32[2,64,128]{2,1,0:T(8,128)S(1)}, f32[2,64,128]{2,1,0:T(8,128)S(1)}, u32[]{:S(2)}, u32[]{:S(2)}) collective-permute-start(f32[2,64,128]{2,1,0:T(8,128)S(1)} %pad_maximum_fusion), channel_id=1, source_target_pairs={{0,6},{1,7},{2,4},{3,5},{4,2},{5,3},{6,0},{7,1},{8,14},{9,15},{10,... | collective-permute-start | bytes 196616 | tf_op jit(solution)/shard_map/ppermute | solution.py:100
  139.2 2.4 %collective-permute-start.16 = (f32[2,64,128]{2,1,0:T(8,128)S(1)}, f32[2,64,128]{2,1,0:T(8,128)S(1)}, u32[]{:S(2)}, u32[]{:S(2)}) collective-permute-start(f32[2,64,128]{2,1,0:T(8,128)S(1)} %pad_maximum_fusion), channel_id=1, source_target_pairs={{0,7},{1,6},{2,5},{3,4},{4,3},{5,2},{6,1},{7,0},{8,15},{9,14},{10,... | collective-permute-start | bytes 196616 | tf_op jit(solution)/shard_map/ppermute | solution.py:100
  141.7 2.3 %collective-permute-done.13 = f32[2,64,128]{2,1,0:T(8,128)S(1)} collective-permute-done((f32[2,64,128]{2,1,0:T(8,128)S(1)}, f32[2,64,128]{2,1,0:T(8,128)S(1)}, u32[]{:S(2)}, u32[]{:S(2)}) %collective-permute-start.13) | collective-permute-done | bytes 65568 | tf_op jit(solution)/shard_map/ppermute | solution.py:100
  144.0 2.5 %collective-permute-done.14 = f32[2,64,128]{2,1,0:T(8,128)S(1)} collective-permute-done((f32[2,64,128]{2,1,0:T(8,128)S(1)}, f32[2,64,128]{2,1,0:T(8,128)S(1)}, u32[]{:S(2)}, u32[]{:S(2)}) %collective-permute-start.14) | collective-permute-done | bytes 65568 | tf_op jit(solution)/shard_map/ppermute | solution.py:100
  146.5 0.6 gather_fusion
  147.1 0.8 slice_multiply_fusion
  (40 shorter events, 1.1 us)
Async XLA Ops:
  7.2 69.9 %all-gather.2.cloned.1.call-start = ((), (), s32[]{:S(2)}) async-start(), calls=%async_computation | async-start | bytes 1179648 | tf_op jit(solution)/shard_map/all_gather | solution.py:303
  7.2 48.9 %collective-permute-start = (bf16[8,2,128,512]{3,2,1,0:T(8,128)(2,1)}, bf16[8,2,128,512]{3,2,1,0:T(8,128)(2,1)S(1)}, u32[]{:S(2)}, u32[]{:S(2)}) collective-permute-start(bf16[8,2,128,512]{3,2,1,0:T(8,128)(2,1)} %param.5), channel_id=1, source_target_pairs={{0,16},{8,24},{16,0},{24,8},{1,17},{9,25},{17,1},{25,9},{2,18},{10... | collective-permute-start | bytes 6291464 | tf_op jit(solution)/shard_map/ppermute | solution.py:306
  10.2 69.7 %collective-permute-start.2 = (bf16[8,2,128,512]{3,2,1,0:T(8,128)(2,1)}, bf16[8,2,128,512]{3,2,1,0:T(8,128)(2,1)}, u32[]{:S(2)}, u32[]{:S(2)}) collective-permute-start(bf16[8,2,128,512]{3,2,1,0:T(8,128)(2,1)} %param.5), channel_id=1, source_target_pairs={{0,8},{8,0},{16,24},{24,16},{1,9},{9,1},{17,25},{25,17},{2,10},{10... | collective-permute-start | bytes 6291464 | tf_op jit(solution)/shard_map/ppermute | solution.py:305
  56.1 19.4 %copy-start = (bf16[8,2,128,512]{3,2,1,0:T(8,128)(2,1)}, bf16[8,2,128,512]{3,2,1,0:T(8,128)(2,1)S(1)}, u32[]{:S(2)}) copy-start(bf16[8,2,128,512]{3,2,1,0:T(8,128)(2,1)S(1)} %collective-permute-done) | copy-start | bytes 6291460
  56.1 38.4 %collective-permute-start.1 = (bf16[8,2,128,512]{3,2,1,0:T(8,128)(2,1)S(1)}, bf16[8,2,128,512]{3,2,1,0:T(8,128)(2,1)}, u32[]{:S(2)}, u32[]{:S(2)}) collective-permute-start(bf16[8,2,128,512]{3,2,1,0:T(8,128)(2,1)S(1)} %collective-permute-done), channel_id=1, source_target_pairs={{0,8},{8,0},{16,24},{24,16},{1,9},{9,1},{17,25},{25,17},{2,10},{10... | collective-permute-start | bytes 6291464 | tf_op jit(solution)/shard_map/ppermute | solution.py:307
  110.8 7.3 %collective-permute-start.3 = (f32[2,64,128]{2,1,0:T(8,128)S(1)}, f32[2,64,128]{2,1,0:T(8,128)S(1)}, u32[]{:S(2)}, u32[]{:S(2)}) collective-permute-start(f32[2,64,128]{2,1,0:T(8,128)S(1)} %get-tuple-element.6), channel_id=1, source_target_pairs={{0,1},{1,0},{2,3},{3,2},{4,5},{5,4},{6,7},{7,6},{8,9},{9,8},{10,11... | collective-permute-start | bytes 196616 | tf_op jit(solution)/shard_map/ppermute | solution.py:91
  110.8 11.2 %collective-permute-start.4 = (f32[2,64,128]{2,1,0:T(8,128)S(1)}, f32[2,64,128]{2,1,0:T(8,128)S(1)}, u32[]{:S(2)}, u32[]{:S(2)}) collective-permute-start(f32[2,64,128]{2,1,0:T(8,128)S(1)} %get-tuple-element.12), channel_id=1, source_target_pairs={{0,2},{1,3},{2,0},{3,1},{4,6},{5,7},{6,4},{7,5},{8,10},{9,11},{10,... | collective-permute-start | bytes 196616 | tf_op jit(solution)/shard_map/ppermute | solution.py:91
  114.1 8.0 %collective-permute-start.5 = (f32[2,64,128]{2,1,0:T(8,128)S(1)}, f32[2,64,128]{2,1,0:T(8,128)S(1)}, u32[]{:S(2)}, u32[]{:S(2)}) collective-permute-start(f32[2,64,128]{2,1,0:T(8,128)S(1)} %get-tuple-element.11), channel_id=1, source_target_pairs={{0,3},{1,2},{2,1},{3,0},{4,7},{5,6},{6,5},{7,4},{8,11},{9,10},{10,... | collective-permute-start | bytes 196616 | tf_op jit(solution)/shard_map/ppermute | solution.py:91
  114.3 7.7 %collective-permute-start.6 = (f32[2,64,128]{2,1,0:T(8,128)S(1)}, f32[2,64,128]{2,1,0:T(8,128)S(1)}, u32[]{:S(2)}, u32[]{:S(2)}) collective-permute-start(f32[2,64,128]{2,1,0:T(8,128)S(1)} %get-tuple-element.10), channel_id=1, source_target_pairs={{0,4},{1,5},{2,6},{3,7},{4,0},{5,1},{6,2},{7,3},{8,12},{9,13},{10,... | collective-permute-start | bytes 196616 | tf_op jit(solution)/shard_map/ppermute | solution.py:91
  117.2 10.1 %collective-permute-start.7 = (f32[2,64,128]{2,1,0:T(8,128)S(1)}, f32[2,64,128]{2,1,0:T(8,128)S(1)}, u32[]{:S(2)}, u32[]{:S(2)}) collective-permute-start(f32[2,64,128]{2,1,0:T(8,128)S(1)} %get-tuple-element.9), channel_id=1, source_target_pairs={{0,5},{1,4},{2,7},{3,6},{4,1},{5,0},{6,3},{7,2},{8,13},{9,12},{10,... | collective-permute-start | bytes 196616 | tf_op jit(solution)/shard_map/ppermute | solution.py:91
  118.1 9.2 %collective-permute-start.8 = (f32[2,64,128]{2,1,0:T(8,128)S(1)}, f32[2,64,128]{2,1,0:T(8,128)S(1)}, u32[]{:S(2)}, u32[]{:S(2)}) collective-permute-start(f32[2,64,128]{2,1,0:T(8,128)S(1)} %get-tuple-element.8), channel_id=1, source_target_pairs={{0,6},{1,7},{2,4},{3,5},{4,2},{5,3},{6,0},{7,1},{8,14},{9,15},{10,... | collective-permute-start | bytes 196616 | tf_op jit(solution)/shard_map/ppermute | solution.py:91
  122.0 7.1 %collective-permute-start.9 = (f32[2,64,128]{2,1,0:T(8,128)S(1)}, f32[2,64,128]{2,1,0:T(8,128)S(1)}, u32[]{:S(2)}, u32[]{:S(2)}) collective-permute-start(f32[2,64,128]{2,1,0:T(8,128)S(1)} %get-tuple-element.7), channel_id=1, source_target_pairs={{0,7},{1,6},{2,5},{3,4},{4,3},{5,2},{6,1},{7,0},{8,15},{9,14},{10,... | collective-permute-start | bytes 196616 | tf_op jit(solution)/shard_map/ppermute | solution.py:91
  129.9 6.9 %collective-permute-start.10 = (f32[2,64,128]{2,1,0:T(8,128)S(1)}, f32[2,64,128]{2,1,0:T(8,128)S(1)}, u32[]{:S(2)}, u32[]{:S(2)}) collective-permute-start(f32[2,64,128]{2,1,0:T(8,128)S(1)} %pad_maximum_fusion), channel_id=1, source_target_pairs={{0,1},{1,0},{2,3},{3,2},{4,5},{5,4},{6,7},{7,6},{8,9},{9,8},{10,11... | collective-permute-start | bytes 196616 | tf_op jit(solution)/shard_map/ppermute | solution.py:100
  130.5 8.8 %collective-permute-start.11 = (f32[2,64,128]{2,1,0:T(8,128)S(1)}, f32[2,64,128]{2,1,0:T(8,128)S(1)}, u32[]{:S(2)}, u32[]{:S(2)}) collective-permute-start(f32[2,64,128]{2,1,0:T(8,128)S(1)} %pad_maximum_fusion), channel_id=1, source_target_pairs={{0,2},{1,3},{2,0},{3,1},{4,6},{5,7},{6,4},{7,5},{8,10},{9,11},{10,... | collective-permute-start | bytes 196616 | tf_op jit(solution)/shard_map/ppermute | solution.py:100
  132.9 8.7 %collective-permute-start.12 = (f32[2,64,128]{2,1,0:T(8,128)S(1)}, f32[2,64,128]{2,1,0:T(8,128)S(1)}, u32[]{:S(2)}, u32[]{:S(2)}) collective-permute-start(f32[2,64,128]{2,1,0:T(8,128)S(1)} %pad_maximum_fusion), channel_id=1, source_target_pairs={{0,3},{1,2},{2,1},{3,0},{4,7},{5,6},{6,5},{7,4},{8,11},{9,10},{10,... | collective-permute-start | bytes 196616 | tf_op jit(solution)/shard_map/ppermute | solution.py:100
  133.5 10.5 %collective-permute-start.13 = (f32[2,64,128]{2,1,0:T(8,128)S(1)}, f32[2,64,128]{2,1,0:T(8,128)S(1)}, u32[]{:S(2)}, u32[]{:S(2)}) collective-permute-start(f32[2,64,128]{2,1,0:T(8,128)S(1)} %pad_maximum_fusion), channel_id=1, source_target_pairs={{0,4},{1,5},{2,6},{3,7},{4,0},{5,1},{6,2},{7,3},{8,12},{9,13},{10,... | collective-permute-start | bytes 196616 | tf_op jit(solution)/shard_map/ppermute | solution.py:100
  136.8 9.7 %collective-permute-start.14 = (f32[2,64,128]{2,1,0:T(8,128)S(1)}, f32[2,64,128]{2,1,0:T(8,128)S(1)}, u32[]{:S(2)}, u32[]{:S(2)}) collective-permute-start(f32[2,64,128]{2,1,0:T(8,128)S(1)} %pad_maximum_fusion), channel_id=1, source_target_pairs={{0,5},{1,4},{2,7},{3,6},{4,1},{5,0},{6,3},{7,2},{8,13},{9,12},{10,... | collective-permute-start | bytes 196616 | tf_op jit(solution)/shard_map/ppermute | solution.py:100
  136.8 9.7 %collective-permute-start.15 = (f32[2,64,128]{2,1,0:T(8,128)S(1)}, f32[2,64,128]{2,1,0:T(8,128)S(1)}, u32[]{:S(2)}, u32[]{:S(2)}) collective-permute-start(f32[2,64,128]{2,1,0:T(8,128)S(1)} %pad_maximum_fusion), channel_id=1, source_target_pairs={{0,6},{1,7},{2,4},{3,5},{4,2},{5,3},{6,0},{7,1},{8,14},{9,15},{10,... | collective-permute-start | bytes 196616 | tf_op jit(solution)/shard_map/ppermute | solution.py:100
  139.2 7.2 %collective-permute-start.16 = (f32[2,64,128]{2,1,0:T(8,128)S(1)}, f32[2,64,128]{2,1,0:T(8,128)S(1)}, u32[]{:S(2)}, u32[]{:S(2)}) collective-permute-start(f32[2,64,128]{2,1,0:T(8,128)S(1)} %pad_maximum_fusion), channel_id=1, source_target_pairs={{0,7},{1,6},{2,5},{3,4},{4,3},{5,2},{6,1},{7,0},{8,15},{9,14},{10,... | collective-permute-start | bytes 196616 | tf_op jit(solution)/shard_map/ppermute | solution.py:100
Sparse Core Ops, SparseCore 0:
  10.4 42.5 all-gather.1

commit v13 on v10

--- a/solution.py
+++ b/solution.py
@@ -78,28 +78,33 @@
 def reduce_joined(joined, shape, axis):
     n = lax.axis_size(axis)
     rows = joined.shape[1]
-    if not is_pow2(n) or rows % n != 0:
+    if not is_pow2(n) or n < 2 or rows % n != 0:
         best = lax.pmax(joined[0], axis)
         power = lax.psum(joined[1], axis)
         return best.reshape(shape), power.reshape(shape)
     me = lax.axis_index(axis)
-    piece = rows // n
-    own = lax.dynamic_slice_in_dim(joined, me * piece, piece, axis=1)
-    bests, powers = [own[0]], [own[1]]
-    for k in range(1, n):
-        send = lax.dynamic_slice_in_dim(joined, (me ^ k) * piece, piece, axis=1)
-        got = lax.ppermute(send, axis, xor_pairs(n, k))
-        bests.append(got[0])
-        powers.append(got[1])
-    best = bests[0]
-    power = powers[0]
-    for b, p in zip(bests[1:], powers[1:]):
-        best = jnp.maximum(best, b)
-        power = power + p
+    half = rows // 2
+    bit = me % 2
+    keep = lax.dynamic_slice_in_dim(joined, bit * half, half, axis=1)
+    send = lax.dynamic_slice_in_dim(joined, (1 - bit) * half, half, axis=1)
+    got = lax.ppermute(send, axis, xor_pairs(n, 1))
+    cur = jnp.stack([jnp.maximum(keep[0], got[0]), keep[1] + got[1]])
+    members = n // 2
+    group = me // 2
+    piece = half // members
+    own = lax.dynamic_slice_in_dim(cur, group * piece, piece, axis=1)
+    best, power = own[0], own[1]
+    for m in range(1, members):
+        out = lax.dynamic_slice_in_dim(cur, (group ^ m) * piece, piece, axis=1)
+        got = lax.ppermute(out, axis, xor_pairs(n, 2 * m))
+        best = jnp.maximum(best, got[0])
+        power = power + got[1]
     done = jnp.stack([best, power])
-    slots = [done] + [lax.ppermute(done, axis, xor_pairs(n, k)) for k in range(1, n)]
-    pieces = jnp.stack(slots)[jnp.arange(n, dtype=jnp.int32) ^ me]
-    whole = jnp.moveaxis(pieces, 0, 1).reshape(2, rows, joined.shape[2])
+    slots = [done] + [lax.ppermute(done, axis, xor_pairs(n, 2 * m)) for m in range(1, members)]
+    pieces = jnp.stack(slots)[jnp.arange(members, dtype=jnp.int32) ^ group]
+    mine = jnp.moveaxis(pieces, 0, 1).reshape(2, half, joined.shape[2])
+    other = lax.ppermute(mine, axis, xor_pairs(n, 1))
+    whole = jnp.where(bit == 1, jnp.concatenate([other, mine], axis=1), jnp.concatenate([mine, other], axis=1))
     return whole[0].reshape(shape), whole[1].reshape(shape)
 
 

time: 130 us -> 129 us (level)
  starting transfers between devices: 29.1 us -> 18.5 us
  waiting for transfers between devices: 33.1 us -> 43 us
    ppermute x14 -> x8, starting transfers between devices: 22.6 us -> 12 us  [the longest x3 4.45 us: reduce_joined(): got = lax.ppermute(out, axis, xor_pairs(n, 2 * m))]
    ppermute x14 -> x8, waiting for transfers between devices: 11.1 us -> 21.1 us  [the longest x1 7.02 us: reduce_joined(): got = lax.ppermute(send, axis, xor_pairs(n, 1))]
  transfers between devices with their start and end apart: 19 -> 13, of which waited for: 8 -> 10; matrix products, arithmetic and copies ran while one was open for 16% -> 16% of each run, Pallas kernels for 11% -> 11%
where the time goes in v13:
time: 129 us
  waiting for transfers between devices  43 us (33%)
  Pallas kernels  29.6 us (23%)
  other arithmetic  19.5 us (15%)
  starting transfers between devices  18.5 us (14%)
  between operations  14.2 us (11%)
  local copies, waits for them, and re-layouts  4.37 us (3%)
    pallas_call x2, Pallas kernels, match_rows(): pl.pallas_call(kernel, grid_spec=pltpu.PrefetchScalarGridSpec(num_scalar_...  29.6 us
    all_gather x1, waiting for transfers between devices, local(): tmpl = lax.all_gather(template_spectra, 'tile', axis=0)  13.3 us
    convert_element_type x2, other arithmetic, angle_tables(): jnp.sin(angle).astype(jnp.bfloat16)  10.1 us
    ppermute x3, waiting for transfers between devices, gather_rows(): got = lax.ppermute(blocks, axis, xor_pairs(n, k))  7.94 us
    ppermute x1, waiting for transfers between devices, reduce_joined(): got = lax.ppermute(send, axis, xor_pairs(n, 1))  7.02 us
    ppermute x3, starting transfers between devices, gather_rows(): got = lax.ppermute(blocks, axis, xor_pairs(n, k))  5.92 us
    ppermute x3, waiting for transfers between devices, reduce_joined(): got = lax.ppermute(out, axis, xor_pairs(n, 2 * m))  5.57 us
    ppermute x1, waiting for transfers between devices, reduce_joined(): other = lax.ppermute(mine, axis, xor_pairs(n, 1))  4.85 us
  transfers between devices with their start and end apart: 13, of which 10 were waited for; matrix products, arithmetic and copies ran while one was open for 16% of the time, Pallas kernels for 11%

profile of v13, /device:TPU:0, one launch (start us, length us, event | category | flops | bytes accessed | tf_op | source)
XLA Modules:
  0.0 129.1 jit_solution(18415966605463290895)
XLA Ops:
  7.2 0.7 all-gather.3.cloned.1.call-update
  8.4 3.7 %collective-permute-start = (bf16[1,2,64,512]{3,2,1,0:T(8,128)(2,1)S(1)}, bf16[1,2,64,512]{3,2,1,0:T(8,128)(2,1)S(1)}, u32[]{:S(2)}, u32[]{:S(2)}) collective-permute-start(bf16[1,2,64,512]{3,2,1,0:T(8,128)(2,1)S(1)} %copy-done), channel_id=1, source_target_pairs={{0,4},{1,5},{2,6},{3,7},{4,0},{5,1},{6,2},{7,3},{8,12},{9,13},{10,... | collective-permute-start | bytes 393224 | tf_op jit(solution)/shard_map/ppermute | solution.py:50
  12.2 4.0 %fusion.12 = bf16[4,512,128]{2,1,0:T(8,128)(2,1)S(1)} fusion(s32[4,128]{1,0:T(4,128)S(1)} %get-tuple-element.21), kind=kLoop, calls=%fused_computation.40 | loop fusion | flops 4718592 | bytes 526336 | tf_op jit(solution)/shard_map/neg | solution.py:38
  16.5 2.5 %collective-permute-done = bf16[1,2,64,512]{3,2,1,0:T(8,128)(2,1)S(1)} collective-permute-done((bf16[1,2,64,512]{3,2,1,0:T(8,128)(2,1)S(1)}, bf16[1,2,64,512]{3,2,1,0:T(8,128)(2,1)S(1)}, u32[]{:S(2)}, u32[]{:S(2)}) %collective-permute-start) | collective-permute-done | bytes 131104 | tf_op jit(solution)/shard_map/ppermute | solution.py:50
  19.0 0.8 collective-permute-start.1
  21.0 4.4 %sine_convert_fusion.1 = (bf16[4,512,128]{2,1,0:T(8,128)(2,1)S(1)}, bf16[4,512,128]{2,1,0:T(8,128)(2,1)S(1)}) fusion(s32[4,128]{1,0:T(4,128)S(1)} %get-tuple-element.21), kind=kLoop, calls=%fused_computation.21 | loop fusion | flops 4194304 | bytes 1050624 | tf_op jit(solution)/shard_map/convert_element_type | solution.py:31
  25.4 1.8 %collective-permute-done.1 = bf16[2,2,64,512]{3,2,1,0:T(8,128)(2,1)S(1)} collective-permute-done((bf16[2,2,64,512]{3,2,1,0:T(8,128)(2,1)S(1)}, bf16[2,2,64,512]{3,2,1,0:T(8,128)(2,1)S(1)}, u32[]{:S(2)}, u32[]{:S(2)}) %collective-permute-start.1) | collective-permute-done | bytes 262176 | tf_op jit(solution)/shard_map/ppermute | solution.py:50
  27.2 1.4 %collective-permute-start.2 = (bf16[4,2,64,512]{3,2,1,0:T(8,128)(2,1)S(1)}, bf16[4,2,64,512]{3,2,1,0:T(8,128)(2,1)S(1)}, u32[]{:S(2)}, u32[]{:S(2)}) collective-permute-start(bf16[4,2,64,512]{3,2,1,0:T(8,128)(2,1)S(1)} %pad_maximum_fusion.1), channel_id=1, source_target_pairs={{0,1},{1,0},{2,3},{3,2},{4,5},{5,4},{6,7},{7,6},{8,9},{9,8},{10,11... | collective-permute-start | bytes 1572872 | tf_op jit(solution)/shard_map/ppermute | solution.py:50
  28.6 0.6 add_multiply_fusion.off_ref
  29.3 1.5 %maximum_maximum_fusion.ct_ref = bf16[4,1024,256]{2,1,0:T(8,128)(2,1)} fusion(bf16[4,512,128]{2,1,0:T(8,128)(2,1)S(1)} %get-tuple-element.17, bf16[4,512,128]{2,1,0:T(8,128)(2,1)S(1)} %fusion.12, bf16[4,512,128]{2,1,0:T(8,128)(2,1)S(1)} %get-tuple-element.16), kind=kLoop, calls=%fused_computation.2 | loop fusion | flops 8388608 | bytes 3670016 | tf_op jit(solution)/shard_map/concatenate | solution.py:39
  30.8 5.7 %sine_convert_fusion = (bf16[4,128,512]{2,1,0:T(8,128)(2,1)}, bf16[4,128,512]{2,1,0:T(8,128)(2,1)}) fusion(s32[4,128]{1,0:T(4,128)S(1)} %get-tuple-element.20), kind=kLoop, calls=%fused_computation.17 | loop fusion | flops 4194304 | bytes 1050624 | tf_op jit(solution)/shard_map/convert_element_type | solution.py:31
  36.5 3.7 %collective-permute-done.2 = bf16[4,2,64,512]{3,2,1,0:T(8,128)(2,1)S(1)} collective-permute-done((bf16[4,2,64,512]{3,2,1,0:T(8,128)(2,1)S(1)}, bf16[4,2,64,512]{3,2,1,0:T(8,128)(2,1)S(1)}, u32[]{:S(2)}, u32[]{:S(2)}) %collective-permute-start.2) | collective-permute-done | bytes 524320 | tf_op jit(solution)/shard_map/ppermute | solution.py:50
  40.3 0.6 gather_fusion
  41.2 1.6 %copy.13 = f32[2,8,64,512]{3,2,1,0:T(8,128)} copy(f32[2,8,64,512]{3,2,0,1:T(8,128)S(1)} %convert_bitcast_fusion) | data formatting | bytes 4194304 | tf_op jit(solution)/shard_map/convert_element_type | solution.py:306
  42.8 14.5 %shard_map.68.rest_0_ = f32[4,8,128,128]{3,2,1,0:T(8,128)} custom-call(s32[32]{0:T(128)} %reshape.176.f_ref, s32[1]{0:T(128)} %constant.104.clone.1.ta_ref.tb_ref, s32[1]{0:T(128)} %constant.104.clone.1.ta_ref.tb_ref, s32[1]{0:T(128)} %bitcast.1.rid_ref, s32[2]{0:T(128)} %add_multiply_fusion.off_ref, bf16[1,8,2,128,512]{4,3,2,1,0:T(8,128)(2,1)} %bitcast.11.tma_ref, ...), custom_call_target="tpu_custom_call" | custom-call | flops 4831838208 | bytes 14680064 | tf_op jit(solution)/shard_map/pallas_call | solution.py:267
  57.3 13.3 %all-gather.3.cloned.1.call-done = bf16[32,2,128,512]{3,2,1,0:T(8,128)(2,1)} async-done(((bf16[8,2,128,512]{3,2,1,0:T(8,128)(2,1)}), bf16[32,2,128,512]{3,2,1,0:T(8,128)(2,1)}) %all-gather.3.cloned.1.call-update) | async-done | bytes 8388624 | tf_op jit(solution)/shard_map/all_gather | solution.py:287
  70.6 15.0 %shard_map.69 = f32[2,4,128,128]{3,2,1,0:T(8,128)} custom-call(s32[32]{0:T(128)} %reshape.176.f_ref, s32[1]{0:T(128)S(6)} %mul.65.ta_ref, s32[1]{0:T(128)S(6)} %add.152.tb_ref, s32[1]{0:T(128)S(6)} %convert_element_type.41.rid_ref, s32[2]{0:T(128)} %iota_multiply_fusion.off_ref, bf16[4,8,2,128,512]{4,3,2,1,0:T(8,128)(2,1)} %bitcast.29, ...), custom_call_target="tpu_custom_call" | custom-call | flops 4831838208 | bytes 14680064 | tf_op jit(solution)/shard_map/pallas_call | solution.py:267
  85.7 1.0 constant_dynamic-slice_fusion
  86.6 1.5 %collective-permute-start.4 = (f32[2,256,128]{2,1,0:T(8,128)S(1)}, f32[2,256,128]{2,1,0:T(8,128)S(1)}, u32[]{:S(2)}, u32[]{:S(2)}) collective-permute-start(f32[2,256,128]{2,1,0:T(8,128)S(1)} %constant_dynamic-slice_fusion), channel_id=1, source_target_pairs={{0,1},{1,0},{2,3},{3,2},{4,5},{5,4},{6,7},{7,6},{8,9},{9,8},{10,11... | collective-permute-start | bytes 786440 | tf_op jit(solution)/shard_map/ppermute | solution.py:90
  88.1 7.0 %collective-permute-done.4 = f32[2,256,128]{2,1,0:T(8,128)S(1)} collective-permute-done((f32[2,256,128]{2,1,0:T(8,128)S(1)}, f32[2,256,128]{2,1,0:T(8,128)S(1)}, u32[]{:S(2)}, u32[]{:S(2)}) %collective-permute-start.4) | collective-permute-done | bytes 262176 | tf_op jit(solution)/shard_map/ppermute | solution.py:90
  95.2 1.0 slice_add_fusion
  96.2 1.6 %collective-permute-start.5 = (f32[2,64,128]{2,1,0:T(8,128)S(1)}, f32[2,64,128]{2,1,0:T(8,128)S(1)}, u32[]{:S(2)}, u32[]{:S(2)}) collective-permute-start(f32[2,64,128]{2,1,0:T(8,128)S(1)} %get-tuple-element.9), channel_id=1, source_target_pairs={{0,2},{1,3},{2,0},{3,1},{4,6},{5,7},{6,4},{7,5},{8,10},{9,11},{10,... | collective-permute-start | bytes 196616 | tf_op jit(solution)/shard_map/ppermute | solution.py:99
  97.8 2.4 %collective-permute-start.6 = (f32[2,64,128]{2,1,0:T(8,128)S(1)}, f32[2,64,128]{2,1,0:T(8,128)S(1)}, u32[]{:S(2)}, u32[]{:S(2)}) collective-permute-start(f32[2,64,128]{2,1,0:T(8,128)S(1)} %get-tuple-element.10), channel_id=1, source_target_pairs={{0,4},{1,5},{2,6},{3,7},{4,0},{5,1},{6,2},{7,3},{8,12},{9,13},{10,... | collective-permute-start | bytes 196616 | tf_op jit(solution)/shard_map/ppermute | solution.py:99
  100.7 4.0 %collective-permute-done.6 = f32[2,64,128]{2,1,0:T(8,128)S(1)} collective-permute-done((f32[2,64,128]{2,1,0:T(8,128)S(1)}, f32[2,64,128]{2,1,0:T(8,128)S(1)}, u32[]{:S(2)}, u32[]{:S(2)}) %collective-permute-start.6) | collective-permute-done | bytes 65568 | tf_op jit(solution)/shard_map/ppermute | solution.py:99
  104.7 1.6 %collective-permute-done.7 = f32[2,64,128]{2,1,0:T(8,128)S(1)} collective-permute-done((f32[2,64,128]{2,1,0:T(8,128)S(1)}, f32[2,64,128]{2,1,0:T(8,128)S(1)}, u32[]{:S(2)}, u32[]{:S(2)}) %collective-permute-start.7) | collective-permute-done | bytes 65568 | tf_op jit(solution)/shard_map/ppermute | solution.py:99
  106.3 2.0 %collective-permute-start.9 = (f32[2,64,128]{2,1,0:T(8,128)S(1)}, f32[2,64,128]{2,1,0:T(8,128)S(1)}, u32[]{:S(2)}, u32[]{:S(2)}) collective-permute-start(f32[2,64,128]{2,1,0:T(8,128)S(1)} %get-tuple-element.13), channel_id=1, source_target_pairs={{0,4},{1,5},{2,6},{3,7},{4,0},{5,1},{6,2},{7,3},{8,12},{9,13},{10,... | collective-permute-start | bytes 196616 | tf_op jit(solution)/shard_map/ppermute | solution.py:103
  108.3 2.4 %collective-permute-start.10 = (f32[2,64,128]{2,1,0:T(8,128)S(1)}, f32[2,64,128]{2,1,0:T(8,128)S(1)}, u32[]{:S(2)}, u32[]{:S(2)}) collective-permute-start(f32[2,64,128]{2,1,0:T(8,128)S(1)} %get-tuple-element.13), channel_id=1, source_target_pairs={{0,6},{1,7},{2,4},{3,5},{4,2},{5,3},{6,0},{7,1},{8,14},{9,15},{10,... | collective-permute-start | bytes 196616 | tf_op jit(solution)/shard_map/ppermute | solution.py:103
  110.7 1.3 collective-permute-done.8
  112.0 2.4 %collective-permute-done.10 = f32[2,64,128]{2,1,0:T(8,128)S(1)} collective-permute-done((f32[2,64,128]{2,1,0:T(8,128)S(1)}, f32[2,64,128]{2,1,0:T(8,128)S(1)}, u32[]{:S(2)}, u32[]{:S(2)}) %collective-permute-start.10) | collective-permute-done | bytes 65568 | tf_op jit(solution)/shard_map/ppermute | solution.py:103
  115.0 1.6 %collective-permute-start.11 = (f32[2,256,128]{2,1,0:T(8,128)S(1)}, f32[2,256,128]{2,1,0:T(8,128)S(1)}, u32[]{:S(2)}, u32[]{:S(2)}) collective-permute-start(f32[2,256,128]{2,1,0:T(8,128)S(1)} %bitcast.36), channel_id=1, source_target_pairs={{0,1},{1,0},{2,3},{3,2},{4,5},{5,4},{6,7},{7,6},{8,9},{9,8},{10,11... | collective-permute-start | bytes 786440 | tf_op jit(solution)/shard_map/ppermute | solution.py:106
  116.6 4.9 %collective-permute-done.11 = f32[2,256,128]{2,1,0:T(8,128)S(1)} collective-permute-done((f32[2,256,128]{2,1,0:T(8,128)S(1)}, f32[2,256,128]{2,1,0:T(8,128)S(1)}, u32[]{:S(2)}, u32[]{:S(2)}) %collective-permute-start.11) | collective-permute-done | bytes 262176 | tf_op jit(solution)/shard_map/ppermute | solution.py:106
  121.5 0.8 slice_multiply_fusion
  (36 shorter events, 3.8 us)
Async XLA Ops:
  7.2 1.3 copy-start
  7.2 5.0 %copy-start.2 = (s32[1,4,2]{1,2,0:T(2,128)S(1)}, s32[1,4,2]{1,2,0:T(2,128)}, u32[]{:S(2)}) copy-start(s32[1,4,2]{1,2,0:T(2,128)} %param.7) | copy-start | bytes 100
  7.2 9.1 %copy-start.1 = (s32[1,4,48]{2,1,0:T(4,128)S(1)}, s32[1,4,48]{2,1,0:T(4,128)}, u32[]{:S(2)}) copy-start(s32[1,4,48]{2,1,0:T(4,128)} %param.8) | copy-start | bytes 2308
  7.2 63.4 %all-gather.3.cloned.1.call-start = ((), (), s32[]{:S(2)}) async-start(), calls=%async_computation | async-start | bytes 10485760 | tf_op jit(solution)/shard_map/all_gather | solution.py:287
  7.9 34.9 %collective-permute-start.3 = (bf16[8,2,128,512]{3,2,1,0:T(8,128)(2,1)}, bf16[8,2,128,512]{3,2,1,0:T(8,128)(2,1)}, u32[]{:S(2)}, u32[]{:S(2)}) collective-permute-start(bf16[8,2,128,512]{3,2,1,0:T(8,128)(2,1)} %param.6), channel_id=1, source_target_pairs={{0,8},{8,0},{16,24},{24,16},{1,9},{9,1},{17,25},{25,17},{2,10},{10... | collective-permute-start | bytes 6291464 | tf_op jit(solution)/shard_map/ppermute | solution.py:305
  8.4 10.6 %collective-permute-start = (bf16[1,2,64,512]{3,2,1,0:T(8,128)(2,1)S(1)}, bf16[1,2,64,512]{3,2,1,0:T(8,128)(2,1)S(1)}, u32[]{:S(2)}, u32[]{:S(2)}) collective-permute-start(bf16[1,2,64,512]{3,2,1,0:T(8,128)(2,1)S(1)} %copy-done), channel_id=1, source_target_pairs={{0,4},{1,5},{2,6},{3,7},{4,0},{5,1},{6,2},{7,3},{8,12},{9,13},{10,... | collective-permute-start | bytes 393224 | tf_op jit(solution)/shard_map/ppermute | solution.py:50
  19.0 8.1 %collective-permute-start.1 = (bf16[2,2,64,512]{3,2,1,0:T(8,128)(2,1)S(1)}, bf16[2,2,64,512]{3,2,1,0:T(8,128)(2,1)S(1)}, u32[]{:S(2)}, u32[]{:S(2)}) collective-permute-start(bf16[2,2,64,512]{3,2,1,0:T(8,128)(2,1)S(1)} %pad_maximum_fusion.2), channel_id=1, source_target_pairs={{0,2},{1,3},{2,0},{3,1},{4,6},{5,7},{6,4},{7,5},{8,10},{9,11},{10,... | collective-permute-start | bytes 786440 | tf_op jit(solution)/shard_map/ppermute | solution.py:50
  27.2 13.0 %collective-permute-start.2 = (bf16[4,2,64,512]{3,2,1,0:T(8,128)(2,1)S(1)}, bf16[4,2,64,512]{3,2,1,0:T(8,128)(2,1)S(1)}, u32[]{:S(2)}, u32[]{:S(2)}) collective-permute-start(bf16[4,2,64,512]{3,2,1,0:T(8,128)(2,1)S(1)} %pad_maximum_fusion.1), channel_id=1, source_target_pairs={{0,1},{1,0},{2,3},{3,2},{4,5},{5,4},{6,7},{7,6},{8,9},{9,8},{10,11... | collective-permute-start | bytes 1572872 | tf_op jit(solution)/shard_map/ppermute | solution.py:50
  86.6 8.5 %collective-permute-start.4 = (f32[2,256,128]{2,1,0:T(8,128)S(1)}, f32[2,256,128]{2,1,0:T(8,128)S(1)}, u32[]{:S(2)}, u32[]{:S(2)}) collective-permute-start(f32[2,256,128]{2,1,0:T(8,128)S(1)} %constant_dynamic-slice_fusion), channel_id=1, source_target_pairs={{0,1},{1,0},{2,3},{3,2},{4,5},{5,4},{6,7},{7,6},{8,9},{9,8},{10,11... | collective-permute-start | bytes 786440 | tf_op jit(solution)/shard_map/ppermute | solution.py:90
  96.2 4.5 %collective-permute-start.5 = (f32[2,64,128]{2,1,0:T(8,128)S(1)}, f32[2,64,128]{2,1,0:T(8,128)S(1)}, u32[]{:S(2)}, u32[]{:S(2)}) collective-permute-start(f32[2,64,128]{2,1,0:T(8,128)S(1)} %get-tuple-element.9), channel_id=1, source_target_pairs={{0,2},{1,3},{2,0},{3,1},{4,6},{5,7},{6,4},{7,5},{8,10},{9,11},{10,... | collective-permute-start | bytes 196616 | tf_op jit(solution)/shard_map/ppermute | solution.py:99
  97.8 6.9 %collective-permute-start.6 = (f32[2,64,128]{2,1,0:T(8,128)S(1)}, f32[2,64,128]{2,1,0:T(8,128)S(1)}, u32[]{:S(2)}, u32[]{:S(2)}) collective-permute-start(f32[2,64,128]{2,1,0:T(8,128)S(1)} %get-tuple-element.10), channel_id=1, source_target_pairs={{0,4},{1,5},{2,6},{3,7},{4,0},{5,1},{6,2},{7,3},{8,12},{9,13},{10,... | collective-permute-start | bytes 196616 | tf_op jit(solution)/shard_map/ppermute | solution.py:99
  100.2 6.1 %collective-permute-start.7 = (f32[2,64,128]{2,1,0:T(8,128)S(1)}, f32[2,64,128]{2,1,0:T(8,128)S(1)}, u32[]{:S(2)}, u32[]{:S(2)}) collective-permute-start(f32[2,64,128]{2,1,0:T(8,128)S(1)} %get-tuple-element.11), channel_id=1, source_target_pairs={{0,6},{1,7},{2,4},{3,5},{4,2},{5,3},{6,0},{7,1},{8,14},{9,15},{10,... | collective-permute-start | bytes 196616 | tf_op jit(solution)/shard_map/ppermute | solution.py:99
  106.3 5.7 %collective-permute-start.8 = (f32[2,64,128]{2,1,0:T(8,128)S(1)}, f32[2,64,128]{2,1,0:T(8,128)S(1)}, u32[]{:S(2)}, u32[]{:S(2)}) collective-permute-start(f32[2,64,128]{2,1,0:T(8,128)S(1)} %get-tuple-element.13), channel_id=1, source_target_pairs={{0,2},{1,3},{2,0},{3,1},{4,6},{5,7},{6,4},{7,5},{8,10},{9,11},{10,... | collective-permute-start | bytes 196616 | tf_op jit(solution)/shard_map/ppermute | solution.py:103
  106.3 5.7 %collective-permute-start.9 = (f32[2,64,128]{2,1,0:T(8,128)S(1)}, f32[2,64,128]{2,1,0:T(8,128)S(1)}, u32[]{:S(2)}, u32[]{:S(2)}) collective-permute-start(f32[2,64,128]{2,1,0:T(8,128)S(1)} %get-tuple-element.13), channel_id=1, source_target_pairs={{0,4},{1,5},{2,6},{3,7},{4,0},{5,1},{6,2},{7,3},{8,12},{9,13},{10,... | collective-permute-start | bytes 196616 | tf_op jit(solution)/shard_map/ppermute | solution.py:103
  108.3 6.1 %collective-permute-start.10 = (f32[2,64,128]{2,1,0:T(8,128)S(1)}, f32[2,64,128]{2,1,0:T(8,128)S(1)}, u32[]{:S(2)}, u32[]{:S(2)}) collective-permute-start(f32[2,64,128]{2,1,0:T(8,128)S(1)} %get-tuple-element.13), channel_id=1, source_target_pairs={{0,6},{1,7},{2,4},{3,5},{4,2},{5,3},{6,0},{7,1},{8,14},{9,15},{10,... | collective-permute-start | bytes 196616 | tf_op jit(solution)/shard_map/ppermute | solution.py:103
  115.0 6.4 %collective-permute-start.11 = (f32[2,256,128]{2,1,0:T(8,128)S(1)}, f32[2,256,128]{2,1,0:T(8,128)S(1)}, u32[]{:S(2)}, u32[]{:S(2)}) collective-permute-start(f32[2,256,128]{2,1,0:T(8,128)S(1)} %bitcast.36), channel_id=1, source_target_pairs={{0,1},{1,0},{2,3},{3,2},{4,5},{5,4},{6,7},{7,6},{8,9},{9,8},{10,11... | collective-permute-start | bytes 786440 | tf_op jit(solution)/shard_map/ppermute | solution.py:106
Sparse Core Ops, SparseCore 0:
  9.6 60.9 all-gather.2

commit v14 on v13

--- a/solution.py
+++ b/solution.py
@@ -89,6 +89,14 @@
     send = lax.dynamic_slice_in_dim(joined, (1 - bit) * half, half, axis=1)
     got = lax.ppermute(send, axis, xor_pairs(n, 1))
     cur = jnp.stack([jnp.maximum(keep[0], got[0]), keep[1] + got[1]])
+    return reduce_rest(cur, shape, axis)
+
+
+def reduce_rest(cur, shape, axis):
+    n = lax.axis_size(axis)
+    me = lax.axis_index(axis)
+    bit = me % 2
+    half = cur.shape[1]
     members = n // 2
     group = me // 2
     piece = half // members
@@ -102,7 +110,7 @@
     done = jnp.stack([best, power])
     slots = [done] + [lax.ppermute(done, axis, xor_pairs(n, 2 * m)) for m in range(1, members)]
     pieces = jnp.stack(slots)[jnp.arange(members, dtype=jnp.int32) ^ group]
-    mine = jnp.moveaxis(pieces, 0, 1).reshape(2, half, joined.shape[2])
+    mine = jnp.moveaxis(pieces, 0, 1).reshape(2, half, cur.shape[2])
     other = lax.ppermute(mine, axis, xor_pairs(n, 1))
     whole = jnp.where(bit == 1, jnp.concatenate([other, mine], axis=1), jnp.concatenate([mine, other], axis=1))
     return whole[0].reshape(shape), whole[1].reshape(shape)
@@ -167,10 +175,9 @@
     )(flags, tmpl, spec, col_table, cos_t, sin_t)
 
 
-def rows_kernel(blocks, size, width, rows_t, peaks_n, chunk, n_steps, final, per, f_ref, ta_ref, tb_ref, rid_ref, off_ref, tma_ref, tmb_ref, sp_ref, ct_ref, cr_ref, sr_ref, *rest):
+def rows_kernel(blocks, size, width, rows_t, peaks_n, chunk, n_steps, final, per, f_ref, ta_ref, tb_ref, rid_ref, off_ref, pos_ref, tma_ref, tmb_ref, sp_ref, ct_ref, cr_ref, sr_ref, *rest):
     if final:
         init_ref, out_ref, acc_ref, m_ref = rest
-        best_ref, pow_ref = out_ref.at[0], out_ref.at[1]
     else:
         part_ref, acc_ref, m_ref = rest
     jj = pl.program_id(0)
@@ -180,8 +187,8 @@
     if final:
         @pl.when((jj == 0) & (i == 0))
         def _():
-            best_ref[...] = jnp.full(best_ref.shape, lowest_score, jnp.float32)
-            pow_ref[...] = jnp.zeros(pow_ref.shape, jnp.float32)
+            out_ref[:, 0] = jnp.full((peaks_n, width, width), lowest_score, jnp.float32)
+            out_ref[:, 1] = jnp.zeros((peaks_n, width, width), jnp.float32)
 
         @pl.when(i == 0)
         def _():
@@ -229,13 +236,14 @@
                     @pl.when(f_ref[p * blocks + per * jj + o] > 0)
                     def _():
                         score = acc_ref[p, o] / size
-                        best_ref[p] = jnp.maximum(best_ref[p], score)
-                        pow_ref[p] = pow_ref[p] + score * score
+                        q = pos_ref[p]
+                        out_ref[q, 0] = jnp.maximum(out_ref[q, 0], score)
+                        out_ref[q, 1] = out_ref[q, 1] + score * score
         else:
             part_ref[...] = acc_ref[...]
 
 
-def match_rows(flags, tas, tbs, rids, offs, tmpl_a, tmpl_b, spec, col_table, cos_t, sin_t, init=None):
+def match_rows(flags, tas, tbs, rids, offs, pos, tmpl_a, tmpl_b, spec, col_table, cos_t, sin_t, init=None):
     _, blocks, _, rows_t, size = tmpl_a.shape
     peaks_n, width = cos_t.shape[0], cos_t.shape[1]
     n_steps = tas.shape[0]
@@ -247,27 +255,27 @@
     flops = blocks * peaks_n * n_steps * (2 * span * 2 * size * 2 * width + 2 * 2 * width * span * width)
     cost = pl.CostEstimate(flops=flops, transcendentals=0, bytes_accessed=n_steps * blocks * 2 * span * size * 6 + col_table.size * 2)
     in_specs = [
-        pl.BlockSpec((1, per, 2, rows_t, size), lambda j, i, f, ta, tb, r, o: (ta[i], j, 0, 0, 0)),
-        pl.BlockSpec((1, per, 2, rows_t, size), lambda j, i, f, ta, tb, r, o: (tb[i], j, 0, 0, 0)),
-        pl.BlockSpec((2, span, size), lambda j, i, f, ta, tb, r, o: (0, r[i], 0)),
-        pl.BlockSpec(col_table.shape, lambda j, i, f, ta, tb, r, o: (0, 0, 0)),
-        pl.BlockSpec((peaks_n, width, span), lambda j, i, f, ta, tb, r, o: (0, 0, r[i])),
-        pl.BlockSpec((peaks_n, width, span), lambda j, i, f, ta, tb, r, o: (0, 0, r[i])),
+        pl.BlockSpec((1, per, 2, rows_t, size), lambda j, i, f, ta, tb, r, o, q: (ta[i], j, 0, 0, 0)),
+        pl.BlockSpec((1, per, 2, rows_t, size), lambda j, i, f, ta, tb, r, o, q: (tb[i], j, 0, 0, 0)),
+        pl.BlockSpec((2, span, size), lambda j, i, f, ta, tb, r, o, q: (0, r[i], 0)),
+        pl.BlockSpec(col_table.shape, lambda j, i, f, ta, tb, r, o, q: (0, 0, 0)),
+        pl.BlockSpec((peaks_n, width, span), lambda j, i, f, ta, tb, r, o, q: (0, 0, r[i])),
+        pl.BlockSpec((peaks_n, width, span), lambda j, i, f, ta, tb, r, o, q: (0, 0, r[i])),
     ]
-    args = [flags, tas, tbs, rids, offs, tmpl_a, tmpl_b, spec, col_table, cos_t, sin_t]
-    part_spec = pl.BlockSpec((peaks_n, per, width, width), lambda j, i, f, ta, tb, r, o: (0, j, 0, 0))
+    args = [flags, tas, tbs, rids, offs, pos, tmpl_a, tmpl_b, spec, col_table, cos_t, sin_t]
+    part_spec = pl.BlockSpec((peaks_n, per, width, width), lambda j, i, f, ta, tb, r, o, q: (0, j, 0, 0))
     if final:
         in_specs.append(part_spec)
         args.append(init)
-        out_shape = jax.ShapeDtypeStruct((2, peaks_n, width, width), jnp.float32)
-        out_specs = pl.BlockSpec((2, peaks_n, width, width), lambda j, i, f, ta, tb, r, o: (0, 0, 0, 0))
+        out_shape = jax.ShapeDtypeStruct((peaks_n, 2, width, width), jnp.float32)
+        out_specs = pl.BlockSpec((peaks_n, 2, width, width), lambda j, i, f, ta, tb, r, o, q: (0, 0, 0, 0))
     else:
         out_shape = jax.ShapeDtypeStruct((peaks_n, blocks, width, width), jnp.float32)
         out_specs = part_spec
     return pl.pallas_call(
         kernel,
         grid_spec=pltpu.PrefetchScalarGridSpec(
-            num_scalar_prefetch=5,
+            num_scalar_prefetch=6,
             grid=(blocks // per, n_steps),
             in_specs=in_specs,
             out_specs=out_specs,
@@ -309,14 +317,32 @@
         zero = jnp.zeros((1,), jnp.int32)
         near_offs = jnp.stack([odd, 1 - odd]) * rows_t
         own, sib = template_spectra[None], sibling[None]
-        partial = match_rows(flags, zero, zero, chip[None].astype(jnp.int32), near_offs, own, sib, spec32, col_table, cos_t, sin_t)
+        peaks_n = best_shape[0]
+        if peaks_n % 2 == 0:
+            pos = jnp.arange(peaks_n, dtype=jnp.int32) ^ ((1 - odd_orient()) * (peaks_n // 2))
+        else:
+            pos = jnp.arange(peaks_n, dtype=jnp.int32)
+        partial = match_rows(flags, zero, zero, chip[None].astype(jnp.int32), near_offs, pos, own, sib, spec32, col_table, cos_t, sin_t)
         far = far_chips(chip, tiles // 2)
         far_offs = jnp.array([0, rows_t], jnp.int32)
-        joined = match_rows(flags, far * 2, far * 2 + 1, far, far_offs, tmpl, tmpl, spec32, col_table, cos_t, sin_t, init=partial)
-        best_all, power_all = reduce_joined(joined.reshape(2, -1, width), best_shape, "orient")
+        placed = match_rows(flags, far * 2, far * 2 + 1, far, far_offs, pos, tmpl, tmpl, spec32, col_table, cos_t, sin_t, init=partial)
+        n = lax.axis_size("orient")
+        if peaks_n % 2 == 0 and is_pow2(n) and n >= 2 and (peaks_n * width) % n == 0:
+            half_peaks = peaks_n // 2
+            send, keep = placed[:half_peaks], placed[half_peaks:]
+            got = lax.ppermute(send, "orient", xor_pairs(n, 1))
+            cur = jnp.stack([jnp.maximum(keep[:, 0], got[:, 0]), keep[:, 1] + got[:, 1]])
+            best_all, power_all = reduce_rest(cur.reshape(2, half_peaks * width, width), best_shape, "orient")
+        else:
+            joined = jnp.moveaxis(placed, 1, 0).reshape(2, -1, width)
+            best_all, power_all = reduce_joined(joined, best_shape, "orient")
         return (best_all[None], (power_all / LIST)[None])
     best_all, power_all = reduce_orient(best_part, power_part, "orient")
     return (best_all[None], (power_all / LIST)[None])
+
+
+def odd_orient():
+    return (lax.axis_index("orient") % 2).astype(jnp.int32)
 
 
 def far_chips(chip, chips):

time: 129 us -> 129 us (level)
  transfers between devices with their start and end apart: 13 -> 13, of which waited for: 10 -> 12; matrix products, arithmetic and copies ran while one was open for 16% -> 16% of each run, Pallas kernels for 11% -> 11%
where the time goes in v14:
time: 129 us
  waiting for transfers between devices  42.6 us (33%)
  Pallas kernels  29.6 us (23%)
  other arithmetic  20.1 us (16%)
  starting transfers between devices  18.4 us (14%)
  between operations  14.2 us (11%)
  local copies, waits for them, and re-layouts  4.37 us (3%)
    pallas_call x2, Pallas kernels, match_rows(): pl.pallas_call(kernel, grid_spec=pltpu.PrefetchScalarGridSpec(num_scalar_...  29.6 us
    all_gather x1, waiting for transfers between devices, local(): tmpl = lax.all_gather(template_spectra, 'tile', axis=0)  13.3 us
    convert_element_type x2, other arithmetic, angle_tables(): jnp.sin(angle).astype(jnp.bfloat16)  10.1 us
    ppermute x3, waiting for transfers between devices, gather_rows(): got = lax.ppermute(blocks, axis, xor_pairs(n, k))  7.4 us
    ppermute x1, waiting for transfers between devices, local(): got = lax.ppermute(send, 'orient', xor_pairs(n, 1))  6.99 us
    ppermute x3, starting transfers between devices, gather_rows(): got = lax.ppermute(blocks, axis, xor_pairs(n, k))  5.92 us
    ppermute x3, waiting for transfers between devices, reduce_rest(): got = lax.ppermute(out, axis, xor_pairs(n, 2 * m))  5.59 us
    ppermute x1, waiting for transfers between devices, reduce_rest(): other = lax.ppermute(mine, axis, xor_pairs(n, 1))  4.95 us
  transfers between devices with their start and end apart: 13, of which 12 were waited for; matrix products, arithmetic and copies ran while one was open for 16% of the time, Pallas kernels for 11%

profile of v14, /device:TPU:0, one launch (start us, length us, event | category | flops | bytes accessed | tf_op | source)
XLA Modules:
  0.0 129.3 jit_solution(1432656653885567947)
XLA Ops:
  7.2 0.7 all-gather.3.cloned.1.call-update
  8.4 3.7 %collective-permute-start = (bf16[1,2,64,512]{3,2,1,0:T(8,128)(2,1)S(1)}, bf16[1,2,64,512]{3,2,1,0:T(8,128)(2,1)S(1)}, u32[]{:S(2)}, u32[]{:S(2)}) collective-permute-start(bf16[1,2,64,512]{3,2,1,0:T(8,128)(2,1)S(1)} %copy-done), channel_id=1, source_target_pairs={{0,4},{1,5},{2,6},{3,7},{4,0},{5,1},{6,2},{7,3},{8,12},{9,13},{10,... | collective-permute-start | bytes 393224 | tf_op jit(solution)/shard_map/ppermute | solution.py:50
  12.8 4.0 %fusion.12 = bf16[4,512,128]{2,1,0:T(8,128)(2,1)S(1)} fusion(s32[4,128]{1,0:T(4,128)S(1)} %get-tuple-element.21), kind=kLoop, calls=%fused_computation.40 | loop fusion | flops 4718592 | bytes 526336 | tf_op jit(solution)/shard_map/neg | solution.py:38
  17.1 2.0 %collective-permute-done = bf16[1,2,64,512]{3,2,1,0:T(8,128)(2,1)S(1)} collective-permute-done((bf16[1,2,64,512]{3,2,1,0:T(8,128)(2,1)S(1)}, bf16[1,2,64,512]{3,2,1,0:T(8,128)(2,1)S(1)}, u32[]{:S(2)}, u32[]{:S(2)}) %collective-permute-start) | collective-permute-done | bytes 131104 | tf_op jit(solution)/shard_map/ppermute | solution.py:50
  19.0 0.8 collective-permute-start.1
  21.0 4.4 %sine_convert_fusion.1 = (bf16[4,512,128]{2,1,0:T(8,128)(2,1)S(1)}, bf16[4,512,128]{2,1,0:T(8,128)(2,1)S(1)}) fusion(s32[4,128]{1,0:T(4,128)S(1)} %get-tuple-element.21), kind=kLoop, calls=%fused_computation.21 | loop fusion | flops 4194304 | bytes 1050624 | tf_op jit(solution)/shard_map/convert_element_type | solution.py:31
  25.4 1.7 %collective-permute-done.1 = bf16[2,2,64,512]{3,2,1,0:T(8,128)(2,1)S(1)} collective-permute-done((bf16[2,2,64,512]{3,2,1,0:T(8,128)(2,1)S(1)}, bf16[2,2,64,512]{3,2,1,0:T(8,128)(2,1)S(1)}, u32[]{:S(2)}, u32[]{:S(2)}) %collective-permute-start.1) | collective-permute-done | bytes 262176 | tf_op jit(solution)/shard_map/ppermute | solution.py:50
  27.2 1.4 %collective-permute-start.2 = (bf16[4,2,64,512]{3,2,1,0:T(8,128)(2,1)S(1)}, bf16[4,2,64,512]{3,2,1,0:T(8,128)(2,1)S(1)}, u32[]{:S(2)}, u32[]{:S(2)}) collective-permute-start(bf16[4,2,64,512]{3,2,1,0:T(8,128)(2,1)S(1)} %pad_maximum_fusion.1), channel_id=1, source_target_pairs={{0,1},{1,0},{2,3},{3,2},{4,5},{5,4},{6,7},{7,6},{8,9},{9,8},{10,11... | collective-permute-start | bytes 1572872 | tf_op jit(solution)/shard_map/ppermute | solution.py:50
  28.6 0.6 add_multiply_fusion.off_ref
  29.2 1.5 %maximum_maximum_fusion.ct_ref = bf16[4,1024,256]{2,1,0:T(8,128)(2,1)} fusion(bf16[4,512,128]{2,1,0:T(8,128)(2,1)S(1)} %get-tuple-element.17, bf16[4,512,128]{2,1,0:T(8,128)(2,1)S(1)} %fusion.12, bf16[4,512,128]{2,1,0:T(8,128)(2,1)S(1)} %get-tuple-element.16), kind=kLoop, calls=%fused_computation.2 | loop fusion | flops 8388608 | bytes 3670016 | tf_op jit(solution)/shard_map/concatenate | solution.py:39
  30.8 5.7 %sine_convert_fusion = (bf16[4,128,512]{2,1,0:T(8,128)(2,1)}, bf16[4,128,512]{2,1,0:T(8,128)(2,1)}) fusion(s32[4,128]{1,0:T(4,128)S(1)} %get-tuple-element.20), kind=kLoop, calls=%fused_computation.17 | loop fusion | flops 4194304 | bytes 1050624 | tf_op jit(solution)/shard_map/convert_element_type | solution.py:31
  36.5 3.7 %collective-permute-done.2 = bf16[4,2,64,512]{3,2,1,0:T(8,128)(2,1)S(1)} collective-permute-done((bf16[4,2,64,512]{3,2,1,0:T(8,128)(2,1)S(1)}, bf16[4,2,64,512]{3,2,1,0:T(8,128)(2,1)S(1)}, u32[]{:S(2)}, u32[]{:S(2)}) %collective-permute-start.2) | collective-permute-done | bytes 524320 | tf_op jit(solution)/shard_map/ppermute | solution.py:50
  40.3 0.6 gather_fusion
  41.2 1.6 %copy.13 = f32[2,8,64,512]{3,2,1,0:T(8,128)} copy(f32[2,8,64,512]{3,2,0,1:T(8,128)S(1)} %convert_bitcast_fusion) | data formatting | bytes 4194304 | tf_op jit(solution)/shard_map/convert_element_type | solution.py:314
  42.8 14.5 %shard_map.68.rest_0_ = f32[4,8,128,128]{3,2,1,0:T(8,128)} custom-call(s32[32]{0:T(128)} %reshape.215.f_ref, s32[1]{0:T(128)} %constant.106.clone.1.ta_ref.tb_ref, s32[1]{0:T(128)} %constant.106.clone.1.ta_ref.tb_ref, s32[1]{0:T(128)} %bitcast.1.rid_ref, s32[2]{0:T(128)} %add_multiply_fusion.off_ref, s32[4]{0:T(128)} %iota_xor_fusion.pos_ref, ...), custom_call_target="tpu_custom_call" | custom-call | flops 4831838208 | bytes 14680064 | tf_op jit(solution)/shard_map/pallas_call | solution.py:275
  57.3 13.3 %all-gather.3.cloned.1.call-done = bf16[32,2,128,512]{3,2,1,0:T(8,128)(2,1)} async-done(((bf16[8,2,128,512]{3,2,1,0:T(8,128)(2,1)}), bf16[32,2,128,512]{3,2,1,0:T(8,128)(2,1)}) %all-gather.3.cloned.1.call-update) | async-done | bytes 8388624 | tf_op jit(solution)/shard_map/all_gather | solution.py:295
  70.6 15.1 %shard_map.69 = f32[4,2,128,128]{3,2,1,0:T(8,128)} custom-call(s32[32]{0:T(128)} %reshape.215.f_ref, s32[1]{0:T(128)S(6)} %mul.62.ta_ref, s32[1]{0:T(128)S(6)} %add.157.tb_ref, s32[1]{0:T(128)S(6)} %convert_element_type.41.rid_ref, s32[2]{0:T(128)} %iota_multiply_fusion.off_ref, s32[4]{0:T(128)} %iota_xor_fusion.pos_ref, ...), custom_call_target="tpu_custom_call" | custom-call | flops 4831838208 | bytes 14680064 | tf_op jit(solution)/shard_map/pallas_call | solution.py:275
  85.7 1.0 slice.76
  86.7 1.5 %collective-permute-start.4 = (f32[2,2,128,128]{3,2,1,0:T(8,128)S(1)}, f32[2,2,128,128]{3,2,1,0:T(8,128)S(1)}, u32[]{:S(2)}, u32[]{:S(2)}) collective-permute-start(f32[2,2,128,128]{3,2,1,0:T(8,128)S(1)} %slice.76), channel_id=1, source_target_pairs={{0,1},{1,0},{2,3},{3,2},{4,5},{5,4},{6,7},{7,6},{8,9},{9,8},{10,11... | collective-permute-start | bytes 786440 | tf_op jit(solution)/shard_map/ppermute | solution.py:333
  88.2 7.0 %collective-permute-done.4 = f32[2,2,128,128]{3,2,1,0:T(8,128)S(1)} collective-permute-done((f32[2,2,128,128]{3,2,1,0:T(8,128)S(1)}, f32[2,2,128,128]{3,2,1,0:T(8,128)S(1)}, u32[]{:S(2)}, u32[]{:S(2)}) %collective-permute-start.4) | collective-permute-done | bytes 262176 | tf_op jit(solution)/shard_map/ppermute | solution.py:333
  95.2 1.0 slice_add_fusion
  96.3 1.6 %collective-permute-start.5 = (f32[2,64,128]{2,1,0:T(8,128)S(1)}, f32[2,64,128]{2,1,0:T(8,128)S(1)}, u32[]{:S(2)}, u32[]{:S(2)}) collective-permute-start(f32[2,64,128]{2,1,0:T(8,128)S(1)} %get-tuple-element.9), channel_id=1, source_target_pairs={{0,2},{1,3},{2,0},{3,1},{4,6},{5,7},{6,4},{7,5},{8,10},{9,11},{10,... | collective-permute-start | bytes 196616 | tf_op jit(solution)/shard_map/ppermute | solution.py:107
  97.8 2.4 %collective-permute-start.6 = (f32[2,64,128]{2,1,0:T(8,128)S(1)}, f32[2,64,128]{2,1,0:T(8,128)S(1)}, u32[]{:S(2)}, u32[]{:S(2)}) collective-permute-start(f32[2,64,128]{2,1,0:T(8,128)S(1)} %get-tuple-element.10), channel_id=1, source_target_pairs={{0,4},{1,5},{2,6},{3,7},{4,0},{5,1},{6,2},{7,3},{8,12},{9,13},{10,... | collective-permute-start | bytes 196616 | tf_op jit(solution)/shard_map/ppermute | solution.py:107
  101.1 3.5 %collective-permute-done.6 = f32[2,64,128]{2,1,0:T(8,128)S(1)} collective-permute-done((f32[2,64,128]{2,1,0:T(8,128)S(1)}, f32[2,64,128]{2,1,0:T(8,128)S(1)}, u32[]{:S(2)}, u32[]{:S(2)}) %collective-permute-start.6) | collective-permute-done | bytes 65568 | tf_op jit(solution)/shard_map/ppermute | solution.py:107
  104.7 1.6 %collective-permute-done.7 = f32[2,64,128]{2,1,0:T(8,128)S(1)} collective-permute-done((f32[2,64,128]{2,1,0:T(8,128)S(1)}, f32[2,64,128]{2,1,0:T(8,128)S(1)}, u32[]{:S(2)}, u32[]{:S(2)}) %collective-permute-start.7) | collective-permute-done | bytes 65568 | tf_op jit(solution)/shard_map/ppermute | solution.py:107
  106.4 2.0 %collective-permute-start.9 = (f32[2,64,128]{2,1,0:T(8,128)S(1)}, f32[2,64,128]{2,1,0:T(8,128)S(1)}, u32[]{:S(2)}, u32[]{:S(2)}) collective-permute-start(f32[2,64,128]{2,1,0:T(8,128)S(1)} %get-tuple-element.13), channel_id=1, source_target_pairs={{0,4},{1,5},{2,6},{3,7},{4,0},{5,1},{6,2},{7,3},{8,12},{9,13},{10,... | collective-permute-start | bytes 196616 | tf_op jit(solution)/shard_map/ppermute | solution.py:111
  108.4 2.4 %collective-permute-start.10 = (f32[2,64,128]{2,1,0:T(8,128)S(1)}, f32[2,64,128]{2,1,0:T(8,128)S(1)}, u32[]{:S(2)}, u32[]{:S(2)}) collective-permute-start(f32[2,64,128]{2,1,0:T(8,128)S(1)} %get-tuple-element.13), channel_id=1, source_target_pairs={{0,6},{1,7},{2,4},{3,5},{4,2},{5,3},{6,0},{7,1},{8,14},{9,15},{10,... | collective-permute-start | bytes 196616 | tf_op jit(solution)/shard_map/ppermute | solution.py:111
  110.9 1.2 collective-permute-done.9
  112.1 2.4 %collective-permute-done.10 = f32[2,64,128]{2,1,0:T(8,128)S(1)} collective-permute-done((f32[2,64,128]{2,1,0:T(8,128)S(1)}, f32[2,64,128]{2,1,0:T(8,128)S(1)}, u32[]{:S(2)}, u32[]{:S(2)}) %collective-permute-start.10) | collective-permute-done | bytes 65568 | tf_op jit(solution)/shard_map/ppermute | solution.py:111
  115.1 1.5 %collective-permute-start.11 = (f32[2,256,128]{2,1,0:T(8,128)S(1)}, f32[2,256,128]{2,1,0:T(8,128)S(1)}, u32[]{:S(2)}, u32[]{:S(2)}) collective-permute-start(f32[2,256,128]{2,1,0:T(8,128)S(1)} %bitcast.35), channel_id=1, source_target_pairs={{0,1},{1,0},{2,3},{3,2},{4,5},{5,4},{6,7},{7,6},{8,9},{9,8},{10,11... | collective-permute-start | bytes 786440 | tf_op jit(solution)/shard_map/ppermute | solution.py:114
  116.6 4.9 %collective-permute-done.11 = f32[2,256,128]{2,1,0:T(8,128)S(1)} collective-permute-done((f32[2,256,128]{2,1,0:T(8,128)S(1)}, f32[2,256,128]{2,1,0:T(8,128)S(1)}, u32[]{:S(2)}, u32[]{:S(2)}) %collective-permute-start.11) | collective-permute-done | bytes 262176 | tf_op jit(solution)/shard_map/ppermute | solution.py:114
  121.6 0.8 slice_multiply_fusion
  (37 shorter events, 4.8 us)
Async XLA Ops:
  7.2 1.3 copy-start
  7.2 5.0 %copy-start.2 = (s32[1,4,2]{1,2,0:T(2,128)S(1)}, s32[1,4,2]{1,2,0:T(2,128)}, u32[]{:S(2)}) copy-start(s32[1,4,2]{1,2,0:T(2,128)} %param.7) | copy-start | bytes 100
  7.2 9.6 %copy-start.1 = (s32[1,4,48]{2,1,0:T(4,128)S(1)}, s32[1,4,48]{2,1,0:T(4,128)}, u32[]{:S(2)}) copy-start(s32[1,4,48]{2,1,0:T(4,128)} %param.8) | copy-start | bytes 2308
  7.2 63.4 %all-gather.3.cloned.1.call-start = ((), (), s32[]{:S(2)}) async-start(), calls=%async_computation | async-start | bytes 10485760 | tf_op jit(solution)/shard_map/all_gather | solution.py:295
  7.9 34.9 %collective-permute-start.3 = (bf16[8,2,128,512]{3,2,1,0:T(8,128)(2,1)}, bf16[8,2,128,512]{3,2,1,0:T(8,128)(2,1)}, u32[]{:S(2)}, u32[]{:S(2)}) collective-permute-start(bf16[8,2,128,512]{3,2,1,0:T(8,128)(2,1)} %param.6), channel_id=1, source_target_pairs={{0,8},{8,0},{16,24},{24,16},{1,9},{9,1},{17,25},{25,17},{2,10},{10... | collective-permute-start | bytes 6291464 | tf_op jit(solution)/shard_map/ppermute | solution.py:313
  8.4 10.6 %collective-permute-start = (bf16[1,2,64,512]{3,2,1,0:T(8,128)(2,1)S(1)}, bf16[1,2,64,512]{3,2,1,0:T(8,128)(2,1)S(1)}, u32[]{:S(2)}, u32[]{:S(2)}) collective-permute-start(bf16[1,2,64,512]{3,2,1,0:T(8,128)(2,1)S(1)} %copy-done), channel_id=1, source_target_pairs={{0,4},{1,5},{2,6},{3,7},{4,0},{5,1},{6,2},{7,3},{8,12},{9,13},{10,... | collective-permute-start | bytes 393224 | tf_op jit(solution)/shard_map/ppermute | solution.py:50
  19.0 8.1 %collective-permute-start.1 = (bf16[2,2,64,512]{3,2,1,0:T(8,128)(2,1)S(1)}, bf16[2,2,64,512]{3,2,1,0:T(8,128)(2,1)S(1)}, u32[]{:S(2)}, u32[]{:S(2)}) collective-permute-start(bf16[2,2,64,512]{3,2,1,0:T(8,128)(2,1)S(1)} %pad_maximum_fusion.2), channel_id=1, source_target_pairs={{0,2},{1,3},{2,0},{3,1},{4,6},{5,7},{6,4},{7,5},{8,10},{9,11},{10,... | collective-permute-start | bytes 786440 | tf_op jit(solution)/shard_map/ppermute | solution.py:50
  27.2 13.0 %collective-permute-start.2 = (bf16[4,2,64,512]{3,2,1,0:T(8,128)(2,1)S(1)}, bf16[4,2,64,512]{3,2,1,0:T(8,128)(2,1)S(1)}, u32[]{:S(2)}, u32[]{:S(2)}) collective-permute-start(bf16[4,2,64,512]{3,2,1,0:T(8,128)(2,1)S(1)} %pad_maximum_fusion.1), channel_id=1, source_target_pairs={{0,1},{1,0},{2,3},{3,2},{4,5},{5,4},{6,7},{7,6},{8,9},{9,8},{10,11... | collective-permute-start | bytes 1572872 | tf_op jit(solution)/shard_map/ppermute | solution.py:50
  86.7 8.5 %collective-permute-start.4 = (f32[2,2,128,128]{3,2,1,0:T(8,128)S(1)}, f32[2,2,128,128]{3,2,1,0:T(8,128)S(1)}, u32[]{:S(2)}, u32[]{:S(2)}) collective-permute-start(f32[2,2,128,128]{3,2,1,0:T(8,128)S(1)} %slice.76), channel_id=1, source_target_pairs={{0,1},{1,0},{2,3},{3,2},{4,5},{5,4},{6,7},{7,6},{8,9},{9,8},{10,11... | collective-permute-start | bytes 786440 | tf_op jit(solution)/shard_map/ppermute | solution.py:333
  96.3 4.9 %collective-permute-start.5 = (f32[2,64,128]{2,1,0:T(8,128)S(1)}, f32[2,64,128]{2,1,0:T(8,128)S(1)}, u32[]{:S(2)}, u32[]{:S(2)}) collective-permute-start(f32[2,64,128]{2,1,0:T(8,128)S(1)} %get-tuple-element.9), channel_id=1, source_target_pairs={{0,2},{1,3},{2,0},{3,1},{4,6},{5,7},{6,4},{7,5},{8,10},{9,11},{10,... | collective-permute-start | bytes 196616 | tf_op jit(solution)/shard_map/ppermute | solution.py:107
  97.8 6.9 %collective-permute-start.6 = (f32[2,64,128]{2,1,0:T(8,128)S(1)}, f32[2,64,128]{2,1,0:T(8,128)S(1)}, u32[]{:S(2)}, u32[]{:S(2)}) collective-permute-start(f32[2,64,128]{2,1,0:T(8,128)S(1)} %get-tuple-element.10), channel_id=1, source_target_pairs={{0,4},{1,5},{2,6},{3,7},{4,0},{5,1},{6,2},{7,3},{8,12},{9,13},{10,... | collective-permute-start | bytes 196616 | tf_op jit(solution)/shard_map/ppermute | solution.py:107
  100.2 6.1 %collective-permute-start.7 = (f32[2,64,128]{2,1,0:T(8,128)S(1)}, f32[2,64,128]{2,1,0:T(8,128)S(1)}, u32[]{:S(2)}, u32[]{:S(2)}) collective-permute-start(f32[2,64,128]{2,1,0:T(8,128)S(1)} %get-tuple-element.11), channel_id=1, source_target_pairs={{0,6},{1,7},{2,4},{3,5},{4,2},{5,3},{6,0},{7,1},{8,14},{9,15},{10,... | collective-permute-start | bytes 196616 | tf_op jit(solution)/shard_map/ppermute | solution.py:107
  106.3 4.6 %collective-permute-start.8 = (f32[2,64,128]{2,1,0:T(8,128)S(1)}, f32[2,64,128]{2,1,0:T(8,128)S(1)}, u32[]{:S(2)}, u32[]{:S(2)}) collective-permute-start(f32[2,64,128]{2,1,0:T(8,128)S(1)} %get-tuple-element.13), channel_id=1, source_target_pairs={{0,2},{1,3},{2,0},{3,1},{4,6},{5,7},{6,4},{7,5},{8,10},{9,11},{10,... | collective-permute-start | bytes 196616 | tf_op jit(solution)/shard_map/ppermute | solution.py:111
  106.4 5.7 %collective-permute-start.9 = (f32[2,64,128]{2,1,0:T(8,128)S(1)}, f32[2,64,128]{2,1,0:T(8,128)S(1)}, u32[]{:S(2)}, u32[]{:S(2)}) collective-permute-start(f32[2,64,128]{2,1,0:T(8,128)S(1)} %get-tuple-element.13), channel_id=1, source_target_pairs={{0,4},{1,5},{2,6},{3,7},{4,0},{5,1},{6,2},{7,3},{8,12},{9,13},{10,... | collective-permute-start | bytes 196616 | tf_op jit(solution)/shard_map/ppermute | solution.py:111
  108.4 6.1 %collective-permute-start.10 = (f32[2,64,128]{2,1,0:T(8,128)S(1)}, f32[2,64,128]{2,1,0:T(8,128)S(1)}, u32[]{:S(2)}, u32[]{:S(2)}) collective-permute-start(f32[2,64,128]{2,1,0:T(8,128)S(1)} %get-tuple-element.13), channel_id=1, source_target_pairs={{0,6},{1,7},{2,4},{3,5},{4,2},{5,3},{6,0},{7,1},{8,14},{9,15},{10,... | collective-permute-start | bytes 196616 | tf_op jit(solution)/shard_map/ppermute | solution.py:111
  115.1 6.4 %collective-permute-start.11 = (f32[2,256,128]{2,1,0:T(8,128)S(1)}, f32[2,256,128]{2,1,0:T(8,128)S(1)}, u32[]{:S(2)}, u32[]{:S(2)}) collective-permute-start(f32[2,256,128]{2,1,0:T(8,128)S(1)} %bitcast.35), channel_id=1, source_target_pairs={{0,1},{1,0},{2,3},{3,2},{4,5},{5,4},{6,7},{7,6},{8,9},{9,8},{10,11... | collective-permute-start | bytes 786440 | tf_op jit(solution)/shard_map/ppermute | solution.py:114
Sparse Core Ops, SparseCore 0:
  9.6 60.9 all-gather.2

commit v15 on v13

--- a/solution.py
+++ b/solution.py
@@ -197,8 +197,8 @@
                 row = pl.multiple_of(c * chunk, chunk)
                 in_row = pl.multiple_of(off_ref[u] + c * chunk, chunk)
                 out_row = pl.multiple_of(o * span + off_ref[u] + c * chunk, chunk)
-                image_re = sp_ref[0, pl.ds(in_row, chunk), :]
-                image_im = sp_ref[1, pl.ds(in_row, chunk), :]
+                image_re = sp_ref[0, pl.ds(in_row, chunk), :].astype(jnp.float32)
+                image_im = sp_ref[1, pl.ds(in_row, chunk), :].astype(jnp.float32)
                 tmpl_re = tm_ref[0, o, 0, pl.ds(row, chunk), :].astype(jnp.float32)
                 tmpl_im = tm_ref[0, o, 1, pl.ds(row, chunk), :].astype(jnp.float32)
                 m_ref[pl.ds(out_row, chunk), pl.ds(0, size)] = (image_re * tmpl_re + image_im * tmpl_im).astype(jnp.bfloat16)
@@ -245,7 +245,7 @@
     per = 4 if blocks % 4 == 0 else 2
     kernel = functools.partial(rows_kernel, blocks, size, width, rows_t, peaks_n, chunk, n_steps, final, per)
     flops = blocks * peaks_n * n_steps * (2 * span * 2 * size * 2 * width + 2 * 2 * width * span * width)
-    cost = pl.CostEstimate(flops=flops, transcendentals=0, bytes_accessed=n_steps * blocks * 2 * span * size * 6 + col_table.size * 2)
+    cost = pl.CostEstimate(flops=flops, transcendentals=0, bytes_accessed=n_steps * blocks * 2 * span * size * 4 + col_table.size * 2)
     in_specs = [
         pl.BlockSpec((1, per, 2, rows_t, size), lambda j, i, f, ta, tb, r, o: (ta[i], j, 0, 0, 0)),
         pl.BlockSpec((1, per, 2, rows_t, size), lambda j, i, f, ta, tb, r, o: (tb[i], j, 0, 0, 0)),
@@ -303,16 +303,15 @@
     else:
         me = lax.axis_index("tile")
         sibling = lax.ppermute(template_spectra, "tile", xor_pairs(tiles, 1))
-        spec32 = spec.astype(jnp.float32)
         chip = me // 2
         odd = (me % 2).astype(jnp.int32)
         zero = jnp.zeros((1,), jnp.int32)
         near_offs = jnp.stack([odd, 1 - odd]) * rows_t
         own, sib = template_spectra[None], sibling[None]
-        partial = match_rows(flags, zero, zero, chip[None].astype(jnp.int32), near_offs, own, sib, spec32, col_table, cos_t, sin_t)
+        partial = match_rows(flags, zero, zero, chip[None].astype(jnp.int32), near_offs, own, sib, spec, col_table, cos_t, sin_t)
         far = far_chips(chip, tiles // 2)
         far_offs = jnp.array([0, rows_t], jnp.int32)
-        joined = match_rows(flags, far * 2, far * 2 + 1, far, far_offs, tmpl, tmpl, spec32, col_table, cos_t, sin_t, init=partial)
+        joined = match_rows(flags, far * 2, far * 2 + 1, far, far_offs, tmpl, tmpl, spec, col_table, cos_t, sin_t, init=partial)
         best_all, power_all = reduce_joined(joined.reshape(2, -1, width), best_shape, "orient")
         return (best_all[None], (power_all / LIST)[None])
     best_all, power_all = reduce_orient(best_part, power_part, "orient")

time: 129 us -> 130 us (level)
    convert_element_type x1 -> x0, local copies, waits for them, and re-layouts: 1.59 us -> none  [local(): spec32 = spec.astype(jnp.float32)]
  transfers between devices with their start and end apart: 13 -> 13, of which waited for: 10 -> 11; matrix products, arithmetic and copies ran while one was open for 16% -> 15% of each run, Pallas kernels for 11% -> 11%
where the time goes in v15:
time: 130 us
  waiting for transfers between devices  43.7 us (34%)
  Pallas kernels  30.2 us (23%)
  other arithmetic  19.2 us (15%)
  starting transfers between devices  18.4 us (14%)
  between operations  14.2 us (11%)
  local copies, waits for them, and re-layouts  3.87 us (3%)
    pallas_call x2, Pallas kernels, match_rows(): pl.pallas_call(kernel, grid_spec=pltpu.PrefetchScalarGridSpec(num_scalar_...  30.2 us
    all_gather x1, waiting for transfers between devices, local(): tmpl = lax.all_gather(template_spectra, 'tile', axis=0)  13.8 us
    convert_element_type x2, other arithmetic, angle_tables(): jnp.sin(angle).astype(jnp.bfloat16)  10 us
    ppermute x3, waiting for transfers between devices, gather_rows(): got = lax.ppermute(blocks, axis, xor_pairs(n, k))  7.98 us
    ppermute x1, waiting for transfers between devices, reduce_joined(): got = lax.ppermute(send, axis, xor_pairs(n, 1))  6.99 us
    ppermute x3, starting transfers between devices, gather_rows(): got = lax.ppermute(blocks, axis, xor_pairs(n, k))  5.92 us
    ppermute x3, waiting for transfers between devices, reduce_joined(): got = lax.ppermute(out, axis, xor_pairs(n, 2 * m))  5.59 us
    ppermute x1, waiting for transfers between devices, reduce_joined(): other = lax.ppermute(mine, axis, xor_pairs(n, 1))  4.94 us
  transfers between devices with their start and end apart: 13, of which 11 were waited for; matrix products, arithmetic and copies ran while one was open for 15% of the time, Pallas kernels for 11%

profile of v15, /device:TPU:0, one launch (start us, length us, event | category | flops | bytes accessed | tf_op | source)
XLA Modules:
  0.0 129.6 jit_solution(12858886105219252519)
XLA Ops:
  7.2 0.7 all-gather.3.cloned.1.call-update
  8.4 3.7 %collective-permute-start = (bf16[1,2,64,512]{3,2,1,0:T(8,128)(2,1)S(1)}, bf16[1,2,64,512]{3,2,1,0:T(8,128)(2,1)S(1)}, u32[]{:S(2)}, u32[]{:S(2)}) collective-permute-start(bf16[1,2,64,512]{3,2,1,0:T(8,128)(2,1)S(1)} %copy-done), channel_id=1, source_target_pairs={{0,4},{1,5},{2,6},{3,7},{4,0},{5,1},{6,2},{7,3},{8,12},{9,13},{10,... | collective-permute-start | bytes 393224 | tf_op jit(solution)/shard_map/ppermute | solution.py:50
  12.3 4.0 %fusion.12 = bf16[4,512,128]{2,1,0:T(8,128)(2,1)S(1)} fusion(s32[4,128]{1,0:T(4,128)S(1)} %get-tuple-element.21), kind=kLoop, calls=%fused_computation.39 | loop fusion | flops 4718592 | bytes 526336 | tf_op jit(solution)/shard_map/neg | solution.py:38
  16.5 2.5 %collective-permute-done = bf16[1,2,64,512]{3,2,1,0:T(8,128)(2,1)S(1)} collective-permute-done((bf16[1,2,64,512]{3,2,1,0:T(8,128)(2,1)S(1)}, bf16[1,2,64,512]{3,2,1,0:T(8,128)(2,1)S(1)}, u32[]{:S(2)}, u32[]{:S(2)}) %collective-permute-start) | collective-permute-done | bytes 131104 | tf_op jit(solution)/shard_map/ppermute | solution.py:50
  19.0 0.8 collective-permute-start.1
  20.4 0.6 reshape.177.f_ref
  21.0 4.4 %sine_convert_fusion.1 = (bf16[4,512,128]{2,1,0:T(8,128)(2,1)S(1)}, bf16[4,512,128]{2,1,0:T(8,128)(2,1)S(1)}) fusion(s32[4,128]{1,0:T(4,128)S(1)} %get-tuple-element.21), kind=kLoop, calls=%fused_computation.20 | loop fusion | flops 4194304 | bytes 1050624 | tf_op jit(solution)/shard_map/convert_element_type | solution.py:31
  25.4 1.8 %collective-permute-done.1 = bf16[2,2,64,512]{3,2,1,0:T(8,128)(2,1)S(1)} collective-permute-done((bf16[2,2,64,512]{3,2,1,0:T(8,128)(2,1)S(1)}, bf16[2,2,64,512]{3,2,1,0:T(8,128)(2,1)S(1)}, u32[]{:S(2)}, u32[]{:S(2)}) %collective-permute-start.1) | collective-permute-done | bytes 262176 | tf_op jit(solution)/shard_map/ppermute | solution.py:50
  27.2 1.4 %collective-permute-start.2 = (bf16[4,2,64,512]{3,2,1,0:T(8,128)(2,1)S(1)}, bf16[4,2,64,512]{3,2,1,0:T(8,128)(2,1)S(1)}, u32[]{:S(2)}, u32[]{:S(2)}) collective-permute-start(bf16[4,2,64,512]{3,2,1,0:T(8,128)(2,1)S(1)} %pad_maximum_fusion.1), channel_id=1, source_target_pairs={{0,1},{1,0},{2,3},{3,2},{4,5},{5,4},{6,7},{7,6},{8,9},{9,8},{10,11... | collective-permute-start | bytes 1572872 | tf_op jit(solution)/shard_map/ppermute | solution.py:50
  29.2 1.6 %maximum_maximum_fusion.ct_ref = bf16[4,1024,256]{2,1,0:T(8,128)(2,1)} fusion(bf16[4,512,128]{2,1,0:T(8,128)(2,1)S(1)} %get-tuple-element.17, bf16[4,512,128]{2,1,0:T(8,128)(2,1)S(1)} %fusion.12, bf16[4,512,128]{2,1,0:T(8,128)(2,1)S(1)} %get-tuple-element.16), kind=kLoop, calls=%fused_computation.2 | loop fusion | flops 8388608 | bytes 3670016 | tf_op jit(solution)/shard_map/concatenate | solution.py:39
  30.8 5.6 %sine_convert_fusion = (bf16[4,128,512]{2,1,0:T(8,128)(2,1)}, bf16[4,128,512]{2,1,0:T(8,128)(2,1)}) fusion(s32[4,128]{1,0:T(4,128)S(1)} %get-tuple-element.20), kind=kLoop, calls=%fused_computation.16 | loop fusion | flops 4194304 | bytes 1050624 | tf_op jit(solution)/shard_map/convert_element_type | solution.py:31
  36.5 3.7 %collective-permute-done.2 = bf16[4,2,64,512]{3,2,1,0:T(8,128)(2,1)S(1)} collective-permute-done((bf16[4,2,64,512]{3,2,1,0:T(8,128)(2,1)S(1)}, bf16[4,2,64,512]{3,2,1,0:T(8,128)(2,1)S(1)}, u32[]{:S(2)}, u32[]{:S(2)}) %collective-permute-start.2) | collective-permute-done | bytes 524320 | tf_op jit(solution)/shard_map/ppermute | solution.py:50
  40.3 0.6 gather_fusion
  40.9 1.1 copy.13
  42.0 14.8 %shard_map.68.rest_0_ = f32[4,8,128,128]{3,2,1,0:T(8,128)} custom-call(s32[32]{0:T(128)} %reshape.177.f_ref, s32[1]{0:T(128)} %constant.104.clone.1.ta_ref.tb_ref, s32[1]{0:T(128)} %constant.104.clone.1.ta_ref.tb_ref, s32[1]{0:T(128)} %bitcast.1.rid_ref, s32[2]{0:T(128)} %add_multiply_fusion.off_ref, bf16[1,8,2,128,512]{4,3,2,1,0:T(8,128)(2,1)} %bitcast.11.tma_ref, ...), custom_call_target="tpu_custom_call" | custom-call | flops 4831838208 | bytes 10485760 | tf_op jit(solution)/shard_map/pallas_call | solution.py:267
  56.9 13.8 %all-gather.3.cloned.1.call-done = bf16[32,2,128,512]{3,2,1,0:T(8,128)(2,1)} async-done(((bf16[8,2,128,512]{3,2,1,0:T(8,128)(2,1)}), bf16[32,2,128,512]{3,2,1,0:T(8,128)(2,1)}) %all-gather.3.cloned.1.call-update) | async-done | bytes 8388624 | tf_op jit(solution)/shard_map/all_gather | solution.py:287
  70.6 15.4 %shard_map.69 = f32[2,4,128,128]{3,2,1,0:T(8,128)} custom-call(s32[32]{0:T(128)} %reshape.177.f_ref, s32[1]{0:T(128)S(6)} %mul.65.ta_ref, s32[1]{0:T(128)S(6)} %add.152.tb_ref, s32[1]{0:T(128)S(6)} %convert_element_type.34.rid_ref, s32[2]{0:T(128)} %iota_multiply_fusion.off_ref, bf16[4,8,2,128,512]{4,3,2,1,0:T(8,128)(2,1)} %bitcast.28, ...), custom_call_target="tpu_custom_call" | custom-call | flops 4831838208 | bytes 10485760 | tf_op jit(solution)/shard_map/pallas_call | solution.py:267
  86.0 1.0 constant_dynamic-slice_fusion
  86.9 1.5 %collective-permute-start.4 = (f32[2,256,128]{2,1,0:T(8,128)S(1)}, f32[2,256,128]{2,1,0:T(8,128)S(1)}, u32[]{:S(2)}, u32[]{:S(2)}) collective-permute-start(f32[2,256,128]{2,1,0:T(8,128)S(1)} %constant_dynamic-slice_fusion), channel_id=1, source_target_pairs={{0,1},{1,0},{2,3},{3,2},{4,5},{5,4},{6,7},{7,6},{8,9},{9,8},{10,11... | collective-permute-start | bytes 786440 | tf_op jit(solution)/shard_map/ppermute | solution.py:90
  88.4 7.0 %collective-permute-done.4 = f32[2,256,128]{2,1,0:T(8,128)S(1)} collective-permute-done((f32[2,256,128]{2,1,0:T(8,128)S(1)}, f32[2,256,128]{2,1,0:T(8,128)S(1)}, u32[]{:S(2)}, u32[]{:S(2)}) %collective-permute-start.4) | collective-permute-done | bytes 262176 | tf_op jit(solution)/shard_map/ppermute | solution.py:90
  95.4 1.0 slice_add_fusion
  96.5 1.6 %collective-permute-start.5 = (f32[2,64,128]{2,1,0:T(8,128)S(1)}, f32[2,64,128]{2,1,0:T(8,128)S(1)}, u32[]{:S(2)}, u32[]{:S(2)}) collective-permute-start(f32[2,64,128]{2,1,0:T(8,128)S(1)} %get-tuple-element.9), channel_id=1, source_target_pairs={{0,2},{1,3},{2,0},{3,1},{4,6},{5,7},{6,4},{7,5},{8,10},{9,11},{10,... | collective-permute-start | bytes 196616 | tf_op jit(solution)/shard_map/ppermute | solution.py:99
  98.0 2.4 %collective-permute-start.6 = (f32[2,64,128]{2,1,0:T(8,128)S(1)}, f32[2,64,128]{2,1,0:T(8,128)S(1)}, u32[]{:S(2)}, u32[]{:S(2)}) collective-permute-start(f32[2,64,128]{2,1,0:T(8,128)S(1)} %get-tuple-element.10), channel_id=1, source_target_pairs={{0,4},{1,5},{2,6},{3,7},{4,0},{5,1},{6,2},{7,3},{8,12},{9,13},{10,... | collective-permute-start | bytes 196616 | tf_op jit(solution)/shard_map/ppermute | solution.py:99
  101.5 3.4 %collective-permute-done.6 = f32[2,64,128]{2,1,0:T(8,128)S(1)} collective-permute-done((f32[2,64,128]{2,1,0:T(8,128)S(1)}, f32[2,64,128]{2,1,0:T(8,128)S(1)}, u32[]{:S(2)}, u32[]{:S(2)}) %collective-permute-start.6) | collective-permute-done | bytes 65568 | tf_op jit(solution)/shard_map/ppermute | solution.py:99
  104.9 1.6 %collective-permute-done.7 = f32[2,64,128]{2,1,0:T(8,128)S(1)} collective-permute-done((f32[2,64,128]{2,1,0:T(8,128)S(1)}, f32[2,64,128]{2,1,0:T(8,128)S(1)}, u32[]{:S(2)}, u32[]{:S(2)}) %collective-permute-start.7) | collective-permute-done | bytes 65568 | tf_op jit(solution)/shard_map/ppermute | solution.py:99
  106.6 2.1 %collective-permute-start.9 = (f32[2,64,128]{2,1,0:T(8,128)S(1)}, f32[2,64,128]{2,1,0:T(8,128)S(1)}, u32[]{:S(2)}, u32[]{:S(2)}) collective-permute-start(f32[2,64,128]{2,1,0:T(8,128)S(1)} %get-tuple-element.13), channel_id=1, source_target_pairs={{0,4},{1,5},{2,6},{3,7},{4,0},{5,1},{6,2},{7,3},{8,12},{9,13},{10,... | collective-permute-start | bytes 196616 | tf_op jit(solution)/shard_map/ppermute | solution.py:103
  108.7 2.3 %collective-permute-start.10 = (f32[2,64,128]{2,1,0:T(8,128)S(1)}, f32[2,64,128]{2,1,0:T(8,128)S(1)}, u32[]{:S(2)}, u32[]{:S(2)}) collective-permute-start(f32[2,64,128]{2,1,0:T(8,128)S(1)} %get-tuple-element.13), channel_id=1, source_target_pairs={{0,6},{1,7},{2,4},{3,5},{4,2},{5,3},{6,0},{7,1},{8,14},{9,15},{10,... | collective-permute-start | bytes 196616 | tf_op jit(solution)/shard_map/ppermute | solution.py:103
  111.0 1.4 %collective-permute-done.9 = f32[2,64,128]{2,1,0:T(8,128)S(1)} collective-permute-done((f32[2,64,128]{2,1,0:T(8,128)S(1)}, f32[2,64,128]{2,1,0:T(8,128)S(1)}, u32[]{:S(2)}, u32[]{:S(2)}) %collective-permute-start.9) | collective-permute-done | bytes 65568 | tf_op jit(solution)/shard_map/ppermute | solution.py:103
  112.4 2.4 %collective-permute-done.10 = f32[2,64,128]{2,1,0:T(8,128)S(1)} collective-permute-done((f32[2,64,128]{2,1,0:T(8,128)S(1)}, f32[2,64,128]{2,1,0:T(8,128)S(1)}, u32[]{:S(2)}, u32[]{:S(2)}) %collective-permute-start.10) | collective-permute-done | bytes 65568 | tf_op jit(solution)/shard_map/ppermute | solution.py:103
  115.4 1.5 %collective-permute-start.11 = (f32[2,256,128]{2,1,0:T(8,128)S(1)}, f32[2,256,128]{2,1,0:T(8,128)S(1)}, u32[]{:S(2)}, u32[]{:S(2)}) collective-permute-start(f32[2,256,128]{2,1,0:T(8,128)S(1)} %bitcast.36), channel_id=1, source_target_pairs={{0,1},{1,0},{2,3},{3,2},{4,5},{5,4},{6,7},{7,6},{8,9},{9,8},{10,11... | collective-permute-start | bytes 786440 | tf_op jit(solution)/shard_map/ppermute | solution.py:106
  116.9 4.9 %collective-permute-done.11 = f32[2,256,128]{2,1,0:T(8,128)S(1)} collective-permute-done((f32[2,256,128]{2,1,0:T(8,128)S(1)}, f32[2,256,128]{2,1,0:T(8,128)S(1)}, u32[]{:S(2)}, u32[]{:S(2)}) %collective-permute-start.11) | collective-permute-done | bytes 262176 | tf_op jit(solution)/shard_map/ppermute | solution.py:106
  121.9 0.8 slice_multiply_fusion
  (35 shorter events, 4.0 us)
Async XLA Ops:
  7.2 1.3 copy-start
  7.2 5.0 %copy-start.2 = (s32[1,4,2]{1,2,0:T(2,128)S(1)}, s32[1,4,2]{1,2,0:T(2,128)}, u32[]{:S(2)}) copy-start(s32[1,4,2]{1,2,0:T(2,128)} %param.7) | copy-start | bytes 100
  7.2 9.1 %copy-start.1 = (s32[1,4,48]{2,1,0:T(4,128)S(1)}, s32[1,4,48]{2,1,0:T(4,128)}, u32[]{:S(2)}) copy-start(s32[1,4,48]{2,1,0:T(4,128)} %param.8) | copy-start | bytes 2308
  7.2 63.4 %all-gather.3.cloned.1.call-start = ((), (), s32[]{:S(2)}) async-start(), calls=%async_computation | async-start | bytes 10485760 | tf_op jit(solution)/shard_map/all_gather | solution.py:287
  7.9 34.1 %collective-permute-start.3 = (bf16[8,2,128,512]{3,2,1,0:T(8,128)(2,1)}, bf16[8,2,128,512]{3,2,1,0:T(8,128)(2,1)}, u32[]{:S(2)}, u32[]{:S(2)}) collective-permute-start(bf16[8,2,128,512]{3,2,1,0:T(8,128)(2,1)} %param.6), channel_id=1, source_target_pairs={{0,8},{8,0},{16,24},{24,16},{1,9},{9,1},{17,25},{25,17},{2,10},{10... | collective-permute-start | bytes 6291464 | tf_op jit(solution)/shard_map/ppermute | solution.py:305
  8.4 10.6 %collective-permute-start = (bf16[1,2,64,512]{3,2,1,0:T(8,128)(2,1)S(1)}, bf16[1,2,64,512]{3,2,1,0:T(8,128)(2,1)S(1)}, u32[]{:S(2)}, u32[]{:S(2)}) collective-permute-start(bf16[1,2,64,512]{3,2,1,0:T(8,128)(2,1)S(1)} %copy-done), channel_id=1, source_target_pairs={{0,4},{1,5},{2,6},{3,7},{4,0},{5,1},{6,2},{7,3},{8,12},{9,13},{10,... | collective-permute-start | bytes 393224 | tf_op jit(solution)/shard_map/ppermute | solution.py:50
  19.0 8.1 %collective-permute-start.1 = (bf16[2,2,64,512]{3,2,1,0:T(8,128)(2,1)S(1)}, bf16[2,2,64,512]{3,2,1,0:T(8,128)(2,1)S(1)}, u32[]{:S(2)}, u32[]{:S(2)}) collective-permute-start(bf16[2,2,64,512]{3,2,1,0:T(8,128)(2,1)S(1)} %pad_maximum_fusion.2), channel_id=1, source_target_pairs={{0,2},{1,3},{2,0},{3,1},{4,6},{5,7},{6,4},{7,5},{8,10},{9,11},{10,... | collective-permute-start | bytes 786440 | tf_op jit(solution)/shard_map/ppermute | solution.py:50
  27.2 13.0 %collective-permute-start.2 = (bf16[4,2,64,512]{3,2,1,0:T(8,128)(2,1)S(1)}, bf16[4,2,64,512]{3,2,1,0:T(8,128)(2,1)S(1)}, u32[]{:S(2)}, u32[]{:S(2)}) collective-permute-start(bf16[4,2,64,512]{3,2,1,0:T(8,128)(2,1)S(1)} %pad_maximum_fusion.1), channel_id=1, source_target_pairs={{0,1},{1,0},{2,3},{3,2},{4,5},{5,4},{6,7},{7,6},{8,9},{9,8},{10,11... | collective-permute-start | bytes 1572872 | tf_op jit(solution)/shard_map/ppermute | solution.py:50
  86.9 8.5 %collective-permute-start.4 = (f32[2,256,128]{2,1,0:T(8,128)S(1)}, f32[2,256,128]{2,1,0:T(8,128)S(1)}, u32[]{:S(2)}, u32[]{:S(2)}) collective-permute-start(f32[2,256,128]{2,1,0:T(8,128)S(1)} %constant_dynamic-slice_fusion), channel_id=1, source_target_pairs={{0,1},{1,0},{2,3},{3,2},{4,5},{5,4},{6,7},{7,6},{8,9},{9,8},{10,11... | collective-permute-start | bytes 786440 | tf_op jit(solution)/shard_map/ppermute | solution.py:90
  96.5 5.0 %collective-permute-start.5 = (f32[2,64,128]{2,1,0:T(8,128)S(1)}, f32[2,64,128]{2,1,0:T(8,128)S(1)}, u32[]{:S(2)}, u32[]{:S(2)}) collective-permute-start(f32[2,64,128]{2,1,0:T(8,128)S(1)} %get-tuple-element.9), channel_id=1, source_target_pairs={{0,2},{1,3},{2,0},{3,1},{4,6},{5,7},{6,4},{7,5},{8,10},{9,11},{10,... | collective-permute-start | bytes 196616 | tf_op jit(solution)/shard_map/ppermute | solution.py:99
  98.0 6.8 %collective-permute-start.6 = (f32[2,64,128]{2,1,0:T(8,128)S(1)}, f32[2,64,128]{2,1,0:T(8,128)S(1)}, u32[]{:S(2)}, u32[]{:S(2)}) collective-permute-start(f32[2,64,128]{2,1,0:T(8,128)S(1)} %get-tuple-element.10), channel_id=1, source_target_pairs={{0,4},{1,5},{2,6},{3,7},{4,0},{5,1},{6,2},{7,3},{8,12},{9,13},{10,... | collective-permute-start | bytes 196616 | tf_op jit(solution)/shard_map/ppermute | solution.py:99
  100.5 6.1 %collective-permute-start.7 = (f32[2,64,128]{2,1,0:T(8,128)S(1)}, f32[2,64,128]{2,1,0:T(8,128)S(1)}, u32[]{:S(2)}, u32[]{:S(2)}) collective-permute-start(f32[2,64,128]{2,1,0:T(8,128)S(1)} %get-tuple-element.11), channel_id=1, source_target_pairs={{0,6},{1,7},{2,4},{3,5},{4,2},{5,3},{6,0},{7,1},{8,14},{9,15},{10,... | collective-permute-start | bytes 196616 | tf_op jit(solution)/shard_map/ppermute | solution.py:99
  106.6 4.5 %collective-permute-start.8 = (f32[2,64,128]{2,1,0:T(8,128)S(1)}, f32[2,64,128]{2,1,0:T(8,128)S(1)}, u32[]{:S(2)}, u32[]{:S(2)}) collective-permute-start(f32[2,64,128]{2,1,0:T(8,128)S(1)} %get-tuple-element.13), channel_id=1, source_target_pairs={{0,2},{1,3},{2,0},{3,1},{4,6},{5,7},{6,4},{7,5},{8,10},{9,11},{10,... | collective-permute-start | bytes 196616 | tf_op jit(solution)/shard_map/ppermute | solution.py:103
  106.6 5.8 %collective-permute-start.9 = (f32[2,64,128]{2,1,0:T(8,128)S(1)}, f32[2,64,128]{2,1,0:T(8,128)S(1)}, u32[]{:S(2)}, u32[]{:S(2)}) collective-permute-start(f32[2,64,128]{2,1,0:T(8,128)S(1)} %get-tuple-element.13), channel_id=1, source_target_pairs={{0,4},{1,5},{2,6},{3,7},{4,0},{5,1},{6,2},{7,3},{8,12},{9,13},{10,... | collective-permute-start | bytes 196616 | tf_op jit(solution)/shard_map/ppermute | solution.py:103
  108.7 6.1 %collective-permute-start.10 = (f32[2,64,128]{2,1,0:T(8,128)S(1)}, f32[2,64,128]{2,1,0:T(8,128)S(1)}, u32[]{:S(2)}, u32[]{:S(2)}) collective-permute-start(f32[2,64,128]{2,1,0:T(8,128)S(1)} %get-tuple-element.13), channel_id=1, source_target_pairs={{0,6},{1,7},{2,4},{3,5},{4,2},{5,3},{6,0},{7,1},{8,14},{9,15},{10,... | collective-permute-start | bytes 196616 | tf_op jit(solution)/shard_map/ppermute | solution.py:103
  115.4 6.4 %collective-permute-start.11 = (f32[2,256,128]{2,1,0:T(8,128)S(1)}, f32[2,256,128]{2,1,0:T(8,128)S(1)}, u32[]{:S(2)}, u32[]{:S(2)}) collective-permute-start(f32[2,256,128]{2,1,0:T(8,128)S(1)} %bitcast.36), channel_id=1, source_target_pairs={{0,1},{1,0},{2,3},{3,2},{4,5},{5,4},{6,7},{7,6},{8,9},{9,8},{10,11... | collective-permute-start | bytes 786440 | tf_op jit(solution)/shard_map/ppermute | solution.py:106
Sparse Core Ops, SparseCore 0:
  9.6 60.9 all-gather.2

commit v16 on v15

--- a/solution.py
+++ b/solution.py
@@ -169,10 +169,10 @@
 
 def rows_kernel(blocks, size, width, rows_t, peaks_n, chunk, n_steps, final, per, f_ref, ta_ref, tb_ref, rid_ref, off_ref, tma_ref, tmb_ref, sp_ref, ct_ref, cr_ref, sr_ref, *rest):
     if final:
-        init_ref, out_ref, acc_ref, m_ref = rest
+        init_ref, out_ref, acc_ref, m_ref, table_ref, table_sem = rest
         best_ref, pow_ref = out_ref.at[0], out_ref.at[1]
     else:
-        part_ref, acc_ref, m_ref = rest
+        part_ref, acc_ref, m_ref, table_ref, table_sem = rest
     jj = pl.program_id(0)
     i = pl.program_id(1)
     span = 2 * rows_t
@@ -190,6 +190,13 @@
         @pl.when(i == 0)
         def _():
             acc_ref[...] = jnp.zeros(acc_ref.shape, jnp.float32)
+
+    first = (pl.program_id(0) == 0) & (pl.program_id(1) == 0)
+    table_copy = pltpu.make_async_copy(ct_ref, table_ref, table_sem)
+
+    @pl.when(first)
+    def _():
+        table_copy.start()
 
     for o in range(per):
         for u, tm_ref in enumerate((tma_ref, tmb_ref)):
@@ -207,6 +214,10 @@
 
             lax.fori_loop(0, rows_t // chunk, mix, 0, unroll=4)
 
+    @pl.when(first)
+    def _():
+        table_copy.wait()
+
     for p in range(peaks_n):
         count = f_ref[p * blocks + per * jj]
         for o in range(1, per):
@@ -214,7 +225,7 @@
 
         @pl.when(count > 0)
         def _():
-            g = jnp.dot(m_ref[...], ct_ref[p], preferred_element_type=jnp.float32).astype(jnp.bfloat16)
+            g = jnp.dot(m_ref[...], table_ref[p], preferred_element_type=jnp.float32).astype(jnp.bfloat16)
             for o in range(per):
                 rows = slice(o * span, (o + 1) * span)
                 part = jnp.dot(cr_ref[p], g[rows, :width], preferred_element_type=jnp.float32)
@@ -250,7 +261,7 @@
         pl.BlockSpec((1, per, 2, rows_t, size), lambda j, i, f, ta, tb, r, o: (ta[i], j, 0, 0, 0)),
         pl.BlockSpec((1, per, 2, rows_t, size), lambda j, i, f, ta, tb, r, o: (tb[i], j, 0, 0, 0)),
         pl.BlockSpec((2, span, size), lambda j, i, f, ta, tb, r, o: (0, r[i], 0)),
-        pl.BlockSpec(col_table.shape, lambda j, i, f, ta, tb, r, o: (0, 0, 0)),
+        pl.BlockSpec(memory_space=pl.ANY),
         pl.BlockSpec((peaks_n, width, span), lambda j, i, f, ta, tb, r, o: (0, 0, r[i])),
         pl.BlockSpec((peaks_n, width, span), lambda j, i, f, ta, tb, r, o: (0, 0, r[i])),
     ]
@@ -271,7 +282,8 @@
             grid=(blocks // per, n_steps),
             in_specs=in_specs,
             out_specs=out_specs,
-            scratch_shapes=[pltpu.VMEM((peaks_n, per, width, width), jnp.float32), pltpu.VMEM((per * span, 2 * size), jnp.bfloat16)],
+            scratch_shapes=[pltpu.VMEM((peaks_n, per, width, width), jnp.float32), pltpu.VMEM((per * span, 2 * size), jnp.bfloat16),
+                            pltpu.VMEM(col_table.shape, jnp.bfloat16), pltpu.SemaphoreType.DMA(())],
         ),
         out_shape=out_shape,
         compiler_params=pltpu.CompilerParams(dimension_semantics=("arbitrary", "arbitrary")),

time: 130 us -> 130 us (level)
  transfers between devices with their start and end apart: 13 -> 13, of which waited for: 11 -> 12; matrix products, arithmetic and copies ran while one was open for 15% -> 15% of each run, Pallas kernels for 11% -> 11%
where the time goes in v16:
time: 130 us
  waiting for transfers between devices  43.5 us (33%)
  Pallas kernels  30.4 us (23%)
  other arithmetic  19.2 us (15%)
  starting transfers between devices  18.5 us (14%)
  between operations  14.2 us (11%)
  local copies, waits for them, and re-layouts  3.88 us (3%)
    pallas_call x2, Pallas kernels, match_rows(): pl.pallas_call(kernel, grid_spec=pltpu.PrefetchScalarGridSpec(num_scalar_...  30.4 us
    all_gather x1, waiting for transfers between devices, local(): tmpl = lax.all_gather(template_spectra, 'tile', axis=0)  13.7 us
    convert_element_type x2, other arithmetic, angle_tables(): jnp.sin(angle).astype(jnp.bfloat16)  10 us
    ppermute x3, waiting for transfers between devices, gather_rows(): got = lax.ppermute(blocks, axis, xor_pairs(n, k))  7.98 us
    ppermute x1, waiting for transfers between devices, reduce_joined(): got = lax.ppermute(send, axis, xor_pairs(n, 1))  7.02 us
    ppermute x3, starting transfers between devices, gather_rows(): got = lax.ppermute(blocks, axis, xor_pairs(n, k))  5.92 us
    ppermute x3, waiting for transfers between devices, reduce_joined(): got = lax.ppermute(out, axis, xor_pairs(n, 2 * m))  5.54 us
    ppermute x1, waiting for transfers between devices, reduce_joined(): other = lax.ppermute(mine, axis, xor_pairs(n, 1))  4.86 us
  transfers between devices with their start and end apart: 13, of which 12 were waited for; matrix products, arithmetic and copies ran while one was open for 15% of the time, Pallas kernels for 11%

profile of v16, /device:TPU:0, one launch (start us, length us, event | category | flops | bytes accessed | tf_op | source)
XLA Modules:
  0.0 129.6 jit_solution(9884944751363662074)
XLA Ops:
  7.2 0.7 all-gather.3.cloned.1.call-update
  8.4 3.7 %collective-permute-start = (bf16[1,2,64,512]{3,2,1,0:T(8,128)(2,1)S(1)}, bf16[1,2,64,512]{3,2,1,0:T(8,128)(2,1)S(1)}, u32[]{:S(2)}, u32[]{:S(2)}) collective-permute-start(bf16[1,2,64,512]{3,2,1,0:T(8,128)(2,1)S(1)} %copy-done), channel_id=1, source_target_pairs={{0,4},{1,5},{2,6},{3,7},{4,0},{5,1},{6,2},{7,3},{8,12},{9,13},{10,... | collective-permute-start | bytes 393224 | tf_op jit(solution)/shard_map/ppermute | solution.py:50
  12.3 4.0 %fusion.12 = bf16[4,512,128]{2,1,0:T(8,128)(2,1)S(1)} fusion(s32[4,128]{1,0:T(4,128)S(1)} %get-tuple-element.21), kind=kLoop, calls=%fused_computation.39 | loop fusion | flops 4718592 | bytes 526336 | tf_op jit(solution)/shard_map/neg | solution.py:38
  16.5 2.5 %collective-permute-done = bf16[1,2,64,512]{3,2,1,0:T(8,128)(2,1)S(1)} collective-permute-done((bf16[1,2,64,512]{3,2,1,0:T(8,128)(2,1)S(1)}, bf16[1,2,64,512]{3,2,1,0:T(8,128)(2,1)S(1)}, u32[]{:S(2)}, u32[]{:S(2)}) %collective-permute-start) | collective-permute-done | bytes 131104 | tf_op jit(solution)/shard_map/ppermute | solution.py:50
  19.0 0.8 collective-permute-start.1
  20.4 0.6 reshape.177.f_ref
  21.0 4.4 %sine_convert_fusion.1 = (bf16[4,512,128]{2,1,0:T(8,128)(2,1)S(1)}, bf16[4,512,128]{2,1,0:T(8,128)(2,1)S(1)}) fusion(s32[4,128]{1,0:T(4,128)S(1)} %get-tuple-element.21), kind=kLoop, calls=%fused_computation.20 | loop fusion | flops 4194304 | bytes 1050624 | tf_op jit(solution)/shard_map/convert_element_type | solution.py:31
  25.4 1.8 %collective-permute-done.1 = bf16[2,2,64,512]{3,2,1,0:T(8,128)(2,1)S(1)} collective-permute-done((bf16[2,2,64,512]{3,2,1,0:T(8,128)(2,1)S(1)}, bf16[2,2,64,512]{3,2,1,0:T(8,128)(2,1)S(1)}, u32[]{:S(2)}, u32[]{:S(2)}) %collective-permute-start.1) | collective-permute-done | bytes 262176 | tf_op jit(solution)/shard_map/ppermute | solution.py:50
  27.2 1.4 %collective-permute-start.2 = (bf16[4,2,64,512]{3,2,1,0:T(8,128)(2,1)S(1)}, bf16[4,2,64,512]{3,2,1,0:T(8,128)(2,1)S(1)}, u32[]{:S(2)}, u32[]{:S(2)}) collective-permute-start(bf16[4,2,64,512]{3,2,1,0:T(8,128)(2,1)S(1)} %pad_maximum_fusion.1), channel_id=1, source_target_pairs={{0,1},{1,0},{2,3},{3,2},{4,5},{5,4},{6,7},{7,6},{8,9},{9,8},{10,11... | collective-permute-start | bytes 1572872 | tf_op jit(solution)/shard_map/ppermute | solution.py:50
  29.2 1.6 %maximum_maximum_fusion.ct_ref = bf16[4,1024,256]{2,1,0:T(8,128)(2,1)} fusion(bf16[4,512,128]{2,1,0:T(8,128)(2,1)S(1)} %get-tuple-element.17, bf16[4,512,128]{2,1,0:T(8,128)(2,1)S(1)} %fusion.12, bf16[4,512,128]{2,1,0:T(8,128)(2,1)S(1)} %get-tuple-element.16), kind=kLoop, calls=%fused_computation.2 | loop fusion | flops 8388608 | bytes 3670016 | tf_op jit(solution)/shard_map/concatenate | solution.py:39
  30.8 5.6 %sine_convert_fusion = (bf16[4,128,512]{2,1,0:T(8,128)(2,1)}, bf16[4,128,512]{2,1,0:T(8,128)(2,1)}) fusion(s32[4,128]{1,0:T(4,128)S(1)} %get-tuple-element.20), kind=kLoop, calls=%fused_computation.16 | loop fusion | flops 4194304 | bytes 1050624 | tf_op jit(solution)/shard_map/convert_element_type | solution.py:31
  36.5 3.7 %collective-permute-done.2 = bf16[4,2,64,512]{3,2,1,0:T(8,128)(2,1)S(1)} collective-permute-done((bf16[4,2,64,512]{3,2,1,0:T(8,128)(2,1)S(1)}, bf16[4,2,64,512]{3,2,1,0:T(8,128)(2,1)S(1)}, u32[]{:S(2)}, u32[]{:S(2)}) %collective-permute-start.2) | collective-permute-done | bytes 524320 | tf_op jit(solution)/shard_map/ppermute | solution.py:50
  40.3 0.6 gather_fusion
  40.9 1.1 copy.13
  42.0 14.9 %shard_map.68.rest_0_ = f32[4,8,128,128]{3,2,1,0:T(8,128)} custom-call(s32[32]{0:T(128)} %reshape.177.f_ref, s32[1]{0:T(128)} %constant.104.clone.1.ta_ref.tb_ref, s32[1]{0:T(128)} %constant.104.clone.1.ta_ref.tb_ref, s32[1]{0:T(128)} %bitcast.1.rid_ref, s32[2]{0:T(128)} %add_multiply_fusion.off_ref, bf16[1,8,2,128,512]{4,3,2,1,0:T(8,128)(2,1)} %bitcast.11.tma_ref, ...), custom_call_target="tpu_custom_call" | custom-call | flops 4831838208 | bytes 10485760 | tf_op jit(solution)/shard_map/pallas_call | solution.py:278
  56.9 13.7 %all-gather.3.cloned.1.call-done = bf16[32,2,128,512]{3,2,1,0:T(8,128)(2,1)} async-done(((bf16[8,2,128,512]{3,2,1,0:T(8,128)(2,1)}), bf16[32,2,128,512]{3,2,1,0:T(8,128)(2,1)}) %all-gather.3.cloned.1.call-update) | async-done | bytes 8388624 | tf_op jit(solution)/shard_map/all_gather | solution.py:299
  70.6 15.5 %shard_map.69 = f32[2,4,128,128]{3,2,1,0:T(8,128)} custom-call(s32[32]{0:T(128)} %reshape.177.f_ref, s32[1]{0:T(128)S(6)} %mul.65.ta_ref, s32[1]{0:T(128)S(6)} %add.152.tb_ref, s32[1]{0:T(128)S(6)} %convert_element_type.34.rid_ref, s32[2]{0:T(128)} %iota_multiply_fusion.off_ref, bf16[4,8,2,128,512]{4,3,2,1,0:T(8,128)(2,1)} %bitcast.28, ...), custom_call_target="tpu_custom_call" | custom-call | flops 4831838208 | bytes 10485760 | tf_op jit(solution)/shard_map/pallas_call | solution.py:278
  86.1 1.0 constant_dynamic-slice_fusion
  87.1 1.5 %collective-permute-start.4 = (f32[2,256,128]{2,1,0:T(8,128)S(1)}, f32[2,256,128]{2,1,0:T(8,128)S(1)}, u32[]{:S(2)}, u32[]{:S(2)}) collective-permute-start(f32[2,256,128]{2,1,0:T(8,128)S(1)} %constant_dynamic-slice_fusion), channel_id=1, source_target_pairs={{0,1},{1,0},{2,3},{3,2},{4,5},{5,4},{6,7},{7,6},{8,9},{9,8},{10,11... | collective-permute-start | bytes 786440 | tf_op jit(solution)/shard_map/ppermute | solution.py:90
  88.6 7.0 %collective-permute-done.4 = f32[2,256,128]{2,1,0:T(8,128)S(1)} collective-permute-done((f32[2,256,128]{2,1,0:T(8,128)S(1)}, f32[2,256,128]{2,1,0:T(8,128)S(1)}, u32[]{:S(2)}, u32[]{:S(2)}) %collective-permute-start.4) | collective-permute-done | bytes 262176 | tf_op jit(solution)/shard_map/ppermute | solution.py:90
  95.6 1.0 slice_add_fusion
  96.7 1.5 %collective-permute-start.5 = (f32[2,64,128]{2,1,0:T(8,128)S(1)}, f32[2,64,128]{2,1,0:T(8,128)S(1)}, u32[]{:S(2)}, u32[]{:S(2)}) collective-permute-start(f32[2,64,128]{2,1,0:T(8,128)S(1)} %get-tuple-element.9), channel_id=1, source_target_pairs={{0,2},{1,3},{2,0},{3,1},{4,6},{5,7},{6,4},{7,5},{8,10},{9,11},{10,... | collective-permute-start | bytes 196616 | tf_op jit(solution)/shard_map/ppermute | solution.py:99
  98.2 2.4 %collective-permute-start.6 = (f32[2,64,128]{2,1,0:T(8,128)S(1)}, f32[2,64,128]{2,1,0:T(8,128)S(1)}, u32[]{:S(2)}, u32[]{:S(2)}) collective-permute-start(f32[2,64,128]{2,1,0:T(8,128)S(1)} %get-tuple-element.10), channel_id=1, source_target_pairs={{0,4},{1,5},{2,6},{3,7},{4,0},{5,1},{6,2},{7,3},{8,12},{9,13},{10,... | collective-permute-start | bytes 196616 | tf_op jit(solution)/shard_map/ppermute | solution.py:99
  101.5 3.6 %collective-permute-done.6 = f32[2,64,128]{2,1,0:T(8,128)S(1)} collective-permute-done((f32[2,64,128]{2,1,0:T(8,128)S(1)}, f32[2,64,128]{2,1,0:T(8,128)S(1)}, u32[]{:S(2)}, u32[]{:S(2)}) %collective-permute-start.6) | collective-permute-done | bytes 65568 | tf_op jit(solution)/shard_map/ppermute | solution.py:99
  105.1 1.6 %collective-permute-done.7 = f32[2,64,128]{2,1,0:T(8,128)S(1)} collective-permute-done((f32[2,64,128]{2,1,0:T(8,128)S(1)}, f32[2,64,128]{2,1,0:T(8,128)S(1)}, u32[]{:S(2)}, u32[]{:S(2)}) %collective-permute-start.7) | collective-permute-done | bytes 65568 | tf_op jit(solution)/shard_map/ppermute | solution.py:99
  106.8 2.0 %collective-permute-start.9 = (f32[2,64,128]{2,1,0:T(8,128)S(1)}, f32[2,64,128]{2,1,0:T(8,128)S(1)}, u32[]{:S(2)}, u32[]{:S(2)}) collective-permute-start(f32[2,64,128]{2,1,0:T(8,128)S(1)} %get-tuple-element.13), channel_id=1, source_target_pairs={{0,4},{1,5},{2,6},{3,7},{4,0},{5,1},{6,2},{7,3},{8,12},{9,13},{10,... | collective-permute-start | bytes 196616 | tf_op jit(solution)/shard_map/ppermute | solution.py:103
  108.8 2.4 %collective-permute-start.10 = (f32[2,64,128]{2,1,0:T(8,128)S(1)}, f32[2,64,128]{2,1,0:T(8,128)S(1)}, u32[]{:S(2)}, u32[]{:S(2)}) collective-permute-start(f32[2,64,128]{2,1,0:T(8,128)S(1)} %get-tuple-element.13), channel_id=1, source_target_pairs={{0,6},{1,7},{2,4},{3,5},{4,2},{5,3},{6,0},{7,1},{8,14},{9,15},{10,... | collective-permute-start | bytes 196616 | tf_op jit(solution)/shard_map/ppermute | solution.py:103
  111.4 1.0 collective-permute-done.9
  112.4 2.4 %collective-permute-done.10 = f32[2,64,128]{2,1,0:T(8,128)S(1)} collective-permute-done((f32[2,64,128]{2,1,0:T(8,128)S(1)}, f32[2,64,128]{2,1,0:T(8,128)S(1)}, u32[]{:S(2)}, u32[]{:S(2)}) %collective-permute-start.10) | collective-permute-done | bytes 65568 | tf_op jit(solution)/shard_map/ppermute | solution.py:103
  115.5 1.6 %collective-permute-start.11 = (f32[2,256,128]{2,1,0:T(8,128)S(1)}, f32[2,256,128]{2,1,0:T(8,128)S(1)}, u32[]{:S(2)}, u32[]{:S(2)}) collective-permute-start(f32[2,256,128]{2,1,0:T(8,128)S(1)} %bitcast.36), channel_id=1, source_target_pairs={{0,1},{1,0},{2,3},{3,2},{4,5},{5,4},{6,7},{7,6},{8,9},{9,8},{10,11... | collective-permute-start | bytes 786440 | tf_op jit(solution)/shard_map/ppermute | solution.py:106
  117.1 4.9 %collective-permute-done.11 = f32[2,256,128]{2,1,0:T(8,128)S(1)} collective-permute-done((f32[2,256,128]{2,1,0:T(8,128)S(1)}, f32[2,256,128]{2,1,0:T(8,128)S(1)}, u32[]{:S(2)}, u32[]{:S(2)}) %collective-permute-start.11) | collective-permute-done | bytes 262176 | tf_op jit(solution)/shard_map/ppermute | solution.py:106
  122.0 0.8 slice_multiply_fusion
  (35 shorter events, 4.1 us)
Async XLA Ops:
  7.2 1.3 copy-start
  7.2 5.0 %copy-start.2 = (s32[1,4,2]{1,2,0:T(2,128)S(1)}, s32[1,4,2]{1,2,0:T(2,128)}, u32[]{:S(2)}) copy-start(s32[1,4,2]{1,2,0:T(2,128)} %param.7) | copy-start | bytes 100
  7.2 9.1 %copy-start.1 = (s32[1,4,48]{2,1,0:T(4,128)S(1)}, s32[1,4,48]{2,1,0:T(4,128)}, u32[]{:S(2)}) copy-start(s32[1,4,48]{2,1,0:T(4,128)} %param.8) | copy-start | bytes 2308
  7.2 63.4 %all-gather.3.cloned.1.call-start = ((), (), s32[]{:S(2)}) async-start(), calls=%async_computation | async-start | bytes 10485760 | tf_op jit(solution)/shard_map/all_gather | solution.py:299
  7.9 34.1 %collective-permute-start.3 = (bf16[8,2,128,512]{3,2,1,0:T(8,128)(2,1)}, bf16[8,2,128,512]{3,2,1,0:T(8,128)(2,1)}, u32[]{:S(2)}, u32[]{:S(2)}) collective-permute-start(bf16[8,2,128,512]{3,2,1,0:T(8,128)(2,1)} %param.6), channel_id=1, source_target_pairs={{0,8},{8,0},{16,24},{24,16},{1,9},{9,1},{17,25},{25,17},{2,10},{10... | collective-permute-start | bytes 6291464 | tf_op jit(solution)/shard_map/ppermute | solution.py:317
  8.4 10.6 %collective-permute-start = (bf16[1,2,64,512]{3,2,1,0:T(8,128)(2,1)S(1)}, bf16[1,2,64,512]{3,2,1,0:T(8,128)(2,1)S(1)}, u32[]{:S(2)}, u32[]{:S(2)}) collective-permute-start(bf16[1,2,64,512]{3,2,1,0:T(8,128)(2,1)S(1)} %copy-done), channel_id=1, source_target_pairs={{0,4},{1,5},{2,6},{3,7},{4,0},{5,1},{6,2},{7,3},{8,12},{9,13},{10,... | collective-permute-start | bytes 393224 | tf_op jit(solution)/shard_map/ppermute | solution.py:50
  19.0 8.1 %collective-permute-start.1 = (bf16[2,2,64,512]{3,2,1,0:T(8,128)(2,1)S(1)}, bf16[2,2,64,512]{3,2,1,0:T(8,128)(2,1)S(1)}, u32[]{:S(2)}, u32[]{:S(2)}) collective-permute-start(bf16[2,2,64,512]{3,2,1,0:T(8,128)(2,1)S(1)} %pad_maximum_fusion.2), channel_id=1, source_target_pairs={{0,2},{1,3},{2,0},{3,1},{4,6},{5,7},{6,4},{7,5},{8,10},{9,11},{10,... | collective-permute-start | bytes 786440 | tf_op jit(solution)/shard_map/ppermute | solution.py:50
  27.2 13.0 %collective-permute-start.2 = (bf16[4,2,64,512]{3,2,1,0:T(8,128)(2,1)S(1)}, bf16[4,2,64,512]{3,2,1,0:T(8,128)(2,1)S(1)}, u32[]{:S(2)}, u32[]{:S(2)}) collective-permute-start(bf16[4,2,64,512]{3,2,1,0:T(8,128)(2,1)S(1)} %pad_maximum_fusion.1), channel_id=1, source_target_pairs={{0,1},{1,0},{2,3},{3,2},{4,5},{5,4},{6,7},{7,6},{8,9},{9,8},{10,11... | collective-permute-start | bytes 1572872 | tf_op jit(solution)/shard_map/ppermute | solution.py:50
  87.1 8.5 %collective-permute-start.4 = (f32[2,256,128]{2,1,0:T(8,128)S(1)}, f32[2,256,128]{2,1,0:T(8,128)S(1)}, u32[]{:S(2)}, u32[]{:S(2)}) collective-permute-start(f32[2,256,128]{2,1,0:T(8,128)S(1)} %constant_dynamic-slice_fusion), channel_id=1, source_target_pairs={{0,1},{1,0},{2,3},{3,2},{4,5},{5,4},{6,7},{7,6},{8,9},{9,8},{10,11... | collective-permute-start | bytes 786440 | tf_op jit(solution)/shard_map/ppermute | solution.py:90
  96.7 4.8 %collective-permute-start.5 = (f32[2,64,128]{2,1,0:T(8,128)S(1)}, f32[2,64,128]{2,1,0:T(8,128)S(1)}, u32[]{:S(2)}, u32[]{:S(2)}) collective-permute-start(f32[2,64,128]{2,1,0:T(8,128)S(1)} %get-tuple-element.9), channel_id=1, source_target_pairs={{0,2},{1,3},{2,0},{3,1},{4,6},{5,7},{6,4},{7,5},{8,10},{9,11},{10,... | collective-permute-start | bytes 196616 | tf_op jit(solution)/shard_map/ppermute | solution.py:99
  98.2 6.9 %collective-permute-start.6 = (f32[2,64,128]{2,1,0:T(8,128)S(1)}, f32[2,64,128]{2,1,0:T(8,128)S(1)}, u32[]{:S(2)}, u32[]{:S(2)}) collective-permute-start(f32[2,64,128]{2,1,0:T(8,128)S(1)} %get-tuple-element.10), channel_id=1, source_target_pairs={{0,4},{1,5},{2,6},{3,7},{4,0},{5,1},{6,2},{7,3},{8,12},{9,13},{10,... | collective-permute-start | bytes 196616 | tf_op jit(solution)/shard_map/ppermute | solution.py:99
  100.6 6.1 %collective-permute-start.7 = (f32[2,64,128]{2,1,0:T(8,128)S(1)}, f32[2,64,128]{2,1,0:T(8,128)S(1)}, u32[]{:S(2)}, u32[]{:S(2)}) collective-permute-start(f32[2,64,128]{2,1,0:T(8,128)S(1)} %get-tuple-element.11), channel_id=1, source_target_pairs={{0,6},{1,7},{2,4},{3,5},{4,2},{5,3},{6,0},{7,1},{8,14},{9,15},{10,... | collective-permute-start | bytes 196616 | tf_op jit(solution)/shard_map/ppermute | solution.py:99
  106.7 4.7 %collective-permute-start.8 = (f32[2,64,128]{2,1,0:T(8,128)S(1)}, f32[2,64,128]{2,1,0:T(8,128)S(1)}, u32[]{:S(2)}, u32[]{:S(2)}) collective-permute-start(f32[2,64,128]{2,1,0:T(8,128)S(1)} %get-tuple-element.13), channel_id=1, source_target_pairs={{0,2},{1,3},{2,0},{3,1},{4,6},{5,7},{6,4},{7,5},{8,10},{9,11},{10,... | collective-permute-start | bytes 196616 | tf_op jit(solution)/shard_map/ppermute | solution.py:103
  106.8 5.7 %collective-permute-start.9 = (f32[2,64,128]{2,1,0:T(8,128)S(1)}, f32[2,64,128]{2,1,0:T(8,128)S(1)}, u32[]{:S(2)}, u32[]{:S(2)}) collective-permute-start(f32[2,64,128]{2,1,0:T(8,128)S(1)} %get-tuple-element.13), channel_id=1, source_target_pairs={{0,4},{1,5},{2,6},{3,7},{4,0},{5,1},{6,2},{7,3},{8,12},{9,13},{10,... | collective-permute-start | bytes 196616 | tf_op jit(solution)/shard_map/ppermute | solution.py:103
  108.8 6.1 %collective-permute-start.10 = (f32[2,64,128]{2,1,0:T(8,128)S(1)}, f32[2,64,128]{2,1,0:T(8,128)S(1)}, u32[]{:S(2)}, u32[]{:S(2)}) collective-permute-start(f32[2,64,128]{2,1,0:T(8,128)S(1)} %get-tuple-element.13), channel_id=1, source_target_pairs={{0,6},{1,7},{2,4},{3,5},{4,2},{5,3},{6,0},{7,1},{8,14},{9,15},{10,... | collective-permute-start | bytes 196616 | tf_op jit(solution)/shard_map/ppermute | solution.py:103
  115.5 6.4 %collective-permute-start.11 = (f32[2,256,128]{2,1,0:T(8,128)S(1)}, f32[2,256,128]{2,1,0:T(8,128)S(1)}, u32[]{:S(2)}, u32[]{:S(2)}) collective-permute-start(f32[2,256,128]{2,1,0:T(8,128)S(1)} %bitcast.36), channel_id=1, source_target_pairs={{0,1},{1,0},{2,3},{3,2},{4,5},{5,4},{6,7},{7,6},{8,9},{9,8},{10,11... | collective-permute-start | bytes 786440 | tf_op jit(solution)/shard_map/ppermute | solution.py:106
Sparse Core Ops, SparseCore 0:
  9.6 60.9 all-gather.2

commit v17 on v15

--- a/solution.py
+++ b/solution.py
@@ -242,7 +242,7 @@
     final = init is not None
     chunk = math.gcd(rows_t, 16)
     span = 2 * rows_t
-    per = 4 if blocks % 4 == 0 else 2
+    per = 8 if blocks % 8 == 0 else (4 if blocks % 4 == 0 else 2)
     kernel = functools.partial(rows_kernel, blocks, size, width, rows_t, peaks_n, chunk, n_steps, final, per)
     flops = blocks * peaks_n * n_steps * (2 * span * 2 * size * 2 * width + 2 * 2 * width * span * width)
     cost = pl.CostEstimate(flops=flops, transcendentals=0, bytes_accessed=n_steps * blocks * 2 * span * size * 4 + col_table.size * 2)

time: 130 us -> 129 us (level)
  transfers between devices with their start and end apart: 13 -> 13, of which waited for: 11 -> 10; matrix products, arithmetic and copies ran while one was open for 15% -> 15% of each run, Pallas kernels for 11% -> 11%
where the time goes in v17:
time: 129 us
  waiting for transfers between devices  43.9 us (34%)
  Pallas kernels  29.3 us (23%)
  other arithmetic  19.2 us (15%)
  starting transfers between devices  18.5 us (14%)
  between operations  14.2 us (11%)
  local copies, waits for them, and re-layouts  3.87 us (3%)
    pallas_call x2, Pallas kernels, match_rows(): pl.pallas_call(kernel, grid_spec=pltpu.PrefetchScalarGridSpec(num_scalar_...  29.3 us
    all_gather x1, waiting for transfers between devices, local(): tmpl = lax.all_gather(template_spectra, 'tile', axis=0)  14.2 us
    convert_element_type x2, other arithmetic, angle_tables(): jnp.sin(angle).astype(jnp.bfloat16)  10 us
    ppermute x3, waiting for transfers between devices, gather_rows(): got = lax.ppermute(blocks, axis, xor_pairs(n, k))  7.98 us
    ppermute x1, waiting for transfers between devices, reduce_joined(): got = lax.ppermute(send, axis, xor_pairs(n, 1))  7.01 us
    ppermute x3, starting transfers between devices, gather_rows(): got = lax.ppermute(blocks, axis, xor_pairs(n, k))  5.92 us
    ppermute x3, waiting for transfers between devices, reduce_joined(): got = lax.ppermute(out, axis, xor_pairs(n, 2 * m))  5.6 us
    ppermute x1, waiting for transfers between devices, reduce_joined(): other = lax.ppermute(mine, axis, xor_pairs(n, 1))  4.81 us
  transfers between devices with their start and end apart: 13, of which 10 were waited for; matrix products, arithmetic and copies ran while one was open for 15% of the time, Pallas kernels for 11%

profile of v17, /device:TPU:0, one launch (start us, length us, event | category | flops | bytes accessed | tf_op | source)
XLA Modules:
  0.0 129.0 jit_solution(11803098436584293085)
XLA Ops:
  7.2 0.7 all-gather.3.cloned.1.call-update
  8.4 3.7 %collective-permute-start = (bf16[1,2,64,512]{3,2,1,0:T(8,128)(2,1)S(1)}, bf16[1,2,64,512]{3,2,1,0:T(8,128)(2,1)S(1)}, u32[]{:S(2)}, u32[]{:S(2)}) collective-permute-start(bf16[1,2,64,512]{3,2,1,0:T(8,128)(2,1)S(1)} %copy-done), channel_id=1, source_target_pairs={{0,4},{1,5},{2,6},{3,7},{4,0},{5,1},{6,2},{7,3},{8,12},{9,13},{10,... | collective-permute-start | bytes 393224 | tf_op jit(solution)/shard_map/ppermute | solution.py:50
  12.3 4.0 %fusion.12 = bf16[4,512,128]{2,1,0:T(8,128)(2,1)S(1)} fusion(s32[4,128]{1,0:T(4,128)S(1)} %get-tuple-element.21), kind=kLoop, calls=%fused_computation.39 | loop fusion | flops 4718592 | bytes 526336 | tf_op jit(solution)/shard_map/neg | solution.py:38
  16.5 2.5 %collective-permute-done = bf16[1,2,64,512]{3,2,1,0:T(8,128)(2,1)S(1)} collective-permute-done((bf16[1,2,64,512]{3,2,1,0:T(8,128)(2,1)S(1)}, bf16[1,2,64,512]{3,2,1,0:T(8,128)(2,1)S(1)}, u32[]{:S(2)}, u32[]{:S(2)}) %collective-permute-start) | collective-permute-done | bytes 131104 | tf_op jit(solution)/shard_map/ppermute | solution.py:50
  19.0 0.8 collective-permute-start.1
  20.4 0.6 reshape.177.f_ref
  21.0 4.4 %sine_convert_fusion.1 = (bf16[4,512,128]{2,1,0:T(8,128)(2,1)S(1)}, bf16[4,512,128]{2,1,0:T(8,128)(2,1)S(1)}) fusion(s32[4,128]{1,0:T(4,128)S(1)} %get-tuple-element.21), kind=kLoop, calls=%fused_computation.20 | loop fusion | flops 4194304 | bytes 1050624 | tf_op jit(solution)/shard_map/convert_element_type | solution.py:31
  25.4 1.8 %collective-permute-done.1 = bf16[2,2,64,512]{3,2,1,0:T(8,128)(2,1)S(1)} collective-permute-done((bf16[2,2,64,512]{3,2,1,0:T(8,128)(2,1)S(1)}, bf16[2,2,64,512]{3,2,1,0:T(8,128)(2,1)S(1)}, u32[]{:S(2)}, u32[]{:S(2)}) %collective-permute-start.1) | collective-permute-done | bytes 262176 | tf_op jit(solution)/shard_map/ppermute | solution.py:50
  27.2 1.4 %collective-permute-start.2 = (bf16[4,2,64,512]{3,2,1,0:T(8,128)(2,1)S(1)}, bf16[4,2,64,512]{3,2,1,0:T(8,128)(2,1)S(1)}, u32[]{:S(2)}, u32[]{:S(2)}) collective-permute-start(bf16[4,2,64,512]{3,2,1,0:T(8,128)(2,1)S(1)} %pad_maximum_fusion.1), channel_id=1, source_target_pairs={{0,1},{1,0},{2,3},{3,2},{4,5},{5,4},{6,7},{7,6},{8,9},{9,8},{10,11... | collective-permute-start | bytes 1572872 | tf_op jit(solution)/shard_map/ppermute | solution.py:50
  29.2 1.6 %maximum_maximum_fusion.ct_ref = bf16[4,1024,256]{2,1,0:T(8,128)(2,1)} fusion(bf16[4,512,128]{2,1,0:T(8,128)(2,1)S(1)} %get-tuple-element.17, bf16[4,512,128]{2,1,0:T(8,128)(2,1)S(1)} %fusion.12, bf16[4,512,128]{2,1,0:T(8,128)(2,1)S(1)} %get-tuple-element.16), kind=kLoop, calls=%fused_computation.2 | loop fusion | flops 8388608 | bytes 3670016 | tf_op jit(solution)/shard_map/concatenate | solution.py:39
  30.8 5.6 %sine_convert_fusion = (bf16[4,128,512]{2,1,0:T(8,128)(2,1)}, bf16[4,128,512]{2,1,0:T(8,128)(2,1)}) fusion(s32[4,128]{1,0:T(4,128)S(1)} %get-tuple-element.20), kind=kLoop, calls=%fused_computation.16 | loop fusion | flops 4194304 | bytes 1050624 | tf_op jit(solution)/shard_map/convert_element_type | solution.py:31
  36.5 3.7 %collective-permute-done.2 = bf16[4,2,64,512]{3,2,1,0:T(8,128)(2,1)S(1)} collective-permute-done((bf16[4,2,64,512]{3,2,1,0:T(8,128)(2,1)S(1)}, bf16[4,2,64,512]{3,2,1,0:T(8,128)(2,1)S(1)}, u32[]{:S(2)}, u32[]{:S(2)}) %collective-permute-start.2) | collective-permute-done | bytes 524320 | tf_op jit(solution)/shard_map/ppermute | solution.py:50
  40.3 0.6 gather_fusion
  40.9 1.1 copy.13
  42.0 14.4 %shard_map.68.rest_0_ = f32[4,8,128,128]{3,2,1,0:T(8,128)} custom-call(s32[32]{0:T(128)} %reshape.177.f_ref, s32[1]{0:T(128)} %constant.104.clone.1.ta_ref.tb_ref, s32[1]{0:T(128)} %constant.104.clone.1.ta_ref.tb_ref, s32[1]{0:T(128)} %bitcast.1.rid_ref, s32[2]{0:T(128)} %add_multiply_fusion.off_ref, bf16[1,8,2,128,512]{4,3,2,1,0:T(8,128)(2,1)} %bitcast.11.tma_ref, ...), custom_call_target="tpu_custom_call" | custom-call | flops 4831838208 | bytes 10485760 | tf_op jit(solution)/shard_map/pallas_call | solution.py:267
  56.4 14.2 %all-gather.3.cloned.1.call-done = bf16[32,2,128,512]{3,2,1,0:T(8,128)(2,1)} async-done(((bf16[8,2,128,512]{3,2,1,0:T(8,128)(2,1)}), bf16[32,2,128,512]{3,2,1,0:T(8,128)(2,1)}) %all-gather.3.cloned.1.call-update) | async-done | bytes 8388624 | tf_op jit(solution)/shard_map/all_gather | solution.py:287
  70.6 14.9 %shard_map.69 = f32[2,4,128,128]{3,2,1,0:T(8,128)} custom-call(s32[32]{0:T(128)} %reshape.177.f_ref, s32[1]{0:T(128)S(6)} %mul.65.ta_ref, s32[1]{0:T(128)S(6)} %add.152.tb_ref, s32[1]{0:T(128)S(6)} %convert_element_type.34.rid_ref, s32[2]{0:T(128)} %iota_multiply_fusion.off_ref, bf16[4,8,2,128,512]{4,3,2,1,0:T(8,128)(2,1)} %bitcast.28, ...), custom_call_target="tpu_custom_call" | custom-call | flops 4831838208 | bytes 10485760 | tf_op jit(solution)/shard_map/pallas_call | solution.py:267
  85.5 1.0 constant_dynamic-slice_fusion
  86.4 1.5 %collective-permute-start.4 = (f32[2,256,128]{2,1,0:T(8,128)S(1)}, f32[2,256,128]{2,1,0:T(8,128)S(1)}, u32[]{:S(2)}, u32[]{:S(2)}) collective-permute-start(f32[2,256,128]{2,1,0:T(8,128)S(1)} %constant_dynamic-slice_fusion), channel_id=1, source_target_pairs={{0,1},{1,0},{2,3},{3,2},{4,5},{5,4},{6,7},{7,6},{8,9},{9,8},{10,11... | collective-permute-start | bytes 786440 | tf_op jit(solution)/shard_map/ppermute | solution.py:90
  87.9 7.0 %collective-permute-done.4 = f32[2,256,128]{2,1,0:T(8,128)S(1)} collective-permute-done((f32[2,256,128]{2,1,0:T(8,128)S(1)}, f32[2,256,128]{2,1,0:T(8,128)S(1)}, u32[]{:S(2)}, u32[]{:S(2)}) %collective-permute-start.4) | collective-permute-done | bytes 262176 | tf_op jit(solution)/shard_map/ppermute | solution.py:90
  95.0 1.0 slice_add_fusion
  96.0 1.6 %collective-permute-start.5 = (f32[2,64,128]{2,1,0:T(8,128)S(1)}, f32[2,64,128]{2,1,0:T(8,128)S(1)}, u32[]{:S(2)}, u32[]{:S(2)}) collective-permute-start(f32[2,64,128]{2,1,0:T(8,128)S(1)} %get-tuple-element.9), channel_id=1, source_target_pairs={{0,2},{1,3},{2,0},{3,1},{4,6},{5,7},{6,4},{7,5},{8,10},{9,11},{10,... | collective-permute-start | bytes 196616 | tf_op jit(solution)/shard_map/ppermute | solution.py:99
  97.6 2.4 %collective-permute-start.6 = (f32[2,64,128]{2,1,0:T(8,128)S(1)}, f32[2,64,128]{2,1,0:T(8,128)S(1)}, u32[]{:S(2)}, u32[]{:S(2)}) collective-permute-start(f32[2,64,128]{2,1,0:T(8,128)S(1)} %get-tuple-element.10), channel_id=1, source_target_pairs={{0,4},{1,5},{2,6},{3,7},{4,0},{5,1},{6,2},{7,3},{8,12},{9,13},{10,... | collective-permute-start | bytes 196616 | tf_op jit(solution)/shard_map/ppermute | solution.py:99
  100.5 4.0 %collective-permute-done.6 = f32[2,64,128]{2,1,0:T(8,128)S(1)} collective-permute-done((f32[2,64,128]{2,1,0:T(8,128)S(1)}, f32[2,64,128]{2,1,0:T(8,128)S(1)}, u32[]{:S(2)}, u32[]{:S(2)}) %collective-permute-start.6) | collective-permute-done | bytes 65568 | tf_op jit(solution)/shard_map/ppermute | solution.py:99
  104.5 1.6 %collective-permute-done.7 = f32[2,64,128]{2,1,0:T(8,128)S(1)} collective-permute-done((f32[2,64,128]{2,1,0:T(8,128)S(1)}, f32[2,64,128]{2,1,0:T(8,128)S(1)}, u32[]{:S(2)}, u32[]{:S(2)}) %collective-permute-start.7) | collective-permute-done | bytes 65568 | tf_op jit(solution)/shard_map/ppermute | solution.py:99
  106.2 1.9 %collective-permute-start.9 = (f32[2,64,128]{2,1,0:T(8,128)S(1)}, f32[2,64,128]{2,1,0:T(8,128)S(1)}, u32[]{:S(2)}, u32[]{:S(2)}) collective-permute-start(f32[2,64,128]{2,1,0:T(8,128)S(1)} %get-tuple-element.13), channel_id=1, source_target_pairs={{0,4},{1,5},{2,6},{3,7},{4,0},{5,1},{6,2},{7,3},{8,12},{9,13},{10,... | collective-permute-start | bytes 196616 | tf_op jit(solution)/shard_map/ppermute | solution.py:103
  108.1 2.4 %collective-permute-start.10 = (f32[2,64,128]{2,1,0:T(8,128)S(1)}, f32[2,64,128]{2,1,0:T(8,128)S(1)}, u32[]{:S(2)}, u32[]{:S(2)}) collective-permute-start(f32[2,64,128]{2,1,0:T(8,128)S(1)} %get-tuple-element.13), channel_id=1, source_target_pairs={{0,6},{1,7},{2,4},{3,5},{4,2},{5,3},{6,0},{7,1},{8,14},{9,15},{10,... | collective-permute-start | bytes 196616 | tf_op jit(solution)/shard_map/ppermute | solution.py:103
  110.6 1.3 collective-permute-done.8
  111.8 2.4 %collective-permute-done.10 = f32[2,64,128]{2,1,0:T(8,128)S(1)} collective-permute-done((f32[2,64,128]{2,1,0:T(8,128)S(1)}, f32[2,64,128]{2,1,0:T(8,128)S(1)}, u32[]{:S(2)}, u32[]{:S(2)}) %collective-permute-start.10) | collective-permute-done | bytes 65568 | tf_op jit(solution)/shard_map/ppermute | solution.py:103
  114.8 1.6 %collective-permute-start.11 = (f32[2,256,128]{2,1,0:T(8,128)S(1)}, f32[2,256,128]{2,1,0:T(8,128)S(1)}, u32[]{:S(2)}, u32[]{:S(2)}) collective-permute-start(f32[2,256,128]{2,1,0:T(8,128)S(1)} %bitcast.36), channel_id=1, source_target_pairs={{0,1},{1,0},{2,3},{3,2},{4,5},{5,4},{6,7},{7,6},{8,9},{9,8},{10,11... | collective-permute-start | bytes 786440 | tf_op jit(solution)/shard_map/ppermute | solution.py:106
  116.4 4.8 %collective-permute-done.11 = f32[2,256,128]{2,1,0:T(8,128)S(1)} collective-permute-done((f32[2,256,128]{2,1,0:T(8,128)S(1)}, f32[2,256,128]{2,1,0:T(8,128)S(1)}, u32[]{:S(2)}, u32[]{:S(2)}) %collective-permute-start.11) | collective-permute-done | bytes 262176 | tf_op jit(solution)/shard_map/ppermute | solution.py:106
  121.3 0.8 slice_multiply_fusion
  (35 shorter events, 3.5 us)
Async XLA Ops:
  7.2 1.3 copy-start
  7.2 5.0 %copy-start.2 = (s32[1,4,2]{1,2,0:T(2,128)S(1)}, s32[1,4,2]{1,2,0:T(2,128)}, u32[]{:S(2)}) copy-start(s32[1,4,2]{1,2,0:T(2,128)} %param.7) | copy-start | bytes 100
  7.2 9.1 %copy-start.1 = (s32[1,4,48]{2,1,0:T(4,128)S(1)}, s32[1,4,48]{2,1,0:T(4,128)}, u32[]{:S(2)}) copy-start(s32[1,4,48]{2,1,0:T(4,128)} %param.8) | copy-start | bytes 2308
  7.2 63.4 %all-gather.3.cloned.1.call-start = ((), (), s32[]{:S(2)}) async-start(), calls=%async_computation | async-start | bytes 10485760 | tf_op jit(solution)/shard_map/all_gather | solution.py:287
  7.9 34.1 %collective-permute-start.3 = (bf16[8,2,128,512]{3,2,1,0:T(8,128)(2,1)}, bf16[8,2,128,512]{3,2,1,0:T(8,128)(2,1)}, u32[]{:S(2)}, u32[]{:S(2)}) collective-permute-start(bf16[8,2,128,512]{3,2,1,0:T(8,128)(2,1)} %param.6), channel_id=1, source_target_pairs={{0,8},{8,0},{16,24},{24,16},{1,9},{9,1},{17,25},{25,17},{2,10},{10... | collective-permute-start | bytes 6291464 | tf_op jit(solution)/shard_map/ppermute | solution.py:305
  8.4 10.6 %collective-permute-start = (bf16[1,2,64,512]{3,2,1,0:T(8,128)(2,1)S(1)}, bf16[1,2,64,512]{3,2,1,0:T(8,128)(2,1)S(1)}, u32[]{:S(2)}, u32[]{:S(2)}) collective-permute-start(bf16[1,2,64,512]{3,2,1,0:T(8,128)(2,1)S(1)} %copy-done), channel_id=1, source_target_pairs={{0,4},{1,5},{2,6},{3,7},{4,0},{5,1},{6,2},{7,3},{8,12},{9,13},{10,... | collective-permute-start | bytes 393224 | tf_op jit(solution)/shard_map/ppermute | solution.py:50
  19.0 8.1 %collective-permute-start.1 = (bf16[2,2,64,512]{3,2,1,0:T(8,128)(2,1)S(1)}, bf16[2,2,64,512]{3,2,1,0:T(8,128)(2,1)S(1)}, u32[]{:S(2)}, u32[]{:S(2)}) collective-permute-start(bf16[2,2,64,512]{3,2,1,0:T(8,128)(2,1)S(1)} %pad_maximum_fusion.2), channel_id=1, source_target_pairs={{0,2},{1,3},{2,0},{3,1},{4,6},{5,7},{6,4},{7,5},{8,10},{9,11},{10,... | collective-permute-start | bytes 786440 | tf_op jit(solution)/shard_map/ppermute | solution.py:50
  27.2 13.0 %collective-permute-start.2 = (bf16[4,2,64,512]{3,2,1,0:T(8,128)(2,1)S(1)}, bf16[4,2,64,512]{3,2,1,0:T(8,128)(2,1)S(1)}, u32[]{:S(2)}, u32[]{:S(2)}) collective-permute-start(bf16[4,2,64,512]{3,2,1,0:T(8,128)(2,1)S(1)} %pad_maximum_fusion.1), channel_id=1, source_target_pairs={{0,1},{1,0},{2,3},{3,2},{4,5},{5,4},{6,7},{7,6},{8,9},{9,8},{10,11... | collective-permute-start | bytes 1572872 | tf_op jit(solution)/shard_map/ppermute | solution.py:50
  86.4 8.5 %collective-permute-start.4 = (f32[2,256,128]{2,1,0:T(8,128)S(1)}, f32[2,256,128]{2,1,0:T(8,128)S(1)}, u32[]{:S(2)}, u32[]{:S(2)}) collective-permute-start(f32[2,256,128]{2,1,0:T(8,128)S(1)} %constant_dynamic-slice_fusion), channel_id=1, source_target_pairs={{0,1},{1,0},{2,3},{3,2},{4,5},{5,4},{6,7},{7,6},{8,9},{9,8},{10,11... | collective-permute-start | bytes 786440 | tf_op jit(solution)/shard_map/ppermute | solution.py:90
  96.0 4.5 %collective-permute-start.5 = (f32[2,64,128]{2,1,0:T(8,128)S(1)}, f32[2,64,128]{2,1,0:T(8,128)S(1)}, u32[]{:S(2)}, u32[]{:S(2)}) collective-permute-start(f32[2,64,128]{2,1,0:T(8,128)S(1)} %get-tuple-element.9), channel_id=1, source_target_pairs={{0,2},{1,3},{2,0},{3,1},{4,6},{5,7},{6,4},{7,5},{8,10},{9,11},{10,... | collective-permute-start | bytes 196616 | tf_op jit(solution)/shard_map/ppermute | solution.py:99
  97.6 6.9 %collective-permute-start.6 = (f32[2,64,128]{2,1,0:T(8,128)S(1)}, f32[2,64,128]{2,1,0:T(8,128)S(1)}, u32[]{:S(2)}, u32[]{:S(2)}) collective-permute-start(f32[2,64,128]{2,1,0:T(8,128)S(1)} %get-tuple-element.10), channel_id=1, source_target_pairs={{0,4},{1,5},{2,6},{3,7},{4,0},{5,1},{6,2},{7,3},{8,12},{9,13},{10,... | collective-permute-start | bytes 196616 | tf_op jit(solution)/shard_map/ppermute | solution.py:99
  100.0 6.1 %collective-permute-start.7 = (f32[2,64,128]{2,1,0:T(8,128)S(1)}, f32[2,64,128]{2,1,0:T(8,128)S(1)}, u32[]{:S(2)}, u32[]{:S(2)}) collective-permute-start(f32[2,64,128]{2,1,0:T(8,128)S(1)} %get-tuple-element.11), channel_id=1, source_target_pairs={{0,6},{1,7},{2,4},{3,5},{4,2},{5,3},{6,0},{7,1},{8,14},{9,15},{10,... | collective-permute-start | bytes 196616 | tf_op jit(solution)/shard_map/ppermute | solution.py:99
  106.1 5.7 %collective-permute-start.8 = (f32[2,64,128]{2,1,0:T(8,128)S(1)}, f32[2,64,128]{2,1,0:T(8,128)S(1)}, u32[]{:S(2)}, u32[]{:S(2)}) collective-permute-start(f32[2,64,128]{2,1,0:T(8,128)S(1)} %get-tuple-element.13), channel_id=1, source_target_pairs={{0,2},{1,3},{2,0},{3,1},{4,6},{5,7},{6,4},{7,5},{8,10},{9,11},{10,... | collective-permute-start | bytes 196616 | tf_op jit(solution)/shard_map/ppermute | solution.py:103
  106.2 5.7 %collective-permute-start.9 = (f32[2,64,128]{2,1,0:T(8,128)S(1)}, f32[2,64,128]{2,1,0:T(8,128)S(1)}, u32[]{:S(2)}, u32[]{:S(2)}) collective-permute-start(f32[2,64,128]{2,1,0:T(8,128)S(1)} %get-tuple-element.13), channel_id=1, source_target_pairs={{0,4},{1,5},{2,6},{3,7},{4,0},{5,1},{6,2},{7,3},{8,12},{9,13},{10,... | collective-permute-start | bytes 196616 | tf_op jit(solution)/shard_map/ppermute | solution.py:103
  108.1 6.1 %collective-permute-start.10 = (f32[2,64,128]{2,1,0:T(8,128)S(1)}, f32[2,64,128]{2,1,0:T(8,128)S(1)}, u32[]{:S(2)}, u32[]{:S(2)}) collective-permute-start(f32[2,64,128]{2,1,0:T(8,128)S(1)} %get-tuple-element.13), channel_id=1, source_target_pairs={{0,6},{1,7},{2,4},{3,5},{4,2},{5,3},{6,0},{7,1},{8,14},{9,15},{10,... | collective-permute-start | bytes 196616 | tf_op jit(solution)/shard_map/ppermute | solution.py:103
  114.8 6.4 %collective-permute-start.11 = (f32[2,256,128]{2,1,0:T(8,128)S(1)}, f32[2,256,128]{2,1,0:T(8,128)S(1)}, u32[]{:S(2)}, u32[]{:S(2)}) collective-permute-start(f32[2,256,128]{2,1,0:T(8,128)S(1)} %bitcast.36), channel_id=1, source_target_pairs={{0,1},{1,0},{2,3},{3,2},{4,5},{5,4},{6,7},{7,6},{8,9},{9,8},{10,11... | collective-permute-start | bytes 786440 | tf_op jit(solution)/shard_map/ppermute | solution.py:106
Sparse Core Ops, SparseCore 0:
  9.6 60.9 all-gather.2

commit v18 on v15

--- a/solution.py
+++ b/solution.py
@@ -83,28 +83,28 @@
         power = lax.psum(joined[1], axis)
         return best.reshape(shape), power.reshape(shape)
     me = lax.axis_index(axis)
-    half = rows // 2
     bit = me % 2
-    keep = lax.dynamic_slice_in_dim(joined, bit * half, half, axis=1)
-    send = lax.dynamic_slice_in_dim(joined, (1 - bit) * half, half, axis=1)
-    got = lax.ppermute(send, axis, xor_pairs(n, 1))
-    cur = jnp.stack([jnp.maximum(keep[0], got[0]), keep[1] + got[1]])
     members = n // 2
     group = me // 2
-    piece = half // members
-    own = lax.dynamic_slice_in_dim(cur, group * piece, piece, axis=1)
+    quarter = rows // members
+    own = lax.dynamic_slice_in_dim(joined, group * quarter, quarter, axis=1)
     best, power = own[0], own[1]
     for m in range(1, members):
-        out = lax.dynamic_slice_in_dim(cur, (group ^ m) * piece, piece, axis=1)
+        out = lax.dynamic_slice_in_dim(joined, (group ^ m) * quarter, quarter, axis=1)
         got = lax.ppermute(out, axis, xor_pairs(n, 2 * m))
         best = jnp.maximum(best, got[0])
         power = power + got[1]
-    done = jnp.stack([best, power])
-    slots = [done] + [lax.ppermute(done, axis, xor_pairs(n, 2 * m)) for m in range(1, members)]
+    cur = jnp.stack([best, power])
+    half = quarter // 2
+    keep = lax.dynamic_slice_in_dim(cur, bit * half, half, axis=1)
+    send = lax.dynamic_slice_in_dim(cur, (1 - bit) * half, half, axis=1)
+    got = lax.ppermute(send, axis, xor_pairs(n, 1))
+    done = jnp.stack([jnp.maximum(keep[0], got[0]), keep[1] + got[1]])
+    other = lax.ppermute(done, axis, xor_pairs(n, 1))
+    mine = jnp.where(bit == 1, jnp.concatenate([other, done], axis=1), jnp.concatenate([done, other], axis=1))
+    slots = [mine] + [lax.ppermute(mine, axis, xor_pairs(n, 2 * m)) for m in range(1, members)]
     pieces = jnp.stack(slots)[jnp.arange(members, dtype=jnp.int32) ^ group]
-    mine = jnp.moveaxis(pieces, 0, 1).reshape(2, half, joined.shape[2])
-    other = lax.ppermute(mine, axis, xor_pairs(n, 1))
-    whole = jnp.where(bit == 1, jnp.concatenate([other, mine], axis=1), jnp.concatenate([mine, other], axis=1))
+    whole = jnp.moveaxis(pieces, 0, 1).reshape(2, rows, joined.shape[2])
     return whole[0].reshape(shape), whole[1].reshape(shape)
 
 

time: 130 us -> 132 us (1.015)
  waiting for transfers between devices: 43.7 us -> 45.8 us
    ppermute x3, waiting for transfers between devices: 5.59 us -> 10 us  [reduce_joined(): got = lax.ppermute(out, axis, xor_pairs(n, 2 * m))]
    ppermute x1, waiting for transfers between devices: 6.99 us -> 3.14 us  [reduce_joined(): got = lax.ppermute(send, axis, xor_pairs(n, 1))]
    ppermute x4, waiting for transfers between devices: 8.72 us -> 10.3 us  [the longest x3 7.48 us: reduce_joined(): lax.ppermute(mine, axis, xor_pairs(n, 2 * m))]
  transfers between devices with their start and end apart: 13 -> 13, of which waited for: 11 -> 10; matrix products, arithmetic and copies ran while one was open for 15% -> 15% of each run, Pallas kernels for 11% -> 11%
where the time goes in v18:
time: 132 us
  waiting for transfers between devices  45.8 us (35%)
  Pallas kernels  30.1 us (23%)
  other arithmetic  19.1 us (14%)
  starting transfers between devices  18.6 us (14%)
  between operations  14.2 us (11%)
  local copies, waits for them, and re-layouts  3.97 us (3%)
    pallas_call x2, Pallas kernels, match_rows(): pl.pallas_call(kernel, grid_spec=pltpu.PrefetchScalarGridSpec(num_scalar_...  30.1 us
    all_gather x1, waiting for transfers between devices, local(): tmpl = lax.all_gather(template_spectra, 'tile', axis=0)  13.8 us
    ppermute x3, waiting for transfers between devices, reduce_joined(): got = lax.ppermute(out, axis, xor_pairs(n, 2 * m))  10 us
    convert_element_type x2, other arithmetic, angle_tables(): jnp.sin(angle).astype(jnp.bfloat16)  10 us
    ppermute x3, waiting for transfers between devices, gather_rows(): got = lax.ppermute(blocks, axis, xor_pairs(n, k))  7.96 us
    ppermute x3, waiting for transfers between devices, reduce_joined(): lax.ppermute(mine, axis, xor_pairs(n, 2 * m))  7.48 us
    ppermute x3, starting transfers between devices, gather_rows(): got = lax.ppermute(blocks, axis, xor_pairs(n, k))  5.92 us
    ppermute x3, starting transfers between devices, reduce_joined(): lax.ppermute(mine, axis, xor_pairs(n, 2 * m))  4.55 us
  transfers between devices with their start and end apart: 13, of which 10 were waited for; matrix products, arithmetic and copies ran while one was open for 15% of the time, Pallas kernels for 11%

profile of v18, /device:TPU:0, one launch (start us, length us, event | category | flops | bytes accessed | tf_op | source)
XLA Modules:
  0.0 131.8 jit_solution(13377093956219034454)
XLA Ops:
  7.2 0.7 all-gather.3.cloned.1.call-update
  8.4 3.7 %collective-permute-start = (bf16[1,2,64,512]{3,2,1,0:T(8,128)(2,1)S(1)}, bf16[1,2,64,512]{3,2,1,0:T(8,128)(2,1)S(1)}, u32[]{:S(2)}, u32[]{:S(2)}) collective-permute-start(bf16[1,2,64,512]{3,2,1,0:T(8,128)(2,1)S(1)} %copy-done), channel_id=1, source_target_pairs={{0,4},{1,5},{2,6},{3,7},{4,0},{5,1},{6,2},{7,3},{8,12},{9,13},{10,... | collective-permute-start | bytes 393224 | tf_op jit(solution)/shard_map/ppermute | solution.py:50
  12.3 4.0 %fusion.13 = bf16[4,512,128]{2,1,0:T(8,128)(2,1)S(1)} fusion(s32[4,128]{1,0:T(4,128)S(1)} %get-tuple-element.28), kind=kLoop, calls=%fused_computation.36 | loop fusion | flops 4718592 | bytes 526336 | tf_op jit(solution)/shard_map/neg | solution.py:38
  16.5 2.5 %collective-permute-done = bf16[1,2,64,512]{3,2,1,0:T(8,128)(2,1)S(1)} collective-permute-done((bf16[1,2,64,512]{3,2,1,0:T(8,128)(2,1)S(1)}, bf16[1,2,64,512]{3,2,1,0:T(8,128)(2,1)S(1)}, u32[]{:S(2)}, u32[]{:S(2)}) %collective-permute-start) | collective-permute-done | bytes 131104 | tf_op jit(solution)/shard_map/ppermute | solution.py:50
  19.0 0.8 collective-permute-start.1
  21.0 4.4 %sine_convert_fusion.1 = (bf16[4,512,128]{2,1,0:T(8,128)(2,1)S(1)}, bf16[4,512,128]{2,1,0:T(8,128)(2,1)S(1)}) fusion(s32[4,128]{1,0:T(4,128)S(1)} %get-tuple-element.28), kind=kLoop, calls=%fused_computation.20 | loop fusion | flops 4194304 | bytes 1050624 | tf_op jit(solution)/shard_map/convert_element_type | solution.py:31
  25.4 1.8 %collective-permute-done.1 = bf16[2,2,64,512]{3,2,1,0:T(8,128)(2,1)S(1)} collective-permute-done((bf16[2,2,64,512]{3,2,1,0:T(8,128)(2,1)S(1)}, bf16[2,2,64,512]{3,2,1,0:T(8,128)(2,1)S(1)}, u32[]{:S(2)}, u32[]{:S(2)}) %collective-permute-start.1) | collective-permute-done | bytes 262176 | tf_op jit(solution)/shard_map/ppermute | solution.py:50
  27.2 1.4 %collective-permute-start.2 = (bf16[4,2,64,512]{3,2,1,0:T(8,128)(2,1)S(1)}, bf16[4,2,64,512]{3,2,1,0:T(8,128)(2,1)S(1)}, u32[]{:S(2)}, u32[]{:S(2)}) collective-permute-start(bf16[4,2,64,512]{3,2,1,0:T(8,128)(2,1)S(1)} %pad_maximum_fusion.1), channel_id=1, source_target_pairs={{0,1},{1,0},{2,3},{3,2},{4,5},{5,4},{6,7},{7,6},{8,9},{9,8},{10,11... | collective-permute-start | bytes 1572872 | tf_op jit(solution)/shard_map/ppermute | solution.py:50
  28.6 0.7 add_multiply_fusion.off_ref
  29.3 1.6 %maximum_maximum_fusion.ct_ref = bf16[4,1024,256]{2,1,0:T(8,128)(2,1)} fusion(bf16[4,512,128]{2,1,0:T(8,128)(2,1)S(1)} %get-tuple-element.24, bf16[4,512,128]{2,1,0:T(8,128)(2,1)S(1)} %fusion.13, bf16[4,512,128]{2,1,0:T(8,128)(2,1)S(1)} %get-tuple-element.23), kind=kLoop, calls=%fused_computation.2 | loop fusion | flops 8388608 | bytes 3670016 | tf_op jit(solution)/shard_map/concatenate | solution.py:39
  30.9 5.6 %sine_convert_fusion = (bf16[4,128,512]{2,1,0:T(8,128)(2,1)}, bf16[4,128,512]{2,1,0:T(8,128)(2,1)}) fusion(s32[4,128]{1,0:T(4,128)S(1)} %get-tuple-element.27), kind=kLoop, calls=%fused_computation.16 | loop fusion | flops 4194304 | bytes 1050624 | tf_op jit(solution)/shard_map/convert_element_type | solution.py:31
  36.5 3.7 %collective-permute-done.2 = bf16[4,2,64,512]{3,2,1,0:T(8,128)(2,1)S(1)} collective-permute-done((bf16[4,2,64,512]{3,2,1,0:T(8,128)(2,1)S(1)}, bf16[4,2,64,512]{3,2,1,0:T(8,128)(2,1)S(1)}, u32[]{:S(2)}, u32[]{:S(2)}) %collective-permute-start.2) | collective-permute-done | bytes 524320 | tf_op jit(solution)/shard_map/ppermute | solution.py:50
  40.9 1.1 copy.14
  42.0 14.8 %shard_map.68.rest_0_ = f32[4,8,128,128]{3,2,1,0:T(8,128)} custom-call(s32[32]{0:T(128)} %reshape.221.f_ref, s32[1]{0:T(128)} %constant.104.clone.1.ta_ref.tb_ref, s32[1]{0:T(128)} %constant.104.clone.1.ta_ref.tb_ref, s32[1]{0:T(128)} %bitcast.1.rid_ref, s32[2]{0:T(128)} %add_multiply_fusion.off_ref, bf16[1,8,2,128,512]{4,3,2,1,0:T(8,128)(2,1)} %bitcast.11.tma_ref, ...), custom_call_target="tpu_custom_call" | custom-call | flops 4831838208 | bytes 10485760 | tf_op jit(solution)/shard_map/pallas_call | solution.py:267
  56.8 13.8 %all-gather.3.cloned.1.call-done = bf16[32,2,128,512]{3,2,1,0:T(8,128)(2,1)} async-done(((bf16[8,2,128,512]{3,2,1,0:T(8,128)(2,1)}), bf16[32,2,128,512]{3,2,1,0:T(8,128)(2,1)}) %all-gather.3.cloned.1.call-update) | async-done | bytes 8388624 | tf_op jit(solution)/shard_map/all_gather | solution.py:287
  70.6 15.3 %shard_map.69 = f32[2,4,128,128]{3,2,1,0:T(8,128)} custom-call(s32[32]{0:T(128)} %reshape.221.f_ref, s32[1]{0:T(128)S(6)} %mul.65.ta_ref, s32[1]{0:T(128)S(6)} %add.152.tb_ref, s32[1]{0:T(128)S(6)} %convert_element_type.34.rid_ref, s32[2]{0:T(128)} %iota_multiply_fusion.off_ref, bf16[4,8,2,128,512]{4,3,2,1,0:T(8,128)(2,1)} %bitcast.30, ...), custom_call_target="tpu_custom_call" | custom-call | flops 4831838208 | bytes 10485760 | tf_op jit(solution)/shard_map/pallas_call | solution.py:267
  85.9 1.1 constant_dynamic-slice_fusion.2
  87.0 1.6 %collective-permute-start.4 = (f32[2,128,128]{2,1,0:T(8,128)S(1)}, f32[2,128,128]{2,1,0:T(8,128)S(1)}, u32[]{:S(2)}, u32[]{:S(2)}) collective-permute-start(f32[2,128,128]{2,1,0:T(8,128)S(1)} %get-tuple-element.12), channel_id=1, source_target_pairs={{0,2},{1,3},{2,0},{3,1},{4,6},{5,7},{6,4},{7,5},{8,10},{9,11},{10,... | collective-permute-start | bytes 393224 | tf_op jit(solution)/shard_map/ppermute | solution.py:94
  88.6 2.4 %collective-permute-start.5 = (f32[2,128,128]{2,1,0:T(8,128)S(1)}, f32[2,128,128]{2,1,0:T(8,128)S(1)}, u32[]{:S(2)}, u32[]{:S(2)}) collective-permute-start(f32[2,128,128]{2,1,0:T(8,128)S(1)} %get-tuple-element.14), channel_id=1, source_target_pairs={{0,4},{1,5},{2,6},{3,7},{4,0},{5,1},{6,2},{7,3},{8,12},{9,13},{10,... | collective-permute-start | bytes 393224 | tf_op jit(solution)/shard_map/ppermute | solution.py:94
  91.4 3.3 %collective-permute-done.4 = f32[2,128,128]{2,1,0:T(8,128)S(1)} collective-permute-done((f32[2,128,128]{2,1,0:T(8,128)S(1)}, f32[2,128,128]{2,1,0:T(8,128)S(1)}, u32[]{:S(2)}, u32[]{:S(2)}) %collective-permute-start.4) | collective-permute-done | bytes 131104 | tf_op jit(solution)/shard_map/ppermute | solution.py:94
  94.8 6.7 %collective-permute-done.5 = f32[2,128,128]{2,1,0:T(8,128)S(1)} collective-permute-done((f32[2,128,128]{2,1,0:T(8,128)S(1)}, f32[2,128,128]{2,1,0:T(8,128)S(1)}, u32[]{:S(2)}, u32[]{:S(2)}) %collective-permute-start.5) | collective-permute-done | bytes 131104 | tf_op jit(solution)/shard_map/ppermute | solution.py:94
  101.5 0.9 slice_add_fusion
  102.4 1.5 %collective-permute-start.7 = (f32[2,64,128]{2,1,0:T(8,128)S(1)}, f32[2,64,128]{2,1,0:T(8,128)S(1)}, u32[]{:S(2)}, u32[]{:S(2)}) collective-permute-start(f32[2,64,128]{2,1,0:T(8,128)S(1)} %get-tuple-element.18), channel_id=1, source_target_pairs={{0,1},{1,0},{2,3},{3,2},{4,5},{5,4},{6,7},{7,6},{8,9},{9,8},{10,11... | collective-permute-start | bytes 196616 | tf_op jit(solution)/shard_map/ppermute | solution.py:101
  103.9 3.1 %collective-permute-done.7 = f32[2,64,128]{2,1,0:T(8,128)S(1)} collective-permute-done((f32[2,64,128]{2,1,0:T(8,128)S(1)}, f32[2,64,128]{2,1,0:T(8,128)S(1)}, u32[]{:S(2)}, u32[]{:S(2)}) %collective-permute-start.7) | collective-permute-done | bytes 65568 | tf_op jit(solution)/shard_map/ppermute | solution.py:101
  107.1 1.5 %collective-permute-start.8 = (f32[2,64,128]{2,1,0:T(8,128)S(1)}, f32[2,64,128]{2,1,0:T(8,128)S(1)}, u32[]{:S(2)}, u32[]{:S(2)}) collective-permute-start(f32[2,64,128]{2,1,0:T(8,128)S(1)} %get-tuple-element.20), channel_id=1, source_target_pairs={{0,1},{1,0},{2,3},{3,2},{4,5},{5,4},{6,7},{7,6},{8,9},{9,8},{10,11... | collective-permute-start | bytes 196616 | tf_op jit(solution)/shard_map/ppermute | solution.py:103
  108.7 2.8 %collective-permute-done.8 = f32[2,64,128]{2,1,0:T(8,128)S(1)} collective-permute-done((f32[2,64,128]{2,1,0:T(8,128)S(1)}, f32[2,64,128]{2,1,0:T(8,128)S(1)}, u32[]{:S(2)}, u32[]{:S(2)}) %collective-permute-start.8) | collective-permute-done | bytes 65568 | tf_op jit(solution)/shard_map/ppermute | solution.py:103
  111.5 2.1 %collective-permute-start.9 = (f32[2,128,128]{2,1,0:T(8,128)S(1)}, f32[2,128,128]{2,1,0:T(8,128)S(1)}, u32[]{:S(2)}, u32[]{:S(2)}) collective-permute-start(f32[2,128,128]{2,1,0:T(8,128)S(1)} %maximum_select_fusion.1), channel_id=1, source_target_pairs={{0,2},{1,3},{2,0},{3,1},{4,6},{5,7},{6,4},{7,5},{8,10},{9,11},{10,... | collective-permute-start | bytes 393224 | tf_op jit(solution)/shard_map/ppermute | solution.py:105
  113.6 0.9 collective-permute-start.10
  114.5 1.5 %collective-permute-start.11 = (f32[2,128,128]{2,1,0:T(8,128)S(1)}, f32[2,128,128]{2,1,0:T(8,128)S(1)}, u32[]{:S(2)}, u32[]{:S(2)}) collective-permute-start(f32[2,128,128]{2,1,0:T(8,128)S(1)} %maximum_select_fusion.1), channel_id=1, source_target_pairs={{0,6},{1,7},{2,4},{3,5},{4,2},{5,3},{6,0},{7,1},{8,14},{9,15},{10,... | collective-permute-start | bytes 393224 | tf_op jit(solution)/shard_map/ppermute | solution.py:105
  116.0 2.1 %collective-permute-done.9 = f32[2,128,128]{2,1,0:T(8,128)S(1)} collective-permute-done((f32[2,128,128]{2,1,0:T(8,128)S(1)}, f32[2,128,128]{2,1,0:T(8,128)S(1)}, u32[]{:S(2)}, u32[]{:S(2)}) %collective-permute-start.9) | collective-permute-done | bytes 131104 | tf_op jit(solution)/shard_map/ppermute | solution.py:105
  118.2 5.3 %collective-permute-done.10 = f32[2,128,128]{2,1,0:T(8,128)S(1)} collective-permute-done((f32[2,128,128]{2,1,0:T(8,128)S(1)}, f32[2,128,128]{2,1,0:T(8,128)S(1)}, u32[]{:S(2)}, u32[]{:S(2)}) %collective-permute-start.10) | collective-permute-done | bytes 131104 | tf_op jit(solution)/shard_map/ppermute | solution.py:105
  124.2 0.8 fusion.12
  (35 shorter events, 4.0 us)
Async XLA Ops:
  7.2 1.3 copy-start
  7.2 5.0 %copy-start.2 = (s32[1,4,2]{1,2,0:T(2,128)S(1)}, s32[1,4,2]{1,2,0:T(2,128)}, u32[]{:S(2)}) copy-start(s32[1,4,2]{1,2,0:T(2,128)} %param.7) | copy-start | bytes 100
  7.2 9.1 %copy-start.1 = (s32[1,4,48]{2,1,0:T(4,128)S(1)}, s32[1,4,48]{2,1,0:T(4,128)}, u32[]{:S(2)}) copy-start(s32[1,4,48]{2,1,0:T(4,128)} %param.8) | copy-start | bytes 2308
  7.2 63.4 %all-gather.3.cloned.1.call-start = ((), (), s32[]{:S(2)}) async-start(), calls=%async_computation | async-start | bytes 10485760 | tf_op jit(solution)/shard_map/all_gather | solution.py:287
  7.9 34.1 %collective-permute-start.3 = (bf16[8,2,128,512]{3,2,1,0:T(8,128)(2,1)}, bf16[8,2,128,512]{3,2,1,0:T(8,128)(2,1)}, u32[]{:S(2)}, u32[]{:S(2)}) collective-permute-start(bf16[8,2,128,512]{3,2,1,0:T(8,128)(2,1)} %param.6), channel_id=1, source_target_pairs={{0,8},{8,0},{16,24},{24,16},{1,9},{9,1},{17,25},{25,17},{2,10},{10... | collective-permute-start | bytes 6291464 | tf_op jit(solution)/shard_map/ppermute | solution.py:305
  8.4 10.6 %collective-permute-start = (bf16[1,2,64,512]{3,2,1,0:T(8,128)(2,1)S(1)}, bf16[1,2,64,512]{3,2,1,0:T(8,128)(2,1)S(1)}, u32[]{:S(2)}, u32[]{:S(2)}) collective-permute-start(bf16[1,2,64,512]{3,2,1,0:T(8,128)(2,1)S(1)} %copy-done), channel_id=1, source_target_pairs={{0,4},{1,5},{2,6},{3,7},{4,0},{5,1},{6,2},{7,3},{8,12},{9,13},{10,... | collective-permute-start | bytes 393224 | tf_op jit(solution)/shard_map/ppermute | solution.py:50
  19.0 8.1 %collective-permute-start.1 = (bf16[2,2,64,512]{3,2,1,0:T(8,128)(2,1)S(1)}, bf16[2,2,64,512]{3,2,1,0:T(8,128)(2,1)S(1)}, u32[]{:S(2)}, u32[]{:S(2)}) collective-permute-start(bf16[2,2,64,512]{3,2,1,0:T(8,128)(2,1)S(1)} %pad_maximum_fusion.3), channel_id=1, source_target_pairs={{0,2},{1,3},{2,0},{3,1},{4,6},{5,7},{6,4},{7,5},{8,10},{9,11},{10,... | collective-permute-start | bytes 786440 | tf_op jit(solution)/shard_map/ppermute | solution.py:50
  27.2 13.0 %collective-permute-start.2 = (bf16[4,2,64,512]{3,2,1,0:T(8,128)(2,1)S(1)}, bf16[4,2,64,512]{3,2,1,0:T(8,128)(2,1)S(1)}, u32[]{:S(2)}, u32[]{:S(2)}) collective-permute-start(bf16[4,2,64,512]{3,2,1,0:T(8,128)(2,1)S(1)} %pad_maximum_fusion.1), channel_id=1, source_target_pairs={{0,1},{1,0},{2,3},{3,2},{4,5},{5,4},{6,7},{7,6},{8,9},{9,8},{10,11... | collective-permute-start | bytes 1572872 | tf_op jit(solution)/shard_map/ppermute | solution.py:50
  87.0 7.8 %collective-permute-start.4 = (f32[2,128,128]{2,1,0:T(8,128)S(1)}, f32[2,128,128]{2,1,0:T(8,128)S(1)}, u32[]{:S(2)}, u32[]{:S(2)}) collective-permute-start(f32[2,128,128]{2,1,0:T(8,128)S(1)} %get-tuple-element.12), channel_id=1, source_target_pairs={{0,2},{1,3},{2,0},{3,1},{4,6},{5,7},{6,4},{7,5},{8,10},{9,11},{10,... | collective-permute-start | bytes 393224 | tf_op jit(solution)/shard_map/ppermute | solution.py:94
  88.6 12.9 %collective-permute-start.5 = (f32[2,128,128]{2,1,0:T(8,128)S(1)}, f32[2,128,128]{2,1,0:T(8,128)S(1)}, u32[]{:S(2)}, u32[]{:S(2)}) collective-permute-start(f32[2,128,128]{2,1,0:T(8,128)S(1)} %get-tuple-element.14), channel_id=1, source_target_pairs={{0,4},{1,5},{2,6},{3,7},{4,0},{5,1},{6,2},{7,3},{8,12},{9,13},{10,... | collective-permute-start | bytes 393224 | tf_op jit(solution)/shard_map/ppermute | solution.py:94
  90.9 10.5 %collective-permute-start.6 = (f32[2,128,128]{2,1,0:T(8,128)S(1)}, f32[2,128,128]{2,1,0:T(8,128)S(1)}, u32[]{:S(2)}, u32[]{:S(2)}) collective-permute-start(f32[2,128,128]{2,1,0:T(8,128)S(1)} %get-tuple-element.13), channel_id=1, source_target_pairs={{0,6},{1,7},{2,4},{3,5},{4,2},{5,3},{6,0},{7,1},{8,14},{9,15},{10,... | collective-permute-start | bytes 393224 | tf_op jit(solution)/shard_map/ppermute | solution.py:94
  102.4 4.7 %collective-permute-start.7 = (f32[2,64,128]{2,1,0:T(8,128)S(1)}, f32[2,64,128]{2,1,0:T(8,128)S(1)}, u32[]{:S(2)}, u32[]{:S(2)}) collective-permute-start(f32[2,64,128]{2,1,0:T(8,128)S(1)} %get-tuple-element.18), channel_id=1, source_target_pairs={{0,1},{1,0},{2,3},{3,2},{4,5},{5,4},{6,7},{7,6},{8,9},{9,8},{10,11... | collective-permute-start | bytes 196616 | tf_op jit(solution)/shard_map/ppermute | solution.py:101
  107.1 4.3 %collective-permute-start.8 = (f32[2,64,128]{2,1,0:T(8,128)S(1)}, f32[2,64,128]{2,1,0:T(8,128)S(1)}, u32[]{:S(2)}, u32[]{:S(2)}) collective-permute-start(f32[2,64,128]{2,1,0:T(8,128)S(1)} %get-tuple-element.20), channel_id=1, source_target_pairs={{0,1},{1,0},{2,3},{3,2},{4,5},{5,4},{6,7},{7,6},{8,9},{9,8},{10,11... | collective-permute-start | bytes 196616 | tf_op jit(solution)/shard_map/ppermute | solution.py:103
  111.5 6.7 %collective-permute-start.9 = (f32[2,128,128]{2,1,0:T(8,128)S(1)}, f32[2,128,128]{2,1,0:T(8,128)S(1)}, u32[]{:S(2)}, u32[]{:S(2)}) collective-permute-start(f32[2,128,128]{2,1,0:T(8,128)S(1)} %maximum_select_fusion.1), channel_id=1, source_target_pairs={{0,2},{1,3},{2,0},{3,1},{4,6},{5,7},{6,4},{7,5},{8,10},{9,11},{10,... | collective-permute-start | bytes 393224 | tf_op jit(solution)/shard_map/ppermute | solution.py:105
  113.6 9.9 %collective-permute-start.10 = (f32[2,128,128]{2,1,0:T(8,128)S(1)}, f32[2,128,128]{2,1,0:T(8,128)S(1)}, u32[]{:S(2)}, u32[]{:S(2)}) collective-permute-start(f32[2,128,128]{2,1,0:T(8,128)S(1)} %maximum_select_fusion.1), channel_id=1, source_target_pairs={{0,4},{1,5},{2,6},{3,7},{4,0},{5,1},{6,2},{7,3},{8,12},{9,13},{10,... | collective-permute-start | bytes 393224 | tf_op jit(solution)/shard_map/ppermute | solution.py:105
  114.5 9.0 %collective-permute-start.11 = (f32[2,128,128]{2,1,0:T(8,128)S(1)}, f32[2,128,128]{2,1,0:T(8,128)S(1)}, u32[]{:S(2)}, u32[]{:S(2)}) collective-permute-start(f32[2,128,128]{2,1,0:T(8,128)S(1)} %maximum_select_fusion.1), channel_id=1, source_target_pairs={{0,6},{1,7},{2,4},{3,5},{4,2},{5,3},{6,0},{7,1},{8,14},{9,15},{10,... | collective-permute-start | bytes 393224 | tf_op jit(solution)/shard_map/ppermute | solution.py:105
Sparse Core Ops, SparseCore 0:
  9.6 60.9 all-gather.2

commit v19 on v15

--- a/solution.py
+++ b/solution.py
@@ -64,23 +64,23 @@
     return slot
 
 
-def reduce_orient(best_part, power_part, axis):
+def reduce_orient(best_part, power_part, axis, scale):
     n = lax.axis_size(axis)
     if not is_pow2(n):
         best = lax.pmax(best_part, axis)
         power = lax.psum(power_part, axis)
-        return best, power
+        return best, power / scale
     width = best_part.shape[-1]
     joined = jnp.stack([best_part.reshape(-1, width), power_part.reshape(-1, width)], axis=0)
-    return reduce_joined(joined, best_part.shape, axis)
-
-
-def reduce_joined(joined, shape, axis):
+    return reduce_joined(joined, best_part.shape, axis, scale)
+
+
+def reduce_joined(joined, shape, axis, scale):
     n = lax.axis_size(axis)
     rows = joined.shape[1]
     if not is_pow2(n) or n < 2 or rows % n != 0:
         best = lax.pmax(joined[0], axis)
-        power = lax.psum(joined[1], axis)
+        power = lax.psum(joined[1], axis) / scale
         return best.reshape(shape), power.reshape(shape)
     me = lax.axis_index(axis)
     half = rows // 2
@@ -99,7 +99,7 @@
         got = lax.ppermute(out, axis, xor_pairs(n, 2 * m))
         best = jnp.maximum(best, got[0])
         power = power + got[1]
-    done = jnp.stack([best, power])
+    done = jnp.stack([best, power / scale])
     slots = [done] + [lax.ppermute(done, axis, xor_pairs(n, 2 * m)) for m in range(1, members)]
     pieces = jnp.stack(slots)[jnp.arange(members, dtype=jnp.int32) ^ group]
     mine = jnp.moveaxis(pieces, 0, 1).reshape(2, half, joined.shape[2])
@@ -312,10 +312,10 @@
         far = far_chips(chip, tiles // 2)
         far_offs = jnp.array([0, rows_t], jnp.int32)
         joined = match_rows(flags, far * 2, far * 2 + 1, far, far_offs, tmpl, tmpl, spec, col_table, cos_t, sin_t, init=partial)
-        best_all, power_all = reduce_joined(joined.reshape(2, -1, width), best_shape, "orient")
-        return (best_all[None], (power_all / LIST)[None])
-    best_all, power_all = reduce_orient(best_part, power_part, "orient")
-    return (best_all[None], (power_all / LIST)[None])
+        best_all, power_all = reduce_joined(joined.reshape(2, -1, width), best_shape, "orient", LIST)
+        return (best_all[None], power_all[None])
+    best_all, power_all = reduce_orient(best_part, power_part, "orient", LIST)
+    return (best_all[None], power_all[None])
 
 
 def far_chips(chip, chips):

time: 130 us -> 130 us (level)
  Pallas kernels: 30.2 us -> 28.1 us
    pallas_call x2, Pallas kernels: 30.2 us -> 28.1 us  [match_rows(): pl.pallas_call(kernel, grid_spec=pltpu.PrefetchScalarGridSpec(num_scalar_...]
  transfers between devices with their start and end apart: 13 -> 13, of which waited for: 11 -> 12; matrix products, arithmetic and copies ran while one was open for 15% -> 15% of each run, Pallas kernels for 11% -> 11%
where the time goes in v19:
time: 130 us; the launch traced here: 129 us
  waiting for transfers between devices  44.6 us (34%)
  Pallas kernels  28.1 us (22%)
  starting transfers between devices  19.5 us (15%)
  other arithmetic  18.4 us (14%)
  between operations  14.2 us (11%)
  local copies, waits for them, and re-layouts  4.7 us (4%)
    pallas_call x2, Pallas kernels, match_rows(): pl.pallas_call(kernel, grid_spec=pltpu.PrefetchScalarGridSpec(num_scalar_...  28.1 us
    all_gather x1, waiting for transfers between devices, local(): tmpl = lax.all_gather(template_spectra, 'tile', axis=0)  14.8 us
    convert_element_type x2, other arithmetic, angle_tables(): jnp.sin(angle).astype(jnp.bfloat16)  10 us
    ppermute x3, waiting for transfers between devices, gather_rows(): got = lax.ppermute(blocks, axis, xor_pairs(n, k))  7.98 us
    ppermute x1, waiting for transfers between devices, reduce_joined(): got = lax.ppermute(send, axis, xor_pairs(n, 1))  6.96 us
    ppermute x3, starting transfers between devices, gather_rows(): got = lax.ppermute(blocks, axis, xor_pairs(n, k))  5.92 us
    ppermute x3, waiting for transfers between devices, reduce_joined(): got = lax.ppermute(out, axis, xor_pairs(n, 2 * m))  5.6 us
    ppermute x1, waiting for transfers between devices, reduce_joined(): other = lax.ppermute(mine, axis, xor_pairs(n, 1))  4.85 us
  transfers between devices with their start and end apart: 13, of which 12 were waited for; matrix products, arithmetic and copies ran while one was open for 15% of the time, Pallas kernels for 11%

profile of v19, /device:TPU:0, one launch (start us, length us, event | category | flops | bytes accessed | tf_op | source)
XLA Modules:
  0.0 129.5 jit_solution(7446093100142254097)
XLA Ops:
  7.2 0.7 all-gather.3.cloned.1.call-update
  8.4 3.7 %collective-permute-start = (bf16[1,2,64,512]{3,2,1,0:T(8,128)(2,1)S(1)}, bf16[1,2,64,512]{3,2,1,0:T(8,128)(2,1)S(1)}, u32[]{:S(2)}, u32[]{:S(2)}) collective-permute-start(bf16[1,2,64,512]{3,2,1,0:T(8,128)(2,1)S(1)} %copy-done), channel_id=1, source_target_pairs={{0,4},{1,5},{2,6},{3,7},{4,0},{5,1},{6,2},{7,3},{8,12},{9,13},{10,... | collective-permute-start | bytes 393224 | tf_op jit(solution)/shard_map/ppermute | solution.py:50
  12.3 4.0 %fusion.12 = bf16[4,512,128]{2,1,0:T(8,128)(2,1)S(1)} fusion(s32[4,128]{1,0:T(4,128)S(1)} %get-tuple-element.21), kind=kLoop, calls=%fused_computation.38 | loop fusion | flops 4718592 | bytes 526336 | tf_op jit(solution)/shard_map/neg | solution.py:38
  16.5 2.5 %collective-permute-done = bf16[1,2,64,512]{3,2,1,0:T(8,128)(2,1)S(1)} collective-permute-done((bf16[1,2,64,512]{3,2,1,0:T(8,128)(2,1)S(1)}, bf16[1,2,64,512]{3,2,1,0:T(8,128)(2,1)S(1)}, u32[]{:S(2)}, u32[]{:S(2)}) %collective-permute-start) | collective-permute-done | bytes 131104 | tf_op jit(solution)/shard_map/ppermute | solution.py:50
  19.0 0.8 collective-permute-start.1
  20.4 0.6 reshape.165.f_ref
  21.0 4.4 %sine_convert_fusion.1 = (bf16[4,512,128]{2,1,0:T(8,128)(2,1)S(1)}, bf16[4,512,128]{2,1,0:T(8,128)(2,1)S(1)}) fusion(s32[4,128]{1,0:T(4,128)S(1)} %get-tuple-element.21), kind=kLoop, calls=%fused_computation.20 | loop fusion | flops 4194304 | bytes 1050624 | tf_op jit(solution)/shard_map/convert_element_type | solution.py:31
  25.4 1.8 %collective-permute-done.1 = bf16[2,2,64,512]{3,2,1,0:T(8,128)(2,1)S(1)} collective-permute-done((bf16[2,2,64,512]{3,2,1,0:T(8,128)(2,1)S(1)}, bf16[2,2,64,512]{3,2,1,0:T(8,128)(2,1)S(1)}, u32[]{:S(2)}, u32[]{:S(2)}) %collective-permute-start.1) | collective-permute-done | bytes 262176 | tf_op jit(solution)/shard_map/ppermute | solution.py:50
  27.2 1.4 %collective-permute-start.2 = (bf16[4,2,64,512]{3,2,1,0:T(8,128)(2,1)S(1)}, bf16[4,2,64,512]{3,2,1,0:T(8,128)(2,1)S(1)}, u32[]{:S(2)}, u32[]{:S(2)}) collective-permute-start(bf16[4,2,64,512]{3,2,1,0:T(8,128)(2,1)S(1)} %pad_maximum_fusion.1), channel_id=1, source_target_pairs={{0,1},{1,0},{2,3},{3,2},{4,5},{5,4},{6,7},{7,6},{8,9},{9,8},{10,11... | collective-permute-start | bytes 1572872 | tf_op jit(solution)/shard_map/ppermute | solution.py:50
  29.2 1.6 %maximum_maximum_fusion.ct_ref = bf16[4,1024,256]{2,1,0:T(8,128)(2,1)} fusion(bf16[4,512,128]{2,1,0:T(8,128)(2,1)S(1)} %get-tuple-element.17, bf16[4,512,128]{2,1,0:T(8,128)(2,1)S(1)} %fusion.12, bf16[4,512,128]{2,1,0:T(8,128)(2,1)S(1)} %get-tuple-element.16), kind=kLoop, calls=%fused_computation.2 | loop fusion | flops 8388608 | bytes 3670016 | tf_op jit(solution)/shard_map/concatenate | solution.py:39
  30.8 5.6 %sine_convert_fusion = (bf16[4,128,512]{2,1,0:T(8,128)(2,1)}, bf16[4,128,512]{2,1,0:T(8,128)(2,1)}) fusion(s32[4,128]{1,0:T(4,128)S(1)} %get-tuple-element.20), kind=kLoop, calls=%fused_computation.16 | loop fusion | flops 4194304 | bytes 1050624 | tf_op jit(solution)/shard_map/convert_element_type | solution.py:31
  36.5 3.7 %collective-permute-done.2 = bf16[4,2,64,512]{3,2,1,0:T(8,128)(2,1)S(1)} collective-permute-done((bf16[4,2,64,512]{3,2,1,0:T(8,128)(2,1)S(1)}, bf16[4,2,64,512]{3,2,1,0:T(8,128)(2,1)S(1)}, u32[]{:S(2)}, u32[]{:S(2)}) %collective-permute-start.2) | collective-permute-done | bytes 524320 | tf_op jit(solution)/shard_map/ppermute | solution.py:50
  40.3 0.6 gather_fusion
  40.9 1.1 copy.13
  42.0 13.8 %shard_map.68.rest_0_ = f32[4,8,128,128]{3,2,1,0:T(8,128)} custom-call(s32[32]{0:T(128)} %reshape.165.f_ref, s32[1]{0:T(128)} %constant.104.clone.1.ta_ref.tb_ref, s32[1]{0:T(128)} %constant.104.clone.1.ta_ref.tb_ref, s32[1]{0:T(128)} %bitcast.1.rid_ref, s32[2]{0:T(128)} %add_multiply_fusion.off_ref, bf16[1,8,2,128,512]{4,3,2,1,0:T(8,128)(2,1)} %bitcast.11.tma_ref, ...), custom_call_target="tpu_custom_call" | custom-call | flops 4831838208 | bytes 10485760 | tf_op jit(solution)/shard_map/pallas_call | solution.py:267
  55.8 14.8 %all-gather.3.cloned.1.call-done = bf16[32,2,128,512]{3,2,1,0:T(8,128)(2,1)} async-done(((bf16[8,2,128,512]{3,2,1,0:T(8,128)(2,1)}), bf16[32,2,128,512]{3,2,1,0:T(8,128)(2,1)}) %all-gather.3.cloned.1.call-update) | async-done | bytes 8388624 | tf_op jit(solution)/shard_map/all_gather | solution.py:287
  70.6 14.3 %shard_map.69 = f32[2,4,128,128]{3,2,1,0:T(8,128)} custom-call(s32[32]{0:T(128)} %reshape.165.f_ref, s32[1]{0:T(128)S(6)} %mul.65.ta_ref, s32[1]{0:T(128)S(6)} %add.152.tb_ref, s32[1]{0:T(128)S(6)} %convert_element_type.34.rid_ref, s32[2]{0:T(128)} %iota_multiply_fusion.off_ref, bf16[4,8,2,128,512]{4,3,2,1,0:T(8,128)(2,1)} %bitcast.28, ...), custom_call_target="tpu_custom_call" | custom-call | flops 4831838208 | bytes 10485760 | tf_op jit(solution)/shard_map/pallas_call | solution.py:267
  84.9 1.0 constant_dynamic-slice_fusion
  85.9 2.6 %collective-permute-start.4 = (f32[2,256,128]{2,1,0:T(8,128)S(1)}, f32[2,256,128]{2,1,0:T(8,128)S(1)}, u32[]{:S(2)}, u32[]{:S(2)}) collective-permute-start(f32[2,256,128]{2,1,0:T(8,128)S(1)} %constant_dynamic-slice_fusion), channel_id=1, source_target_pairs={{0,1},{1,0},{2,3},{3,2},{4,5},{5,4},{6,7},{7,6},{8,9},{9,8},{10,11... | collective-permute-start | bytes 786440 | tf_op jit(solution)/shard_map/ppermute | solution.py:90
  88.5 7.0 %collective-permute-done.4 = f32[2,256,128]{2,1,0:T(8,128)S(1)} collective-permute-done((f32[2,256,128]{2,1,0:T(8,128)S(1)}, f32[2,256,128]{2,1,0:T(8,128)S(1)}, u32[]{:S(2)}, u32[]{:S(2)}) %collective-permute-start.4) | collective-permute-done | bytes 262176 | tf_op jit(solution)/shard_map/ppermute | solution.py:90
  95.4 1.0 slice_add_fusion
  96.5 1.6 %collective-permute-start.5 = (f32[2,64,128]{2,1,0:T(8,128)S(1)}, f32[2,64,128]{2,1,0:T(8,128)S(1)}, u32[]{:S(2)}, u32[]{:S(2)}) collective-permute-start(f32[2,64,128]{2,1,0:T(8,128)S(1)} %get-tuple-element.9), channel_id=1, source_target_pairs={{0,2},{1,3},{2,0},{3,1},{4,6},{5,7},{6,4},{7,5},{8,10},{9,11},{10,... | collective-permute-start | bytes 196616 | tf_op jit(solution)/shard_map/ppermute | solution.py:99
  98.0 2.4 %collective-permute-start.6 = (f32[2,64,128]{2,1,0:T(8,128)S(1)}, f32[2,64,128]{2,1,0:T(8,128)S(1)}, u32[]{:S(2)}, u32[]{:S(2)}) collective-permute-start(f32[2,64,128]{2,1,0:T(8,128)S(1)} %get-tuple-element.10), channel_id=1, source_target_pairs={{0,4},{1,5},{2,6},{3,7},{4,0},{5,1},{6,2},{7,3},{8,12},{9,13},{10,... | collective-permute-start | bytes 196616 | tf_op jit(solution)/shard_map/ppermute | solution.py:99
  101.4 3.5 %collective-permute-done.6 = f32[2,64,128]{2,1,0:T(8,128)S(1)} collective-permute-done((f32[2,64,128]{2,1,0:T(8,128)S(1)}, f32[2,64,128]{2,1,0:T(8,128)S(1)}, u32[]{:S(2)}, u32[]{:S(2)}) %collective-permute-start.6) | collective-permute-done | bytes 65568 | tf_op jit(solution)/shard_map/ppermute | solution.py:99
  104.9 1.6 %collective-permute-done.7 = f32[2,64,128]{2,1,0:T(8,128)S(1)} collective-permute-done((f32[2,64,128]{2,1,0:T(8,128)S(1)}, f32[2,64,128]{2,1,0:T(8,128)S(1)}, u32[]{:S(2)}, u32[]{:S(2)}) %collective-permute-start.7) | collective-permute-done | bytes 65568 | tf_op jit(solution)/shard_map/ppermute | solution.py:99
  106.6 2.0 %collective-permute-start.9 = (f32[2,64,128]{2,1,0:T(8,128)S(1)}, f32[2,64,128]{2,1,0:T(8,128)S(1)}, u32[]{:S(2)}, u32[]{:S(2)}) collective-permute-start(f32[2,64,128]{2,1,0:T(8,128)S(1)} %get-tuple-element.13), channel_id=1, source_target_pairs={{0,4},{1,5},{2,6},{3,7},{4,0},{5,1},{6,2},{7,3},{8,12},{9,13},{10,... | collective-permute-start | bytes 196616 | tf_op jit(solution)/shard_map/ppermute | solution.py:103
  108.7 2.4 %collective-permute-start.10 = (f32[2,64,128]{2,1,0:T(8,128)S(1)}, f32[2,64,128]{2,1,0:T(8,128)S(1)}, u32[]{:S(2)}, u32[]{:S(2)}) collective-permute-start(f32[2,64,128]{2,1,0:T(8,128)S(1)} %get-tuple-element.13), channel_id=1, source_target_pairs={{0,6},{1,7},{2,4},{3,5},{4,2},{5,3},{6,0},{7,1},{8,14},{9,15},{10,... | collective-permute-start | bytes 196616 | tf_op jit(solution)/shard_map/ppermute | solution.py:103
  111.2 1.1 collective-permute-done.9
  112.3 2.4 %collective-permute-done.10 = f32[2,64,128]{2,1,0:T(8,128)S(1)} collective-permute-done((f32[2,64,128]{2,1,0:T(8,128)S(1)}, f32[2,64,128]{2,1,0:T(8,128)S(1)}, u32[]{:S(2)}, u32[]{:S(2)}) %collective-permute-start.10) | collective-permute-done | bytes 65568 | tf_op jit(solution)/shard_map/ppermute | solution.py:103
  115.3 1.6 %collective-permute-start.11 = (f32[2,256,128]{2,1,0:T(8,128)S(1)}, f32[2,256,128]{2,1,0:T(8,128)S(1)}, u32[]{:S(2)}, u32[]{:S(2)}) collective-permute-start(f32[2,256,128]{2,1,0:T(8,128)S(1)} %bitcast.36), channel_id=1, source_target_pairs={{0,1},{1,0},{2,3},{3,2},{4,5},{5,4},{6,7},{7,6},{8,9},{9,8},{10,11... | collective-permute-start | bytes 786440 | tf_op jit(solution)/shard_map/ppermute | solution.py:106
  116.9 4.8 %collective-permute-done.11 = f32[2,256,128]{2,1,0:T(8,128)S(1)} collective-permute-done((f32[2,256,128]{2,1,0:T(8,128)S(1)}, f32[2,256,128]{2,1,0:T(8,128)S(1)}, u32[]{:S(2)}, u32[]{:S(2)}) %collective-permute-start.11) | collective-permute-done | bytes 262176 | tf_op jit(solution)/shard_map/ppermute | solution.py:106
  121.8 0.8 fusion.25
  (35 shorter events, 4.0 us)
Async XLA Ops:
  7.2 1.3 copy-start
  7.2 5.0 %copy-start.2 = (s32[1,4,2]{1,2,0:T(2,128)S(1)}, s32[1,4,2]{1,2,0:T(2,128)}, u32[]{:S(2)}) copy-start(s32[1,4,2]{1,2,0:T(2,128)} %param.7) | copy-start | bytes 100
  7.2 9.1 %copy-start.1 = (s32[1,4,48]{2,1,0:T(4,128)S(1)}, s32[1,4,48]{2,1,0:T(4,128)}, u32[]{:S(2)}) copy-start(s32[1,4,48]{2,1,0:T(4,128)} %param.8) | copy-start | bytes 2308
  7.2 63.4 %all-gather.3.cloned.1.call-start = ((), (), s32[]{:S(2)}) async-start(), calls=%async_computation | async-start | bytes 10485760 | tf_op jit(solution)/shard_map/all_gather | solution.py:287
  7.9 34.1 %collective-permute-start.3 = (bf16[8,2,128,512]{3,2,1,0:T(8,128)(2,1)}, bf16[8,2,128,512]{3,2,1,0:T(8,128)(2,1)}, u32[]{:S(2)}, u32[]{:S(2)}) collective-permute-start(bf16[8,2,128,512]{3,2,1,0:T(8,128)(2,1)} %param.6), channel_id=1, source_target_pairs={{0,8},{8,0},{16,24},{24,16},{1,9},{9,1},{17,25},{25,17},{2,10},{10... | collective-permute-start | bytes 6291464 | tf_op jit(solution)/shard_map/ppermute | solution.py:305
  8.4 10.6 %collective-permute-start = (bf16[1,2,64,512]{3,2,1,0:T(8,128)(2,1)S(1)}, bf16[1,2,64,512]{3,2,1,0:T(8,128)(2,1)S(1)}, u32[]{:S(2)}, u32[]{:S(2)}) collective-permute-start(bf16[1,2,64,512]{3,2,1,0:T(8,128)(2,1)S(1)} %copy-done), channel_id=1, source_target_pairs={{0,4},{1,5},{2,6},{3,7},{4,0},{5,1},{6,2},{7,3},{8,12},{9,13},{10,... | collective-permute-start | bytes 393224 | tf_op jit(solution)/shard_map/ppermute | solution.py:50
  19.0 8.1 %collective-permute-start.1 = (bf16[2,2,64,512]{3,2,1,0:T(8,128)(2,1)S(1)}, bf16[2,2,64,512]{3,2,1,0:T(8,128)(2,1)S(1)}, u32[]{:S(2)}, u32[]{:S(2)}) collective-permute-start(bf16[2,2,64,512]{3,2,1,0:T(8,128)(2,1)S(1)} %pad_maximum_fusion.2), channel_id=1, source_target_pairs={{0,2},{1,3},{2,0},{3,1},{4,6},{5,7},{6,4},{7,5},{8,10},{9,11},{10,... | collective-permute-start | bytes 786440 | tf_op jit(solution)/shard_map/ppermute | solution.py:50
  27.2 13.0 %collective-permute-start.2 = (bf16[4,2,64,512]{3,2,1,0:T(8,128)(2,1)S(1)}, bf16[4,2,64,512]{3,2,1,0:T(8,128)(2,1)S(1)}, u32[]{:S(2)}, u32[]{:S(2)}) collective-permute-start(bf16[4,2,64,512]{3,2,1,0:T(8,128)(2,1)S(1)} %pad_maximum_fusion.1), channel_id=1, source_target_pairs={{0,1},{1,0},{2,3},{3,2},{4,5},{5,4},{6,7},{7,6},{8,9},{9,8},{10,11... | collective-permute-start | bytes 1572872 | tf_op jit(solution)/shard_map/ppermute | solution.py:50
  85.9 9.5 %collective-permute-start.4 = (f32[2,256,128]{2,1,0:T(8,128)S(1)}, f32[2,256,128]{2,1,0:T(8,128)S(1)}, u32[]{:S(2)}, u32[]{:S(2)}) collective-permute-start(f32[2,256,128]{2,1,0:T(8,128)S(1)} %constant_dynamic-slice_fusion), channel_id=1, source_target_pairs={{0,1},{1,0},{2,3},{3,2},{4,5},{5,4},{6,7},{7,6},{8,9},{9,8},{10,11... | collective-permute-start | bytes 786440 | tf_op jit(solution)/shard_map/ppermute | solution.py:90
  96.5 4.9 %collective-permute-start.5 = (f32[2,64,128]{2,1,0:T(8,128)S(1)}, f32[2,64,128]{2,1,0:T(8,128)S(1)}, u32[]{:S(2)}, u32[]{:S(2)}) collective-permute-start(f32[2,64,128]{2,1,0:T(8,128)S(1)} %get-tuple-element.9), channel_id=1, source_target_pairs={{0,2},{1,3},{2,0},{3,1},{4,6},{5,7},{6,4},{7,5},{8,10},{9,11},{10,... | collective-permute-start | bytes 196616 | tf_op jit(solution)/shard_map/ppermute | solution.py:99
  98.0 6.9 %collective-permute-start.6 = (f32[2,64,128]{2,1,0:T(8,128)S(1)}, f32[2,64,128]{2,1,0:T(8,128)S(1)}, u32[]{:S(2)}, u32[]{:S(2)}) collective-permute-start(f32[2,64,128]{2,1,0:T(8,128)S(1)} %get-tuple-element.10), channel_id=1, source_target_pairs={{0,4},{1,5},{2,6},{3,7},{4,0},{5,1},{6,2},{7,3},{8,12},{9,13},{10,... | collective-permute-start | bytes 196616 | tf_op jit(solution)/shard_map/ppermute | solution.py:99
  100.5 6.1 %collective-permute-start.7 = (f32[2,64,128]{2,1,0:T(8,128)S(1)}, f32[2,64,128]{2,1,0:T(8,128)S(1)}, u32[]{:S(2)}, u32[]{:S(2)}) collective-permute-start(f32[2,64,128]{2,1,0:T(8,128)S(1)} %get-tuple-element.11), channel_id=1, source_target_pairs={{0,6},{1,7},{2,4},{3,5},{4,2},{5,3},{6,0},{7,1},{8,14},{9,15},{10,... | collective-permute-start | bytes 196616 | tf_op jit(solution)/shard_map/ppermute | solution.py:99
  106.6 4.6 %collective-permute-start.8 = (f32[2,64,128]{2,1,0:T(8,128)S(1)}, f32[2,64,128]{2,1,0:T(8,128)S(1)}, u32[]{:S(2)}, u32[]{:S(2)}) collective-permute-start(f32[2,64,128]{2,1,0:T(8,128)S(1)} %get-tuple-element.13), channel_id=1, source_target_pairs={{0,2},{1,3},{2,0},{3,1},{4,6},{5,7},{6,4},{7,5},{8,10},{9,11},{10,... | collective-permute-start | bytes 196616 | tf_op jit(solution)/shard_map/ppermute | solution.py:103
  106.6 5.7 %collective-permute-start.9 = (f32[2,64,128]{2,1,0:T(8,128)S(1)}, f32[2,64,128]{2,1,0:T(8,128)S(1)}, u32[]{:S(2)}, u32[]{:S(2)}) collective-permute-start(f32[2,64,128]{2,1,0:T(8,128)S(1)} %get-tuple-element.13), channel_id=1, source_target_pairs={{0,4},{1,5},{2,6},{3,7},{4,0},{5,1},{6,2},{7,3},{8,12},{9,13},{10,... | collective-permute-start | bytes 196616 | tf_op jit(solution)/shard_map/ppermute | solution.py:103
  108.7 6.1 %collective-permute-start.10 = (f32[2,64,128]{2,1,0:T(8,128)S(1)}, f32[2,64,128]{2,1,0:T(8,128)S(1)}, u32[]{:S(2)}, u32[]{:S(2)}) collective-permute-start(f32[2,64,128]{2,1,0:T(8,128)S(1)} %get-tuple-element.13), channel_id=1, source_target_pairs={{0,6},{1,7},{2,4},{3,5},{4,2},{5,3},{6,0},{7,1},{8,14},{9,15},{10,... | collective-permute-start | bytes 196616 | tf_op jit(solution)/shard_map/ppermute | solution.py:103
  115.3 6.4 %collective-permute-start.11 = (f32[2,256,128]{2,1,0:T(8,128)S(1)}, f32[2,256,128]{2,1,0:T(8,128)S(1)}, u32[]{:S(2)}, u32[]{:S(2)}) collective-permute-start(f32[2,256,128]{2,1,0:T(8,128)S(1)} %bitcast.36), channel_id=1, source_target_pairs={{0,1},{1,0},{2,3},{3,2},{4,5},{5,4},{6,7},{7,6},{8,9},{9,8},{10,11... | collective-permute-start | bytes 786440 | tf_op jit(solution)/shard_map/ppermute | solution.py:106
Sparse Core Ops, SparseCore 0:
  9.6 60.9 all-gather.2
